TPU v7x, 128 devices: a whole 4x4x4 slice. The times are simulated.
128 devices in a mesh: comp: 4 (over z), band: 32 (over y, x, core).
Axes of the slice: x: 4, y: 4, z: 4, core: 2. Of those that a mesh axis runs over, the one named last changes fastest.
Arguments:
- layer_temp: float32 [4, 2048, 16, 256], P('comp', 'band'), may hold values from -6 to 6
- diffusivity: float32 [4, 2048, 256], P('comp', 'band'), may hold values from 0.02 to 0.11
- owner_band: int32 [4, 2048, 1], P('comp', 'band'), may hold values from 0 to 31, as said below
- block_index: int32 [4, 2048], P('comp', 'band'), may hold values from 0 to 63
- remap_blocks: bfloat16 [4, 2048, 256, 256], P('comp', 'band'), may hold values from -0.375 to 0.375
Outputs:
- temp_out: float32 [4, 2048, 16, 256], P('comp', 'band')
- surface_temp: bfloat16 [4, 2048, 4, 256], P('comp', 'band')
Inputs may be any that keep to these rules, and one draw needn't show every extreme that they name: `owner_band`: among the rows of one device no band is named by more than 4 rows, and some band is named by exactly 4.
All inputs are finite; a program needn't handle non-finite values.
Results may differ from a plain program's by a relative error of at most 0.0055.
Values may be sent and summed in bfloat16 or wider, within the bound.
No kernel may reach another device: no remote copies, remote signals or barrier semaphores. Data moves between devices by JAX's collectives and lax.ppermute only.
A program may use at most 64 MiB of HBM per device.

v0:
```python
import jax
import jax.numpy as jnp
from jax import lax
from jax.sharding import PartitionSpec as P

NF = 4
NSTEPS = 4


COUPLING = 0.25
VERTICAL = 0.15
HIGHEST = lax.Precision.HIGHEST


def padded_2(block, sides, width):
    for axis, dim in sides:
        count = lax.axis_size(axis)
        forward = [(i, i + 1) for i in range(count - 1)]
        backward = [(target, source) for source, target in forward]
        low = lax.ppermute(
            lax.slice_in_dim(block, block.shape[dim] - width, None, axis=dim), axis, forward
        )
        high = lax.ppermute(lax.slice_in_dim(block, 0, width, axis=dim), axis, backward)
        block = jnp.concatenate([low, block, high], axis=dim)
    return block


def advance(padded, diffusivity):
    fields = padded[:, 1:-1]
    row_north = padded[:, :-2]
    row_south = padded[:, 2:]
    col_east = jnp.roll(fields, 1, axis=3)
    col_west = jnp.roll(fields, -1, axis=3)
    level_below = jnp.concatenate([fields[:, :, :1], fields[:, :, :-1]], axis=2)
    level_above = jnp.concatenate([fields[:, :, 1:], fields[:, :, -1:]], axis=2)
    horizontal = row_north + row_south + col_east + col_west - 4.0 * fields
    return (
        fields
        + diffusivity[:, :, None, :] * horizontal
        + VERTICAL * (level_below + level_above - 2.0 * fields)
    )


def accumulate(values, row_target, row_count):
    flat_target = row_target.reshape(-1)
    matches = (flat_target[:, None] == jnp.arange(row_count, dtype=jnp.int32)[None, :]).astype(
        jnp.float32
    )
    flat_values = values.reshape(flat_target.shape[0], values.shape[2], values.shape[3])
    return jnp.einsum("kr,kfc->rfc", matches, flat_values, precision=HIGHEST)


def select_rows(source_table, row_target):
    flat_target = row_target.reshape(-1)
    row_count = source_table.shape[0]
    matches = (flat_target[:, None] == jnp.arange(row_count, dtype=jnp.int32)[None, :]).astype(
        jnp.bfloat16
    )
    picked = jnp.einsum("kr,rfc->kfc", matches, source_table, preferred_element_type=jnp.float32)
    return picked.astype(jnp.bfloat16).reshape(row_target.shape + source_table.shape[1:])


def body(layer_temp, diffusivity, owner_band, block_index, remap_blocks):
    n_sections = lax.axis_size("comp")
    n_bands = lax.axis_size("band")
    section = lax.axis_index("comp")
    row_count = layer_temp.shape[1]
    columns = layer_temp.shape[3]
    surf_count = NF
    slot_cap = max(2, 2 * row_count // n_bands)
    is_ocean = section == n_sections - 1
    surface_layers = layer_temp[0, :, :surf_count, :].astype(jnp.bfloat16)
    weights_local = remap_blocks[0]
    surf_flux = lax.cond(
        is_ocean,
        lambda: jnp.zeros((row_count, surf_count, columns), jnp.float32),
        lambda: jnp.einsum(
            "rfc,rcd->rfd", surface_layers, weights_local, preferred_element_type=jnp.float32
        ),
    )
    destination = owner_band[0, :, 0]
    dest_onehot = (destination[:, None] == jnp.arange(n_bands, dtype=jnp.int32)[None, :]).astype(
        jnp.float32
    )
    positions = jnp.arange(row_count, dtype=jnp.int32)
    earlier_mask = (positions[:, None] > positions[None, :]).astype(jnp.float32)
    earlier = jnp.dot(earlier_mask, dest_onehot, precision=HIGHEST)
    slot_rank = jnp.sum(earlier * dest_onehot, axis=1).astype(jnp.int32)
    slot_onehot = (slot_rank[:, None] == jnp.arange(slot_cap, dtype=jnp.int32)[None, :]).astype(
        jnp.float32
    )
    selector = (dest_onehot[:, :, None] * slot_onehot[:, None, :]).reshape(
        row_count, n_bands * slot_cap
    )
    sending = jnp.einsum("rk,rfc->kfc", selector, surf_flux, precision=HIGHEST)
    sending = sending.reshape(n_bands, slot_cap, surf_count, columns)
    send_index = jnp.dot(block_index[0].astype(jnp.float32), selector, precision=HIGHEST)
    send_index = send_index.astype(jnp.int32).reshape(n_bands, slot_cap)
    fields = layer_temp
    for step_index in range(NSTEPS):
        padded = padded_2(fields, (("band", 1),), 1)
        fields = advance(padded, diffusivity)
    lead = (n_sections - 1) * n_bands
    outgoing = jnp.concatenate(
        [jnp.zeros((lead, slot_cap, surf_count, columns), jnp.float32), sending], axis=0
    )
    outgoing_index = jnp.concatenate([jnp.zeros((lead, slot_cap), jnp.int32), send_index], axis=0)
    received, got_index = (
        lax.all_to_all(outgoing, ("comp", "band"), split_axis=0, concat_axis=0, tiled=True),
        lax.all_to_all(outgoing_index, ("comp", "band"), split_axis=0, concat_axis=0, tiled=True),
    )
    ocean_heat = accumulate(received, got_index, row_count)
    heating = jnp.where(is_ocean, COUPLING * ocean_heat, 0.0)
    temp_out = fields.at[0, :, :surf_count].add(heating)
    sea_surface = temp_out[0, :, :surf_count].astype(jnp.bfloat16)
    returned = lax.cond(
        is_ocean,
        lambda: jnp.einsum(
            "rfc,rcd->rfd", sea_surface, weights_local, preferred_element_type=jnp.float32
        ).astype(jnp.bfloat16),
        lambda: jnp.zeros((row_count, surf_count, columns), jnp.bfloat16),
    )
    reply_rows = select_rows(returned, got_index)
    came_back = lax.all_to_all(
        reply_rows, ("comp", "band"), split_axis=0, concat_axis=0, tiled=True
    )
    arrived = came_back[(n_sections - 1) * n_bands :]
    arrived_flat = arrived.reshape(n_bands * slot_cap, surf_count, columns)
    seen = jnp.einsum(
        "rk,kfc->rfc",
        selector.astype(jnp.bfloat16),
        arrived_flat,
        preferred_element_type=jnp.float32,
    )
    seen = seen.astype(jnp.bfloat16)
    surface_temp = jnp.where(is_ocean, returned, seen)[None]
    return (temp_out, surface_temp)


def solution(mesh):
    return jax.shard_map(
        body,
        mesh=mesh,
        in_specs=(
            P("comp", "band", None, None),
            P("comp", "band", None),
            P("comp", "band", None),
            P("comp", "band"),
            P("comp", "band", None, None),
        ),
        out_specs=(P("comp", "band", None, None), P("comp", "band", None, None)),
        check_vma=False,
    )
```

profile of v0, /device:TPU:1, one launch (start us, length us, event | category | flops | bytes accessed | tf_op | source)
XLA Modules:
  0.0 131.6 jit_solution(18365904185499350231)
XLA Ops:
  0.6 0.8 fusion.94
  1.5 4.5 %collective-permute-start = (f32[1,1,16,256]{3,1,2,0:T(1,128)S(1)}, f32[1,1,16,256]{3,1,2,0:T(1,128)S(1)}, u32[]{:S(2)}, u32[]{:S(2)}) collective-permute-start(f32[1,1,16,256]{3,1,2,0:T(1,128)S(1)} %copy.55), channel_id=1, source_target_pairs={{0,1},{1,2},{2,3},{3,4},{4,5},{5,6},{6,7},{7,8},{8,9},{9,10},{10,1... | collective-permute-start | bytes 49160 | tf_op jit(solution)/shard_map/ppermute | solution.py:20
  6.0 1.9 %collective-permute-start.1 = (f32[1,1,16,256]{3,1,2,0:T(1,128)S(1)}, f32[1,1,16,256]{3,1,2,0:T(1,128)S(1)}, u32[]{:S(2)}, u32[]{:S(2)}) collective-permute-start(f32[1,1,16,256]{3,1,2,0:T(1,128)S(1)} %copy.57), channel_id=1, source_target_pairs={{1,0},{2,1},{3,2},{4,3},{5,4},{6,5},{7,6},{8,7},{9,8},{10,9},{11,1... | collective-permute-start | bytes 49160 | tf_op jit(solution)/shard_map/ppermute | solution.py:23
  7.9 0.7 fusion.70
  8.6 0.9 fusion.20
  9.5 0.6 multiply_convert_fusion
  10.1 0.8 fusion.21
  11.1 0.6 concatenate.174
  11.8 10.6 %all-to-all-start = ((s32[128,1,4]{2,1,0:T(1,128)}), s32[128,1,4]{2,1,0:T(1,128)S(1)}, u32[]{:S(2)}, u32[]{:S(2)}) async-start(s32[128,1,4]{2,1,0:T(1,128)} %bitcast.9), calls=%async_computation | async-start | bytes 131072 | tf_op jit(solution)/shard_map/all_to_all | solution.py:110
  22.4 1.8 %copy.64 = f32[1,64,16,256]{3,1,2,0:T(8,128)S(1)} copy(f32[1,64,16,256]{3,2,1,0:T(8,128)} %param.11) | data formatting | bytes 2097152 | tf_op args[0]
  24.2 1.7 %fusion.92 = (f32[1,64,16,255]{3,1,2,0:T(8,128)}, f32[1,64,16,255]{3,1,2,0:T(8,128)}) fusion(f32[1,64,16,256]{3,1,2,0:T(8,128)S(1)} %copy.64), kind=kLoop, calls=%fused_computation.108 | loop fusion | bytes 4177920 | tf_op jit(solution)/shard_map/jit(_roll_static)/slice | solution.py:33
  25.9 1.5 %fusion.90 = (f32[1,64,15,256]{3,1,2,0:T(8,128)}, f32[1,64,15,256]{3,1,2,0:T(8,128)}) fusion(f32[1,64,16,256]{3,1,2,0:T(8,128)S(1)} %copy.64), kind=kLoop, calls=%fused_computation.106 | loop fusion | bytes 3932160 | tf_op jit(solution)/shard_map/slice | solution.py:35
  27.5 1.1 fusion.93
  28.6 4.6 %conditional.2 = (f32[64,4,256]{2,1,0:T(4,128)S(1)}) conditional(s32[]{:T(128)} %convert_element_type.68, (f32[1,64,16,256]{3,2,1,0:T(8,128)S(1)}, bf16[64,256,256]{2,1,0:T(8,128)(2,1)}) %tuple.65, () %tuple.25), branch_computations={%region_1.0_spmd, %region_2.0_spmd} | conditional | flops 33554432 | bytes 8781832 | solution.py:74
  28.6 4.6 %fusion.1 = f32[64,4,256]{2,1,0:T(4,128)S(1)} fusion(bf16[64,256,256]{2,1,0:T(8,128)(2,1)} %get-tuple-element.32, f32[1,64,16,256]{3,2,1,0:T(8,128)S(1)} %get-tuple-element.31), kind=kOutput, calls=%fused_computation.2 | convolution fusion | flops 33554432 | bytes 8781824 | tf_op jit(solution)/shard_map/cond/branch_0_fun/rfc,rcd->rfd/dot_general | solution.py:77
  33.2 0.6 fusion.59
  33.8 0.3 copy.90
  34.2 1.8 %concatenate.175.clone = f32[128,4,4,256]{3,2,1,0:T(4,128)} pad(f32[32,4,4,256]{3,2,1,0:T(4,128)S(1)} %copy.90, f32[]{:T(128)} %constant.52.clone.1), padding=96_0x0_0x0_0x0_0 | pad | bytes 2621444 | tf_op jit(solution)/shard_map/concatenate | solution.py:104
  36.0 9.8 %all-to-all-start.1 = ((f32[128,4,4,256]{3,2,1,0:T(4,128)}), f32[128,4,4,256]{3,2,1,0:T(4,128)S(1)}, u32[]{:S(2)}, u32[]{:S(2)}) async-start(f32[128,4,4,256]{3,2,1,0:T(4,128)} %concatenate.175.clone), calls=%async_computation.1 | async-start | bytes 4194304 | tf_op jit(solution)/shard_map/all_to_all | solution.py:109
  45.8 0.5 broadcast.103
  46.3 0.8 reduce.5
  47.3 3.2 %fusion.49 = f32[1,64,16,256]{3,1,2,0:T(8,128)S(1)} fusion(f32[1,64,16,256]{3,1,2,0:T(8,128)S(1)} %copy.64, f32[1,1,16,256]{3,1,2,0:T(1,128)S(1)} %collective-permute-done.1, f32[1,1,16,256]{3,1,2,0:T(1,128)S(1)} %collective-permute-done, f32[1,64,16,255]{3,1,2,0:T(8,128)} %get-tuple-element.85, f32[1,64,16,1]{3,1,2,0:T(8,128)} %get-tuple-element.87, ...), kind=kLoop, calls=%fused_computation.54 | loop fusion | flops 4718592 | bytes 6389760 | tf_op jit(solution)/shard_map/add | solution.py:38
  50.5 0.4 fusion.87
  51.4 3.5 %collective-permute-start.2 = (f32[1,1,16,256]{3,1,2,0:T(1,128)S(1)}, f32[1,1,16,256]{3,1,2,0:T(1,128)S(1)}, u32[]{:S(2)}, u32[]{:S(2)}) collective-permute-start(f32[1,1,16,256]{3,1,2,0:T(1,128)S(1)} %get-tuple-element.78), channel_id=1, source_target_pairs={{0,1},{1,2},{2,3},{3,4},{4,5},{5,6},{6,7},{7,8},{8,9},{9,10},{10,1... | collective-permute-start | bytes 49160 | tf_op jit(solution)/shard_map/ppermute | solution.py:20
  54.9 1.9 %collective-permute-start.3 = (f32[1,1,16,256]{3,1,2,0:T(1,128)S(1)}, f32[1,1,16,256]{3,1,2,0:T(1,128)S(1)}, u32[]{:S(2)}, u32[]{:S(2)}) collective-permute-start(f32[1,1,16,256]{3,1,2,0:T(1,128)S(1)} %get-tuple-element.79), channel_id=1, source_target_pairs={{1,0},{2,1},{3,2},{4,3},{5,4},{6,5},{7,6},{8,7},{9,8},{10,9},{11,1... | collective-permute-start | bytes 49160 | tf_op jit(solution)/shard_map/ppermute | solution.py:23
  56.9 10.5 %collective-permute-done.2 = f32[1,1,16,256]{3,1,2,0:T(1,128)S(1)} collective-permute-done((f32[1,1,16,256]{3,1,2,0:T(1,128)S(1)}, f32[1,1,16,256]{3,1,2,0:T(1,128)S(1)}, u32[]{:S(2)}, u32[]{:S(2)}) %collective-permute-start.2) | collective-permute-done | bytes 16416 | tf_op jit(solution)/shard_map/ppermute | solution.py:20
  67.3 3.0 %collective-permute-done.3 = f32[1,1,16,256]{3,1,2,0:T(1,128)S(1)} collective-permute-done((f32[1,1,16,256]{3,1,2,0:T(1,128)S(1)}, f32[1,1,16,256]{3,1,2,0:T(1,128)S(1)}, u32[]{:S(2)}, u32[]{:S(2)}) %collective-permute-start.3) | collective-permute-done | bytes 16416 | tf_op jit(solution)/shard_map/ppermute | solution.py:23
  70.4 0.8 fusion.42
  71.2 0.4 fusion.82
  72.1 1.9 %collective-permute-start.4 = (f32[1,1,16,256]{3,1,2,0:T(1,128)S(1)}, f32[1,1,16,256]{3,1,2,0:T(1,128)S(1)}, u32[]{:S(2)}, u32[]{:S(2)}) collective-permute-start(f32[1,1,16,256]{3,1,2,0:T(1,128)S(1)} %get-tuple-element.68), channel_id=1, source_target_pairs={{0,1},{1,2},{2,3},{3,4},{4,5},{5,6},{6,7},{7,8},{8,9},{9,10},{10,1... | collective-permute-start | bytes 49160 | tf_op jit(solution)/shard_map/ppermute | solution.py:20
  74.0 2.4 %collective-permute-start.5 = (f32[1,1,16,256]{3,1,2,0:T(1,128)S(1)}, f32[1,1,16,256]{3,1,2,0:T(1,128)S(1)}, u32[]{:S(2)}, u32[]{:S(2)}) collective-permute-start(f32[1,1,16,256]{3,1,2,0:T(1,128)S(1)} %get-tuple-element.69), channel_id=1, source_target_pairs={{1,0},{2,1},{3,2},{4,3},{5,4},{6,5},{7,6},{8,7},{9,8},{10,9},{11,1... | collective-permute-start | bytes 49160 | tf_op jit(solution)/shard_map/ppermute | solution.py:23
  76.5 2.6 %collective-permute-done.5 = f32[1,1,16,256]{3,1,2,0:T(1,128)S(1)} collective-permute-done((f32[1,1,16,256]{3,1,2,0:T(1,128)S(1)}, f32[1,1,16,256]{3,1,2,0:T(1,128)S(1)}, u32[]{:S(2)}, u32[]{:S(2)}) %collective-permute-start.5) | collective-permute-done | bytes 16416 | tf_op jit(solution)/shard_map/ppermute | solution.py:23
  79.1 0.8 fusion.35
  80.0 1.9 %collective-permute-start.6 = (f32[1,1,16,256]{3,1,2,0:T(1,128)S(1)}, f32[1,1,16,256]{3,1,2,0:T(1,128)S(1)}, u32[]{:S(2)}, u32[]{:S(2)}) collective-permute-start(f32[1,1,16,256]{3,1,2,0:T(1,128)S(1)} %get-tuple-element.58), channel_id=1, source_target_pairs={{0,1},{1,2},{2,3},{3,4},{4,5},{5,6},{6,7},{7,8},{8,9},{9,10},{10,1... | collective-permute-start | bytes 49160 | tf_op jit(solution)/shard_map/ppermute | solution.py:20
  81.9 2.6 %collective-permute-start.7 = (f32[1,1,16,256]{3,1,2,0:T(1,128)S(1)}, f32[1,1,16,256]{3,1,2,0:T(1,128)S(1)}, u32[]{:S(2)}, u32[]{:S(2)}) collective-permute-start(f32[1,1,16,256]{3,1,2,0:T(1,128)S(1)} %get-tuple-element.59), channel_id=1, source_target_pairs={{1,0},{2,1},{3,2},{4,3},{5,4},{6,5},{7,6},{8,7},{9,8},{10,9},{11,1... | collective-permute-start | bytes 49160 | tf_op jit(solution)/shard_map/ppermute | solution.py:23
  84.7 0.3 fusion.75
  85.0 0.4 fusion.77
  85.4 1.6 %collective-permute-done.7 = f32[1,1,16,256]{3,1,2,0:T(1,128)S(1)} collective-permute-done((f32[1,1,16,256]{3,1,2,0:T(1,128)S(1)}, f32[1,1,16,256]{3,1,2,0:T(1,128)S(1)}, u32[]{:S(2)}, u32[]{:S(2)}) %collective-permute-start.7) | collective-permute-done | bytes 16416 | tf_op jit(solution)/shard_map/ppermute | solution.py:23
  87.0 0.8 fusion.28
  87.8 1.1 fusion.14
  89.0 0.5 convolution_convert_fusion.1
  89.5 0.3 reshape.340
  89.7 1.3 %copy.77 = bf16[128,4,4,256]{3,1,2,0:T(4,128)(2,1)} copy(bf16[128,4,4,256]{3,1,0,2:T(4,128)(2,1)S(1)} %reshape.340) | data formatting | bytes 2097152 | tf_op jit(solution)/shard_map/reshape | solution.py:60
  91.1 19.4 %all-to-all-start.2 = ((bf16[128,4,4,256]{3,1,2,0:T(4,128)(2,1)}), bf16[128,4,4,256]{3,1,2,0:T(4,128)(2,1)S(1)}, u32[]{:S(2)}, u32[]{:S(2)}) async-start(bf16[128,4,4,256]{3,1,2,0:T(4,128)(2,1)} %copy.77), calls=%async_computation.2 | async-start | bytes 2097152 | tf_op jit(solution)/shard_map/all_to_all | solution.py:124
  110.5 1.6 %copy.81 = f32[1,64,16,256]{3,2,1,0:T(8,128)} copy(f32[1,64,16,256]{3,1,2,0:T(8,128)S(1)} %constant_dynamic-update-slice_fusion) | data formatting | bytes 2097152
  112.1 17.6 %all-to-all-done.2 = bf16[128,4,4,256]{3,1,2,0:T(4,128)(2,1)S(1)} async-done(((bf16[128,4,4,256]{3,1,2,0:T(4,128)(2,1)}), bf16[128,4,4,256]{3,1,2,0:T(4,128)(2,1)S(1)}, u32[]{:S(2)}, u32[]{:S(2)}) %all-to-all-start.2) | async-done | bytes 1048608 | tf_op jit(solution)/shard_map/all_to_all | solution.py:124
  129.8 1.0 fusion.19
  130.8 0.8 copy.82
  (32 shorter events, 1.7 us)
Async XLA Ops:
  0.6 28.0 %copy-start = (f32[1,64,16,256]{3,2,1,0:T(8,128)S(1)}, f32[1,64,16,256]{3,2,1,0:T(8,128)}, u32[]{:S(2)}) copy-start(f32[1,64,16,256]{3,2,1,0:T(8,128)} %param.11) | copy-start | bytes 3145732
  1.5 45.7 %collective-permute-start = (f32[1,1,16,256]{3,1,2,0:T(1,128)S(1)}, f32[1,1,16,256]{3,1,2,0:T(1,128)S(1)}, u32[]{:S(2)}, u32[]{:S(2)}) collective-permute-start(f32[1,1,16,256]{3,1,2,0:T(1,128)S(1)} %copy.55), channel_id=1, source_target_pairs={{0,1},{1,2},{2,3},{3,4},{4,5},{5,6},{6,7},{7,8},{8,9},{9,10},{10,1... | collective-permute-start | bytes 49160 | tf_op jit(solution)/shard_map/ppermute | solution.py:20
  6.0 41.2 %collective-permute-start.1 = (f32[1,1,16,256]{3,1,2,0:T(1,128)S(1)}, f32[1,1,16,256]{3,1,2,0:T(1,128)S(1)}, u32[]{:S(2)}, u32[]{:S(2)}) collective-permute-start(f32[1,1,16,256]{3,1,2,0:T(1,128)S(1)} %copy.57), channel_id=1, source_target_pairs={{1,0},{2,1},{3,2},{4,3},{5,4},{6,5},{7,6},{8,7},{9,8},{10,9},{11,1... | collective-permute-start | bytes 49160 | tf_op jit(solution)/shard_map/ppermute | solution.py:23
  11.8 24.2 %all-to-all-start = ((s32[128,1,4]{2,1,0:T(1,128)}), s32[128,1,4]{2,1,0:T(1,128)S(1)}, u32[]{:S(2)}, u32[]{:S(2)}) async-start(s32[128,1,4]{2,1,0:T(1,128)} %bitcast.9), calls=%async_computation | async-start | bytes 131072 | tf_op jit(solution)/shard_map/all_to_all | solution.py:110
  28.6 18.6 %copy-start.1 = (f32[1,64,256]{2,1,0:T(8,128)S(1)}, f32[1,64,256]{2,1,0:T(8,128)}, u32[]{:S(2)}) copy-start(f32[1,64,256]{2,1,0:T(8,128)} %param.12) | copy-start | bytes 196612
  36.0 51.8 %all-to-all-start.1 = ((f32[128,4,4,256]{3,2,1,0:T(4,128)}), f32[128,4,4,256]{3,2,1,0:T(4,128)S(1)}, u32[]{:S(2)}, u32[]{:S(2)}) async-start(f32[128,4,4,256]{3,2,1,0:T(4,128)} %concatenate.175.clone), calls=%async_computation.1 | async-start | bytes 4194304 | tf_op jit(solution)/shard_map/all_to_all | solution.py:109
  51.4 16.0 %collective-permute-start.2 = (f32[1,1,16,256]{3,1,2,0:T(1,128)S(1)}, f32[1,1,16,256]{3,1,2,0:T(1,128)S(1)}, u32[]{:S(2)}, u32[]{:S(2)}) collective-permute-start(f32[1,1,16,256]{3,1,2,0:T(1,128)S(1)} %get-tuple-element.78), channel_id=1, source_target_pairs={{0,1},{1,2},{2,3},{3,4},{4,5},{5,6},{6,7},{7,8},{8,9},{9,10},{10,1... | collective-permute-start | bytes 49160 | tf_op jit(solution)/shard_map/ppermute | solution.py:20
  54.9 15.5 %collective-permute-start.3 = (f32[1,1,16,256]{3,1,2,0:T(1,128)S(1)}, f32[1,1,16,256]{3,1,2,0:T(1,128)S(1)}, u32[]{:S(2)}, u32[]{:S(2)}) collective-permute-start(f32[1,1,16,256]{3,1,2,0:T(1,128)S(1)} %get-tuple-element.79), channel_id=1, source_target_pairs={{1,0},{2,1},{3,2},{4,3},{5,4},{6,5},{7,6},{8,7},{9,8},{10,9},{11,1... | collective-permute-start | bytes 49160 | tf_op jit(solution)/shard_map/ppermute | solution.py:23
  72.1 4.4 %collective-permute-start.4 = (f32[1,1,16,256]{3,1,2,0:T(1,128)S(1)}, f32[1,1,16,256]{3,1,2,0:T(1,128)S(1)}, u32[]{:S(2)}, u32[]{:S(2)}) collective-permute-start(f32[1,1,16,256]{3,1,2,0:T(1,128)S(1)} %get-tuple-element.68), channel_id=1, source_target_pairs={{0,1},{1,2},{2,3},{3,4},{4,5},{5,6},{6,7},{7,8},{8,9},{9,10},{10,1... | collective-permute-start | bytes 49160 | tf_op jit(solution)/shard_map/ppermute | solution.py:20
  74.0 5.1 %collective-permute-start.5 = (f32[1,1,16,256]{3,1,2,0:T(1,128)S(1)}, f32[1,1,16,256]{3,1,2,0:T(1,128)S(1)}, u32[]{:S(2)}, u32[]{:S(2)}) collective-permute-start(f32[1,1,16,256]{3,1,2,0:T(1,128)S(1)} %get-tuple-element.69), channel_id=1, source_target_pairs={{1,0},{2,1},{3,2},{4,3},{5,4},{6,5},{7,6},{8,7},{9,8},{10,9},{11,1... | collective-permute-start | bytes 49160 | tf_op jit(solution)/shard_map/ppermute | solution.py:23
  80.0 5.4 %collective-permute-start.6 = (f32[1,1,16,256]{3,1,2,0:T(1,128)S(1)}, f32[1,1,16,256]{3,1,2,0:T(1,128)S(1)}, u32[]{:S(2)}, u32[]{:S(2)}) collective-permute-start(f32[1,1,16,256]{3,1,2,0:T(1,128)S(1)} %get-tuple-element.58), channel_id=1, source_target_pairs={{0,1},{1,2},{2,3},{3,4},{4,5},{5,6},{6,7},{7,8},{8,9},{9,10},{10,1... | collective-permute-start | bytes 49160 | tf_op jit(solution)/shard_map/ppermute | solution.py:20
  81.9 5.1 %collective-permute-start.7 = (f32[1,1,16,256]{3,1,2,0:T(1,128)S(1)}, f32[1,1,16,256]{3,1,2,0:T(1,128)S(1)}, u32[]{:S(2)}, u32[]{:S(2)}) collective-permute-start(f32[1,1,16,256]{3,1,2,0:T(1,128)S(1)} %get-tuple-element.59), channel_id=1, source_target_pairs={{1,0},{2,1},{3,2},{4,3},{5,4},{6,5},{7,6},{8,7},{9,8},{10,9},{11,1... | collective-permute-start | bytes 49160 | tf_op jit(solution)/shard_map/ppermute | solution.py:23
  91.1 38.6 %all-to-all-start.2 = ((bf16[128,4,4,256]{3,1,2,0:T(4,128)(2,1)}), bf16[128,4,4,256]{3,1,2,0:T(4,128)(2,1)S(1)}, u32[]{:S(2)}, u32[]{:S(2)}) async-start(bf16[128,4,4,256]{3,1,2,0:T(4,128)(2,1)} %copy.77), calls=%async_computation.2 | async-start | bytes 2097152 | tf_op jit(solution)/shard_map/all_to_all | solution.py:124
where the time goes:
time: 132 us
  starting transfers between devices  60.5 us (46%)
  waiting for transfers between devices  35.4 us (27%)
  local copies, waits for them, and re-layouts  17.3 us (13%)
  matrix products  9.43 us (7%)
  other arithmetic  7.9 us (6%)
    all_to_all x1, starting transfers between devices, body(): lax.all_to_all(reply_rows, ('comp', 'band'), split_axis=0, concat_axis=0,...  19.4 us
    all_to_all x1, waiting for transfers between devices, body(): lax.all_to_all(reply_rows, ('comp', 'band'), split_axis=0, concat_axis=0,...  17.6 us
    ppermute x4, starting transfers between devices, padded_2(): lax.ppermute(lax.slice_in_dim(block, block.shape[dim] - width, None, axis...  11.9 us
    all_to_all x1, starting transfers between devices, body(): lax.all_to_all(outgoing_index, ('comp', 'band'), split_axis=0, concat_axi...  10.6 us
    ppermute x4, waiting for transfers between devices, padded_2(): lax.ppermute(lax.slice_in_dim(block, block.shape[dim] - width, None, axis...  10.5 us
    all_to_all x1, starting transfers between devices, body(): lax.all_to_all(outgoing, ('comp', 'band'), split_axis=0, concat_axis=0, t...  9.76 us
    ppermute x4, starting transfers between devices, padded_2(): lax.ppermute(lax.slice_in_dim(block, 0, width, axis=dim), axis, backward)  8.81 us
    ppermute x4, waiting for transfers between devices, padded_2(): lax.ppermute(lax.slice_in_dim(block, 0, width, axis=dim), axis, backward)  7.28 us
  transfers between devices with their start and end apart: 11, of which 5 were waited for; matrix products, arithmetic and copies ran while one was open for 22% of the time, Pallas kernels for 0%

commit v1 on v0

v1 whole, which is shorter than its diff:
```python
import jax
import jax.numpy as jnp
from jax import lax
from jax.sharding import PartitionSpec as P

NF = 4
NSTEPS = 4
CAP = 4

COUPLING = 0.25
VERTICAL = 0.15
HIGHEST = lax.Precision.HIGHEST


def diffuse(layer_temp, diffusivity):
    n_bands = lax.axis_size("band")
    band = lax.axis_index("band")
    rows = layer_temp.shape[1]
    lev = layer_temp.shape[2]
    halo = NSTEPS
    comb = jnp.concatenate([layer_temp[0], diffusivity[0][:, None, :]], axis=1)
    forward = [(i, i + 1) for i in range(n_bands - 1)]
    backward = [(i + 1, i) for i in range(n_bands - 1)]
    above = lax.ppermute(comb[rows - halo:], "band", forward)
    below = lax.ppermute(comb[:halo], "band", backward)
    padded = jnp.concatenate([above, comb, below], axis=0)
    fields = padded[:, :lev]
    diff = padded[:, lev]
    grow = band * rows - halo + jnp.arange(rows + 2 * halo, dtype=jnp.int32)
    valid = ((grow >= 0) & (grow < n_bands * rows))[:, None, None]
    for _ in range(NSTEPS):
        row_north = jnp.roll(fields, 1, axis=0)
        row_south = jnp.roll(fields, -1, axis=0)
        col_east = jnp.roll(fields, 1, axis=2)
        col_west = jnp.roll(fields, -1, axis=2)
        level_below = jnp.concatenate([fields[:, :1], fields[:, :-1]], axis=1)
        level_above = jnp.concatenate([fields[:, 1:], fields[:, -1:]], axis=1)
        horizontal = row_north + row_south + col_east + col_west - 4.0 * fields
        fields = (
            fields
            + diff[:, None, :] * horizontal
            + VERTICAL * (level_below + level_above - 2.0 * fields)
        )
        fields = jnp.where(valid, fields, 0.0)
    return fields[halo:halo + rows]


def body(layer_temp, diffusivity, owner_band, block_index, remap_blocks):
    n_sections = lax.axis_size("comp")
    n_bands = lax.axis_size("band")
    section = lax.axis_index("comp")
    rows = layer_temp.shape[1]
    cols = layer_temp.shape[3]
    width = NF * cols
    is_ocean = section == n_sections - 1
    weights_local = remap_blocks[0]

    surface_layers = layer_temp[0, :, :NF, :].astype(jnp.bfloat16)
    flux = lax.cond(
        is_ocean,
        lambda: jnp.zeros((rows, NF, cols), jnp.float32),
        lambda: jnp.einsum(
            "rfc,rcd->rfd", surface_layers, weights_local, preferred_element_type=jnp.float32
        ),
    )

    destination = owner_band[0, :, 0]
    dest_onehot = (destination[:, None] == jnp.arange(n_bands, dtype=jnp.int32)[None, :]).astype(
        jnp.float32
    )
    positions = jnp.arange(rows, dtype=jnp.int32)
    earlier_mask = (positions[:, None] > positions[None, :]).astype(jnp.float32)
    earlier = jnp.dot(earlier_mask, dest_onehot, precision=HIGHEST)
    slot_rank = jnp.sum(earlier * dest_onehot, axis=1).astype(jnp.int32)
    slot_onehot = (slot_rank[:, None] == jnp.arange(CAP, dtype=jnp.int32)[None, :]).astype(
        jnp.float32
    )
    selector = (dest_onehot[:, :, None] * slot_onehot[:, None, :]).reshape(rows, n_bands * CAP)

    index_lanes = jnp.broadcast_to(block_index[0].astype(jnp.float32)[:, None], (rows, 128))
    payload = jnp.concatenate([flux.reshape(rows, width), index_lanes], axis=1)
    sending = jnp.einsum("rk,rx->kx", selector, payload, precision=HIGHEST)
    sending = sending.reshape(n_bands, CAP, width + 128)
    received = lax.all_to_all(sending, "band", 0, 0, tiled=True)
    received = received.reshape(n_bands * CAP, width + 128)
    got_index = received[:, width].astype(jnp.int32)
    match = (got_index[:, None] == positions[None, :]).astype(jnp.float32)
    partial = jnp.einsum("kr,kx->rx", match, received[:, :width], precision=HIGHEST)
    ocean_heat = lax.psum(partial, "comp")

    fields = diffuse(layer_temp, diffusivity)
    heating = jnp.where(is_ocean, COUPLING * ocean_heat, 0.0).reshape(rows, NF, cols)
    temp_out = fields.at[:, :NF].add(heating)
    sea_surface = temp_out[:, :NF].astype(jnp.bfloat16)
    returned = lax.cond(
        is_ocean,
        lambda: jnp.einsum(
            "rfc,rcd->rfd", sea_surface, weights_local, preferred_element_type=jnp.float32
        ).astype(jnp.bfloat16),
        lambda: jnp.zeros((rows, NF, cols), jnp.bfloat16),
    )

    gathered = lax.all_gather(returned, "comp", axis=0, tiled=False)
    ocean_rows = gathered[n_sections - 1].reshape(rows, width)
    reply = jnp.einsum(
        "kr,rx->kx", match.astype(jnp.bfloat16), ocean_rows, preferred_element_type=jnp.float32
    ).astype(jnp.bfloat16)
    reply = reply.reshape(n_bands, CAP, width)
    came_back = lax.all_to_all(reply, "band", 0, 0, tiled=True)
    came_back = came_back.reshape(n_bands * CAP, width)
    seen = jnp.einsum(
        "rk,kx->rx", selector.astype(jnp.bfloat16), came_back, preferred_element_type=jnp.float32
    ).astype(jnp.bfloat16)
    surface_temp = jnp.where(is_ocean, returned, seen.reshape(rows, NF, cols))
    return temp_out[None], surface_temp[None]


def solution(mesh):
    return jax.shard_map(
        body,
        mesh=mesh,
        in_specs=(
            P("comp", "band", None, None),
            P("comp", "band", None),
            P("comp", "band", None),
            P("comp", "band"),
            P("comp", "band", None, None),
        ),
        out_specs=(P("comp", "band", None, None), P("comp", "band", None, None)),
        check_vma=False,
    )
```

time: 132 us -> 137 us (1.038)
  starting transfers between devices: 60.5 us -> 26.8 us
  blocking collectives: 0 us -> 13.5 us
  between operations: 1 us -> 14.5 us
  waiting for transfers between devices: 35.4 us -> 46.7 us
  other arithmetic: 7.9 us -> 13 us
  local copies, waits for them, and re-layouts: 17.3 us -> 14.7 us
  matrix products: 9.43 us -> 6.92 us
    psum x0 -> x1, waiting for transfers between devices: none -> 38.1 us  [body(): ocean_heat = lax.psum(partial, 'comp')]
    all_to_all x3 -> x2, starting transfers between devices: 39.8 us -> 20.3 us  [the longest x1 12.6 us: body(): came_back = lax.all_to_all(reply, 'band', 0, 0, tiled=True)]
    ppermute x8 -> x2, waiting for transfers between devices: 17.8 us -> 0.01 us  [the longest x1 0.01 us: diffuse(): above = lax.ppermute(comb[rows - halo:], 'band', forward)]
    ppermute x8 -> x2, starting transfers between devices: 20.7 us -> 6.42 us  [the longest x1 4.5 us: diffuse(): above = lax.ppermute(comb[rows - halo:], 'band', forward)]
    all_gather x0 -> x1, blocking collectives: none -> 13.5 us  [body(): gathered = lax.all_gather(returned, 'comp', axis=0, tiled=False)]
    select_n x0 -> x5, other arithmetic: none -> 10.2 us  [the longest x4 9.22 us: diffuse(): fields = jnp.where(valid, fields, 0.0)]
    all_to_all x3 -> x2, waiting for transfers between devices: 17.6 us -> 8.65 us  [the longest x1 8.65 us: body(): came_back = lax.all_to_all(reply, 'band', 0, 0, tiled=True)]
    add x4 -> x0, other arithmetic: 5.8 us -> none  [advance(): fields + diffusivity[:, :, None, :] * horizontal]
  transfers between devices with their start and end apart: 11 -> 5, of which waited for: 5 -> 2; matrix products, arithmetic and copies ran while one was open for 22% -> 21% of each run, Pallas kernels for 0% -> 0%
where the time goes in v1:
time: 137 us; the launch traced here: 136 us
  waiting for transfers between devices  46.7 us (34%)
  starting transfers between devices  26.8 us (20%)
  local copies, waits for them, and re-layouts  14.7 us (11%)
  between operations  14.5 us (11%)
  blocking collectives  13.5 us (10%)
  other arithmetic  13 us (9%)
  matrix products  6.92 us (5%)
    psum x1, waiting for transfers between devices, body(): ocean_heat = lax.psum(partial, 'comp')  38.1 us
    all_gather x1, blocking collectives, body(): gathered = lax.all_gather(returned, 'comp', axis=0, tiled=False)  13.5 us
    all_to_all x1, starting transfers between devices, body(): came_back = lax.all_to_all(reply, 'band', 0, 0, tiled=True)  12.6 us
    select_n x4, other arithmetic, diffuse(): fields = jnp.where(valid, fields, 0.0)  9.22 us
    all_to_all x1, waiting for transfers between devices, body(): came_back = lax.all_to_all(reply, 'band', 0, 0, tiled=True)  8.65 us
    all_to_all x1, starting transfers between devices, body(): received = lax.all_to_all(sending, 'band', 0, 0, tiled=True)  7.72 us
    slice x8, local copies, waits for them, and re-layouts, diffuse(): col_west = jnp.roll(fields, -1, axis=2)  4.96 us
    dot_general x1, matrix products, body(): jnp.einsum('rfc,rcd->rfd', surface_layers, weights_local, preferred_eleme...  4.57 us
  transfers between devices with their start and end apart: 5, of which 2 were waited for; matrix products, arithmetic and copies ran while one was open for 21% of the time, Pallas kernels for 0%

profile of v1, /device:TPU:1, one launch (start us, length us, event | category | flops | bytes accessed | tf_op | source)
XLA Modules:
  0.0 136.2 jit_solution(354215395123963199)
XLA Ops:
  7.2 1.0 broadcast_in_dim_squeeze.4
  8.2 0.9 pad_maximum_fusion.2
  9.1 4.5 %collective-permute-start = (f32[4,17,256]{2,1,0:T(8,128)S(1)}, f32[4,17,256]{2,1,0:T(8,128)S(1)}, u32[]{:S(2)}, u32[]{:S(2)}) collective-permute-start(f32[4,17,256]{2,1,0:T(8,128)S(1)} %get-tuple-element.81), channel_id=1, source_target_pairs={{0,1},{1,2},{2,3},{3,4},{4,5},{5,6},{6,7},{7,8},{8,9},{9,10},{10,1... | collective-permute-start | bytes 208904 | tf_op jit(solution)/shard_map/ppermute | solution.py:24
  13.6 1.9 %collective-permute-start.1 = (f32[4,17,256]{2,1,0:T(8,128)S(1)}, f32[4,17,256]{2,1,0:T(8,128)S(1)}, u32[]{:S(2)}, u32[]{:S(2)}) collective-permute-start(f32[4,17,256]{2,1,0:T(8,128)S(1)} %get-tuple-element.80), channel_id=1, source_target_pairs={{1,0},{2,1},{3,2},{4,3},{5,4},{6,5},{7,6},{8,7},{9,8},{10,9},{11,1... | collective-permute-start | bytes 208904 | tf_op jit(solution)/shard_map/ppermute | solution.py:25
  15.5 0.1 fusion.50
  15.7 0.6 multiply_convert_fusion
  16.3 4.6 %conditional.2 = (f32[64,1024]{1,0:T(8,128)S(1)}) conditional(s32[]{:T(128)} %convert_element_type.70, (f32[1,64,16,256]{3,2,1,0:T(8,128)S(1)}, bf16[64,256,256]{2,1,0:T(8,128)(2,1)}) %tuple.63, () %tuple.27), branch_computations={%region_1.0_spmd, %region_2.0_spmd} | conditional | flops 33554432 | bytes 9306120 | solution.py:59
  16.3 4.6 %fusion.1 = f32[64,4,256]{2,1,0:T(4,128)S(1)} fusion(bf16[64,256,256]{2,1,0:T(8,128)(2,1)} %get-tuple-element.31, f32[1,64,16,256]{3,2,1,0:T(8,128)S(1)} %get-tuple-element.30), kind=kOutput, calls=%fused_computation.2 | convolution fusion | flops 33554432 | bytes 8781824 | tf_op jit(solution)/shard_map/cond/branch_0_fun/rfc,rcd->rfd/dot_general | solution.py:62
  21.1 0.6 fusion.53
  21.7 1.2 copy.17
  22.9 7.7 %all-to-all-start = ((f32[32,4,1152]{2,1,0:T(4,128)}), f32[32,4,1152]{2,1,0:T(4,128)S(1)}, u32[]{:S(2)}, u32[]{:S(2)}) async-start(f32[32,4,1152]{2,1,0:T(4,128)} %copy.17), calls=%async_computation | async-start | bytes 1179648 | tf_op jit(solution)/shard_map/all_to_all | solution.py:84
  30.7 0.1 pad_maximum_fusion
  30.9 0.2 fusion.67
  31.1 0.4 fusion.68
  31.5 0.3 fusion.70
  31.9 0.2 fusion.69
  32.2 1.9 %fusion.10 = f32[72,16,256]{2,1,0:T(8,128)S(1)} fusion(f32[4,17,256]{2,1,0:T(8,128)S(1)} %collective-permute-done, f32[4,17,256]{2,1,0:T(8,128)S(1)} %collective-permute-done.1, f32[64,1,256]{2,1,0:T(1,128)S(1)} %broadcast_in_dim_squeeze.4, f32[64,16,256]{2,1,0:T(8,128)S(1)} %bitcast.43, f32[71,16,256]{2,1,0:T(8,128)S(1)} %get-tuple-element.43, ...), kind=kLoop, calls=%fused_computation.19 | loop fusion | flops 10027008 | bytes 10616904 | tf_op jit(solution)/shard_map/jit(_where)/select_n | solution.py:44
  34.1 0.2 fusion.83
  34.3 0.4 fusion.85
  34.7 0.3 fusion.87
  35.0 0.2 fusion.86
  35.4 1.7 %fusion.28 = f32[72,16,256]{2,1,0:T(8,128)S(1)} fusion(f32[72,16,256]{2,1,0:T(8,128)S(1)} %fusion.10, f32[71,16,256]{2,1,0:T(8,128)S(1)} %get-tuple-element.77, f32[1,16,256]{2,1,0:T(8,128)S(1)} %get-tuple-element.79, f32[1,16,256]{2,1,0:T(8,128)S(1)} %get-tuple-element.78, f32[71,16,256]{2,1,0:T(8,128)S(1)} %get-tuple-element.76, ...), kind=kLoop, calls=%fused_computation.41 | loop fusion | flops 5603328 | bytes 9510984 | tf_op jit(solution)/shard_map/jit(_where)/select_n | solution.py:44
  37.1 0.2 fusion.77
  37.3 0.4 fusion.79
  37.7 0.3 fusion.81
  38.0 0.2 fusion.80
  38.2 0.1 fusion.78
  38.4 1.7 %fusion.37 = f32[72,16,256]{2,1,0:T(8,128)S(1)} fusion(f32[72,16,256]{2,1,0:T(8,128)S(1)} %fusion.28, f32[71,16,256]{2,1,0:T(8,128)S(1)} %get-tuple-element.65, f32[1,16,256]{2,1,0:T(8,128)S(1)} %get-tuple-element.67, f32[1,16,256]{2,1,0:T(8,128)S(1)} %get-tuple-element.66, f32[71,16,256]{2,1,0:T(8,128)S(1)} %get-tuple-element.64, ...), kind=kLoop, calls=%fused_computation.52 | loop fusion | flops 5603328 | bytes 9510984 | tf_op jit(solution)/shard_map/jit(_where)/select_n | solution.py:44
  40.1 1.2 fusion.71
  41.3 1.7 %fusion.75 = (f32[71,16,256]{2,1,0:T(8,128)}, f32[71,16,256]{2,1,0:T(8,128)}) fusion(f32[72,16,256]{2,1,0:T(8,128)S(1)} %fusion.37), kind=kLoop, calls=%fused_computation.115 | loop fusion | bytes 4653056 | tf_op jit(solution)/shard_map/jit(_roll_static)/slice | solution.py:33
  43.0 0.8 fusion.72
  43.8 0.6 fusion.76
  44.4 1.2 fusion.74
  45.6 1.8 %fusion.73 = (f32[72,16,255]{2,1,0:T(8,128)}, f32[72,16,255]{2,1,0:T(8,128)}) fusion(f32[72,16,256]{2,1,0:T(8,128)S(1)} %fusion.37), kind=kLoop, calls=%fused_computation.113 | loop fusion | bytes 4700160 | tf_op jit(solution)/shard_map/jit(_roll_static)/slice | solution.py:35
  47.4 0.2 reshape.125
  47.8 1.1 fusion.51
  48.9 3.9 %fusion.46 = f32[72,16,256]{2,1,0:T(8,128)S(1)} fusion(f32[72,16,256]{2,1,0:T(8,128)S(1)} %fusion.37, f32[71,16,256]{2,1,0:T(8,128)} %get-tuple-element.53, f32[1,16,256]{2,1,0:T(8,128)} %get-tuple-element.55, f32[1,16,256]{2,1,0:T(8,128)S(1)} %get-tuple-element.54, f32[71,16,256]{2,1,0:T(8,128)} %get-tuple-element.52, f32[72,16,255]{2,1,0:T(8,128)} %get-tuple-element.49, ...), kind=kLoop, calls=%fused_computation.63 | loop fusion | flops 5603328 | bytes 9510984 | tf_op jit(solution)/shard_map/jit(_where)/select_n | solution.py:44
  52.8 38.1 %all-reduce.2.cloned.1.call-done = f32[64,1024]{1,0:T(8,128)} async-done(((f32[64,1024]{1,0:T(8,128)}), f32[64,1024]{1,0:T(8,128)}) %all-reduce.2.cloned.1.call-update) | async-done | bytes 262160 | tf_op jit(solution)/shard_map/psum | solution.py:89
  90.9 1.0 multiply_select_fusion
  91.9 0.1 reshape.126
  92.2 13.5 %all-gather = bf16[256,4,256]{2,1,0:T(4,128)(2,1)S(1)} all-gather(bf16[64,4,256]{2,1,0:T(4,128)(2,1)S(1)} %get-tuple-element.85), channel_id=2, replica_groups=mesh['comp'=4,'band'=32] {'comp'}, dimensions={0}, use_global_device_ids=true | all-gather | bytes 655360 | tf_op jit(solution)/shard_map/all_gather | solution.py:103
  105.7 0.3 convolution_convert_fusion.1
  106.0 0.8 reshape.127
  106.8 12.6 %all-to-all-start.1 = ((bf16[32,4,1024]{2,1,0:T(4,128)(2,1)}), bf16[32,4,1024]{2,1,0:T(4,128)(2,1)S(1)}, u32[]{:S(2)}, u32[]{:S(2)}) async-start(bf16[32,4,1024]{2,1,0:T(4,128)(2,1)} %reshape.127), calls=%async_computation.1 | async-start | bytes 524288 | tf_op jit(solution)/shard_map/all_to_all | solution.py:109
  119.5 0.1 bitcast_dynamic-update-slice_fusion
  119.6 8.6 %all-to-all-done.1 = bf16[32,4,1024]{2,1,0:T(4,128)(2,1)S(1)} async-done(((bf16[32,4,1024]{2,1,0:T(4,128)(2,1)}), bf16[32,4,1024]{2,1,0:T(4,128)(2,1)S(1)}, u32[]{:S(2)}, u32[]{:S(2)}) %all-to-all-start.1) | async-done | bytes 262176 | tf_op jit(solution)/shard_map/all_to_all | solution.py:109
  128.3 0.2 fusion.49
  128.6 0.7 select_bitcast_fusion
  (45 shorter events, 0.9 us)
Async XLA Ops:
  7.2 8.6 %copy-start = (f32[1,64,16,256]{3,2,1,0:T(8,128)S(1)}, f32[1,64,16,256]{3,2,1,0:T(8,128)}, u32[]{:S(2)}) copy-start(f32[1,64,16,256]{3,2,1,0:T(8,128)} %param.11) | copy-start | bytes 3145732
  7.2 8.3 %copy-start.7 = (s32[1,64,1]{1,2,0:T(1,128)S(1)}, s32[1,64,1]{1,2,0:T(1,128)}, u32[]{:S(2)}) copy-start(s32[1,64,1]{1,2,0:T(1,128)} %param.13) | copy-start | bytes 772
  7.2 8.5 %copy-start.8 = (s32[1,64]{1,0:T(1,128)S(1)}, s32[1,64]{1,0:T(1,128)}, u32[]{:S(2)}) copy-start(s32[1,64]{1,0:T(1,128)} %param.14) | copy-start | bytes 772
  9.1 21.6 %collective-permute-start = (f32[4,17,256]{2,1,0:T(8,128)S(1)}, f32[4,17,256]{2,1,0:T(8,128)S(1)}, u32[]{:S(2)}, u32[]{:S(2)}) collective-permute-start(f32[4,17,256]{2,1,0:T(8,128)S(1)} %get-tuple-element.81), channel_id=1, source_target_pairs={{0,1},{1,2},{2,3},{3,4},{4,5},{5,6},{6,7},{7,8},{8,9},{9,10},{10,1... | collective-permute-start | bytes 208904 | tf_op jit(solution)/shard_map/ppermute | solution.py:24
  13.6 17.1 %collective-permute-start.1 = (f32[4,17,256]{2,1,0:T(8,128)S(1)}, f32[4,17,256]{2,1,0:T(8,128)S(1)}, u32[]{:S(2)}, u32[]{:S(2)}) collective-permute-start(f32[4,17,256]{2,1,0:T(8,128)S(1)} %get-tuple-element.80), channel_id=1, source_target_pairs={{1,0},{2,1},{3,2},{4,3},{5,4},{6,5},{7,6},{8,7},{9,8},{10,9},{11,1... | collective-permute-start | bytes 208904 | tf_op jit(solution)/shard_map/ppermute | solution.py:25
  22.9 24.5 %all-to-all-start = ((f32[32,4,1152]{2,1,0:T(4,128)}), f32[32,4,1152]{2,1,0:T(4,128)S(1)}, u32[]{:S(2)}, u32[]{:S(2)}) async-start(f32[32,4,1152]{2,1,0:T(4,128)} %copy.17), calls=%async_computation | async-start | bytes 1179648 | tf_op jit(solution)/shard_map/all_to_all | solution.py:84
  30.6 60.3 %all-reduce.2.cloned.1.call-start = ((), (), s32[]{:S(2)}) async-start(), calls=%async_computation.2 | async-start | bytes 524288 | tf_op jit(solution)/shard_map/psum | solution.py:89
  30.7 7.7 %copy-start.4 = (pred[72]{0:T(512)(128)(4,1)}, pred[72]{0:T(512)(128)(4,1)S(1)}, u32[]{:S(2)}) copy-start(pred[72]{0:T(512)(128)(4,1)S(1)} %compare_and_fusion) | copy-start | bytes 220
  32.2 6.2 %copy-start.1 = (f32[72,1,256]{2,0,1:T(8,128)}, f32[72,1,256]{2,0,1:T(8,128)S(1)}, u32[]{:S(2)}) copy-start(f32[72,1,256]{2,0,1:T(8,128)S(1)} %copy.30) | copy-start | bytes 221188
  47.7 1.1 copy-start.5
  92.2 13.6 %copy-start.6 = (s32[128]{0:T(128)S(1)}, s32[128]{0:T(128)}, u32[]{:S(2)}) copy-start(s32[128]{0:T(128)} %copy-done.5) | copy-start | bytes 1540
  106.8 21.5 %all-to-all-start.1 = ((bf16[32,4,1024]{2,1,0:T(4,128)(2,1)}), bf16[32,4,1024]{2,1,0:T(4,128)(2,1)S(1)}, u32[]{:S(2)}, u32[]{:S(2)}) async-start(bf16[32,4,1024]{2,1,0:T(4,128)(2,1)} %reshape.127), calls=%async_computation.1 | async-start | bytes 524288 | tf_op jit(solution)/shard_map/all_to_all | solution.py:109
  119.4 8.9 %copy-start.3 = (bf16[64,32,4]{0,2,1:T(4,128)(2,1)S(1)}, bf16[64,32,4]{0,2,1:T(4,128)(2,1)}, u32[]{:S(2)}) copy-start(bf16[64,32,4]{0,2,1:T(4,128)(2,1)} %get-tuple-element.82) | copy-start | bytes 49156
  119.6 9.7 %copy-start.2 = (f32[1,64,16,256]{3,2,1,0:T(8,128)}, f32[1,64,16,256]{3,2,1,0:T(8,128)S(1)}, u32[]{:S(2)}) copy-start(f32[1,64,16,256]{3,2,1,0:T(8,128)S(1)} %bitcast_dynamic-update-slice_fusion) | copy-start | bytes 3145732
Sparse Core Ops, SparseCore 0:
  49.0 41.8 all-reduce.1

commit v2 on v1

--- a/solution.py
+++ b/solution.py
@@ -86,7 +86,10 @@
     got_index = received[:, width].astype(jnp.int32)
     match = (got_index[:, None] == positions[None, :]).astype(jnp.float32)
     partial = jnp.einsum("kr,kx->rx", match, received[:, :width], precision=HIGHEST)
-    ocean_heat = lax.psum(partial, "comp")
+    last = n_sections - 1
+    ocean_heat = partial
+    for source in range(last):
+        ocean_heat = ocean_heat + lax.ppermute(partial, "comp", [(source, last)])
 
     fields = diffuse(layer_temp, diffusivity)
     heating = jnp.where(is_ocean, COUPLING * ocean_heat, 0.0).reshape(rows, NF, cols)
@@ -100,8 +103,10 @@
         lambda: jnp.zeros((rows, NF, cols), jnp.bfloat16),
     )
 
-    gathered = lax.all_gather(returned, "comp", axis=0, tiled=False)
-    ocean_rows = gathered[n_sections - 1].reshape(rows, width)
+    ocean_rows = returned
+    for target in range(last):
+        ocean_rows = ocean_rows + lax.ppermute(returned, "comp", [(last, target)])
+    ocean_rows = ocean_rows.reshape(rows, width)
     reply = jnp.einsum(
         "kr,rx->kx", match.astype(jnp.bfloat16), ocean_rows, preferred_element_type=jnp.float32
     ).astype(jnp.bfloat16)

time: 137 us -> 90.6 us (0.66)
  waiting for transfers between devices: 46.7 us -> 26.6 us
  blocking collectives: 13.5 us -> 0 us
  between operations: 14.5 us -> 1.19 us
    psum x1 -> x0, waiting for transfers between devices: 38.1 us -> none  [body(): ocean_heat = lax.psum(partial, 'comp')]
    ppermute x0 -> x6, waiting for transfers between devices: none -> 18 us  [the longest x3 12.1 us: body(): ocean_rows = ocean_rows + lax.ppermute(returned, 'comp', [(last, target)])]
    all_gather x1 -> x0, blocking collectives: 13.5 us -> none  [body(): gathered = lax.all_gather(returned, 'comp', axis=0, tiled=False)]
    ppermute x0 -> x6, starting transfers between devices: none -> 5.29 us  [the longest x3 2.66 us: body(): ocean_heat = ocean_heat + lax.ppermute(partial, 'comp', [(source, last)])]
    all_to_all x1, starting transfers between devices: 12.6 us -> 8.4 us  [body(): came_back = lax.all_to_all(reply, 'band', 0, 0, tiled=True)]
  transfers between devices with their start and end apart: 5 -> 10, of which waited for: 2 -> 3; matrix products, arithmetic and copies ran while one was open for 21% -> 31% of each run, Pallas kernels for 0% -> 0%
where the time goes in v2:
time: 90.6 us; the launch traced here: 90 us
  starting transfers between devices  27.9 us (31%)
  waiting for transfers between devices  26.6 us (29%)
  local copies, waits for them, and re-layouts  15.8 us (17%)
  other arithmetic  12.1 us (13%)
  matrix products  6.2 us (7%)
  between operations  1.19 us (1%)
    ppermute x3, waiting for transfers between devices, body(): ocean_rows = ocean_rows + lax.ppermute(returned, 'comp', [(last, target)])  12.1 us
    select_n x4, other arithmetic, diffuse(): fields = jnp.where(valid, fields, 0.0)  9.21 us
    all_to_all x1, waiting for transfers between devices, body(): came_back = lax.all_to_all(reply, 'band', 0, 0, tiled=True)  8.65 us
    all_to_all x1, starting transfers between devices, body(): came_back = lax.all_to_all(reply, 'band', 0, 0, tiled=True)  8.4 us
    all_to_all x1, starting transfers between devices, body(): received = lax.all_to_all(sending, 'band', 0, 0, tiled=True)  7.77 us
    ppermute x3, waiting for transfers between devices, body(): ocean_heat = ocean_heat + lax.ppermute(partial, 'comp', [(source, last)])  5.87 us
    slice x8, local copies, waits for them, and re-layouts, diffuse(): col_west = jnp.roll(fields, -1, axis=2)  4.97 us
    dot_general x1, matrix products, body(): jnp.einsum('rfc,rcd->rfd', surface_layers, weights_local, preferred_eleme...  4.57 us
  transfers between devices with their start and end apart: 10, of which 3 were waited for; matrix products, arithmetic and copies ran while one was open for 31% of the time, Pallas kernels for 0%

profile of v2, /device:TPU:1, one launch (start us, length us, event | category | flops | bytes accessed | tf_op | source)
XLA Modules:
  0.0 90.0 jit_solution(3348221129113750526)
XLA Ops:
  0.7 1.0 %broadcast_in_dim_squeeze.4 = f32[64,1,256]{2,1,0:T(1,128)S(1)} reshape(f32[1,64,256]{2,1,0:T(8,128)} %param.12) | data formatting | bytes 131072 | tf_op jit(solution)/shard_map/broadcast_in_dim;squeeze | solution.py:21
  1.6 0.9 pad_maximum_fusion.2
  2.5 4.5 %collective-permute-start = (f32[4,17,256]{2,1,0:T(8,128)S(1)}, f32[4,17,256]{2,1,0:T(8,128)S(1)}, u32[]{:S(2)}, u32[]{:S(2)}) collective-permute-start(f32[4,17,256]{2,1,0:T(8,128)S(1)} %get-tuple-element.81), channel_id=1, source_target_pairs={{0,1},{1,2},{2,3},{3,4},{4,5},{5,6},{6,7},{7,8},{8,9},{9,10},{10,1... | collective-permute-start | bytes 208904 | tf_op jit(solution)/shard_map/ppermute | solution.py:24
  7.0 1.9 %collective-permute-start.1 = (f32[4,17,256]{2,1,0:T(8,128)S(1)}, f32[4,17,256]{2,1,0:T(8,128)S(1)}, u32[]{:S(2)}, u32[]{:S(2)}) collective-permute-start(f32[4,17,256]{2,1,0:T(8,128)S(1)} %get-tuple-element.80), channel_id=1, source_target_pairs={{1,0},{2,1},{3,2},{4,3},{5,4},{6,5},{7,6},{8,7},{9,8},{10,9},{11,1... | collective-permute-start | bytes 208904 | tf_op jit(solution)/shard_map/ppermute | solution.py:25
  9.2 0.6 multiply_convert_fusion
  9.8 4.6 %conditional.2 = (f32[64,1024]{1,0:T(8,128)S(1)}) conditional(s32[]{:T(128)} %convert_element_type.70, (f32[1,64,16,256]{3,2,1,0:T(8,128)S(1)}, bf16[64,256,256]{2,1,0:T(8,128)(2,1)}) %tuple.61, () %tuple.27), branch_computations={%region_1.0_spmd, %region_2.0_spmd} | conditional | flops 33554432 | bytes 9306120 | solution.py:59
  9.8 4.6 %fusion.1 = f32[64,4,256]{2,1,0:T(4,128)S(1)} fusion(bf16[64,256,256]{2,1,0:T(8,128)(2,1)} %get-tuple-element.31, f32[1,64,16,256]{3,2,1,0:T(8,128)S(1)} %get-tuple-element.30), kind=kOutput, calls=%fused_computation.2 | convolution fusion | flops 33554432 | bytes 8781824 | tf_op jit(solution)/shard_map/cond/branch_0_fun/rfc,rcd->rfd/dot_general | solution.py:62
  14.5 0.6 fusion.53
  15.1 1.2 %copy.17 = f32[32,4,1152]{2,1,0:T(4,128)} copy(f32[32,4,1152]{2,0,1:T(8,128)S(1)} %fusion.53) | data formatting | bytes 1179648 | tf_op jit(solution)/shard_map/rk,rx->kx/dot_general | solution.py:82
  16.4 7.8 %all-to-all-start = ((f32[32,4,1152]{2,1,0:T(4,128)}), f32[32,4,1152]{2,1,0:T(4,128)}, u32[]{:S(2)}, u32[]{:S(2)}) async-start(f32[32,4,1152]{2,1,0:T(4,128)} %copy.17), calls=%async_computation | async-start | bytes 1179648 | tf_op jit(solution)/shard_map/all_to_all | solution.py:84
  24.4 0.2 fusion.67
  24.6 0.4 fusion.68
  25.0 0.3 fusion.70
  25.4 0.2 fusion.69
  25.7 1.9 %fusion.10 = f32[72,16,256]{2,1,0:T(8,128)S(1)} fusion(f32[4,17,256]{2,1,0:T(8,128)S(1)} %collective-permute-done, f32[4,17,256]{2,1,0:T(8,128)S(1)} %collective-permute-done.1, f32[64,1,256]{2,1,0:T(1,128)S(1)} %broadcast_in_dim_squeeze.4, f32[64,16,256]{2,1,0:T(8,128)S(1)} %bitcast.48, f32[71,16,256]{2,1,0:T(8,128)S(1)} %get-tuple-element.43, ...), kind=kLoop, calls=%fused_computation.19 | loop fusion | flops 10027008 | bytes 10616904 | tf_op jit(solution)/shard_map/jit(_where)/select_n | solution.py:44
  27.8 0.4 fusion.85
  28.2 0.3 fusion.87
  28.5 0.2 fusion.86
  28.9 1.7 %fusion.28 = f32[72,16,256]{2,1,0:T(8,128)S(1)} fusion(f32[72,16,256]{2,1,0:T(8,128)S(1)} %fusion.10, f32[71,16,256]{2,1,0:T(8,128)S(1)} %get-tuple-element.77, f32[1,16,256]{2,1,0:T(8,128)S(1)} %get-tuple-element.79, f32[1,16,256]{2,1,0:T(8,128)S(1)} %get-tuple-element.78, f32[71,16,256]{2,1,0:T(8,128)S(1)} %get-tuple-element.76, ...), kind=kLoop, calls=%fused_computation.41 | loop fusion | flops 5603328 | bytes 9510984 | tf_op jit(solution)/shard_map/jit(_where)/select_n | solution.py:44
  30.6 0.2 fusion.77
  30.8 0.4 fusion.79
  31.2 0.3 fusion.81
  31.5 0.2 fusion.80
  31.9 1.7 %fusion.37 = f32[72,16,256]{2,1,0:T(8,128)S(1)} fusion(f32[72,16,256]{2,1,0:T(8,128)S(1)} %fusion.28, f32[71,16,256]{2,1,0:T(8,128)S(1)} %get-tuple-element.65, f32[1,16,256]{2,1,0:T(8,128)S(1)} %get-tuple-element.67, f32[1,16,256]{2,1,0:T(8,128)S(1)} %get-tuple-element.66, f32[71,16,256]{2,1,0:T(8,128)S(1)} %get-tuple-element.64, ...), kind=kLoop, calls=%fused_computation.52 | loop fusion | flops 5603328 | bytes 9510984 | tf_op jit(solution)/shard_map/jit(_where)/select_n | solution.py:44
  33.6 1.2 %fusion.71 = (f32[72,15,256]{2,1,0:T(8,128)S(1)}, f32[72,15,256]{2,1,0:T(8,128)}) fusion(f32[72,16,256]{2,1,0:T(8,128)S(1)} %fusion.37), kind=kLoop, calls=%fused_computation.112 | loop fusion | bytes 4423680 | tf_op jit(solution)/shard_map/slice | solution.py:37
  34.8 1.7 %fusion.75 = (f32[71,16,256]{2,1,0:T(8,128)}, f32[71,16,256]{2,1,0:T(8,128)}) fusion(f32[72,16,256]{2,1,0:T(8,128)S(1)} %fusion.37), kind=kLoop, calls=%fused_computation.116 | loop fusion | bytes 4653056 | tf_op jit(solution)/shard_map/jit(_roll_static)/slice | solution.py:33
  36.5 0.8 fusion.72
  37.3 0.6 fusion.76
  37.9 1.2 %fusion.74 = (f32[72,16,1]{2,1,0:T(8,128)}, f32[72,16,1]{2,1,0:T(8,128)}) fusion(f32[72,16,256]{2,1,0:T(8,128)S(1)} %fusion.37), kind=kLoop, calls=%fused_computation.115 | loop fusion | bytes 18432 | tf_op jit(solution)/shard_map/jit(_roll_static)/slice | solution.py:35
  39.1 1.8 %fusion.73 = (f32[72,16,255]{2,1,0:T(8,128)}, f32[72,16,255]{2,1,0:T(8,128)}) fusion(f32[72,16,256]{2,1,0:T(8,128)S(1)} %fusion.37), kind=kLoop, calls=%fused_computation.114 | loop fusion | bytes 4700160 | tf_op jit(solution)/shard_map/jit(_roll_static)/slice | solution.py:35
  40.9 1.3 %reshape.128 = f32[128,1152]{1,0:T(8,128)S(1)} reshape(f32[32,4,1152]{2,1,0:T(4,128)} %all-to-all-done) | data formatting | bytes 1179648 | tf_op jit(solution)/shard_map/reshape | solution.py:85
  42.3 0.4 fusion.51
  42.7 1.3 %collective-permute-start.2 = (f32[64,1024]{1,0:T(8,128)S(1)}, f32[64,1024]{1,0:T(8,128)S(1)}, u32[]{:S(2)}, u32[]{:S(2)}) collective-permute-start(f32[64,1024]{1,0:T(8,128)S(1)} %fusion.51), channel_id=1, source_target_pairs={{0,96},{1,97},{2,98},{3,99},{4,100},{5,101},{6,102},{7,103},{8,104... | collective-permute-start | bytes 786440 | tf_op jit(solution)/shard_map/ppermute | solution.py:92
  44.0 0.7 collective-permute-start.3
  44.7 0.7 collective-permute-start.4
  45.4 3.9 %fusion.46 = f32[72,16,256]{2,1,0:T(8,128)S(1)} fusion(f32[72,16,256]{2,1,0:T(8,128)S(1)} %fusion.37, f32[71,16,256]{2,1,0:T(8,128)} %get-tuple-element.53, f32[1,16,256]{2,1,0:T(8,128)} %get-tuple-element.55, f32[1,16,256]{2,1,0:T(8,128)S(1)} %get-tuple-element.54, f32[71,16,256]{2,1,0:T(8,128)} %get-tuple-element.52, f32[72,16,255]{2,1,0:T(8,128)} %get-tuple-element.49, ...), kind=kLoop, calls=%fused_computation.63 | loop fusion | flops 5603328 | bytes 9510984 | tf_op jit(solution)/shard_map/jit(_where)/select_n | solution.py:44
  49.4 5.9 %collective-permute-done.2 = f32[64,1024]{1,0:T(8,128)S(1)} collective-permute-done((f32[64,1024]{1,0:T(8,128)S(1)}, f32[64,1024]{1,0:T(8,128)S(1)}, u32[]{:S(2)}, u32[]{:S(2)}) %collective-permute-start.2) | collective-permute-done | bytes 262176 | tf_op jit(solution)/shard_map/ppermute | solution.py:92
  55.5 0.2 conditional.3
  55.8 0.7 collective-permute-start.7
  56.4 0.7 collective-permute-start.6
  57.1 1.3 %collective-permute-start.5 = (bf16[64,4,256]{2,1,0:T(4,128)(2,1)S(1)}, bf16[64,4,256]{2,1,0:T(4,128)(2,1)S(1)}, u32[]{:S(2)}, u32[]{:S(2)}) collective-permute-start(bf16[64,4,256]{2,1,0:T(4,128)(2,1)S(1)} %get-tuple-element.85), channel_id=1, source_target_pairs={{96,0},{97,1},{98,2},{99,3},{100,4},{101,5},{102,6},{103,7},{104,8... | collective-permute-start | bytes 393224 | tf_op jit(solution)/shard_map/ppermute | solution.py:108
  58.4 12.1 %collective-permute-done.5 = bf16[64,4,256]{2,1,0:T(4,128)(2,1)S(1)} collective-permute-done((bf16[64,4,256]{2,1,0:T(4,128)(2,1)S(1)}, bf16[64,4,256]{2,1,0:T(4,128)(2,1)S(1)}, u32[]{:S(2)}, u32[]{:S(2)}) %collective-permute-start.5) | collective-permute-done | bytes 131104 | tf_op jit(solution)/shard_map/ppermute | solution.py:108
  70.6 0.3 convolution_convert_fusion.1
  70.9 0.8 reshape.131
  71.7 8.4 %all-to-all-start.1 = ((bf16[32,4,1024]{2,1,0:T(4,128)(2,1)}), bf16[32,4,1024]{2,1,0:T(4,128)(2,1)S(1)}, u32[]{:S(2)}, u32[]{:S(2)}) async-start(bf16[32,4,1024]{2,1,0:T(4,128)(2,1)} %reshape.131), calls=%async_computation.1 | async-start | bytes 524288 | tf_op jit(solution)/shard_map/all_to_all | solution.py:114
  80.3 8.6 %all-to-all-done.1 = bf16[32,4,1024]{2,1,0:T(4,128)(2,1)S(1)} async-done(((bf16[32,4,1024]{2,1,0:T(4,128)(2,1)}), bf16[32,4,1024]{2,1,0:T(4,128)(2,1)S(1)}, u32[]{:S(2)}, u32[]{:S(2)}) %all-to-all-start.1) | async-done | bytes 262176 | tf_op jit(solution)/shard_map/all_to_all | solution.py:114
  89.0 0.2 fusion.49
  89.3 0.7 select_bitcast_fusion
  (53 shorter events, 1.7 us)
Async XLA Ops:
  0.6 8.6 %copy-start = (f32[1,64,16,256]{3,2,1,0:T(8,128)S(1)}, f32[1,64,16,256]{3,2,1,0:T(8,128)}, u32[]{:S(2)}) copy-start(f32[1,64,16,256]{3,2,1,0:T(8,128)} %param.11) | copy-start | bytes 3145732
  0.6 8.3 %copy-start.7 = (s32[1,64,1]{1,2,0:T(1,128)S(1)}, s32[1,64,1]{1,2,0:T(1,128)}, u32[]{:S(2)}) copy-start(s32[1,64,1]{1,2,0:T(1,128)} %param.13) | copy-start | bytes 772
  0.7 8.5 %copy-start.8 = (s32[1,64]{1,0:T(1,128)S(1)}, s32[1,64]{1,0:T(1,128)}, u32[]{:S(2)}) copy-start(s32[1,64]{1,0:T(1,128)} %param.14) | copy-start | bytes 772
  2.5 21.6 %collective-permute-start = (f32[4,17,256]{2,1,0:T(8,128)S(1)}, f32[4,17,256]{2,1,0:T(8,128)S(1)}, u32[]{:S(2)}, u32[]{:S(2)}) collective-permute-start(f32[4,17,256]{2,1,0:T(8,128)S(1)} %get-tuple-element.81), channel_id=1, source_target_pairs={{0,1},{1,2},{2,3},{3,4},{4,5},{5,6},{6,7},{7,8},{8,9},{9,10},{10,1... | collective-permute-start | bytes 208904 | tf_op jit(solution)/shard_map/ppermute | solution.py:24
  7.0 17.1 %collective-permute-start.1 = (f32[4,17,256]{2,1,0:T(8,128)S(1)}, f32[4,17,256]{2,1,0:T(8,128)S(1)}, u32[]{:S(2)}, u32[]{:S(2)}) collective-permute-start(f32[4,17,256]{2,1,0:T(8,128)S(1)} %get-tuple-element.80), channel_id=1, source_target_pairs={{1,0},{2,1},{3,2},{4,3},{5,4},{6,5},{7,6},{8,7},{9,8},{10,9},{11,1... | collective-permute-start | bytes 208904 | tf_op jit(solution)/shard_map/ppermute | solution.py:25
  16.4 24.6 %all-to-all-start = ((f32[32,4,1152]{2,1,0:T(4,128)}), f32[32,4,1152]{2,1,0:T(4,128)}, u32[]{:S(2)}, u32[]{:S(2)}) async-start(f32[32,4,1152]{2,1,0:T(4,128)} %copy.17), calls=%async_computation | async-start | bytes 1179648 | tf_op jit(solution)/shard_map/all_to_all | solution.py:84
  24.1 7.7 %copy-start.4 = (pred[72]{0:T(512)(128)(4,1)}, pred[72]{0:T(512)(128)(4,1)S(1)}, u32[]{:S(2)}) copy-start(pred[72]{0:T(512)(128)(4,1)S(1)} %compare_and_fusion) | copy-start | bytes 220
  25.7 6.2 %copy-start.1 = (f32[72,1,256]{2,0,1:T(8,128)}, f32[72,1,256]{2,0,1:T(8,128)S(1)}, u32[]{:S(2)}) copy-start(f32[72,1,256]{2,0,1:T(8,128)S(1)} %copy.30) | copy-start | bytes 221188
  42.3 3.1 %copy-start.5 = (s32[128]{0:T(128)}, s32[128]{0:T(128)S(1)}, u32[]{:S(2)}) copy-start(s32[128]{0:T(128)S(1)} %fusion.58) | copy-start | bytes 1540
  42.7 12.5 %collective-permute-start.2 = (f32[64,1024]{1,0:T(8,128)S(1)}, f32[64,1024]{1,0:T(8,128)S(1)}, u32[]{:S(2)}, u32[]{:S(2)}) collective-permute-start(f32[64,1024]{1,0:T(8,128)S(1)} %fusion.51), channel_id=1, source_target_pairs={{0,96},{1,97},{2,98},{3,99},{4,100},{5,101},{6,102},{7,103},{8,104... | collective-permute-start | bytes 786440 | tf_op jit(solution)/shard_map/ppermute | solution.py:92
  44.0 11.2 %collective-permute-start.3 = (f32[64,1024]{1,0:T(8,128)S(1)}, f32[64,1024]{1,0:T(8,128)S(1)}, u32[]{:S(2)}, u32[]{:S(2)}) collective-permute-start(f32[64,1024]{1,0:T(8,128)S(1)} %fusion.51), channel_id=1, source_target_pairs={{32,96},{33,97},{34,98},{35,99},{36,100},{37,101},{38,102},{39,103... | collective-permute-start | bytes 786440 | tf_op jit(solution)/shard_map/ppermute | solution.py:92
  44.7 10.5 %collective-permute-start.4 = (f32[64,1024]{1,0:T(8,128)S(1)}, f32[64,1024]{1,0:T(8,128)S(1)}, u32[]{:S(2)}, u32[]{:S(2)}) collective-permute-start(f32[64,1024]{1,0:T(8,128)S(1)} %fusion.51), channel_id=1, source_target_pairs={{64,96},{65,97},{66,98},{67,99},{68,100},{69,101},{70,102},{71,103... | collective-permute-start | bytes 786440 | tf_op jit(solution)/shard_map/ppermute | solution.py:92
  55.5 15.1 %copy-start.6 = (s32[128]{0:T(128)S(1)}, s32[128]{0:T(128)}, u32[]{:S(2)}) copy-start(s32[128]{0:T(128)} %copy-done.5) | copy-start | bytes 1540
  55.8 2.7 %collective-permute-start.7 = (bf16[64,4,256]{2,1,0:T(4,128)(2,1)S(1)}, bf16[64,4,256]{2,1,0:T(4,128)(2,1)S(1)}, u32[]{:S(2)}, u32[]{:S(2)}) collective-permute-start(bf16[64,4,256]{2,1,0:T(4,128)(2,1)S(1)} %get-tuple-element.85), channel_id=1, source_target_pairs={{96,64},{97,65},{98,66},{99,67},{100,68},{101,69},{102,70},{103,71... | collective-permute-start | bytes 393224 | tf_op jit(solution)/shard_map/ppermute | solution.py:108
  56.4 2.0 %collective-permute-start.6 = (bf16[64,4,256]{2,1,0:T(4,128)(2,1)S(1)}, bf16[64,4,256]{2,1,0:T(4,128)(2,1)S(1)}, u32[]{:S(2)}, u32[]{:S(2)}) collective-permute-start(bf16[64,4,256]{2,1,0:T(4,128)(2,1)S(1)} %get-tuple-element.85), channel_id=1, source_target_pairs={{96,32},{97,33},{98,34},{99,35},{100,36},{101,37},{102,38},{103,39... | collective-permute-start | bytes 393224 | tf_op jit(solution)/shard_map/ppermute | solution.py:108
  57.1 13.4 %collective-permute-start.5 = (bf16[64,4,256]{2,1,0:T(4,128)(2,1)S(1)}, bf16[64,4,256]{2,1,0:T(4,128)(2,1)S(1)}, u32[]{:S(2)}, u32[]{:S(2)}) collective-permute-start(bf16[64,4,256]{2,1,0:T(4,128)(2,1)S(1)} %get-tuple-element.85), channel_id=1, source_target_pairs={{96,0},{97,1},{98,2},{99,3},{100,4},{101,5},{102,6},{103,7},{104,8... | collective-permute-start | bytes 393224 | tf_op jit(solution)/shard_map/ppermute | solution.py:108
  71.7 17.3 %all-to-all-start.1 = ((bf16[32,4,1024]{2,1,0:T(4,128)(2,1)}), bf16[32,4,1024]{2,1,0:T(4,128)(2,1)S(1)}, u32[]{:S(2)}, u32[]{:S(2)}) async-start(bf16[32,4,1024]{2,1,0:T(4,128)(2,1)} %reshape.131), calls=%async_computation.1 | async-start | bytes 524288 | tf_op jit(solution)/shard_map/all_to_all | solution.py:114
  80.1 8.9 %copy-start.3 = (bf16[64,32,4]{0,2,1:T(4,128)(2,1)S(1)}, bf16[64,32,4]{0,2,1:T(4,128)(2,1)}, u32[]{:S(2)}) copy-start(bf16[64,32,4]{0,2,1:T(4,128)(2,1)} %get-tuple-element.82) | copy-start | bytes 49156
  80.3 9.7 %copy-start.2 = (f32[1,64,16,256]{3,2,1,0:T(8,128)}, f32[1,64,16,256]{3,2,1,0:T(8,128)S(1)}, u32[]{:S(2)}) copy-start(f32[1,64,16,256]{3,2,1,0:T(8,128)S(1)} %bitcast_dynamic-update-slice_fusion) | copy-start | bytes 3145732

commit v3 on v2

--- a/solution.py
+++ b/solution.py
@@ -2,6 +2,8 @@
 import jax.numpy as jnp
 from jax import lax
 from jax.sharding import PartitionSpec as P
+from jax.experimental import pallas as pl
+from jax.experimental.pallas import tpu as pltpu
 
 NF = 4
 NSTEPS = 4
@@ -12,12 +14,62 @@
 HIGHEST = lax.Precision.HIGHEST
 
 
+def _advance_rows(src, dst, d_ref, r0, count, out_r0, bounds):
+    lev, cols = src.shape[1], src.shape[2]
+    fields = src[pl.ds(r0, count)]
+    row_north = src[pl.ds(r0 - 1, count)]
+    row_south = src[pl.ds(r0 + 1, count)]
+    diff = d_ref[pl.ds(r0, count)]
+    level = lax.broadcasted_iota(jnp.int32, (count, lev, cols), 1)
+    col_east = pltpu.roll(fields, 1, 2)
+    col_west = pltpu.roll(fields, cols - 1, 2)
+    level_below = jnp.where(level == 0, fields, pltpu.roll(fields, 1, 1))
+    level_above = jnp.where(level == lev - 1, fields, pltpu.roll(fields, lev - 1, 1))
+    horizontal = row_north + row_south + col_east + col_west - 4.0 * fields
+    new = fields + diff * horizontal + VERTICAL * (level_below + level_above - 2.0 * fields)
+    if bounds is not None:
+        row = r0 + lax.broadcasted_iota(jnp.int32, (count, 1, 1), 0)
+        new = jnp.where((row >= bounds[0]) & (row < bounds[1]), new, 0.0)
+    dst[pl.ds(out_r0, count)] = new
+
+
+def _diffusion_kernel(bounds_ref, f_ref, d_ref, o_ref, buf_a, buf_b):
+    total = f_ref.shape[0]
+    rows = o_ref.shape[0]
+    halo = (total - rows) // 2
+    bounds = (bounds_ref[0], bounds_ref[1])
+    chunk = 5 if (total - 2) % 5 == 0 else 1
+    src = f_ref
+    targets = (buf_a, buf_b)
+    for step in range(NSTEPS - 1):
+        dst = targets[step % 2]
+        dst[0] = src[0]
+        dst[total - 1] = src[total - 1]
+
+        def one(i, carry, src=src, dst=dst):
+            r0 = 1 + i * chunk
+            _advance_rows(src, dst, d_ref, r0, chunk, r0, bounds)
+            return carry
+
+        lax.fori_loop(0, (total - 2) // chunk, one, 0)
+        src = dst
+    last = 8 if rows % 8 == 0 else 1
+
+    def final(i, carry):
+        _advance_rows(src, o_ref, d_ref, halo + i * last, last, i * last, None)
+        return carry
+
+    lax.fori_loop(0, rows // last, final, 0)
+
+
 def diffuse(layer_temp, diffusivity):
     n_bands = lax.axis_size("band")
     band = lax.axis_index("band")
     rows = layer_temp.shape[1]
     lev = layer_temp.shape[2]
+    cols = layer_temp.shape[3]
     halo = NSTEPS
+    total = rows + 2 * halo
     comb = jnp.concatenate([layer_temp[0], diffusivity[0][:, None, :]], axis=1)
     forward = [(i, i + 1) for i in range(n_bands - 1)]
     backward = [(i + 1, i) for i in range(n_bands - 1)]
@@ -25,24 +77,21 @@
     below = lax.ppermute(comb[:halo], "band", backward)
     padded = jnp.concatenate([above, comb, below], axis=0)
     fields = padded[:, :lev]
-    diff = padded[:, lev]
-    grow = band * rows - halo + jnp.arange(rows + 2 * halo, dtype=jnp.int32)
-    valid = ((grow >= 0) & (grow < n_bands * rows))[:, None, None]
-    for _ in range(NSTEPS):
-        row_north = jnp.roll(fields, 1, axis=0)
-        row_south = jnp.roll(fields, -1, axis=0)
-        col_east = jnp.roll(fields, 1, axis=2)
-        col_west = jnp.roll(fields, -1, axis=2)
-        level_below = jnp.concatenate([fields[:, :1], fields[:, :-1]], axis=1)
-        level_above = jnp.concatenate([fields[:, 1:], fields[:, -1:]], axis=1)
-        horizontal = row_north + row_south + col_east + col_west - 4.0 * fields
-        fields = (
-            fields
-            + diff[:, None, :] * horizontal
-            + VERTICAL * (level_below + level_above - 2.0 * fields)
-        )
-        fields = jnp.where(valid, fields, 0.0)
-    return fields[halo:halo + rows]
+    diff = padded[:, lev:]
+    first = jnp.where(band == 0, halo, 0)
+    stop = jnp.where(band == n_bands - 1, halo + rows, total)
+    bounds = jnp.stack([first, stop]).astype(jnp.int32)
+    return pl.pallas_call(
+        _diffusion_kernel,
+        out_shape=jax.ShapeDtypeStruct((rows, lev, cols), jnp.float32),
+        in_specs=[
+            pl.BlockSpec(memory_space=pltpu.SMEM),
+            pl.BlockSpec(memory_space=pltpu.VMEM),
+            pl.BlockSpec(memory_space=pltpu.VMEM),
+        ],
+        out_specs=pl.BlockSpec(memory_space=pltpu.VMEM),
+        scratch_shapes=[pltpu.VMEM((total, lev, cols), jnp.float32)] * 2,
+    )(bounds, fields, diff)
 
 
 def body(layer_temp, diffusivity, owner_band, block_index, remap_blocks):

time: 90.6 us -> 77.9 us (0.86)
  local copies, waits for them, and re-layouts: 15.8 us -> 4.47 us
  Pallas kernels: 0 us -> 8.92 us
  other arithmetic: 12.1 us -> 3.95 us
  starting transfers between devices: 27.9 us -> 24.9 us
  matrix products: 6.2 us -> 7.13 us
    slice x24 -> x1, local copies, waits for them, and re-layouts: 11 us -> 1.21 us  [diffuse(): fields = padded[:, :lev]]
    select_n x4 -> x0, other arithmetic: 9.21 us -> none  [diffuse(): fields = jnp.where(valid, fields, 0.0)]
    pallas_call x0 -> x1, Pallas kernels: none -> 8.92 us  [diffuse(): pl.pallas_call(_diffusion_kernel, out_shape=jax.ShapeDtypeStruct((rows, l...]
    all_to_all x1, waiting for transfers between devices: 0.01 us -> 5.84 us  [body(): received = lax.all_to_all(sending, 'band', 0, 0, tiled=True)]
    ppermute x3, waiting for transfers between devices: 5.87 us -> 0.47 us  [body(): ocean_heat = ocean_heat + lax.ppermute(partial, 'comp', [(source, last)])]
    all_to_all x1, starting transfers between devices: 8.4 us -> 4.66 us  [body(): came_back = lax.all_to_all(reply, 'band', 0, 0, tiled=True)]
    ppermute x1, starting transfers between devices: 4.5 us -> 3.42 us  [diffuse(): above = lax.ppermute(comb[rows - halo:], 'band', forward)]
    reshape x1, local copies, waits for them, and re-layouts: 1.27 us -> 0.2 us  [body(): received = received.reshape(n_bands * CAP, width + 128)]
  transfers between devices with their start and end apart: 10 -> 10, of which waited for: 3 -> 4; matrix products, arithmetic and copies ran while one was open for 31% -> 5% of each run, Pallas kernels for 0% -> 12%
where the time goes in v3:
time: 77.9 us; the launch traced here: 77.4 us
  waiting for transfers between devices  27 us (35%)
  starting transfers between devices  24.9 us (32%)
  Pallas kernels  8.92 us (11%)
  matrix products  7.13 us (9%)
  local copies, waits for them, and re-layouts  4.47 us (6%)
  other arithmetic  3.95 us (5%)
  between operations  0.94 us (1%)
    ppermute x3, waiting for transfers between devices, body(): ocean_rows = ocean_rows + lax.ppermute(returned, 'comp', [(last, target)])  12 us
    pallas_call x1, Pallas kernels, diffuse(): pl.pallas_call(_diffusion_kernel, out_shape=jax.ShapeDtypeStruct((rows, l...  8.92 us
    all_to_all x1, waiting for transfers between devices, body(): came_back = lax.all_to_all(reply, 'band', 0, 0, tiled=True)  8.68 us
    all_to_all x1, starting transfers between devices, body(): received = lax.all_to_all(sending, 'band', 0, 0, tiled=True)  8.58 us
    all_to_all x1, waiting for transfers between devices, body(): received = lax.all_to_all(sending, 'band', 0, 0, tiled=True)  5.84 us
    dot_general x1, matrix products, body(): jnp.einsum('rfc,rcd->rfd', surface_layers, weights_local, preferred_eleme...  4.76 us
    all_to_all x1, starting transfers between devices, body(): came_back = lax.all_to_all(reply, 'band', 0, 0, tiled=True)  4.66 us
    ppermute x3, starting transfers between devices, body(): ocean_heat = ocean_heat + lax.ppermute(partial, 'comp', [(source, last)])  3.47 us
  transfers between devices with their start and end apart: 10, of which 4 were waited for; matrix products, arithmetic and copies ran while one was open for 5% of the time, Pallas kernels for 12%

profile of v3, /device:TPU:1, one launch (start us, length us, event | category | flops | bytes accessed | tf_op | source)
XLA Modules:
  0.0 77.4 jit_solution(9854076805107166865)
XLA Ops:
  0.6 0.9 %fusion.4 = f32[64]{0:T(128)S(1)} fusion(s32[64]{0:T(128)} %bitcast.55), kind=kOutput, calls=%fused_computation.9 | convolution fusion | flops 274368 | bytes 512 | tf_op jit(solution)/shard_map/dot_general | solution.py:122
  1.5 0.7 fusion.17
  2.2 0.7 convert_bitcast_fusion
  2.9 4.8 %conditional.2 = (f32[64,1024]{1,0:T(8,128)S(1)}) conditional(s32[]{:T(128)} %convert_element_type.70, (f32[1,64,16,256]{3,2,1,0:T(8,128)}, bf16[64,256,256]{2,1,0:T(8,128)(2,1)}) %tuple.37, () %tuple.27), branch_computations={%region_1.0_spmd, %region_2.0_spmd} | conditional | flops 33554432 | bytes 9306120 | solution.py:108
  2.9 4.8 %fusion.1 = f32[64,4,256]{2,1,0:T(4,128)S(1)} fusion(bf16[64,256,256]{2,1,0:T(8,128)(2,1)} %get-tuple-element.31, f32[1,64,16,256]{3,2,1,0:T(8,128)} %get-tuple-element.30), kind=kOutput, calls=%fused_computation.2 | convolution fusion | flops 33554432 | bytes 8781824 | tf_op jit(solution)/shard_map/cond/branch_0_fun/rfc,rcd->rfd/dot_general | solution.py:111
  7.6 0.1 copy.20
  7.7 0.0 copy-start.3
  7.7 0.0 copy-start
  7.7 0.1 broadcast_in_dim.12
  7.8 0.6 fusion.7
  8.4 1.2 %copy.17 = f32[32,4,1152]{2,1,0:T(4,128)} copy(f32[32,4,1152]{2,0,1:T(8,128)S(1)} %fusion.7) | data formatting | bytes 1179648 | tf_op jit(solution)/shard_map/rk,rx->kx/dot_general | solution.py:131
  9.6 8.6 %all-to-all-start = ((f32[32,4,1152]{2,1,0:T(4,128)}), f32[32,4,1152]{2,1,0:T(4,128)S(1)}, u32[]{:S(2)}, u32[]{:S(2)}) async-start(f32[32,4,1152]{2,1,0:T(4,128)} %copy.17), calls=%async_computation | async-start | bytes 1179648 | tf_op jit(solution)/shard_map/all_to_all | solution.py:133
  18.3 2.1 %collective-permute-start.1 = (f32[4,17,256]{2,1,0:T(8,128)S(1)}, f32[4,17,256]{2,1,0:T(8,128)S(1)}, u32[]{:S(2)}, u32[]{:S(2)}) collective-permute-start(f32[4,17,256]{2,1,0:T(8,128)S(1)} %get-tuple-element.37), channel_id=1, source_target_pairs={{1,0},{2,1},{3,2},{4,3},{5,4},{6,5},{7,6},{8,7},{9,8},{10,9},{11,1... | collective-permute-start | bytes 208904 | tf_op jit(solution)/shard_map/ppermute | solution.py:77
  20.5 3.4 %collective-permute-start = (f32[4,17,256]{2,1,0:T(8,128)S(1)}, f32[4,17,256]{2,1,0:T(8,128)S(1)}, u32[]{:S(2)}, u32[]{:S(2)}) collective-permute-start(f32[4,17,256]{2,1,0:T(8,128)S(1)} %get-tuple-element.36), channel_id=1, source_target_pairs={{0,1},{1,2},{2,3},{3,4},{4,5},{5,6},{6,7},{7,8},{8,9},{9,10},{10,1... | collective-permute-start | bytes 208904 | tf_op jit(solution)/shard_map/ppermute | solution.py:76
  23.9 0.6 pad_add_fusion.bounds_ref
  24.5 5.8 %all-to-all-done = f32[32,4,1152]{2,1,0:T(4,128)S(1)} async-done(((f32[32,4,1152]{2,1,0:T(4,128)}), f32[32,4,1152]{2,1,0:T(4,128)S(1)}, u32[]{:S(2)}, u32[]{:S(2)}) %all-to-all-start) | async-done | bytes 589856 | tf_op jit(solution)/shard_map/all_to_all | solution.py:133
  30.4 0.2 reshape.121
  30.6 0.1 fusion.12
  30.7 0.4 fusion.5
  31.1 0.7 collective-permute-start.4
  31.8 0.7 collective-permute-start.3
  32.4 2.1 %collective-permute-start.2 = (f32[64,1024]{1,0:T(8,128)S(1)}, f32[64,1024]{1,0:T(8,128)S(1)}, u32[]{:S(2)}, u32[]{:S(2)}) collective-permute-start(f32[64,1024]{1,0:T(8,128)S(1)} %fusion.5), channel_id=1, source_target_pairs={{0,96},{1,97},{2,98},{3,99},{4,100},{5,101},{6,102},{7,103},{8,104... | collective-permute-start | bytes 786440 | tf_op jit(solution)/shard_map/ppermute | solution.py:141
  34.6 0.0 collective-permute-done.1
  34.6 0.2 pad_maximum_fusion
  34.7 1.2 %slice.56.f_ref = f32[72,16,256]{2,1,0:T(8,128)} slice(f32[72,17,256]{2,1,0:T(8,128)S(1)} %pad_maximum_fusion), slice={[0:72], [0:16], [0:256]} | slice | bytes 2359296 | tf_op jit(solution)/shard_map/slice | solution.py:79
  36.0 0.7 pad_maximum_fusion.3.d_ref
  36.6 8.9 %shard_map.68 = f32[64,16,256]{2,1,0:T(8,128)} custom-call(s32[2]{0:T(128)} %pad_add_fusion.bounds_ref, f32[72,16,256]{2,1,0:T(8,128)} %slice.56.f_ref, f32[72,1,256]{2,1,0:T(1,128)} %pad_maximum_fusion.3.d_ref), custom_call_target="tpu_custom_call" | custom-call | tf_op jit(solution)/shard_map/pallas_call | solution.py:84
  45.6 0.0 collective-permute-done.4
  45.6 0.5 collective-permute-done.2
  46.0 0.1 multiply_select_fusion
  46.1 0.1 reshape.122
  46.2 0.5 copy-done.1
  46.8 0.1 fusion.11
  46.9 0.1 conditional.3
  46.9 0.7 collective-permute-start.7
  47.6 0.7 collective-permute-start.6
  48.3 1.3 %collective-permute-start.5 = (bf16[64,4,256]{2,1,0:T(4,128)(2,1)S(1)}, bf16[64,4,256]{2,1,0:T(4,128)(2,1)S(1)}, u32[]{:S(2)}, u32[]{:S(2)}) collective-permute-start(bf16[64,4,256]{2,1,0:T(4,128)(2,1)S(1)} %get-tuple-element.41), channel_id=1, source_target_pairs={{96,0},{97,1},{98,2},{99,3},{100,4},{101,5},{102,6},{103,7},{104,8... | collective-permute-start | bytes 393224 | tf_op jit(solution)/shard_map/ppermute | solution.py:157
  49.6 12.0 %collective-permute-done.5 = bf16[64,4,256]{2,1,0:T(4,128)(2,1)S(1)} collective-permute-done((bf16[64,4,256]{2,1,0:T(4,128)(2,1)S(1)}, bf16[64,4,256]{2,1,0:T(4,128)(2,1)S(1)}, u32[]{:S(2)}, u32[]{:S(2)}) %collective-permute-start.5) | collective-permute-done | bytes 131104 | tf_op jit(solution)/shard_map/ppermute | solution.py:157
  61.7 0.3 convolution_convert_fusion.1
  62.0 0.8 %reshape.124 = bf16[32,4,1024]{2,1,0:T(4,128)(2,1)} reshape(bf16[128,1024]{1,0:T(8,128)(2,1)S(1)} %convolution_convert_fusion.1) | data formatting | bytes 524288 | tf_op jit(solution)/shard_map/reshape | solution.py:162
  62.8 4.7 %all-to-all-start.1 = ((bf16[32,4,1024]{2,1,0:T(4,128)(2,1)}), bf16[32,4,1024]{2,1,0:T(4,128)(2,1)S(1)}, u32[]{:S(2)}, u32[]{:S(2)}) async-start(bf16[32,4,1024]{2,1,0:T(4,128)(2,1)} %reshape.124), calls=%async_computation.1 | async-start | bytes 524288 | tf_op jit(solution)/shard_map/all_to_all | solution.py:163
  67.4 0.1 copy.30
  67.5 0.1 bitcast_dynamic-update-slice_fusion
  67.6 0.0 copy-start.2
  67.6 8.7 %all-to-all-done.1 = bf16[32,4,1024]{2,1,0:T(4,128)(2,1)S(1)} async-done(((bf16[32,4,1024]{2,1,0:T(4,128)(2,1)}), bf16[32,4,1024]{2,1,0:T(4,128)(2,1)S(1)}, u32[]{:S(2)}, u32[]{:S(2)}) %all-to-all-start.1) | async-done | bytes 262176 | tf_op jit(solution)/shard_map/all_to_all | solution.py:163
  76.3 0.2 fusion.3
  76.6 0.1 reshape.125
  76.6 0.7 select_bitcast_fusion
  (16 shorter events, 0.2 us)
Async XLA Ops:
  7.7 10.5 %copy-start.3 = (f32[1,64,256]{2,1,0:T(8,128)S(1)}, f32[1,64,256]{2,1,0:T(8,128)}, u32[]{:S(2)}) copy-start(f32[1,64,256]{2,1,0:T(8,128)} %param.12) | copy-start | bytes 196612
  7.7 10.6 %copy-start = (f32[1,64,16,256]{3,2,1,0:T(8,128)S(1)}, f32[1,64,16,256]{3,2,1,0:T(8,128)}, u32[]{:S(2)}) copy-start(f32[1,64,16,256]{3,2,1,0:T(8,128)} %param.11) | copy-start | bytes 3145732
  9.6 20.7 %all-to-all-start = ((f32[32,4,1152]{2,1,0:T(4,128)}), f32[32,4,1152]{2,1,0:T(4,128)S(1)}, u32[]{:S(2)}, u32[]{:S(2)}) async-start(f32[32,4,1152]{2,1,0:T(4,128)} %copy.17), calls=%async_computation | async-start | bytes 1179648 | tf_op jit(solution)/shard_map/all_to_all | solution.py:133
  18.3 16.2 %collective-permute-start.1 = (f32[4,17,256]{2,1,0:T(8,128)S(1)}, f32[4,17,256]{2,1,0:T(8,128)S(1)}, u32[]{:S(2)}, u32[]{:S(2)}) collective-permute-start(f32[4,17,256]{2,1,0:T(8,128)S(1)} %get-tuple-element.37), channel_id=1, source_target_pairs={{1,0},{2,1},{3,2},{4,3},{5,4},{6,5},{7,6},{8,7},{9,8},{10,9},{11,1... | collective-permute-start | bytes 208904 | tf_op jit(solution)/shard_map/ppermute | solution.py:77
  20.5 14.1 %collective-permute-start = (f32[4,17,256]{2,1,0:T(8,128)S(1)}, f32[4,17,256]{2,1,0:T(8,128)S(1)}, u32[]{:S(2)}, u32[]{:S(2)}) collective-permute-start(f32[4,17,256]{2,1,0:T(8,128)S(1)} %get-tuple-element.36), channel_id=1, source_target_pairs={{0,1},{1,2},{2,3},{3,4},{4,5},{5,6},{6,7},{7,8},{8,9},{9,10},{10,1... | collective-permute-start | bytes 208904 | tf_op jit(solution)/shard_map/ppermute | solution.py:76
  31.1 14.5 %collective-permute-start.4 = (f32[64,1024]{1,0:T(8,128)S(1)}, f32[64,1024]{1,0:T(8,128)S(1)}, u32[]{:S(2)}, u32[]{:S(2)}) collective-permute-start(f32[64,1024]{1,0:T(8,128)S(1)} %fusion.5), channel_id=1, source_target_pairs={{64,96},{65,97},{66,98},{67,99},{68,100},{69,101},{70,102},{71,103... | collective-permute-start | bytes 786440 | tf_op jit(solution)/shard_map/ppermute | solution.py:141
  31.8 13.8 %collective-permute-start.3 = (f32[64,1024]{1,0:T(8,128)S(1)}, f32[64,1024]{1,0:T(8,128)S(1)}, u32[]{:S(2)}, u32[]{:S(2)}) collective-permute-start(f32[64,1024]{1,0:T(8,128)S(1)} %fusion.5), channel_id=1, source_target_pairs={{32,96},{33,97},{34,98},{35,99},{36,100},{37,101},{38,102},{39,103... | collective-permute-start | bytes 786440 | tf_op jit(solution)/shard_map/ppermute | solution.py:141
  32.4 13.6 %collective-permute-start.2 = (f32[64,1024]{1,0:T(8,128)S(1)}, f32[64,1024]{1,0:T(8,128)S(1)}, u32[]{:S(2)}, u32[]{:S(2)}) collective-permute-start(f32[64,1024]{1,0:T(8,128)S(1)} %fusion.5), channel_id=1, source_target_pairs={{0,96},{1,97},{2,98},{3,99},{4,100},{5,101},{6,102},{7,103},{8,104... | collective-permute-start | bytes 786440 | tf_op jit(solution)/shard_map/ppermute | solution.py:141
  45.6 1.2 %copy-start.1 = (f32[64,16,256]{2,1,0:T(8,128)S(1)}, f32[64,16,256]{2,1,0:T(8,128)}, u32[]{:S(2)}) copy-start(f32[64,16,256]{2,1,0:T(8,128)} %shard_map.68) | copy-start | bytes 3145732
  46.9 2.7 %collective-permute-start.7 = (bf16[64,4,256]{2,1,0:T(4,128)(2,1)S(1)}, bf16[64,4,256]{2,1,0:T(4,128)(2,1)S(1)}, u32[]{:S(2)}, u32[]{:S(2)}) collective-permute-start(bf16[64,4,256]{2,1,0:T(4,128)(2,1)S(1)} %get-tuple-element.41), channel_id=1, source_target_pairs={{96,64},{97,65},{98,66},{99,67},{100,68},{101,69},{102,70},{103,71... | collective-permute-start | bytes 393224 | tf_op jit(solution)/shard_map/ppermute | solution.py:157
  47.6 2.0 %collective-permute-start.6 = (bf16[64,4,256]{2,1,0:T(4,128)(2,1)S(1)}, bf16[64,4,256]{2,1,0:T(4,128)(2,1)S(1)}, u32[]{:S(2)}, u32[]{:S(2)}) collective-permute-start(bf16[64,4,256]{2,1,0:T(4,128)(2,1)S(1)} %get-tuple-element.41), channel_id=1, source_target_pairs={{96,32},{97,33},{98,34},{99,35},{100,36},{101,37},{102,38},{103,39... | collective-permute-start | bytes 393224 | tf_op jit(solution)/shard_map/ppermute | solution.py:157
  48.3 13.3 %collective-permute-start.5 = (bf16[64,4,256]{2,1,0:T(4,128)(2,1)S(1)}, bf16[64,4,256]{2,1,0:T(4,128)(2,1)S(1)}, u32[]{:S(2)}, u32[]{:S(2)}) collective-permute-start(bf16[64,4,256]{2,1,0:T(4,128)(2,1)S(1)} %get-tuple-element.41), channel_id=1, source_target_pairs={{96,0},{97,1},{98,2},{99,3},{100,4},{101,5},{102,6},{103,7},{104,8... | collective-permute-start | bytes 393224 | tf_op jit(solution)/shard_map/ppermute | solution.py:157
  62.8 13.6 %all-to-all-start.1 = ((bf16[32,4,1024]{2,1,0:T(4,128)(2,1)}), bf16[32,4,1024]{2,1,0:T(4,128)(2,1)S(1)}, u32[]{:S(2)}, u32[]{:S(2)}) async-start(bf16[32,4,1024]{2,1,0:T(4,128)(2,1)} %reshape.124), calls=%async_computation.1 | async-start | bytes 524288 | tf_op jit(solution)/shard_map/all_to_all | solution.py:163
  67.6 9.7 %copy-start.2 = (f32[1,64,16,256]{3,2,1,0:T(8,128)}, f32[1,64,16,256]{3,2,1,0:T(8,128)S(1)}, u32[]{:S(2)}) copy-start(f32[1,64,16,256]{3,2,1,0:T(8,128)S(1)} %bitcast_dynamic-update-slice_fusion) | copy-start | bytes 3145732

commit v4 on v3

--- a/solution.py
+++ b/solution.py
@@ -12,6 +12,7 @@
 COUPLING = 0.25
 VERTICAL = 0.15
 HIGHEST = lax.Precision.HIGHEST
+LINK = jnp.float16
 
 
 def _advance_rows(src, dst, d_ref, r0, count, out_r0, bounds):
@@ -129,19 +130,20 @@
     index_lanes = jnp.broadcast_to(block_index[0].astype(jnp.float32)[:, None], (rows, 128))
     payload = jnp.concatenate([flux.reshape(rows, width), index_lanes], axis=1)
     sending = jnp.einsum("rk,rx->kx", selector, payload, precision=HIGHEST)
-    sending = sending.reshape(n_bands, CAP, width + 128)
+    sending = sending.reshape(n_bands, CAP, width + 128).astype(LINK)
     received = lax.all_to_all(sending, "band", 0, 0, tiled=True)
-    received = received.reshape(n_bands * CAP, width + 128)
+    received = received.reshape(n_bands * CAP, width + 128).astype(jnp.float32)
     got_index = received[:, width].astype(jnp.int32)
     match = (got_index[:, None] == positions[None, :]).astype(jnp.float32)
     partial = jnp.einsum("kr,kx->rx", match, received[:, :width], precision=HIGHEST)
     last = n_sections - 1
-    ocean_heat = partial
+    scaled = (COUPLING * partial).astype(LINK)
+    heating = scaled.astype(jnp.float32)
     for source in range(last):
-        ocean_heat = ocean_heat + lax.ppermute(partial, "comp", [(source, last)])
+        heating = heating + lax.ppermute(scaled, "comp", [(source, last)]).astype(jnp.float32)
 
     fields = diffuse(layer_temp, diffusivity)
-    heating = jnp.where(is_ocean, COUPLING * ocean_heat, 0.0).reshape(rows, NF, cols)
+    heating = jnp.where(is_ocean, heating, 0.0).reshape(rows, NF, cols)
     temp_out = fields.at[:, :NF].add(heating)
     sea_surface = temp_out[:, :NF].astype(jnp.bfloat16)
     returned = lax.cond(

time: 77.9 us -> 71.5 us (0.918)
  waiting for transfers between devices: 27 us -> 20.3 us
  other arithmetic: 3.95 us -> 5 us
  local copies, waits for them, and re-layouts: 4.47 us -> 3.53 us
    ppermute x3, waiting for transfers between devices: 12 us -> 8.75 us  [body(): ocean_rows = ocean_rows + lax.ppermute(returned, 'comp', [(last, target)])]
    all_to_all x1, waiting for transfers between devices: 5.84 us -> 2.9 us  [body(): received = lax.all_to_all(sending, 'band', 0, 0, tiled=True)]
    dot_general x1 -> x0, local copies, waits for them, and re-layouts: 1.2 us -> none  [body(): sending = jnp.einsum('rk,rx->kx', selector, payload, precision=HIGHEST)]
    convert_element_type x1, other arithmetic: 0.08 us -> 1.11 us  [body(): sea_surface = temp_out[:, :NF].astype(jnp.bfloat16)]
    convert_element_type x0 -> x1, local copies, waits for them, and re-layouts: none -> 0.91 us  [body(): sending = sending.reshape(n_bands, CAP, width + 128).astype(LINK)]
  transfers between devices with their start and end apart: 10 -> 10, of which waited for: 4 -> 3; matrix products, arithmetic and copies ran while one was open for 5% -> 5% of each run, Pallas kernels for 12% -> 13%
where the time goes in v4:
time: 71.5 us; the launch traced here: 71 us
  starting transfers between devices  25.1 us (35%)
  waiting for transfers between devices  20.3 us (28%)
  Pallas kernels  8.92 us (12%)
  matrix products  7.1 us (10%)
  other arithmetic  5 us (7%)
  local copies, waits for them, and re-layouts  3.53 us (5%)
  between operations  0.95 us (1%)
    pallas_call x1, Pallas kernels, diffuse(): pl.pallas_call(_diffusion_kernel, out_shape=jax.ShapeDtypeStruct((rows, l...  8.92 us
    ppermute x3, waiting for transfers between devices, body(): ocean_rows = ocean_rows + lax.ppermute(returned, 'comp', [(last, target)])  8.75 us
    all_to_all x1, waiting for transfers between devices, body(): came_back = lax.all_to_all(reply, 'band', 0, 0, tiled=True)  8.65 us
    all_to_all x1, starting transfers between devices, body(): received = lax.all_to_all(sending, 'band', 0, 0, tiled=True)  8.58 us
    all_to_all x1, starting transfers between devices, body(): came_back = lax.all_to_all(reply, 'band', 0, 0, tiled=True)  4.76 us
    dot_general x1, matrix products, body(): jnp.einsum('rfc,rcd->rfd', surface_layers, weights_local, preferred_eleme...  4.76 us
    ppermute x3, starting transfers between devices, body(): lax.ppermute(scaled, 'comp', [(source, last)]).astype(jnp.float32)  3.46 us
    ppermute x1, starting transfers between devices, diffuse(): above = lax.ppermute(comb[rows - halo:], 'band', forward)  3.42 us
  transfers between devices with their start and end apart: 10, of which 3 were waited for; matrix products, arithmetic and copies ran while one was open for 5% of the time, Pallas kernels for 13%

profile of v4, /device:TPU:1, one launch (start us, length us, event | category | flops | bytes accessed | tf_op | source)
XLA Modules:
  0.0 71.0 jit_solution(6417070148003963333)
XLA Ops:
  0.6 0.9 %fusion.5 = f32[64]{0:T(128)S(1)} fusion(s32[64]{0:T(128)} %bitcast.55), kind=kOutput, calls=%fused_computation.12 | convolution fusion | flops 274368 | bytes 512 | tf_op jit(solution)/shard_map/dot_general | solution.py:123
  1.5 0.7 fusion.15
  2.2 0.7 convert_bitcast_fusion
  2.9 4.8 %conditional.2 = (f32[64,1024]{1,0:T(8,128)S(1)}) conditional(s32[]{:T(128)} %convert_element_type.89, (f32[1,64,16,256]{3,2,1,0:T(8,128)}, bf16[64,256,256]{2,1,0:T(8,128)(2,1)}) %tuple.37, () %tuple.27), branch_computations={%region_1.0_spmd, %region_2.0_spmd} | conditional | flops 33554432 | bytes 9306120 | solution.py:109
  2.9 4.8 %fusion.1 = f32[64,4,256]{2,1,0:T(4,128)S(1)} fusion(bf16[64,256,256]{2,1,0:T(8,128)(2,1)} %get-tuple-element.31, f32[1,64,16,256]{3,2,1,0:T(8,128)} %get-tuple-element.30), kind=kOutput, calls=%fused_computation.2 | convolution fusion | flops 33554432 | bytes 8781824 | tf_op jit(solution)/shard_map/cond/branch_0_fun/rfc,rcd->rfd/dot_general | solution.py:112
  7.6 0.1 copy.20
  7.7 0.0 copy-start.3
  7.7 0.0 copy-start
  7.7 0.1 broadcast_in_dim.12
  7.8 0.6 convolution_convert_fusion.1
  8.4 0.9 %copy.17 = f16[32,4,1152]{2,1,0:T(4,128)(2,1)} copy(f16[32,4,1152]{2,0,1:T(8,128)(2,1)S(1)} %convolution_convert_fusion.1) | data formatting | bytes 589824 | tf_op jit(solution)/shard_map/convert_element_type | solution.py:133
  9.3 8.6 %all-to-all-start = ((f16[32,4,1152]{2,1,0:T(4,128)(2,1)}), f16[32,4,1152]{2,1,0:T(4,128)(2,1)S(1)}, u32[]{:S(2)}, u32[]{:S(2)}) async-start(f16[32,4,1152]{2,1,0:T(4,128)(2,1)} %copy.17), calls=%async_computation | async-start | bytes 589824 | tf_op jit(solution)/shard_map/all_to_all | solution.py:134
  18.0 2.1 %collective-permute-start.1 = (f32[4,17,256]{2,1,0:T(8,128)S(1)}, f32[4,17,256]{2,1,0:T(8,128)S(1)}, u32[]{:S(2)}, u32[]{:S(2)}) collective-permute-start(f32[4,17,256]{2,1,0:T(8,128)S(1)} %get-tuple-element.37), channel_id=1, source_target_pairs={{1,0},{2,1},{3,2},{4,3},{5,4},{6,5},{7,6},{8,7},{9,8},{10,9},{11,1... | collective-permute-start | bytes 208904 | tf_op jit(solution)/shard_map/ppermute | solution.py:78
  20.2 3.4 %collective-permute-start = (f32[4,17,256]{2,1,0:T(8,128)S(1)}, f32[4,17,256]{2,1,0:T(8,128)S(1)}, u32[]{:S(2)}, u32[]{:S(2)}) collective-permute-start(f32[4,17,256]{2,1,0:T(8,128)S(1)} %get-tuple-element.36), channel_id=1, source_target_pairs={{0,1},{1,2},{2,3},{3,4},{4,5},{5,6},{6,7},{7,8},{8,9},{9,10},{10,1... | collective-permute-start | bytes 208904 | tf_op jit(solution)/shard_map/ppermute | solution.py:77
  23.6 0.6 pad_add_fusion.bounds_ref
  24.2 2.9 %all-to-all-done = f16[32,4,1152]{2,1,0:T(4,128)(2,1)S(1)} async-done(((f16[32,4,1152]{2,1,0:T(4,128)(2,1)}), f16[32,4,1152]{2,1,0:T(4,128)(2,1)S(1)}, u32[]{:S(2)}, u32[]{:S(2)}) %all-to-all-start) | async-done | bytes 294944 | tf_op jit(solution)/shard_map/all_to_all | solution.py:134
  27.1 0.1 reshape.121
  27.2 0.1 convert_reduce_fusion
  27.3 0.4 fusion.4
  27.7 0.7 collective-permute-start.4
  28.4 0.7 collective-permute-start.3
  29.1 2.1 %collective-permute-start.2 = (f16[64,1024]{1,0:T(8,128)(2,1)S(1)}, f16[64,1024]{1,0:T(8,128)(2,1)S(1)}, u32[]{:S(2)}, u32[]{:S(2)}) collective-permute-start(f16[64,1024]{1,0:T(8,128)(2,1)S(1)} %fusion.4), channel_id=1, source_target_pairs={{0,96},{1,97},{2,98},{3,99},{4,100},{5,101},{6,102},{7,103},{8,104... | collective-permute-start | bytes 393224 | tf_op jit(solution)/shard_map/ppermute | solution.py:143
  31.2 0.0 collective-permute-done.1
  31.2 0.2 pad_maximum_fusion
  31.4 1.2 %slice.60.f_ref = f32[72,16,256]{2,1,0:T(8,128)} slice(f32[72,17,256]{2,1,0:T(8,128)S(1)} %pad_maximum_fusion), slice={[0:72], [0:16], [0:256]} | slice | bytes 2359296 | tf_op jit(solution)/shard_map/slice | solution.py:80
  32.6 0.7 pad_maximum_fusion.3.d_ref
  33.3 8.9 %shard_map.68 = f32[64,16,256]{2,1,0:T(8,128)} custom-call(s32[2]{0:T(128)} %pad_add_fusion.bounds_ref, f32[72,16,256]{2,1,0:T(8,128)} %slice.60.f_ref, f32[72,1,256]{2,1,0:T(1,128)} %pad_maximum_fusion.3.d_ref), custom_call_target="tpu_custom_call" | custom-call | tf_op jit(solution)/shard_map/pallas_call | solution.py:85
  42.2 0.1 add_select_fusion
  42.3 0.1 reshape.122
  42.4 1.1 %fusion.10 = bf16[64,4,256]{2,1,0:T(4,128)(2,1)S(1)} fusion(f32[64,4,256]{2,1,0:T(4,128)S(1)} %reshape.122, f32[64,16,256]{2,1,0:T(8,128)} %shard_map.68), kind=kLoop, calls=%fused_computation.28 | loop fusion | flops 131072 | bytes 655360 | tf_op jit(solution)/shard_map/convert_element_type | solution.py:148
  43.5 0.1 conditional.3
  43.6 0.0 copy-start.1
  43.6 0.8 %collective-permute-start.7 = (bf16[64,4,256]{2,1,0:T(4,128)(2,1)S(1)}, bf16[64,4,256]{2,1,0:T(4,128)(2,1)S(1)}, u32[]{:S(2)}, u32[]{:S(2)}) collective-permute-start(bf16[64,4,256]{2,1,0:T(4,128)(2,1)S(1)} %get-tuple-element.41), channel_id=1, source_target_pairs={{96,64},{97,65},{98,66},{99,67},{100,68},{101,69},{102,70},{103,71... | collective-permute-start | bytes 393224 | tf_op jit(solution)/shard_map/ppermute | solution.py:159
  44.4 0.7 collective-permute-start.6
  45.1 1.3 %collective-permute-start.5 = (bf16[64,4,256]{2,1,0:T(4,128)(2,1)S(1)}, bf16[64,4,256]{2,1,0:T(4,128)(2,1)S(1)}, u32[]{:S(2)}, u32[]{:S(2)}) collective-permute-start(bf16[64,4,256]{2,1,0:T(4,128)(2,1)S(1)} %get-tuple-element.41), channel_id=1, source_target_pairs={{96,0},{97,1},{98,2},{99,3},{100,4},{101,5},{102,6},{103,7},{104,8... | collective-permute-start | bytes 393224 | tf_op jit(solution)/shard_map/ppermute | solution.py:159
  46.4 0.0 collective-permute-done.7
  46.4 0.0 collective-permute-done.6
  46.4 8.7 %collective-permute-done.5 = bf16[64,4,256]{2,1,0:T(4,128)(2,1)S(1)} collective-permute-done((bf16[64,4,256]{2,1,0:T(4,128)(2,1)S(1)}, bf16[64,4,256]{2,1,0:T(4,128)(2,1)S(1)}, u32[]{:S(2)}, u32[]{:S(2)}) %collective-permute-start.5) | collective-permute-done | bytes 131104 | tf_op jit(solution)/shard_map/ppermute | solution.py:159
  55.2 0.3 convolution_convert_fusion.2
  55.5 0.8 %reshape.124 = bf16[32,4,1024]{2,1,0:T(4,128)(2,1)} reshape(bf16[128,1024]{1,0:T(8,128)(2,1)S(1)} %convolution_convert_fusion.2) | data formatting | bytes 524288 | tf_op jit(solution)/shard_map/reshape | solution.py:164
  56.3 4.8 %all-to-all-start.1 = ((bf16[32,4,1024]{2,1,0:T(4,128)(2,1)}), bf16[32,4,1024]{2,1,0:T(4,128)(2,1)S(1)}, u32[]{:S(2)}, u32[]{:S(2)}) async-start(bf16[32,4,1024]{2,1,0:T(4,128)(2,1)} %reshape.124), calls=%async_computation.1 | async-start | bytes 524288 | tf_op jit(solution)/shard_map/all_to_all | solution.py:165
  61.1 0.1 copy.30
  61.2 0.1 bitcast_dynamic-update-slice_fusion
  61.3 0.0 copy-start.2
  61.3 8.6 %all-to-all-done.1 = bf16[32,4,1024]{2,1,0:T(4,128)(2,1)S(1)} async-done(((bf16[32,4,1024]{2,1,0:T(4,128)(2,1)}), bf16[32,4,1024]{2,1,0:T(4,128)(2,1)S(1)}, u32[]{:S(2)}, u32[]{:S(2)}) %all-to-all-start.1) | async-done | bytes 262176 | tf_op jit(solution)/shard_map/all_to_all | solution.py:165
  69.9 0.2 fusion.3
  70.2 0.1 reshape.125
  70.2 0.7 %select_bitcast_fusion = bf16[1,64,4,256]{3,2,1,0:T(4,128)(2,1)} fusion(bf16[64,4,256]{2,1,0:T(4,128)(2,1)S(1)} %get-tuple-element.41, bf16[64,4,256]{2,1,0:T(4,128)(2,1)S(1)} %reshape.125, pred[]{:T(512)S(6)} %eq.62), kind=kLoop, calls=%fused_computation.21 | loop fusion | flops 65536 | bytes 393217 | tf_op jit(solution)/shard_map/broadcast_in_dim | solution.py:171
  (16 shorter events, 0.2 us)
Async XLA Ops:
  7.7 10.2 %copy-start.3 = (f32[1,64,256]{2,1,0:T(8,128)S(1)}, f32[1,64,256]{2,1,0:T(8,128)}, u32[]{:S(2)}) copy-start(f32[1,64,256]{2,1,0:T(8,128)} %param.12) | copy-start | bytes 196612
  7.7 10.3 %copy-start = (f32[1,64,16,256]{3,2,1,0:T(8,128)S(1)}, f32[1,64,16,256]{3,2,1,0:T(8,128)}, u32[]{:S(2)}) copy-start(f32[1,64,16,256]{3,2,1,0:T(8,128)} %param.11) | copy-start | bytes 3145732
  9.3 17.8 %all-to-all-start = ((f16[32,4,1152]{2,1,0:T(4,128)(2,1)}), f16[32,4,1152]{2,1,0:T(4,128)(2,1)S(1)}, u32[]{:S(2)}, u32[]{:S(2)}) async-start(f16[32,4,1152]{2,1,0:T(4,128)(2,1)} %copy.17), calls=%async_computation | async-start | bytes 589824 | tf_op jit(solution)/shard_map/all_to_all | solution.py:134
  18.0 13.2 %collective-permute-start.1 = (f32[4,17,256]{2,1,0:T(8,128)S(1)}, f32[4,17,256]{2,1,0:T(8,128)S(1)}, u32[]{:S(2)}, u32[]{:S(2)}) collective-permute-start(f32[4,17,256]{2,1,0:T(8,128)S(1)} %get-tuple-element.37), channel_id=1, source_target_pairs={{1,0},{2,1},{3,2},{4,3},{5,4},{6,5},{7,6},{8,7},{9,8},{10,9},{11,1... | collective-permute-start | bytes 208904 | tf_op jit(solution)/shard_map/ppermute | solution.py:78
  20.2 11.0 %collective-permute-start = (f32[4,17,256]{2,1,0:T(8,128)S(1)}, f32[4,17,256]{2,1,0:T(8,128)S(1)}, u32[]{:S(2)}, u32[]{:S(2)}) collective-permute-start(f32[4,17,256]{2,1,0:T(8,128)S(1)} %get-tuple-element.36), channel_id=1, source_target_pairs={{0,1},{1,2},{2,3},{3,4},{4,5},{5,6},{6,7},{7,8},{8,9},{9,10},{10,1... | collective-permute-start | bytes 208904 | tf_op jit(solution)/shard_map/ppermute | solution.py:77
  27.7 14.5 %collective-permute-start.4 = (f16[64,1024]{1,0:T(8,128)(2,1)S(1)}, f16[64,1024]{1,0:T(8,128)(2,1)S(1)}, u32[]{:S(2)}, u32[]{:S(2)}) collective-permute-start(f16[64,1024]{1,0:T(8,128)(2,1)S(1)} %fusion.4), channel_id=1, source_target_pairs={{64,96},{65,97},{66,98},{67,99},{68,100},{69,101},{70,102},{71,103... | collective-permute-start | bytes 393224 | tf_op jit(solution)/shard_map/ppermute | solution.py:143
  28.4 13.8 %collective-permute-start.3 = (f16[64,1024]{1,0:T(8,128)(2,1)S(1)}, f16[64,1024]{1,0:T(8,128)(2,1)S(1)}, u32[]{:S(2)}, u32[]{:S(2)}) collective-permute-start(f16[64,1024]{1,0:T(8,128)(2,1)S(1)} %fusion.4), channel_id=1, source_target_pairs={{32,96},{33,97},{34,98},{35,99},{36,100},{37,101},{38,102},{39,103... | collective-permute-start | bytes 393224 | tf_op jit(solution)/shard_map/ppermute | solution.py:143
  29.1 13.1 %collective-permute-start.2 = (f16[64,1024]{1,0:T(8,128)(2,1)S(1)}, f16[64,1024]{1,0:T(8,128)(2,1)S(1)}, u32[]{:S(2)}, u32[]{:S(2)}) collective-permute-start(f16[64,1024]{1,0:T(8,128)(2,1)S(1)} %fusion.4), channel_id=1, source_target_pairs={{0,96},{1,97},{2,98},{3,99},{4,100},{5,101},{6,102},{7,103},{8,104... | collective-permute-start | bytes 393224 | tf_op jit(solution)/shard_map/ppermute | solution.py:143
  43.6 17.5 %copy-start.1 = (f32[64,16,256]{2,1,0:T(8,128)S(1)}, f32[64,16,256]{2,1,0:T(8,128)}, u32[]{:S(2)}) copy-start(f32[64,16,256]{2,1,0:T(8,128)} %shard_map.68) | copy-start | bytes 3145732
  43.6 2.8 %collective-permute-start.7 = (bf16[64,4,256]{2,1,0:T(4,128)(2,1)S(1)}, bf16[64,4,256]{2,1,0:T(4,128)(2,1)S(1)}, u32[]{:S(2)}, u32[]{:S(2)}) collective-permute-start(bf16[64,4,256]{2,1,0:T(4,128)(2,1)S(1)} %get-tuple-element.41), channel_id=1, source_target_pairs={{96,64},{97,65},{98,66},{99,67},{100,68},{101,69},{102,70},{103,71... | collective-permute-start | bytes 393224 | tf_op jit(solution)/shard_map/ppermute | solution.py:159
  44.4 2.0 %collective-permute-start.6 = (bf16[64,4,256]{2,1,0:T(4,128)(2,1)S(1)}, bf16[64,4,256]{2,1,0:T(4,128)(2,1)S(1)}, u32[]{:S(2)}, u32[]{:S(2)}) collective-permute-start(bf16[64,4,256]{2,1,0:T(4,128)(2,1)S(1)} %get-tuple-element.41), channel_id=1, source_target_pairs={{96,32},{97,33},{98,34},{99,35},{100,36},{101,37},{102,38},{103,39... | collective-permute-start | bytes 393224 | tf_op jit(solution)/shard_map/ppermute | solution.py:159
  45.1 10.1 %collective-permute-start.5 = (bf16[64,4,256]{2,1,0:T(4,128)(2,1)S(1)}, bf16[64,4,256]{2,1,0:T(4,128)(2,1)S(1)}, u32[]{:S(2)}, u32[]{:S(2)}) collective-permute-start(bf16[64,4,256]{2,1,0:T(4,128)(2,1)S(1)} %get-tuple-element.41), channel_id=1, source_target_pairs={{96,0},{97,1},{98,2},{99,3},{100,4},{101,5},{102,6},{103,7},{104,8... | collective-permute-start | bytes 393224 | tf_op jit(solution)/shard_map/ppermute | solution.py:159
  56.3 13.6 %all-to-all-start.1 = ((bf16[32,4,1024]{2,1,0:T(4,128)(2,1)}), bf16[32,4,1024]{2,1,0:T(4,128)(2,1)S(1)}, u32[]{:S(2)}, u32[]{:S(2)}) async-start(bf16[32,4,1024]{2,1,0:T(4,128)(2,1)} %reshape.124), calls=%async_computation.1 | async-start | bytes 524288 | tf_op jit(solution)/shard_map/all_to_all | solution.py:165
  61.3 9.7 %copy-start.2 = (f32[1,64,16,256]{3,2,1,0:T(8,128)}, f32[1,64,16,256]{3,2,1,0:T(8,128)S(1)}, u32[]{:S(2)}) copy-start(f32[1,64,16,256]{3,2,1,0:T(8,128)S(1)} %bitcast_dynamic-update-slice_fusion) | copy-start | bytes 3145732

commit v5 on v4

--- a/solution.py
+++ b/solution.py
@@ -63,12 +63,11 @@
     lax.fori_loop(0, rows // last, final, 0)
 
 
-def diffuse(layer_temp, diffusivity):
+def exchange_halo(layer_temp, diffusivity):
     n_bands = lax.axis_size("band")
     band = lax.axis_index("band")
     rows = layer_temp.shape[1]
     lev = layer_temp.shape[2]
-    cols = layer_temp.shape[3]
     halo = NSTEPS
     total = rows + 2 * halo
     comb = jnp.concatenate([layer_temp[0], diffusivity[0][:, None, :]], axis=1)
@@ -77,11 +76,17 @@
     above = lax.ppermute(comb[rows - halo:], "band", forward)
     below = lax.ppermute(comb[:halo], "band", backward)
     padded = jnp.concatenate([above, comb, below], axis=0)
-    fields = padded[:, :lev]
-    diff = padded[:, lev:]
     first = jnp.where(band == 0, halo, 0)
     stop = jnp.where(band == n_bands - 1, halo + rows, total)
     bounds = jnp.stack([first, stop]).astype(jnp.int32)
+    return padded, bounds
+
+
+def diffuse(padded, bounds, lev):
+    total, _, cols = padded.shape
+    rows = total - 2 * NSTEPS
+    fields = padded[:, :lev]
+    diff = padded[:, lev:]
     return pl.pallas_call(
         _diffusion_kernel,
         out_shape=jax.ShapeDtypeStruct((rows, lev, cols), jnp.float32),
@@ -105,12 +110,17 @@
     is_ocean = section == n_sections - 1
     weights_local = remap_blocks[0]
 
+    lev = layer_temp.shape[2]
+    padded, bounds = exchange_halo(layer_temp, diffusivity)
     surface_layers = layer_temp[0, :, :NF, :].astype(jnp.bfloat16)
-    flux = lax.cond(
+    flux, fields_early = lax.cond(
         is_ocean,
-        lambda: jnp.zeros((rows, NF, cols), jnp.float32),
-        lambda: jnp.einsum(
-            "rfc,rcd->rfd", surface_layers, weights_local, preferred_element_type=jnp.float32
+        lambda: (jnp.zeros((rows, NF, cols), jnp.float32), diffuse(padded, bounds, lev)),
+        lambda: (
+            jnp.einsum(
+                "rfc,rcd->rfd", surface_layers, weights_local, preferred_element_type=jnp.float32
+            ),
+            jnp.zeros((rows, lev, cols), jnp.float32),
         ),
     )
 
@@ -142,7 +152,10 @@
     for source in range(last):
         heating = heating + lax.ppermute(scaled, "comp", [(source, last)]).astype(jnp.float32)
 
-    fields = diffuse(layer_temp, diffusivity)
+    padded_late, _ = lax.optimization_barrier((padded, scaled))
+    fields = lax.cond(
+        is_ocean, lambda: fields_early, lambda: diffuse(padded_late, bounds, lev)
+    )
     heating = jnp.where(is_ocean, heating, 0.0).reshape(rows, NF, cols)
     temp_out = fields.at[:, :NF].add(heating)
     sea_surface = temp_out[:, :NF].astype(jnp.bfloat16)

time: 71.5 us -> 87.4 us (1.22)
  blocking collectives: 0 us -> 17.7 us
  waiting for transfers between devices: 20.3 us -> 18.2 us
  starting transfers between devices: 25.1 us -> 27 us
  other arithmetic: 5 us -> 3.61 us
  local copies, waits for them, and re-layouts: 3.53 us -> 4.52 us
  Pallas kernels: 8.92 us -> 7.94 us
    all_to_all x0 -> x1, blocking collectives: none -> 17.7 us  [body(): received = lax.all_to_all(sending, 'band', 0, 0, tiled=True)]
    ppermute x3, starting transfers between devices: 3.46 us -> 13.4 us  [body(): lax.ppermute(scaled, 'comp', [(source, last)]).astype(jnp.float32)]
    all_to_all x1 -> x0, starting transfers between devices: 8.58 us -> none  [body(): received = lax.all_to_all(sending, 'band', 0, 0, tiled=True)]
    all_to_all x1 -> x0, waiting for transfers between devices: 2.9 us -> none  [body(): received = lax.all_to_all(sending, 'band', 0, 0, tiled=True)]
    ppermute x2, waiting for transfers between devices: 0.01 us -> 1.68 us  [the longest x1 1.68 us: exchange_halo(): below = lax.ppermute(comb[:halo], 'band', backward)]
    another operation x3 -> x4, local copies, waits for them, and re-layouts: 0.21 us -> 1.25 us  [the longest x1 0.97 us: exchange_halo(): comb = jnp.concatenate([layer_temp[0], diffusivity[0][:, None, :]], axis=1)]
    ppermute x3, waiting for transfers between devices: 8.75 us -> 7.72 us  [body(): ocean_rows = ocean_rows + lax.ppermute(returned, 'comp', [(last, target)])]
    convert_element_type x1, other arithmetic: 1.11 us -> 0.08 us  [body(): sea_surface = temp_out[:, :NF].astype(jnp.bfloat16)]
  transfers between devices with their start and end apart: 10 -> 9, of which waited for: 3 -> 3; matrix products, arithmetic and copies ran while one was open for 5% -> 5% of each run, Pallas kernels for 13% -> 9%
where the time goes in v5:
time: 87.4 us; the launch traced here: 86.9 us
  starting transfers between devices  27 us (31%)
  waiting for transfers between devices  18.2 us (21%)
  blocking collectives  17.7 us (20%)
  Pallas kernels  7.94 us (9%)
  matrix products  6.91 us (8%)
  local copies, waits for them, and re-layouts  4.52 us (5%)
  other arithmetic  3.61 us (4%)
  between operations  0.92 us (1%)
    all_to_all x1, blocking collectives, body(): received = lax.all_to_all(sending, 'band', 0, 0, tiled=True)  17.7 us
    ppermute x3, starting transfers between devices, body(): lax.ppermute(scaled, 'comp', [(source, last)]).astype(jnp.float32)  13.4 us
    all_to_all x1, waiting for transfers between devices, body(): came_back = lax.all_to_all(reply, 'band', 0, 0, tiled=True)  8.77 us
    pallas_call x1, Pallas kernels, diffuse(): pl.pallas_call(_diffusion_kernel, out_shape=jax.ShapeDtypeStruct((rows, l...  7.94 us
    ppermute x3, waiting for transfers between devices, body(): ocean_rows = ocean_rows + lax.ppermute(returned, 'comp', [(last, target)])  7.72 us
    dot_general x1, matrix products, body(): jnp.einsum('rfc,rcd->rfd', surface_layers, weights_local, preferred_eleme...  4.57 us
    all_to_all x1, starting transfers between devices, body(): came_back = lax.all_to_all(reply, 'band', 0, 0, tiled=True)  4.55 us
    ppermute x1, starting transfers between devices, exchange_halo(): above = lax.ppermute(comb[rows - halo:], 'band', forward)  4.5 us
  transfers between devices with their start and end apart: 9, of which 3 were waited for; matrix products, arithmetic and copies ran while one was open for 5% of the time, Pallas kernels for 9%

profile of v5, /device:TPU:1, one launch (start us, length us, event | category | flops | bytes accessed | tf_op | source)
XLA Modules:
  0.0 86.9 jit_solution(3954708671530055724)
XLA Ops:
  0.6 0.0 copy-start
  0.6 1.0 %broadcast_in_dim_squeeze.4 = f32[64,1,256]{2,1,0:T(1,128)S(1)} reshape(f32[1,64,256]{2,1,0:T(8,128)} %param.14) | data formatting | bytes 131072 | tf_op jit(solution)/shard_map/broadcast_in_dim;squeeze | solution.py:73
  1.6 0.9 %pad_maximum_fusion.2 = (f32[4,17,256]{2,1,0:T(8,128)S(1)}, f32[4,17,256]{2,1,0:T(8,128)S(1)}) fusion(f32[64,1,256]{2,1,0:T(1,128)S(1)} %broadcast_in_dim_squeeze.4, f32[64,16,256]{2,1,0:T(8,128)} %bitcast.43), kind=kLoop, calls=%fused_computation.24 | loop fusion | flops 34816 | bytes 1253376 | tf_op jit(solution)/shard_map/slice | solution.py:76
  2.5 4.5 %collective-permute-start = (f32[4,17,256]{2,1,0:T(8,128)S(1)}, f32[4,17,256]{2,1,0:T(8,128)S(1)}, u32[]{:S(2)}, u32[]{:S(2)}) collective-permute-start(f32[4,17,256]{2,1,0:T(8,128)S(1)} %get-tuple-element.59), channel_id=1, source_target_pairs={{0,1},{1,2},{2,3},{3,4},{4,5},{5,6},{6,7},{7,8},{8,9},{9,10},{10,1... | collective-permute-start | bytes 208904 | tf_op jit(solution)/shard_map/ppermute | solution.py:76
  7.0 1.9 %collective-permute-start.1 = (f32[4,17,256]{2,1,0:T(8,128)S(1)}, f32[4,17,256]{2,1,0:T(8,128)S(1)}, u32[]{:S(2)}, u32[]{:S(2)}) collective-permute-start(f32[4,17,256]{2,1,0:T(8,128)S(1)} %get-tuple-element.60), channel_id=1, source_target_pairs={{1,0},{2,1},{3,2},{4,3},{5,4},{6,5},{7,6},{8,7},{9,8},{10,9},{11,1... | collective-permute-start | bytes 208904 | tf_op jit(solution)/shard_map/ppermute | solution.py:77
  9.0 0.9 %fusion.5 = f32[64]{0:T(128)S(1)} fusion(s32[64]{0:T(128)} %bitcast.54), kind=kOutput, calls=%fused_computation.12 | convolution fusion | flops 274368 | bytes 512 | tf_op jit(solution)/shard_map/dot_general | solution.py:133
  9.8 0.7 fusion.15
  10.5 0.7 convert_bitcast_fusion
  11.2 0.1 pad_add_fusion
  11.3 0.0 collective-permute-done
  11.3 1.7 %collective-permute-done.1 = f32[4,17,256]{2,1,0:T(8,128)S(1)} collective-permute-done((f32[4,17,256]{2,1,0:T(8,128)S(1)}, f32[4,17,256]{2,1,0:T(8,128)S(1)}, u32[]{:S(2)}, u32[]{:S(2)}) %collective-permute-start.1) | collective-permute-done | bytes 69664 | tf_op jit(solution)/shard_map/ppermute | solution.py:77
  13.0 0.2 pad_maximum_fusion
  13.1 4.8 %conditional.3 = (f32[64,1024]{1,0:T(8,128)S(1)}, f32[64,16,256]{2,1,0:T(8,128)S(1)}) conditional(s32[]{:T(128)} %convert_element_type.87, (f32[1,64,16,256]{3,2,1,0:T(8,128)S(1)}, bf16[64,256,256]{2,1,0:T(8,128)(2,1)}) %tuple.61, (f32[72,17,256]{2,1,0:T(8,128)S(1)}, s32[2]{0:T(128)S(1)}) %tuple.45), branch_computations={%region_1.2_spmd, %region_2.3_spmd} | conditional | flops 33554432 | bytes 10354708 | solution.py:116
  13.1 4.6 %fusion.1 = f32[64,4,256]{2,1,0:T(4,128)S(1)} fusion(bf16[64,256,256]{2,1,0:T(8,128)(2,1)} %get-tuple-element.44, f32[1,64,16,256]{3,2,1,0:T(8,128)S(1)} %get-tuple-element.43), kind=kOutput, calls=%fused_computation.2 | convolution fusion | flops 33554432 | bytes 8781824 | tf_op jit(solution)/shard_map/cond/branch_0_fun/rfc,rcd->rfd/dot_general | solution.py:120
  17.7 0.1 copy.20
  17.8 0.1 broadcast.61
  17.9 0.1 broadcast_in_dim.11
  18.0 0.6 convolution_convert_fusion.1
  18.6 0.2 copy.17
  18.8 17.7 %all_to_all.10 = f16[32,4,1152]{2,1,0:T(4,128)(2,1)S(1)} all-to-all(f16[32,4,1152]{2,1,0:T(4,128)(2,1)S(1)} %copy.17), channel_id=1, replica_groups=mesh['comp'=4,'band'=32] {'band'}, dimensions={0} | all-to-all | bytes 589824 | tf_op jit(solution)/shard_map/all_to_all | solution.py:144
  36.5 0.1 reshape.121
  36.6 0.1 convert_reduce_fusion
  36.8 0.4 fusion.4
  37.1 0.7 collective-permute-start.4
  37.8 0.7 collective-permute-start.3
  38.5 12.0 %collective-permute-start.2 = (f16[64,1024]{1,0:T(8,128)(2,1)S(1)}, f16[64,1024]{1,0:T(8,128)(2,1)S(1)}, u32[]{:S(2)}, u32[]{:S(2)}) collective-permute-start(f16[64,1024]{1,0:T(8,128)(2,1)S(1)} %fusion.4), channel_id=1, source_target_pairs={{0,96},{1,97},{2,98},{3,99},{4,100},{5,101},{6,102},{7,103},{8,104... | collective-permute-start | bytes 393224 | tf_op jit(solution)/shard_map/ppermute | solution.py:153
  50.5 9.8 %conditional.4 = (f32[64,16,256]{2,1,0:T(8,128)S(1)}) conditional(s32[]{:T(128)} %convert_element_type.87, (f32[72,17,256]{2,1,0:T(8,128)S(1)}, s32[2]{0:T(128)S(1)}) %tuple.47, f32[64,16,256]{2,1,0:T(8,128)S(1)} %get-tuple-element.58), branch_computations={%region_3.4_spmd, %region_4.5_spmd} | conditional | bytes 2506760 | solution.py:156
  50.5 0.7 slice.52.d_ref
  51.2 1.2 %slice.51.f_ref = f32[72,16,256]{2,1,0:T(8,128)} slice(f32[72,17,256]{2,1,0:T(8,128)S(1)} %get-tuple-element.48), slice={[0:72], [0:16], [0:256]} | slice | bytes 2359296 | tf_op jit(solution)/shard_map/cond/branch_0_fun/slice | solution.py:88
  52.4 7.9 %branch_0_fun.1 = f32[64,16,256]{2,1,0:T(8,128)S(1)} custom-call(s32[2]{0:T(128)S(1)} %get-tuple-element.47.bounds_ref, f32[72,16,256]{2,1,0:T(8,128)} %slice.51.f_ref, f32[72,1,256]{2,1,0:T(1,128)} %slice.52.d_ref), custom_call_target="tpu_custom_call" | custom-call | tf_op jit(solution)/shard_map/cond/branch_0_fun/pallas_call | solution.py:90
  60.4 0.1 add_select_fusion
  60.5 0.1 reshape.122
  60.6 0.1 fusion.10
  60.7 0.1 conditional.5
  60.8 0.7 collective-permute-start.7
  61.4 0.7 collective-permute-start.6
  62.1 1.3 %collective-permute-start.5 = (bf16[64,4,256]{2,1,0:T(4,128)(2,1)S(1)}, bf16[64,4,256]{2,1,0:T(4,128)(2,1)S(1)}, u32[]{:S(2)}, u32[]{:S(2)}) collective-permute-start(bf16[64,4,256]{2,1,0:T(4,128)(2,1)S(1)} %get-tuple-element.68), channel_id=1, source_target_pairs={{96,0},{97,1},{98,2},{99,3},{100,4},{101,5},{102,6},{103,7},{104,8... | collective-permute-start | bytes 393224 | tf_op jit(solution)/shard_map/ppermute | solution.py:172
  63.4 7.7 %collective-permute-done.5 = bf16[64,4,256]{2,1,0:T(4,128)(2,1)S(1)} collective-permute-done((bf16[64,4,256]{2,1,0:T(4,128)(2,1)S(1)}, bf16[64,4,256]{2,1,0:T(4,128)(2,1)S(1)}, u32[]{:S(2)}, u32[]{:S(2)}) %collective-permute-start.5) | collective-permute-done | bytes 131104 | tf_op jit(solution)/shard_map/ppermute | solution.py:172
  71.2 0.3 convolution_convert_fusion.2
  71.5 0.8 reshape.124
  72.3 4.6 %all-to-all-start.1 = ((bf16[32,4,1024]{2,1,0:T(4,128)(2,1)}), bf16[32,4,1024]{2,1,0:T(4,128)(2,1)S(1)}, u32[]{:S(2)}, u32[]{:S(2)}) async-start(bf16[32,4,1024]{2,1,0:T(4,128)(2,1)} %reshape.124), calls=%async_computation.1 | async-start | bytes 524288 | tf_op jit(solution)/shard_map/all_to_all | solution.py:178
  76.8 0.1 copy.34
  76.9 0.1 bitcast_dynamic-update-slice_fusion
  77.0 0.0 copy-start.1
  77.0 8.8 %all-to-all-done.1 = bf16[32,4,1024]{2,1,0:T(4,128)(2,1)S(1)} async-done(((bf16[32,4,1024]{2,1,0:T(4,128)(2,1)}), bf16[32,4,1024]{2,1,0:T(4,128)(2,1)S(1)}, u32[]{:S(2)}, u32[]{:S(2)}) %all-to-all-start.1) | async-done | bytes 262176 | tf_op jit(solution)/shard_map/all_to_all | solution.py:178
  85.8 0.2 fusion.3
  86.0 0.1 reshape.125
  86.1 0.7 select_bitcast_fusion
  (13 shorter events, 0.1 us)
Async XLA Ops:
  0.6 12.3 %copy-start = (f32[1,64,16,256]{3,2,1,0:T(8,128)S(1)}, f32[1,64,16,256]{3,2,1,0:T(8,128)}, u32[]{:S(2)}) copy-start(f32[1,64,16,256]{3,2,1,0:T(8,128)} %param.13) | copy-start | bytes 3145732
  2.5 8.8 %collective-permute-start = (f32[4,17,256]{2,1,0:T(8,128)S(1)}, f32[4,17,256]{2,1,0:T(8,128)S(1)}, u32[]{:S(2)}, u32[]{:S(2)}) collective-permute-start(f32[4,17,256]{2,1,0:T(8,128)S(1)} %get-tuple-element.59), channel_id=1, source_target_pairs={{0,1},{1,2},{2,3},{3,4},{4,5},{5,6},{6,7},{7,8},{8,9},{9,10},{10,1... | collective-permute-start | bytes 208904 | tf_op jit(solution)/shard_map/ppermute | solution.py:76
  7.0 5.9 %collective-permute-start.1 = (f32[4,17,256]{2,1,0:T(8,128)S(1)}, f32[4,17,256]{2,1,0:T(8,128)S(1)}, u32[]{:S(2)}, u32[]{:S(2)}) collective-permute-start(f32[4,17,256]{2,1,0:T(8,128)S(1)} %get-tuple-element.60), channel_id=1, source_target_pairs={{1,0},{2,1},{3,2},{4,3},{5,4},{6,5},{7,6},{8,7},{9,8},{10,9},{11,1... | collective-permute-start | bytes 208904 | tf_op jit(solution)/shard_map/ppermute | solution.py:77
  37.1 23.2 %collective-permute-start.4 = (f16[64,1024]{1,0:T(8,128)(2,1)S(1)}, f16[64,1024]{1,0:T(8,128)(2,1)S(1)}, u32[]{:S(2)}, u32[]{:S(2)}) collective-permute-start(f16[64,1024]{1,0:T(8,128)(2,1)S(1)} %fusion.4), channel_id=1, source_target_pairs={{64,96},{65,97},{66,98},{67,99},{68,100},{69,101},{70,102},{71,103... | collective-permute-start | bytes 393224 | tf_op jit(solution)/shard_map/ppermute | solution.py:153
  37.8 22.6 %collective-permute-start.3 = (f16[64,1024]{1,0:T(8,128)(2,1)S(1)}, f16[64,1024]{1,0:T(8,128)(2,1)S(1)}, u32[]{:S(2)}, u32[]{:S(2)}) collective-permute-start(f16[64,1024]{1,0:T(8,128)(2,1)S(1)} %fusion.4), channel_id=1, source_target_pairs={{32,96},{33,97},{34,98},{35,99},{36,100},{37,101},{38,102},{39,103... | collective-permute-start | bytes 393224 | tf_op jit(solution)/shard_map/ppermute | solution.py:153
  38.5 21.9 %collective-permute-start.2 = (f16[64,1024]{1,0:T(8,128)(2,1)S(1)}, f16[64,1024]{1,0:T(8,128)(2,1)S(1)}, u32[]{:S(2)}, u32[]{:S(2)}) collective-permute-start(f16[64,1024]{1,0:T(8,128)(2,1)S(1)} %fusion.4), channel_id=1, source_target_pairs={{0,96},{1,97},{2,98},{3,99},{4,100},{5,101},{6,102},{7,103},{8,104... | collective-permute-start | bytes 393224 | tf_op jit(solution)/shard_map/ppermute | solution.py:153
  60.8 2.7 %collective-permute-start.7 = (bf16[64,4,256]{2,1,0:T(4,128)(2,1)S(1)}, bf16[64,4,256]{2,1,0:T(4,128)(2,1)S(1)}, u32[]{:S(2)}, u32[]{:S(2)}) collective-permute-start(bf16[64,4,256]{2,1,0:T(4,128)(2,1)S(1)} %get-tuple-element.68), channel_id=1, source_target_pairs={{96,64},{97,65},{98,66},{99,67},{100,68},{101,69},{102,70},{103,71... | collective-permute-start | bytes 393224 | tf_op jit(solution)/shard_map/ppermute | solution.py:172
  61.4 2.0 %collective-permute-start.6 = (bf16[64,4,256]{2,1,0:T(4,128)(2,1)S(1)}, bf16[64,4,256]{2,1,0:T(4,128)(2,1)S(1)}, u32[]{:S(2)}, u32[]{:S(2)}) collective-permute-start(bf16[64,4,256]{2,1,0:T(4,128)(2,1)S(1)} %get-tuple-element.68), channel_id=1, source_target_pairs={{96,32},{97,33},{98,34},{99,35},{100,36},{101,37},{102,38},{103,39... | collective-permute-start | bytes 393224 | tf_op jit(solution)/shard_map/ppermute | solution.py:172
  62.1 9.0 %collective-permute-start.5 = (bf16[64,4,256]{2,1,0:T(4,128)(2,1)S(1)}, bf16[64,4,256]{2,1,0:T(4,128)(2,1)S(1)}, u32[]{:S(2)}, u32[]{:S(2)}) collective-permute-start(bf16[64,4,256]{2,1,0:T(4,128)(2,1)S(1)} %get-tuple-element.68), channel_id=1, source_target_pairs={{96,0},{97,1},{98,2},{99,3},{100,4},{101,5},{102,6},{103,7},{104,8... | collective-permute-start | bytes 393224 | tf_op jit(solution)/shard_map/ppermute | solution.py:172
  72.3 13.5 %all-to-all-start.1 = ((bf16[32,4,1024]{2,1,0:T(4,128)(2,1)}), bf16[32,4,1024]{2,1,0:T(4,128)(2,1)S(1)}, u32[]{:S(2)}, u32[]{:S(2)}) async-start(bf16[32,4,1024]{2,1,0:T(4,128)(2,1)} %reshape.124), calls=%async_computation.1 | async-start | bytes 524288 | tf_op jit(solution)/shard_map/all_to_all | solution.py:178
  77.0 9.8 %copy-start.1 = (f32[1,64,16,256]{3,2,1,0:T(8,128)}, f32[1,64,16,256]{3,2,1,0:T(8,128)S(1)}, u32[]{:S(2)}) copy-start(f32[1,64,16,256]{3,2,1,0:T(8,128)S(1)} %bitcast_dynamic-update-slice_fusion) | copy-start | bytes 3145732

commit v6 on v4

--- a/solution.py
+++ b/solution.py
@@ -16,11 +16,11 @@
 
 
 def _advance_rows(src, dst, d_ref, r0, count, out_r0, bounds):
-    lev, cols = src.shape[1], src.shape[2]
-    fields = src[pl.ds(r0, count)]
-    row_north = src[pl.ds(r0 - 1, count)]
-    row_south = src[pl.ds(r0 + 1, count)]
-    diff = d_ref[pl.ds(r0, count)]
+    lev, cols = dst.shape[1], dst.shape[2]
+    fields = src[pl.ds(r0, count), pl.ds(0, lev)]
+    row_north = src[pl.ds(r0 - 1, count), pl.ds(0, lev)]
+    row_south = src[pl.ds(r0 + 1, count), pl.ds(0, lev)]
+    diff = d_ref[pl.ds(r0, count), pl.ds(lev, 1)]
     level = lax.broadcasted_iota(jnp.int32, (count, lev, cols), 1)
     col_east = pltpu.roll(fields, 1, 2)
     col_west = pltpu.roll(fields, cols - 1, 2)
@@ -34,30 +34,34 @@
     dst[pl.ds(out_r0, count)] = new
 
 
-def _diffusion_kernel(bounds_ref, f_ref, d_ref, o_ref, buf_a, buf_b):
-    total = f_ref.shape[0]
-    rows = o_ref.shape[0]
+def _largest_divisor(n, limit):
+    return max(k for k in range(1, limit + 1) if n % k == 0)
+
+
+def _diffusion_kernel(bounds_ref, p_ref, o_ref, buf_a, buf_b):
+    total = p_ref.shape[0]
+    rows, lev = o_ref.shape[0], o_ref.shape[1]
     halo = (total - rows) // 2
     bounds = (bounds_ref[0], bounds_ref[1])
-    chunk = 5 if (total - 2) % 5 == 0 else 1
-    src = f_ref
+    chunk = _largest_divisor(total - 2, 16)
+    src = p_ref
     targets = (buf_a, buf_b)
     for step in range(NSTEPS - 1):
         dst = targets[step % 2]
-        dst[0] = src[0]
-        dst[total - 1] = src[total - 1]
+        dst[0] = src[0, pl.ds(0, lev)]
+        dst[total - 1] = src[total - 1, pl.ds(0, lev)]
 
         def one(i, carry, src=src, dst=dst):
             r0 = 1 + i * chunk
-            _advance_rows(src, dst, d_ref, r0, chunk, r0, bounds)
+            _advance_rows(src, dst, p_ref, r0, chunk, r0, bounds)
             return carry
 
         lax.fori_loop(0, (total - 2) // chunk, one, 0)
         src = dst
-    last = 8 if rows % 8 == 0 else 1
+    last = _largest_divisor(rows, 16)
 
     def final(i, carry):
-        _advance_rows(src, o_ref, d_ref, halo + i * last, last, i * last, None)
+        _advance_rows(src, o_ref, p_ref, halo + i * last, last, i * last, None)
         return carry
 
     lax.fori_loop(0, rows // last, final, 0)
@@ -77,8 +81,6 @@
     above = lax.ppermute(comb[rows - halo:], "band", forward)
     below = lax.ppermute(comb[:halo], "band", backward)
     padded = jnp.concatenate([above, comb, below], axis=0)
-    fields = padded[:, :lev]
-    diff = padded[:, lev:]
     first = jnp.where(band == 0, halo, 0)
     stop = jnp.where(band == n_bands - 1, halo + rows, total)
     bounds = jnp.stack([first, stop]).astype(jnp.int32)
@@ -88,11 +90,10 @@
         in_specs=[
             pl.BlockSpec(memory_space=pltpu.SMEM),
             pl.BlockSpec(memory_space=pltpu.VMEM),
-            pl.BlockSpec(memory_space=pltpu.VMEM),
         ],
         out_specs=pl.BlockSpec(memory_space=pltpu.VMEM),
         scratch_shapes=[pltpu.VMEM((total, lev, cols), jnp.float32)] * 2,
-    )(bounds, fields, diff)
+    )(bounds, padded)
 
 
 def body(layer_temp, diffusivity, owner_band, block_index, remap_blocks):

time: 71.5 us -> 70.3 us (0.983)
  Pallas kernels: 8.92 us -> 7.42 us
  local copies, waits for them, and re-layouts: 3.53 us -> 2.32 us
  waiting for transfers between devices: 20.3 us -> 21.1 us
    pallas_call x1, Pallas kernels: 8.92 us -> 7.42 us  [diffuse(): pl.pallas_call(_diffusion_kernel, out_shape=jax.ShapeDtypeStruct((rows, l...]
    concatenate x1, other arithmetic: 0.15 us -> 1.38 us  [diffuse(): padded = jnp.concatenate([above, comb, below], axis=0)]
    slice x1 -> x0, local copies, waits for them, and re-layouts: 1.21 us -> none  [diffuse(): fields = padded[:, :lev]]
    ppermute x3, waiting for transfers between devices: 8.75 us -> 9.61 us  [body(): ocean_rows = ocean_rows + lax.ppermute(returned, 'comp', [(last, target)])]
  transfers between devices with their start and end apart: 10 -> 10, of which waited for: 3 -> 3; matrix products, arithmetic and copies ran while one was open for 5% -> 4% of each run, Pallas kernels for 13% -> 11%
where the time goes in v6:
time: 70.3 us; the launch traced here: 69.8 us
  starting transfers between devices  25.2 us (36%)
  waiting for transfers between devices  21.1 us (30%)
  Pallas kernels  7.42 us (11%)
  matrix products  7.1 us (10%)
  other arithmetic  5.59 us (8%)
  local copies, waits for them, and re-layouts  2.32 us (3%)
  between operations  0.95 us (1%)
    ppermute x3, waiting for transfers between devices, body(): ocean_rows = ocean_rows + lax.ppermute(returned, 'comp', [(last, target)])  9.61 us
    all_to_all x1, waiting for transfers between devices, body(): came_back = lax.all_to_all(reply, 'band', 0, 0, tiled=True)  8.65 us
    all_to_all x1, starting transfers between devices, body(): received = lax.all_to_all(sending, 'band', 0, 0, tiled=True)  8.58 us
    pallas_call x1, Pallas kernels, diffuse(): pl.pallas_call(_diffusion_kernel, out_shape=jax.ShapeDtypeStruct((rows, l...  7.42 us
    all_to_all x1, starting transfers between devices, body(): came_back = lax.all_to_all(reply, 'band', 0, 0, tiled=True)  4.86 us
    dot_general x1, matrix products, body(): jnp.einsum('rfc,rcd->rfd', surface_layers, weights_local, preferred_eleme...  4.76 us
    ppermute x3, starting transfers between devices, body(): lax.ppermute(scaled, 'comp', [(source, last)]).astype(jnp.float32)  3.46 us
    ppermute x1, starting transfers between devices, diffuse(): above = lax.ppermute(comb[rows - halo:], 'band', forward)  3.42 us
  transfers between devices with their start and end apart: 10, of which 3 were waited for; matrix products, arithmetic and copies ran while one was open for 4% of the time, Pallas kernels for 11%

profile of v6, /device:TPU:1, one launch (start us, length us, event | category | flops | bytes accessed | tf_op | source)
XLA Modules:
  0.0 69.8 jit_solution(7869026888767470362)
XLA Ops:
  0.6 0.9 %fusion.5 = f32[64]{0:T(128)S(1)} fusion(s32[64]{0:T(128)} %bitcast.54), kind=kOutput, calls=%fused_computation.12 | convolution fusion | flops 274368 | bytes 512 | tf_op jit(solution)/shard_map/dot_general | solution.py:124
  1.5 0.7 fusion.15
  2.2 0.7 convert_bitcast_fusion
  2.9 4.8 %conditional.2 = (f32[64,1024]{1,0:T(8,128)S(1)}) conditional(s32[]{:T(128)} %convert_element_type.89, (f32[1,64,16,256]{3,2,1,0:T(8,128)}, bf16[64,256,256]{2,1,0:T(8,128)(2,1)}) %tuple.37, () %tuple.27), branch_computations={%region_1.0_spmd, %region_2.0_spmd} | conditional | flops 33554432 | bytes 9306120 | solution.py:110
  2.9 4.8 %fusion.1 = f32[64,4,256]{2,1,0:T(4,128)S(1)} fusion(bf16[64,256,256]{2,1,0:T(8,128)(2,1)} %get-tuple-element.31, f32[1,64,16,256]{3,2,1,0:T(8,128)} %get-tuple-element.30), kind=kOutput, calls=%fused_computation.2 | convolution fusion | flops 33554432 | bytes 8781824 | tf_op jit(solution)/shard_map/cond/branch_0_fun/rfc,rcd->rfd/dot_general | solution.py:113
  7.6 0.1 copy.20
  7.7 0.0 copy-start.3
  7.7 0.0 copy-start
  7.7 0.1 broadcast_in_dim.12
  7.8 0.6 convolution_convert_fusion.1
  8.4 0.9 %copy.17 = f16[32,4,1152]{2,1,0:T(4,128)(2,1)} copy(f16[32,4,1152]{2,0,1:T(8,128)(2,1)S(1)} %convolution_convert_fusion.1) | data formatting | bytes 589824 | tf_op jit(solution)/shard_map/convert_element_type | solution.py:134
  9.3 8.6 %all-to-all-start = ((f16[32,4,1152]{2,1,0:T(4,128)(2,1)}), f16[32,4,1152]{2,1,0:T(4,128)(2,1)S(1)}, u32[]{:S(2)}, u32[]{:S(2)}) async-start(f16[32,4,1152]{2,1,0:T(4,128)(2,1)} %copy.17), calls=%async_computation | async-start | bytes 589824 | tf_op jit(solution)/shard_map/all_to_all | solution.py:135
  18.0 2.1 %collective-permute-start.1 = (f32[4,17,256]{2,1,0:T(8,128)S(1)}, f32[4,17,256]{2,1,0:T(8,128)S(1)}, u32[]{:S(2)}, u32[]{:S(2)}) collective-permute-start(f32[4,17,256]{2,1,0:T(8,128)S(1)} %get-tuple-element.37), channel_id=1, source_target_pairs={{1,0},{2,1},{3,2},{4,3},{5,4},{6,5},{7,6},{8,7},{9,8},{10,9},{11,1... | collective-permute-start | bytes 208904 | tf_op jit(solution)/shard_map/ppermute | solution.py:82
  20.2 3.4 %collective-permute-start = (f32[4,17,256]{2,1,0:T(8,128)S(1)}, f32[4,17,256]{2,1,0:T(8,128)S(1)}, u32[]{:S(2)}, u32[]{:S(2)}) collective-permute-start(f32[4,17,256]{2,1,0:T(8,128)S(1)} %get-tuple-element.36), channel_id=1, source_target_pairs={{0,1},{1,2},{2,3},{3,4},{4,5},{5,6},{6,7},{7,8},{8,9},{9,10},{10,1... | collective-permute-start | bytes 208904 | tf_op jit(solution)/shard_map/ppermute | solution.py:81
  23.6 0.7 pad_add_fusion.bounds_ref
  24.3 2.8 %all-to-all-done = f16[32,4,1152]{2,1,0:T(4,128)(2,1)S(1)} async-done(((f16[32,4,1152]{2,1,0:T(4,128)(2,1)}), f16[32,4,1152]{2,1,0:T(4,128)(2,1)S(1)}, u32[]{:S(2)}, u32[]{:S(2)}) %all-to-all-start) | async-done | bytes 294944 | tf_op jit(solution)/shard_map/all_to_all | solution.py:135
  27.1 0.1 reshape.121
  27.2 0.1 convert_reduce_fusion
  27.3 0.4 fusion.4
  27.7 0.7 collective-permute-start.4
  28.4 0.7 collective-permute-start.3
  29.1 2.1 %collective-permute-start.2 = (f16[64,1024]{1,0:T(8,128)(2,1)S(1)}, f16[64,1024]{1,0:T(8,128)(2,1)S(1)}, u32[]{:S(2)}, u32[]{:S(2)}) collective-permute-start(f16[64,1024]{1,0:T(8,128)(2,1)S(1)} %fusion.4), channel_id=1, source_target_pairs={{0,96},{1,97},{2,98},{3,99},{4,100},{5,101},{6,102},{7,103},{8,104... | collective-permute-start | bytes 393224 | tf_op jit(solution)/shard_map/ppermute | solution.py:144
  31.2 0.0 collective-permute-done.1
  31.2 0.0 collective-permute-done
  31.2 1.4 %pad_maximum_fusion.p_ref = f32[72,17,256]{2,1,0:T(8,128)} fusion(f32[4,17,256]{2,1,0:T(8,128)S(1)} %collective-permute-done.1, f32[64,1,256]{2,1,0:T(1,128)S(1)} %broadcast_in_dim_squeeze.4, f32[64,16,256]{2,1,0:T(8,128)S(1)} %bitcast.44, f32[4,17,256]{2,1,0:T(8,128)S(1)} %collective-permute-done), kind=kLoop, calls=%fused_computation.5 | loop fusion | flops 940032 | bytes 2506752 | tf_op jit(solution)/shard_map/concatenate | solution.py:83
  32.6 7.4 %shard_map.68 = f32[64,16,256]{2,1,0:T(8,128)} custom-call(s32[2]{0:T(128)} %pad_add_fusion.bounds_ref, f32[72,17,256]{2,1,0:T(8,128)} %pad_maximum_fusion.p_ref), custom_call_target="tpu_custom_call" | custom-call | tf_op jit(solution)/shard_map/pallas_call | solution.py:87
  40.0 0.0 collective-permute-done.4
  40.0 0.1 add_select_fusion
  40.1 0.1 reshape.122
  40.2 1.1 %fusion.10 = bf16[64,4,256]{2,1,0:T(4,128)(2,1)S(1)} fusion(f32[64,4,256]{2,1,0:T(4,128)S(1)} %reshape.122, f32[64,16,256]{2,1,0:T(8,128)} %shard_map.68), kind=kLoop, calls=%fused_computation.27 | loop fusion | flops 131072 | bytes 655360 | tf_op jit(solution)/shard_map/convert_element_type | solution.py:149
  41.4 0.1 conditional.3
  41.4 0.0 copy-start.1
  41.4 0.8 %collective-permute-start.7 = (bf16[64,4,256]{2,1,0:T(4,128)(2,1)S(1)}, bf16[64,4,256]{2,1,0:T(4,128)(2,1)S(1)}, u32[]{:S(2)}, u32[]{:S(2)}) collective-permute-start(bf16[64,4,256]{2,1,0:T(4,128)(2,1)S(1)} %get-tuple-element.41), channel_id=1, source_target_pairs={{96,64},{97,65},{98,66},{99,67},{100,68},{101,69},{102,70},{103,71... | collective-permute-start | bytes 393224 | tf_op jit(solution)/shard_map/ppermute | solution.py:160
  42.2 0.7 collective-permute-start.6
  42.9 1.3 %collective-permute-start.5 = (bf16[64,4,256]{2,1,0:T(4,128)(2,1)S(1)}, bf16[64,4,256]{2,1,0:T(4,128)(2,1)S(1)}, u32[]{:S(2)}, u32[]{:S(2)}) collective-permute-start(bf16[64,4,256]{2,1,0:T(4,128)(2,1)S(1)} %get-tuple-element.41), channel_id=1, source_target_pairs={{96,0},{97,1},{98,2},{99,3},{100,4},{101,5},{102,6},{103,7},{104,8... | collective-permute-start | bytes 393224 | tf_op jit(solution)/shard_map/ppermute | solution.py:160
  44.2 0.0 collective-permute-done.7
  44.2 0.0 collective-permute-done.6
  44.2 9.6 %collective-permute-done.5 = bf16[64,4,256]{2,1,0:T(4,128)(2,1)S(1)} collective-permute-done((bf16[64,4,256]{2,1,0:T(4,128)(2,1)S(1)}, bf16[64,4,256]{2,1,0:T(4,128)(2,1)S(1)}, u32[]{:S(2)}, u32[]{:S(2)}) %collective-permute-start.5) | collective-permute-done | bytes 131104 | tf_op jit(solution)/shard_map/ppermute | solution.py:160
  53.9 0.3 convolution_convert_fusion.2
  54.2 0.8 %reshape.124 = bf16[32,4,1024]{2,1,0:T(4,128)(2,1)} reshape(bf16[128,1024]{1,0:T(8,128)(2,1)S(1)} %convolution_convert_fusion.2) | data formatting | bytes 524288 | tf_op jit(solution)/shard_map/reshape | solution.py:165
  55.0 4.9 %all-to-all-start.1 = ((bf16[32,4,1024]{2,1,0:T(4,128)(2,1)}), bf16[32,4,1024]{2,1,0:T(4,128)(2,1)S(1)}, u32[]{:S(2)}, u32[]{:S(2)}) async-start(bf16[32,4,1024]{2,1,0:T(4,128)(2,1)} %reshape.124), calls=%async_computation.1 | async-start | bytes 524288 | tf_op jit(solution)/shard_map/all_to_all | solution.py:166
  59.9 0.1 copy.30
  59.9 0.1 bitcast_dynamic-update-slice_fusion
  60.1 0.0 copy-start.2
  60.1 8.6 %all-to-all-done.1 = bf16[32,4,1024]{2,1,0:T(4,128)(2,1)S(1)} async-done(((bf16[32,4,1024]{2,1,0:T(4,128)(2,1)}), bf16[32,4,1024]{2,1,0:T(4,128)(2,1)S(1)}, u32[]{:S(2)}, u32[]{:S(2)}) %all-to-all-start.1) | async-done | bytes 262176 | tf_op jit(solution)/shard_map/all_to_all | solution.py:166
  68.7 0.2 fusion.3
  68.9 0.1 reshape.125
  69.0 0.7 %select_bitcast_fusion = bf16[1,64,4,256]{3,2,1,0:T(4,128)(2,1)} fusion(bf16[64,4,256]{2,1,0:T(4,128)(2,1)S(1)} %get-tuple-element.41, bf16[64,4,256]{2,1,0:T(4,128)(2,1)S(1)} %reshape.125, pred[]{:T(512)S(6)} %eq.62), kind=kLoop, calls=%fused_computation.21 | loop fusion | flops 65536 | bytes 393217 | tf_op jit(solution)/shard_map/broadcast_in_dim | solution.py:172
  (14 shorter events, 0.2 us)
Async XLA Ops:
  7.7 10.2 %copy-start.3 = (f32[1,64,256]{2,1,0:T(8,128)S(1)}, f32[1,64,256]{2,1,0:T(8,128)}, u32[]{:S(2)}) copy-start(f32[1,64,256]{2,1,0:T(8,128)} %param.12) | copy-start | bytes 196612
  7.7 10.3 %copy-start = (f32[1,64,16,256]{3,2,1,0:T(8,128)S(1)}, f32[1,64,16,256]{3,2,1,0:T(8,128)}, u32[]{:S(2)}) copy-start(f32[1,64,16,256]{3,2,1,0:T(8,128)} %param.11) | copy-start | bytes 3145732
  9.3 17.8 %all-to-all-start = ((f16[32,4,1152]{2,1,0:T(4,128)(2,1)}), f16[32,4,1152]{2,1,0:T(4,128)(2,1)S(1)}, u32[]{:S(2)}, u32[]{:S(2)}) async-start(f16[32,4,1152]{2,1,0:T(4,128)(2,1)} %copy.17), calls=%async_computation | async-start | bytes 589824 | tf_op jit(solution)/shard_map/all_to_all | solution.py:135
  18.0 13.2 %collective-permute-start.1 = (f32[4,17,256]{2,1,0:T(8,128)S(1)}, f32[4,17,256]{2,1,0:T(8,128)S(1)}, u32[]{:S(2)}, u32[]{:S(2)}) collective-permute-start(f32[4,17,256]{2,1,0:T(8,128)S(1)} %get-tuple-element.37), channel_id=1, source_target_pairs={{1,0},{2,1},{3,2},{4,3},{5,4},{6,5},{7,6},{8,7},{9,8},{10,9},{11,1... | collective-permute-start | bytes 208904 | tf_op jit(solution)/shard_map/ppermute | solution.py:82
  20.2 11.0 %collective-permute-start = (f32[4,17,256]{2,1,0:T(8,128)S(1)}, f32[4,17,256]{2,1,0:T(8,128)S(1)}, u32[]{:S(2)}, u32[]{:S(2)}) collective-permute-start(f32[4,17,256]{2,1,0:T(8,128)S(1)} %get-tuple-element.36), channel_id=1, source_target_pairs={{0,1},{1,2},{2,3},{3,4},{4,5},{5,6},{6,7},{7,8},{8,9},{9,10},{10,1... | collective-permute-start | bytes 208904 | tf_op jit(solution)/shard_map/ppermute | solution.py:81
  27.7 12.3 %collective-permute-start.4 = (f16[64,1024]{1,0:T(8,128)(2,1)S(1)}, f16[64,1024]{1,0:T(8,128)(2,1)S(1)}, u32[]{:S(2)}, u32[]{:S(2)}) collective-permute-start(f16[64,1024]{1,0:T(8,128)(2,1)S(1)} %fusion.4), channel_id=1, source_target_pairs={{64,96},{65,97},{66,98},{67,99},{68,100},{69,101},{70,102},{71,103... | collective-permute-start | bytes 393224 | tf_op jit(solution)/shard_map/ppermute | solution.py:144
  28.4 11.6 %collective-permute-start.3 = (f16[64,1024]{1,0:T(8,128)(2,1)S(1)}, f16[64,1024]{1,0:T(8,128)(2,1)S(1)}, u32[]{:S(2)}, u32[]{:S(2)}) collective-permute-start(f16[64,1024]{1,0:T(8,128)(2,1)S(1)} %fusion.4), channel_id=1, source_target_pairs={{32,96},{33,97},{34,98},{35,99},{36,100},{37,101},{38,102},{39,103... | collective-permute-start | bytes 393224 | tf_op jit(solution)/shard_map/ppermute | solution.py:144
  29.1 11.0 %collective-permute-start.2 = (f16[64,1024]{1,0:T(8,128)(2,1)S(1)}, f16[64,1024]{1,0:T(8,128)(2,1)S(1)}, u32[]{:S(2)}, u32[]{:S(2)}) collective-permute-start(f16[64,1024]{1,0:T(8,128)(2,1)S(1)} %fusion.4), channel_id=1, source_target_pairs={{0,96},{1,97},{2,98},{3,99},{4,100},{5,101},{6,102},{7,103},{8,104... | collective-permute-start | bytes 393224 | tf_op jit(solution)/shard_map/ppermute | solution.py:144
  41.4 18.4 %copy-start.1 = (f32[64,16,256]{2,1,0:T(8,128)S(1)}, f32[64,16,256]{2,1,0:T(8,128)}, u32[]{:S(2)}) copy-start(f32[64,16,256]{2,1,0:T(8,128)} %shard_map.68) | copy-start | bytes 3145732
  41.4 2.8 %collective-permute-start.7 = (bf16[64,4,256]{2,1,0:T(4,128)(2,1)S(1)}, bf16[64,4,256]{2,1,0:T(4,128)(2,1)S(1)}, u32[]{:S(2)}, u32[]{:S(2)}) collective-permute-start(bf16[64,4,256]{2,1,0:T(4,128)(2,1)S(1)} %get-tuple-element.41), channel_id=1, source_target_pairs={{96,64},{97,65},{98,66},{99,67},{100,68},{101,69},{102,70},{103,71... | collective-permute-start | bytes 393224 | tf_op jit(solution)/shard_map/ppermute | solution.py:160
  42.2 2.0 %collective-permute-start.6 = (bf16[64,4,256]{2,1,0:T(4,128)(2,1)S(1)}, bf16[64,4,256]{2,1,0:T(4,128)(2,1)S(1)}, u32[]{:S(2)}, u32[]{:S(2)}) collective-permute-start(bf16[64,4,256]{2,1,0:T(4,128)(2,1)S(1)} %get-tuple-element.41), channel_id=1, source_target_pairs={{96,32},{97,33},{98,34},{99,35},{100,36},{101,37},{102,38},{103,39... | collective-permute-start | bytes 393224 | tf_op jit(solution)/shard_map/ppermute | solution.py:160
  42.9 10.9 %collective-permute-start.5 = (bf16[64,4,256]{2,1,0:T(4,128)(2,1)S(1)}, bf16[64,4,256]{2,1,0:T(4,128)(2,1)S(1)}, u32[]{:S(2)}, u32[]{:S(2)}) collective-permute-start(bf16[64,4,256]{2,1,0:T(4,128)(2,1)S(1)} %get-tuple-element.41), channel_id=1, source_target_pairs={{96,0},{97,1},{98,2},{99,3},{100,4},{101,5},{102,6},{103,7},{104,8... | collective-permute-start | bytes 393224 | tf_op jit(solution)/shard_map/ppermute | solution.py:160
  55.0 13.7 %all-to-all-start.1 = ((bf16[32,4,1024]{2,1,0:T(4,128)(2,1)}), bf16[32,4,1024]{2,1,0:T(4,128)(2,1)S(1)}, u32[]{:S(2)}, u32[]{:S(2)}) async-start(bf16[32,4,1024]{2,1,0:T(4,128)(2,1)} %reshape.124), calls=%async_computation.1 | async-start | bytes 524288 | tf_op jit(solution)/shard_map/all_to_all | solution.py:166
  60.1 9.7 %copy-start.2 = (f32[1,64,16,256]{3,2,1,0:T(8,128)}, f32[1,64,16,256]{3,2,1,0:T(8,128)S(1)}, u32[]{:S(2)}) copy-start(f32[1,64,16,256]{3,2,1,0:T(8,128)S(1)} %bitcast_dynamic-update-slice_fusion) | copy-start | bytes 3145732

commit v7 on v6

--- a/solution.py
+++ b/solution.py
@@ -126,17 +126,29 @@
     slot_onehot = (slot_rank[:, None] == jnp.arange(CAP, dtype=jnp.int32)[None, :]).astype(
         jnp.float32
     )
-    selector = (dest_onehot[:, :, None] * slot_onehot[:, None, :]).reshape(rows, n_bands * CAP)
+    selector = dest_onehot[:, :, None] * slot_onehot[:, None, :]
+    chunk = width + 128
 
     index_lanes = jnp.broadcast_to(block_index[0].astype(jnp.float32)[:, None], (rows, 128))
     payload = jnp.concatenate([flux.reshape(rows, width), index_lanes], axis=1)
-    sending = jnp.einsum("rk,rx->kx", selector, payload, precision=HIGHEST)
-    sending = sending.reshape(n_bands, CAP, width + 128).astype(LINK)
-    received = lax.all_to_all(sending, "band", 0, 0, tiled=True)
-    received = received.reshape(n_bands * CAP, width + 128).astype(jnp.float32)
-    got_index = received[:, width].astype(jnp.int32)
-    match = (got_index[:, None] == positions[None, :]).astype(jnp.float32)
-    partial = jnp.einsum("kr,kx->rx", match, received[:, :width], precision=HIGHEST)
+    sending = jnp.concatenate(
+        [
+            jnp.einsum("rb,rx->bx", selector[:, :, k], payload, precision=HIGHEST)
+            for k in range(CAP)
+        ],
+        axis=1,
+    ).astype(LINK)
+    received = lax.all_to_all(sending, "band", 0, 0, tiled=True).astype(jnp.float32)
+    matches = []
+    partial = None
+    for k in range(CAP):
+        got_index = received[:, k * chunk + width].astype(jnp.int32)
+        match = (got_index[:, None] == positions[None, :]).astype(jnp.float32)
+        matches.append(match)
+        term = jnp.einsum(
+            "br,bx->rx", match, received[:, k * chunk:k * chunk + width], precision=HIGHEST
+        )
+        partial = term if partial is None else partial + term
     last = n_sections - 1
     scaled = (COUPLING * partial).astype(LINK)
     heating = scaled.astype(jnp.float32)
@@ -145,8 +157,8 @@
 
     fields = diffuse(layer_temp, diffusivity)
     heating = jnp.where(is_ocean, heating, 0.0).reshape(rows, NF, cols)
+    sea_surface = (fields[:, :NF] + heating).astype(jnp.bfloat16)
     temp_out = fields.at[:, :NF].add(heating)
-    sea_surface = temp_out[:, :NF].astype(jnp.bfloat16)
     returned = lax.cond(
         is_ocean,
         lambda: jnp.einsum(
@@ -159,15 +171,29 @@
     for target in range(last):
         ocean_rows = ocean_rows + lax.ppermute(returned, "comp", [(last, target)])
     ocean_rows = ocean_rows.reshape(rows, width)
-    reply = jnp.einsum(
-        "kr,rx->kx", match.astype(jnp.bfloat16), ocean_rows, preferred_element_type=jnp.float32
-    ).astype(jnp.bfloat16)
-    reply = reply.reshape(n_bands, CAP, width)
+    reply = jnp.concatenate(
+        [
+            jnp.einsum(
+                "br,rx->bx",
+                match.astype(jnp.bfloat16),
+                ocean_rows,
+                preferred_element_type=jnp.float32,
+            ).astype(jnp.bfloat16)
+            for match in matches
+        ],
+        axis=1,
+    )
     came_back = lax.all_to_all(reply, "band", 0, 0, tiled=True)
-    came_back = came_back.reshape(n_bands * CAP, width)
-    seen = jnp.einsum(
-        "rk,kx->rx", selector.astype(jnp.bfloat16), came_back, preferred_element_type=jnp.float32
-    ).astype(jnp.bfloat16)
+    seen = None
+    for k in range(CAP):
+        term = jnp.einsum(
+            "rb,bx->rx",
+            selector[:, :, k].astype(jnp.bfloat16),
+            came_back[:, k * width:(k + 1) * width],
+            preferred_element_type=jnp.float32,
+        )
+        seen = term if seen is None else seen + term
+    seen = seen.astype(jnp.bfloat16)
     surface_temp = jnp.where(is_ocean, returned, seen.reshape(rows, NF, cols))
     return temp_out[None], surface_temp[None]
 

time: 70.3 us -> 76.4 us (1.087)
  matrix products: 7.1 us -> 9.76 us
  local copies, waits for them, and re-layouts: 2.32 us -> 4.07 us
  other arithmetic: 5.59 us -> 7.33 us
    dot_general x4 -> x16, matrix products: 1.47 us -> 4.13 us  [the longest x4 1.37 us: body(): jnp.einsum('br,bx->rx', match, received[:, k * chunk:k * chunk + width],...]
    unnamed x10 -> x15, local copies, waits for them, and re-layouts: 0.11 us -> 2.63 us
    concatenate x0 -> x2, other arithmetic: none -> 0.91 us  [body(): jnp.concatenate([jnp.einsum('rb,rx->bx', selector[:, :, k], payload, prec...]
    convert_element_type x1 -> x0, local copies, waits for them, and re-layouts: 0.91 us -> none  [body(): sending = sending.reshape(n_bands, CAP, width + 128).astype(LINK)]
    reshape x2 -> x0, local copies, waits for them, and re-layouts: 0.89 us -> none  [the longest x1 0.8 us: body(): reply = reply.reshape(n_bands, CAP, width)]
    all_to_all x0 -> x2, other arithmetic: none -> 0.81 us  [body(): came_back = lax.all_to_all(reply, 'band', 0, 0, tiled=True)]
  transfers between devices with their start and end apart: 10 -> 10, of which waited for: 3 -> 3; matrix products, arithmetic and copies ran while one was open for 4% -> 5% of each run, Pallas kernels for 11% -> 10%
where the time goes in v7:
time: 76.4 us; the launch traced here: 75.8 us
  starting transfers between devices  24.7 us (32%)
  waiting for transfers between devices  21.4 us (28%)
  matrix products  9.76 us (13%)
  Pallas kernels  7.42 us (10%)
  other arithmetic  7.33 us (10%)
  local copies, waits for them, and re-layouts  4.07 us (5%)
  between operations  1.08 us (1%)
    ppermute x3, waiting for transfers between devices, body(): ocean_rows = ocean_rows + lax.ppermute(returned, 'comp', [(last, target)])  9.62 us
    all_to_all x1, waiting for transfers between devices, body(): came_back = lax.all_to_all(reply, 'band', 0, 0, tiled=True)  8.76 us
    all_to_all x1, starting transfers between devices, body(): lax.all_to_all(sending, 'band', 0, 0, tiled=True).astype(jnp.float32)  8.58 us
    pallas_call x1, Pallas kernels, diffuse(): pl.pallas_call(_diffusion_kernel, out_shape=jax.ShapeDtypeStruct((rows, l...  7.42 us
    dot_general x1, matrix products, body(): jnp.einsum('rfc,rcd->rfd', surface_layers, weights_local, preferred_eleme...  4.76 us
    all_to_all x1, starting transfers between devices, body(): came_back = lax.all_to_all(reply, 'band', 0, 0, tiled=True)  4.55 us
    ppermute x1, starting transfers between devices, diffuse(): above = lax.ppermute(comb[rows - halo:], 'band', forward)  3.54 us
    ppermute x3, starting transfers between devices, body(): lax.ppermute(scaled, 'comp', [(source, last)]).astype(jnp.float32)  3.48 us
  transfers between devices with their start and end apart: 10, of which 3 were waited for; matrix products, arithmetic and copies ran while one was open for 5% of the time, Pallas kernels for 10%

profile of v7, /device:TPU:1, one launch (start us, length us, event | category | flops | bytes accessed | tf_op | source)
XLA Modules:
  0.0 75.8 jit_solution(15008737165091613486)
XLA Ops:
  0.6 0.9 %fusion.10 = f32[64]{0:T(128)S(1)} fusion(s32[64]{0:T(128)} %bitcast.91), kind=kOutput, calls=%fused_computation.27 | convolution fusion | flops 274368 | bytes 512 | tf_op jit(solution)/shard_map/dot_general | solution.py:124
  1.5 0.7 fusion.26
  2.2 0.7 convert_bitcast_fusion
  2.9 4.8 %conditional.2 = (f32[64,1024]{1,0:T(8,128)S(1)}) conditional(s32[]{:T(128)} %convert_element_type.143, (f32[1,64,16,256]{3,2,1,0:T(8,128)}, bf16[64,256,256]{2,1,0:T(8,128)(2,1)}) %tuple.40, () %tuple.27), branch_computations={%region_1.0_spmd, %region_2.0_spmd} | conditional | flops 33554432 | bytes 9306120 | solution.py:110
  2.9 4.8 %fusion.1 = f32[64,4,256]{2,1,0:T(4,128)S(1)} fusion(bf16[64,256,256]{2,1,0:T(8,128)(2,1)} %get-tuple-element.31, f32[1,64,16,256]{3,2,1,0:T(8,128)} %get-tuple-element.30), kind=kOutput, calls=%fused_computation.2 | convolution fusion | flops 33554432 | bytes 8781824 | tf_op jit(solution)/shard_map/cond/branch_0_fun/rfc,rcd->rfd/dot_general | solution.py:113
  7.8 0.3 fusion.4
  8.1 0.3 fusion.5
  8.4 0.3 fusion.6
  8.7 0.3 fusion.3
  9.1 0.5 broadcast.66
  9.6 0.8 %reduce.10 = f16[32,4608]{1,0:T(8,128)(2,1)S(1)} reduce(f16[32,1,4608]{2,0,1:T(8,128)(2,1)S(1)} %pad_maximum_fusion.2, f16[]{:T(256)} %broadcast.66), dimensions={1}, to_apply=%copy.10.reduce_sub_computation | reduce | bytes 589826 | tf_op jit(solution)/shard_map/concatenate | solution.py:134
  10.4 0.8 %reshape.177 = f16[32,2,2304]{2,1,0:T(2,128)(2,1)} reshape(f16[32,4608]{1,0:T(8,128)(2,1)S(1)} %reduce.10) | data formatting | bytes 589824
  11.2 8.6 %all-to-all-start = ((f16[32,2,2304]{2,1,0:T(2,128)(2,1)}), f16[32,2,2304]{2,1,0:T(2,128)(2,1)S(1)}, u32[]{:S(2)}, u32[]{:S(2)}) async-start(f16[32,2,2304]{2,1,0:T(2,128)(2,1)} %reshape.177), calls=%async_computation | async-start | bytes 589824 | tf_op jit(solution)/shard_map/all_to_all | solution.py:141
  19.9 3.5 %collective-permute-start = (f32[4,17,256]{2,1,0:T(8,128)S(1)}, f32[4,17,256]{2,1,0:T(8,128)S(1)}, u32[]{:S(2)}, u32[]{:S(2)}) collective-permute-start(f32[4,17,256]{2,1,0:T(8,128)S(1)} %get-tuple-element.42), channel_id=1, source_target_pairs={{0,1},{1,2},{2,3},{3,4},{4,5},{5,6},{6,7},{7,8},{8,9},{9,10},{10,1... | collective-permute-start | bytes 208904 | tf_op jit(solution)/shard_map/ppermute | solution.py:81
  23.4 1.9 %collective-permute-start.1 = (f32[4,17,256]{2,1,0:T(8,128)S(1)}, f32[4,17,256]{2,1,0:T(8,128)S(1)}, u32[]{:S(2)}, u32[]{:S(2)}) collective-permute-start(f32[4,17,256]{2,1,0:T(8,128)S(1)} %get-tuple-element.43), channel_id=1, source_target_pairs={{1,0},{2,1},{3,2},{4,3},{5,4},{6,5},{7,6},{8,7},{9,8},{10,9},{11,1... | collective-permute-start | bytes 208904 | tf_op jit(solution)/shard_map/ppermute | solution.py:82
  25.4 0.6 pad_add_fusion.bounds_ref
  26.0 3.0 %all-to-all-done = f16[32,2,2304]{2,1,0:T(2,128)(2,1)S(1)} async-done(((f16[32,2,2304]{2,1,0:T(2,128)(2,1)}), f16[32,2,2304]{2,1,0:T(2,128)(2,1)S(1)}, u32[]{:S(2)}, u32[]{:S(2)}) %all-to-all-start) | async-done | bytes 294944 | tf_op jit(solution)/shard_map/all_to_all | solution.py:141
  29.0 0.3 reshape.178
  29.5 0.3 fusion.20
  29.9 0.3 convolution_add_fusion.5
  30.2 0.3 convolution_add_fusion.4
  30.5 0.3 fusion.8
  30.9 0.7 collective-permute-start.4
  31.6 0.7 collective-permute-start.3
  32.3 2.1 %collective-permute-start.2 = (f16[64,1024]{1,0:T(8,128)(2,1)S(1)}, f16[64,1024]{1,0:T(8,128)(2,1)S(1)}, u32[]{:S(2)}, u32[]{:S(2)}) collective-permute-start(f16[64,1024]{1,0:T(8,128)(2,1)S(1)} %fusion.8), channel_id=1, source_target_pairs={{0,96},{1,97},{2,98},{3,99},{4,100},{5,101},{6,102},{7,103},{8,104... | collective-permute-start | bytes 393224 | tf_op jit(solution)/shard_map/ppermute | solution.py:156
  34.4 1.4 %pad_maximum_fusion.p_ref = f32[72,17,256]{2,1,0:T(8,128)} fusion(f32[4,17,256]{2,1,0:T(8,128)S(1)} %collective-permute-done.1, f32[64,1,256]{2,1,0:T(1,128)S(1)} %broadcast_in_dim_squeeze.4, f32[64,16,256]{2,1,0:T(8,128)S(1)} %bitcast.74, f32[4,17,256]{2,1,0:T(8,128)S(1)} %collective-permute-done), kind=kLoop, calls=%fused_computation.12 | loop fusion | flops 940032 | bytes 2506752 | tf_op jit(solution)/shard_map/concatenate | solution.py:83
  35.8 7.4 %shard_map.68 = f32[64,16,256]{2,1,0:T(8,128)} custom-call(s32[2]{0:T(128)} %pad_add_fusion.bounds_ref, f32[72,17,256]{2,1,0:T(8,128)} %pad_maximum_fusion.p_ref), custom_call_target="tpu_custom_call" | custom-call | tf_op jit(solution)/shard_map/pallas_call | solution.py:87
  43.5 1.1 %fusion.11 = bf16[64,4,256]{2,1,0:T(4,128)(2,1)S(1)} fusion(f32[64,4,256]{2,1,0:T(4,128)S(1)} %reshape.170, f32[64,16,256]{2,1,0:T(8,128)} %shard_map.68), kind=kLoop, calls=%fused_computation.40 | loop fusion | flops 131072 | bytes 655360 | tf_op jit(solution)/shard_map/convert_element_type | solution.py:160
  44.6 0.7 collective-permute-start.7
  45.3 0.7 collective-permute-start.6
  46.0 1.3 %collective-permute-start.5 = (bf16[64,4,256]{2,1,0:T(4,128)(2,1)S(1)}, bf16[64,4,256]{2,1,0:T(4,128)(2,1)S(1)}, u32[]{:S(2)}, u32[]{:S(2)}) collective-permute-start(bf16[64,4,256]{2,1,0:T(4,128)(2,1)S(1)} %get-tuple-element.45), channel_id=1, source_target_pairs={{96,0},{97,1},{98,2},{99,3},{100,4},{101,5},{102,6},{103,7},{104,8... | collective-permute-start | bytes 393224 | tf_op jit(solution)/shard_map/ppermute | solution.py:172
  47.3 9.6 %collective-permute-done.5 = bf16[64,4,256]{2,1,0:T(4,128)(2,1)S(1)} collective-permute-done((bf16[64,4,256]{2,1,0:T(4,128)(2,1)S(1)}, bf16[64,4,256]{2,1,0:T(4,128)(2,1)S(1)}, u32[]{:S(2)}, u32[]{:S(2)}) %collective-permute-start.5) | collective-permute-done | bytes 131104 | tf_op jit(solution)/shard_map/ppermute | solution.py:172
  57.0 0.2 convolution_convert_fusion.5
  57.2 0.2 convolution_convert_fusion.6
  57.4 0.2 convolution_convert_fusion.7
  57.6 0.2 convolution_convert_fusion.8
  57.9 0.5 broadcast.67
  58.4 0.8 %reduce.11 = bf16[32,4096]{1,0:T(8,128)(2,1)S(1)} reduce(bf16[32,1,4096]{2,0,1:T(8,128)(2,1)S(1)} %maximum_bitcast_fusion, bf16[]{:T(256)} %broadcast.67), dimensions={1}, to_apply=%copy.11.reduce_sub_computation | reduce | bytes 524290 | tf_op jit(solution)/shard_map/all_to_all | solution.py:186
  59.2 0.9 %reshape.179 = bf16[32,2,2048]{2,1,0:T(2,128)(2,1)} reshape(bf16[32,4096]{1,0:T(8,128)(2,1)S(1)} %reduce.11) | data formatting | bytes 524288
  60.0 4.5 %all-to-all-start.1 = ((bf16[32,2,2048]{2,1,0:T(2,128)(2,1)}), bf16[32,2,2048]{2,1,0:T(2,128)(2,1)S(1)}, u32[]{:S(2)}, u32[]{:S(2)}) async-start(bf16[32,2,2048]{2,1,0:T(2,128)(2,1)} %reshape.179), calls=%async_computation.1 | async-start | bytes 524288 | tf_op jit(solution)/shard_map/all_to_all | solution.py:186
  64.8 8.8 %all-to-all-done.1 = bf16[32,2,2048]{2,1,0:T(2,128)(2,1)S(1)} async-done(((bf16[32,2,2048]{2,1,0:T(2,128)(2,1)}), bf16[32,2,2048]{2,1,0:T(2,128)(2,1)S(1)}, u32[]{:S(2)}, u32[]{:S(2)}) %all-to-all-start.1) | async-done | bytes 262176 | tf_op jit(solution)/shard_map/all_to_all | solution.py:186
  73.6 0.3 reshape.180
  73.8 0.3 copy.19
  74.1 0.2 fusion.15
  74.3 0.2 convolution_add_fusion.2
  74.6 0.2 convolution_add_fusion.1
  74.8 0.2 fusion.9
  75.1 0.7 select_bitcast_fusion
  (35 shorter events, 1.2 us)
Async XLA Ops:
  8.1 11.7 %copy-start.3 = (f32[1,64,256]{2,1,0:T(8,128)S(1)}, f32[1,64,256]{2,1,0:T(8,128)}, u32[]{:S(2)}) copy-start(f32[1,64,256]{2,1,0:T(8,128)} %param.12) | copy-start | bytes 196612
  8.1 11.8 %copy-start = (f32[1,64,16,256]{3,2,1,0:T(8,128)S(1)}, f32[1,64,16,256]{3,2,1,0:T(8,128)}, u32[]{:S(2)}) copy-start(f32[1,64,16,256]{3,2,1,0:T(8,128)} %param.11) | copy-start | bytes 3145732
  11.2 17.8 %all-to-all-start = ((f16[32,2,2304]{2,1,0:T(2,128)(2,1)}), f16[32,2,2304]{2,1,0:T(2,128)(2,1)S(1)}, u32[]{:S(2)}, u32[]{:S(2)}) async-start(f16[32,2,2304]{2,1,0:T(2,128)(2,1)} %reshape.177), calls=%async_computation | async-start | bytes 589824 | tf_op jit(solution)/shard_map/all_to_all | solution.py:141
  19.9 14.5 %collective-permute-start = (f32[4,17,256]{2,1,0:T(8,128)S(1)}, f32[4,17,256]{2,1,0:T(8,128)S(1)}, u32[]{:S(2)}, u32[]{:S(2)}) collective-permute-start(f32[4,17,256]{2,1,0:T(8,128)S(1)} %get-tuple-element.42), channel_id=1, source_target_pairs={{0,1},{1,2},{2,3},{3,4},{4,5},{5,6},{6,7},{7,8},{8,9},{9,10},{10,1... | collective-permute-start | bytes 208904 | tf_op jit(solution)/shard_map/ppermute | solution.py:81
  23.4 11.0 %collective-permute-start.1 = (f32[4,17,256]{2,1,0:T(8,128)S(1)}, f32[4,17,256]{2,1,0:T(8,128)S(1)}, u32[]{:S(2)}, u32[]{:S(2)}) collective-permute-start(f32[4,17,256]{2,1,0:T(8,128)S(1)} %get-tuple-element.43), channel_id=1, source_target_pairs={{1,0},{2,1},{3,2},{4,3},{5,4},{6,5},{7,6},{8,7},{9,8},{10,9},{11,1... | collective-permute-start | bytes 208904 | tf_op jit(solution)/shard_map/ppermute | solution.py:82
  30.9 12.3 %collective-permute-start.4 = (f16[64,1024]{1,0:T(8,128)(2,1)S(1)}, f16[64,1024]{1,0:T(8,128)(2,1)S(1)}, u32[]{:S(2)}, u32[]{:S(2)}) collective-permute-start(f16[64,1024]{1,0:T(8,128)(2,1)S(1)} %fusion.8), channel_id=1, source_target_pairs={{64,96},{65,97},{66,98},{67,99},{68,100},{69,101},{70,102},{71,103... | collective-permute-start | bytes 393224 | tf_op jit(solution)/shard_map/ppermute | solution.py:156
  31.6 11.7 %collective-permute-start.3 = (f16[64,1024]{1,0:T(8,128)(2,1)S(1)}, f16[64,1024]{1,0:T(8,128)(2,1)S(1)}, u32[]{:S(2)}, u32[]{:S(2)}) collective-permute-start(f16[64,1024]{1,0:T(8,128)(2,1)S(1)} %fusion.8), channel_id=1, source_target_pairs={{32,96},{33,97},{34,98},{35,99},{36,100},{37,101},{38,102},{39,103... | collective-permute-start | bytes 393224 | tf_op jit(solution)/shard_map/ppermute | solution.py:156
  32.3 11.0 %collective-permute-start.2 = (f16[64,1024]{1,0:T(8,128)(2,1)S(1)}, f16[64,1024]{1,0:T(8,128)(2,1)S(1)}, u32[]{:S(2)}, u32[]{:S(2)}) collective-permute-start(f16[64,1024]{1,0:T(8,128)(2,1)S(1)} %fusion.8), channel_id=1, source_target_pairs={{0,96},{1,97},{2,98},{3,99},{4,100},{5,101},{6,102},{7,103},{8,104... | collective-permute-start | bytes 393224 | tf_op jit(solution)/shard_map/ppermute | solution.py:156
  44.6 2.7 %collective-permute-start.7 = (bf16[64,4,256]{2,1,0:T(4,128)(2,1)S(1)}, bf16[64,4,256]{2,1,0:T(4,128)(2,1)S(1)}, u32[]{:S(2)}, u32[]{:S(2)}) collective-permute-start(bf16[64,4,256]{2,1,0:T(4,128)(2,1)S(1)} %get-tuple-element.45), channel_id=1, source_target_pairs={{96,64},{97,65},{98,66},{99,67},{100,68},{101,69},{102,70},{103,71... | collective-permute-start | bytes 393224 | tf_op jit(solution)/shard_map/ppermute | solution.py:172
  45.3 2.0 %collective-permute-start.6 = (bf16[64,4,256]{2,1,0:T(4,128)(2,1)S(1)}, bf16[64,4,256]{2,1,0:T(4,128)(2,1)S(1)}, u32[]{:S(2)}, u32[]{:S(2)}) collective-permute-start(bf16[64,4,256]{2,1,0:T(4,128)(2,1)S(1)} %get-tuple-element.45), channel_id=1, source_target_pairs={{96,32},{97,33},{98,34},{99,35},{100,36},{101,37},{102,38},{103,39... | collective-permute-start | bytes 393224 | tf_op jit(solution)/shard_map/ppermute | solution.py:172
  46.0 10.9 %collective-permute-start.5 = (bf16[64,4,256]{2,1,0:T(4,128)(2,1)S(1)}, bf16[64,4,256]{2,1,0:T(4,128)(2,1)S(1)}, u32[]{:S(2)}, u32[]{:S(2)}) collective-permute-start(bf16[64,4,256]{2,1,0:T(4,128)(2,1)S(1)} %get-tuple-element.45), channel_id=1, source_target_pairs={{96,0},{97,1},{98,2},{99,3},{100,4},{101,5},{102,6},{103,7},{104,8... | collective-permute-start | bytes 393224 | tf_op jit(solution)/shard_map/ppermute | solution.py:172
  56.9 7.7 %copy-start.1 = (f32[64,16,256]{2,1,0:T(8,128)S(1)}, f32[64,16,256]{2,1,0:T(8,128)}, u32[]{:S(2)}) copy-start(f32[64,16,256]{2,1,0:T(8,128)} %shard_map.68) | copy-start | bytes 3145732
  60.0 13.5 %all-to-all-start.1 = ((bf16[32,2,2048]{2,1,0:T(2,128)(2,1)}), bf16[32,2,2048]{2,1,0:T(2,128)(2,1)S(1)}, u32[]{:S(2)}, u32[]{:S(2)}) async-start(bf16[32,2,2048]{2,1,0:T(2,128)(2,1)} %reshape.179), calls=%async_computation.1 | async-start | bytes 524288 | tf_op jit(solution)/shard_map/all_to_all | solution.py:186
  64.8 10.2 %copy-start.2 = (f32[1,64,16,256]{3,2,1,0:T(8,128)}, f32[1,64,16,256]{3,2,1,0:T(8,128)S(1)}, u32[]{:S(2)}) copy-start(f32[1,64,16,256]{3,2,1,0:T(8,128)S(1)} %bitcast_dynamic-update-slice_fusion) | copy-start | bytes 3145732

commit v8 on v6

--- a/solution.py
+++ b/solution.py
@@ -121,7 +121,11 @@
     )
     positions = jnp.arange(rows, dtype=jnp.int32)
     earlier_mask = (positions[:, None] > positions[None, :]).astype(jnp.float32)
-    earlier = jnp.dot(earlier_mask, dest_onehot, precision=HIGHEST)
+    earlier = jnp.dot(
+        earlier_mask.astype(jnp.bfloat16),
+        dest_onehot.astype(jnp.bfloat16),
+        preferred_element_type=jnp.float32,
+    )
     slot_rank = jnp.sum(earlier * dest_onehot, axis=1).astype(jnp.int32)
     slot_onehot = (slot_rank[:, None] == jnp.arange(CAP, dtype=jnp.int32)[None, :]).astype(
         jnp.float32

time: 70.3 us -> 70.3 us (level)
  no operation moved by 1% of the time
where the time goes in v8:
time: 70.3 us; the launch traced here: 69.8 us
  starting transfers between devices  25.2 us (36%)
  waiting for transfers between devices  21.1 us (30%)
  Pallas kernels  7.42 us (11%)
  matrix products  7.09 us (10%)
  other arithmetic  5.59 us (8%)
  local copies, waits for them, and re-layouts  2.32 us (3%)
  between operations  0.95 us (1%)
    ppermute x3, waiting for transfers between devices, body(): ocean_rows = ocean_rows + lax.ppermute(returned, 'comp', [(last, target)])  9.61 us
    all_to_all x1, waiting for transfers between devices, body(): came_back = lax.all_to_all(reply, 'band', 0, 0, tiled=True)  8.65 us
    all_to_all x1, starting transfers between devices, body(): received = lax.all_to_all(sending, 'band', 0, 0, tiled=True)  8.58 us
    pallas_call x1, Pallas kernels, diffuse(): pl.pallas_call(_diffusion_kernel, out_shape=jax.ShapeDtypeStruct((rows, l...  7.42 us
    all_to_all x1, starting transfers between devices, body(): came_back = lax.all_to_all(reply, 'band', 0, 0, tiled=True)  4.86 us
    dot_general x1, matrix products, body(): jnp.einsum('rfc,rcd->rfd', surface_layers, weights_local, preferred_eleme...  4.76 us
    ppermute x3, starting transfers between devices, body(): lax.ppermute(scaled, 'comp', [(source, last)]).astype(jnp.float32)  3.46 us
    ppermute x1, starting transfers between devices, diffuse(): above = lax.ppermute(comb[rows - halo:], 'band', forward)  3.42 us
  transfers between devices with their start and end apart: 10, of which 3 were waited for; matrix products, arithmetic and copies ran while one was open for 4% of the time, Pallas kernels for 11%

profile of v8, /device:TPU:1, one launch (start us, length us, event | category | flops | bytes accessed | tf_op | source)
XLA Modules:
  0.0 69.8 jit_solution(15358597106596214117)
XLA Ops:
  0.6 0.9 %fusion.5 = f32[64]{0:T(128)S(1)} fusion(s32[64]{0:T(128)} %bitcast.54), kind=kOutput, calls=%fused_computation.12 | convolution fusion | flops 286656 | bytes 512 | tf_op jit(solution)/shard_map/dot_general | solution.py:124
  1.5 0.7 fusion.15
  2.2 0.7 convert_bitcast_fusion
  2.9 4.8 %conditional.2 = (f32[64,1024]{1,0:T(8,128)S(1)}) conditional(s32[]{:T(128)} %convert_element_type.100, (f32[1,64,16,256]{3,2,1,0:T(8,128)}, bf16[64,256,256]{2,1,0:T(8,128)(2,1)}) %tuple.37, () %tuple.27), branch_computations={%region_1.0_spmd, %region_2.0_spmd} | conditional | flops 33554432 | bytes 9306120 | solution.py:110
  2.9 4.8 %fusion.1 = f32[64,4,256]{2,1,0:T(4,128)S(1)} fusion(bf16[64,256,256]{2,1,0:T(8,128)(2,1)} %get-tuple-element.31, f32[1,64,16,256]{3,2,1,0:T(8,128)} %get-tuple-element.30), kind=kOutput, calls=%fused_computation.2 | convolution fusion | flops 33554432 | bytes 8781824 | tf_op jit(solution)/shard_map/cond/branch_0_fun/rfc,rcd->rfd/dot_general | solution.py:113
  7.6 0.1 copy.20
  7.7 0.0 copy-start.3
  7.7 0.0 copy-start
  7.7 0.1 broadcast_in_dim.12
  7.8 0.6 convolution_convert_fusion.1
  8.4 0.9 %copy.17 = f16[32,4,1152]{2,1,0:T(4,128)(2,1)} copy(f16[32,4,1152]{2,0,1:T(8,128)(2,1)S(1)} %convolution_convert_fusion.1) | data formatting | bytes 589824 | tf_op jit(solution)/shard_map/convert_element_type | solution.py:138
  9.3 8.6 %all-to-all-start = ((f16[32,4,1152]{2,1,0:T(4,128)(2,1)}), f16[32,4,1152]{2,1,0:T(4,128)(2,1)S(1)}, u32[]{:S(2)}, u32[]{:S(2)}) async-start(f16[32,4,1152]{2,1,0:T(4,128)(2,1)} %copy.17), calls=%async_computation | async-start | bytes 589824 | tf_op jit(solution)/shard_map/all_to_all | solution.py:139
  18.0 2.1 %collective-permute-start.1 = (f32[4,17,256]{2,1,0:T(8,128)S(1)}, f32[4,17,256]{2,1,0:T(8,128)S(1)}, u32[]{:S(2)}, u32[]{:S(2)}) collective-permute-start(f32[4,17,256]{2,1,0:T(8,128)S(1)} %get-tuple-element.37), channel_id=1, source_target_pairs={{1,0},{2,1},{3,2},{4,3},{5,4},{6,5},{7,6},{8,7},{9,8},{10,9},{11,1... | collective-permute-start | bytes 208904 | tf_op jit(solution)/shard_map/ppermute | solution.py:82
  20.2 3.4 %collective-permute-start = (f32[4,17,256]{2,1,0:T(8,128)S(1)}, f32[4,17,256]{2,1,0:T(8,128)S(1)}, u32[]{:S(2)}, u32[]{:S(2)}) collective-permute-start(f32[4,17,256]{2,1,0:T(8,128)S(1)} %get-tuple-element.36), channel_id=1, source_target_pairs={{0,1},{1,2},{2,3},{3,4},{4,5},{5,6},{6,7},{7,8},{8,9},{9,10},{10,1... | collective-permute-start | bytes 208904 | tf_op jit(solution)/shard_map/ppermute | solution.py:81
  23.6 0.7 pad_add_fusion.bounds_ref
  24.3 2.8 %all-to-all-done = f16[32,4,1152]{2,1,0:T(4,128)(2,1)S(1)} async-done(((f16[32,4,1152]{2,1,0:T(4,128)(2,1)}), f16[32,4,1152]{2,1,0:T(4,128)(2,1)S(1)}, u32[]{:S(2)}, u32[]{:S(2)}) %all-to-all-start) | async-done | bytes 294944 | tf_op jit(solution)/shard_map/all_to_all | solution.py:139
  27.1 0.1 reshape.121
  27.2 0.1 convert_reduce_fusion
  27.3 0.4 fusion.4
  27.7 0.7 collective-permute-start.4
  28.4 0.7 collective-permute-start.3
  29.1 2.1 %collective-permute-start.2 = (f16[64,1024]{1,0:T(8,128)(2,1)S(1)}, f16[64,1024]{1,0:T(8,128)(2,1)S(1)}, u32[]{:S(2)}, u32[]{:S(2)}) collective-permute-start(f16[64,1024]{1,0:T(8,128)(2,1)S(1)} %fusion.4), channel_id=1, source_target_pairs={{0,96},{1,97},{2,98},{3,99},{4,100},{5,101},{6,102},{7,103},{8,104... | collective-permute-start | bytes 393224 | tf_op jit(solution)/shard_map/ppermute | solution.py:148
  31.2 0.0 collective-permute-done.1
  31.2 0.0 collective-permute-done
  31.2 1.4 %pad_maximum_fusion.p_ref = f32[72,17,256]{2,1,0:T(8,128)} fusion(f32[4,17,256]{2,1,0:T(8,128)S(1)} %collective-permute-done.1, f32[64,1,256]{2,1,0:T(1,128)S(1)} %broadcast_in_dim_squeeze.4, f32[64,16,256]{2,1,0:T(8,128)S(1)} %bitcast.44, f32[4,17,256]{2,1,0:T(8,128)S(1)} %collective-permute-done), kind=kLoop, calls=%fused_computation.5 | loop fusion | flops 940032 | bytes 2506752 | tf_op jit(solution)/shard_map/concatenate | solution.py:83
  32.6 7.4 %shard_map.68 = f32[64,16,256]{2,1,0:T(8,128)} custom-call(s32[2]{0:T(128)} %pad_add_fusion.bounds_ref, f32[72,17,256]{2,1,0:T(8,128)} %pad_maximum_fusion.p_ref), custom_call_target="tpu_custom_call" | custom-call | tf_op jit(solution)/shard_map/pallas_call | solution.py:87
  40.0 0.0 collective-permute-done.4
  40.0 0.1 add_select_fusion
  40.1 0.1 reshape.122
  40.2 1.1 %fusion.10 = bf16[64,4,256]{2,1,0:T(4,128)(2,1)S(1)} fusion(f32[64,4,256]{2,1,0:T(4,128)S(1)} %reshape.122, f32[64,16,256]{2,1,0:T(8,128)} %shard_map.68), kind=kLoop, calls=%fused_computation.27 | loop fusion | flops 131072 | bytes 655360 | tf_op jit(solution)/shard_map/convert_element_type | solution.py:153
  41.4 0.1 conditional.3
  41.4 0.0 copy-start.1
  41.4 0.8 %collective-permute-start.7 = (bf16[64,4,256]{2,1,0:T(4,128)(2,1)S(1)}, bf16[64,4,256]{2,1,0:T(4,128)(2,1)S(1)}, u32[]{:S(2)}, u32[]{:S(2)}) collective-permute-start(bf16[64,4,256]{2,1,0:T(4,128)(2,1)S(1)} %get-tuple-element.41), channel_id=1, source_target_pairs={{96,64},{97,65},{98,66},{99,67},{100,68},{101,69},{102,70},{103,71... | collective-permute-start | bytes 393224 | tf_op jit(solution)/shard_map/ppermute | solution.py:164
  42.2 0.7 collective-permute-start.6
  42.9 1.3 %collective-permute-start.5 = (bf16[64,4,256]{2,1,0:T(4,128)(2,1)S(1)}, bf16[64,4,256]{2,1,0:T(4,128)(2,1)S(1)}, u32[]{:S(2)}, u32[]{:S(2)}) collective-permute-start(bf16[64,4,256]{2,1,0:T(4,128)(2,1)S(1)} %get-tuple-element.41), channel_id=1, source_target_pairs={{96,0},{97,1},{98,2},{99,3},{100,4},{101,5},{102,6},{103,7},{104,8... | collective-permute-start | bytes 393224 | tf_op jit(solution)/shard_map/ppermute | solution.py:164
  44.2 0.0 collective-permute-done.7
  44.2 0.0 collective-permute-done.6
  44.2 9.6 %collective-permute-done.5 = bf16[64,4,256]{2,1,0:T(4,128)(2,1)S(1)} collective-permute-done((bf16[64,4,256]{2,1,0:T(4,128)(2,1)S(1)}, bf16[64,4,256]{2,1,0:T(4,128)(2,1)S(1)}, u32[]{:S(2)}, u32[]{:S(2)}) %collective-permute-start.5) | collective-permute-done | bytes 131104 | tf_op jit(solution)/shard_map/ppermute | solution.py:164
  53.9 0.3 convolution_convert_fusion.2
  54.2 0.8 %reshape.124 = bf16[32,4,1024]{2,1,0:T(4,128)(2,1)} reshape(bf16[128,1024]{1,0:T(8,128)(2,1)S(1)} %convolution_convert_fusion.2) | data formatting | bytes 524288 | tf_op jit(solution)/shard_map/reshape | solution.py:169
  55.0 4.9 %all-to-all-start.1 = ((bf16[32,4,1024]{2,1,0:T(4,128)(2,1)}), bf16[32,4,1024]{2,1,0:T(4,128)(2,1)S(1)}, u32[]{:S(2)}, u32[]{:S(2)}) async-start(bf16[32,4,1024]{2,1,0:T(4,128)(2,1)} %reshape.124), calls=%async_computation.1 | async-start | bytes 524288 | tf_op jit(solution)/shard_map/all_to_all | solution.py:170
  59.9 0.1 copy.30
  59.9 0.1 bitcast_dynamic-update-slice_fusion
  60.1 0.0 copy-start.2
  60.1 8.6 %all-to-all-done.1 = bf16[32,4,1024]{2,1,0:T(4,128)(2,1)S(1)} async-done(((bf16[32,4,1024]{2,1,0:T(4,128)(2,1)}), bf16[32,4,1024]{2,1,0:T(4,128)(2,1)S(1)}, u32[]{:S(2)}, u32[]{:S(2)}) %all-to-all-start.1) | async-done | bytes 262176 | tf_op jit(solution)/shard_map/all_to_all | solution.py:170
  68.7 0.2 fusion.3
  68.9 0.1 reshape.125
  69.0 0.7 %select_bitcast_fusion = bf16[1,64,4,256]{3,2,1,0:T(4,128)(2,1)} fusion(bf16[64,4,256]{2,1,0:T(4,128)(2,1)S(1)} %get-tuple-element.41, bf16[64,4,256]{2,1,0:T(4,128)(2,1)S(1)} %reshape.125, pred[]{:T(512)S(6)} %eq.62), kind=kLoop, calls=%fused_computation.21 | loop fusion | flops 65536 | bytes 393217 | tf_op jit(solution)/shard_map/broadcast_in_dim | solution.py:176
  (14 shorter events, 0.2 us)
Async XLA Ops:
  7.7 10.2 %copy-start.3 = (f32[1,64,256]{2,1,0:T(8,128)S(1)}, f32[1,64,256]{2,1,0:T(8,128)}, u32[]{:S(2)}) copy-start(f32[1,64,256]{2,1,0:T(8,128)} %param.12) | copy-start | bytes 196612
  7.7 10.3 %copy-start = (f32[1,64,16,256]{3,2,1,0:T(8,128)S(1)}, f32[1,64,16,256]{3,2,1,0:T(8,128)}, u32[]{:S(2)}) copy-start(f32[1,64,16,256]{3,2,1,0:T(8,128)} %param.11) | copy-start | bytes 3145732
  9.3 17.8 %all-to-all-start = ((f16[32,4,1152]{2,1,0:T(4,128)(2,1)}), f16[32,4,1152]{2,1,0:T(4,128)(2,1)S(1)}, u32[]{:S(2)}, u32[]{:S(2)}) async-start(f16[32,4,1152]{2,1,0:T(4,128)(2,1)} %copy.17), calls=%async_computation | async-start | bytes 589824 | tf_op jit(solution)/shard_map/all_to_all | solution.py:139
  18.0 13.2 %collective-permute-start.1 = (f32[4,17,256]{2,1,0:T(8,128)S(1)}, f32[4,17,256]{2,1,0:T(8,128)S(1)}, u32[]{:S(2)}, u32[]{:S(2)}) collective-permute-start(f32[4,17,256]{2,1,0:T(8,128)S(1)} %get-tuple-element.37), channel_id=1, source_target_pairs={{1,0},{2,1},{3,2},{4,3},{5,4},{6,5},{7,6},{8,7},{9,8},{10,9},{11,1... | collective-permute-start | bytes 208904 | tf_op jit(solution)/shard_map/ppermute | solution.py:82
  20.2 11.0 %collective-permute-start = (f32[4,17,256]{2,1,0:T(8,128)S(1)}, f32[4,17,256]{2,1,0:T(8,128)S(1)}, u32[]{:S(2)}, u32[]{:S(2)}) collective-permute-start(f32[4,17,256]{2,1,0:T(8,128)S(1)} %get-tuple-element.36), channel_id=1, source_target_pairs={{0,1},{1,2},{2,3},{3,4},{4,5},{5,6},{6,7},{7,8},{8,9},{9,10},{10,1... | collective-permute-start | bytes 208904 | tf_op jit(solution)/shard_map/ppermute | solution.py:81
  27.7 12.3 %collective-permute-start.4 = (f16[64,1024]{1,0:T(8,128)(2,1)S(1)}, f16[64,1024]{1,0:T(8,128)(2,1)S(1)}, u32[]{:S(2)}, u32[]{:S(2)}) collective-permute-start(f16[64,1024]{1,0:T(8,128)(2,1)S(1)} %fusion.4), channel_id=1, source_target_pairs={{64,96},{65,97},{66,98},{67,99},{68,100},{69,101},{70,102},{71,103... | collective-permute-start | bytes 393224 | tf_op jit(solution)/shard_map/ppermute | solution.py:148
  28.4 11.6 %collective-permute-start.3 = (f16[64,1024]{1,0:T(8,128)(2,1)S(1)}, f16[64,1024]{1,0:T(8,128)(2,1)S(1)}, u32[]{:S(2)}, u32[]{:S(2)}) collective-permute-start(f16[64,1024]{1,0:T(8,128)(2,1)S(1)} %fusion.4), channel_id=1, source_target_pairs={{32,96},{33,97},{34,98},{35,99},{36,100},{37,101},{38,102},{39,103... | collective-permute-start | bytes 393224 | tf_op jit(solution)/shard_map/ppermute | solution.py:148
  29.1 11.0 %collective-permute-start.2 = (f16[64,1024]{1,0:T(8,128)(2,1)S(1)}, f16[64,1024]{1,0:T(8,128)(2,1)S(1)}, u32[]{:S(2)}, u32[]{:S(2)}) collective-permute-start(f16[64,1024]{1,0:T(8,128)(2,1)S(1)} %fusion.4), channel_id=1, source_target_pairs={{0,96},{1,97},{2,98},{3,99},{4,100},{5,101},{6,102},{7,103},{8,104... | collective-permute-start | bytes 393224 | tf_op jit(solution)/shard_map/ppermute | solution.py:148
  41.4 18.4 %copy-start.1 = (f32[64,16,256]{2,1,0:T(8,128)S(1)}, f32[64,16,256]{2,1,0:T(8,128)}, u32[]{:S(2)}) copy-start(f32[64,16,256]{2,1,0:T(8,128)} %shard_map.68) | copy-start | bytes 3145732
  41.4 2.8 %collective-permute-start.7 = (bf16[64,4,256]{2,1,0:T(4,128)(2,1)S(1)}, bf16[64,4,256]{2,1,0:T(4,128)(2,1)S(1)}, u32[]{:S(2)}, u32[]{:S(2)}) collective-permute-start(bf16[64,4,256]{2,1,0:T(4,128)(2,1)S(1)} %get-tuple-element.41), channel_id=1, source_target_pairs={{96,64},{97,65},{98,66},{99,67},{100,68},{101,69},{102,70},{103,71... | collective-permute-start | bytes 393224 | tf_op jit(solution)/shard_map/ppermute | solution.py:164
  42.2 2.0 %collective-permute-start.6 = (bf16[64,4,256]{2,1,0:T(4,128)(2,1)S(1)}, bf16[64,4,256]{2,1,0:T(4,128)(2,1)S(1)}, u32[]{:S(2)}, u32[]{:S(2)}) collective-permute-start(bf16[64,4,256]{2,1,0:T(4,128)(2,1)S(1)} %get-tuple-element.41), channel_id=1, source_target_pairs={{96,32},{97,33},{98,34},{99,35},{100,36},{101,37},{102,38},{103,39... | collective-permute-start | bytes 393224 | tf_op jit(solution)/shard_map/ppermute | solution.py:164
  42.9 10.9 %collective-permute-start.5 = (bf16[64,4,256]{2,1,0:T(4,128)(2,1)S(1)}, bf16[64,4,256]{2,1,0:T(4,128)(2,1)S(1)}, u32[]{:S(2)}, u32[]{:S(2)}) collective-permute-start(bf16[64,4,256]{2,1,0:T(4,128)(2,1)S(1)} %get-tuple-element.41), channel_id=1, source_target_pairs={{96,0},{97,1},{98,2},{99,3},{100,4},{101,5},{102,6},{103,7},{104,8... | collective-permute-start | bytes 393224 | tf_op jit(solution)/shard_map/ppermute | solution.py:164
  55.0 13.7 %all-to-all-start.1 = ((bf16[32,4,1024]{2,1,0:T(4,128)(2,1)}), bf16[32,4,1024]{2,1,0:T(4,128)(2,1)S(1)}, u32[]{:S(2)}, u32[]{:S(2)}) async-start(bf16[32,4,1024]{2,1,0:T(4,128)(2,1)} %reshape.124), calls=%async_computation.1 | async-start | bytes 524288 | tf_op jit(solution)/shard_map/all_to_all | solution.py:170
  60.1 9.7 %copy-start.2 = (f32[1,64,16,256]{3,2,1,0:T(8,128)}, f32[1,64,16,256]{3,2,1,0:T(8,128)S(1)}, u32[]{:S(2)}) copy-start(f32[1,64,16,256]{3,2,1,0:T(8,128)S(1)} %bitcast_dynamic-update-slice_fusion) | copy-start | bytes 3145732

commit v9 on v8

--- a/solution.py
+++ b/solution.py
@@ -142,10 +142,22 @@
     match = (got_index[:, None] == positions[None, :]).astype(jnp.float32)
     partial = jnp.einsum("kr,kx->rx", match, received[:, :width], precision=HIGHEST)
     last = n_sections - 1
-    scaled = (COUPLING * partial).astype(LINK)
-    heating = scaled.astype(jnp.float32)
-    for source in range(last):
-        heating = heating + lax.ppermute(scaled, "comp", [(source, last)]).astype(jnp.float32)
+    part = COUPLING * partial
+    if n_sections == 4:
+        half = rows // 2
+        up = lax.ppermute(part[:half].astype(LINK), "comp", [(1, 2)])
+        down = lax.ppermute(part[half:].astype(LINK), "comp", [(1, 0)])
+        carried = jnp.concatenate([up, down], axis=0).astype(jnp.float32)
+        merged = (part + carried).astype(LINK)
+        heating = lax.ppermute(merged, "comp", [(2, last)]).astype(jnp.float32)
+        heating = heating + lax.ppermute(merged, "comp", [(0, last)]).astype(jnp.float32)
+    else:
+        scaled = part.astype(LINK)
+        heating = scaled.astype(jnp.float32)
+        for source in range(last):
+            heating = heating + lax.ppermute(scaled, "comp", [(source, last)]).astype(
+                jnp.float32
+            )
 
     fields = diffuse(layer_temp, diffusivity)
     heating = jnp.where(is_ocean, heating, 0.0).reshape(rows, NF, cols)

time: 70.3 us -> 75.6 us (1.075)
  starting transfers between devices: 25.2 us -> 27.9 us
  waiting for transfers between devices: 21.1 us -> 23.7 us
    ppermute x3 -> x4, waiting for transfers between devices: 0.01 us -> 2.78 us  [the longest x1 2.77 us: body(): down = lax.ppermute(part[half:].astype(LINK), 'comp', [(1, 0)])]
    all_to_all x1, starting transfers between devices: 4.86 us -> 7.07 us  [body(): came_back = lax.all_to_all(reply, 'band', 0, 0, tiled=True)]
    ppermute x3, waiting for transfers between devices: 9.61 us -> 8.74 us  [body(): ocean_rows = ocean_rows + lax.ppermute(returned, 'comp', [(last, target)])]
    ppermute x3 -> x4, starting transfers between devices: 3.46 us -> 3.92 us  [the longest x1 1.3 us: body(): lax.ppermute(merged, 'comp', [(0, last)]).astype(jnp.float32)]
  transfers between devices with their start and end apart: 10 -> 11, of which waited for: 3 -> 4; matrix products, arithmetic and copies ran while one was open for 4% -> 4% of each run, Pallas kernels for 11% -> 10%
where the time goes in v9:
time: 75.6 us; the launch traced here: 75 us
  starting transfers between devices  27.9 us (37%)
  waiting for transfers between devices  23.7 us (31%)
  Pallas kernels  7.42 us (10%)
  matrix products  7.09 us (9%)
  other arithmetic  5.57 us (7%)
  local copies, waits for them, and re-layouts  2.34 us (3%)
  between operations  0.96 us (1%)
    ppermute x3, waiting for transfers between devices, body(): ocean_rows = ocean_rows + lax.ppermute(returned, 'comp', [(last, target)])  8.74 us
    all_to_all x1, waiting for transfers between devices, body(): came_back = lax.all_to_all(reply, 'band', 0, 0, tiled=True)  8.65 us
    all_to_all x1, starting transfers between devices, body(): received = lax.all_to_all(sending, 'band', 0, 0, tiled=True)  8.58 us
    pallas_call x1, Pallas kernels, diffuse(): pl.pallas_call(_diffusion_kernel, out_shape=jax.ShapeDtypeStruct((rows, l...  7.42 us
    all_to_all x1, starting transfers between devices, body(): came_back = lax.all_to_all(reply, 'band', 0, 0, tiled=True)  7.07 us
    dot_general x1, matrix products, body(): jnp.einsum('rfc,rcd->rfd', surface_layers, weights_local, preferred_eleme...  4.76 us
    all_to_all x1, waiting for transfers between devices, body(): received = lax.all_to_all(sending, 'band', 0, 0, tiled=True)  3.5 us
    ppermute x1, starting transfers between devices, diffuse(): above = lax.ppermute(comb[rows - halo:], 'band', forward)  3.42 us
  transfers between devices with their start and end apart: 11, of which 4 were waited for; matrix products, arithmetic and copies ran while one was open for 4% of the time, Pallas kernels for 10%

profile of v9, /device:TPU:1, one launch (start us, length us, event | category | flops | bytes accessed | tf_op | source)
XLA Modules:
  0.0 75.0 jit_solution(15247375730218566469)
XLA Ops:
  0.6 0.9 %fusion.4 = f32[64]{0:T(128)S(1)} fusion(s32[64]{0:T(128)} %bitcast.54), kind=kOutput, calls=%fused_computation.11 | convolution fusion | flops 286656 | bytes 512 | tf_op jit(solution)/shard_map/dot_general | solution.py:124
  1.5 0.7 fusion.14
  2.2 0.7 convert_bitcast_fusion
  2.9 4.8 %conditional.2 = (f32[64,1024]{1,0:T(8,128)S(1)}) conditional(s32[]{:T(128)} %convert_element_type.99, (f32[1,64,16,256]{3,2,1,0:T(8,128)}, bf16[64,256,256]{2,1,0:T(8,128)(2,1)}) %tuple.39, () %tuple.27), branch_computations={%region_1.0_spmd, %region_2.0_spmd} | conditional | flops 33554432 | bytes 9306120 | solution.py:110
  2.9 4.8 %fusion.1 = f32[64,4,256]{2,1,0:T(4,128)S(1)} fusion(bf16[64,256,256]{2,1,0:T(8,128)(2,1)} %get-tuple-element.31, f32[1,64,16,256]{3,2,1,0:T(8,128)} %get-tuple-element.30), kind=kOutput, calls=%fused_computation.2 | convolution fusion | flops 33554432 | bytes 8781824 | tf_op jit(solution)/shard_map/cond/branch_0_fun/rfc,rcd->rfd/dot_general | solution.py:113
  7.6 0.1 copy.20
  7.7 0.0 copy-start.3
  7.7 0.0 copy-start
  7.7 0.1 broadcast_in_dim.12
  7.8 0.6 convolution_convert_fusion.1
  8.4 0.9 %copy.17 = f16[32,4,1152]{2,1,0:T(4,128)(2,1)} copy(f16[32,4,1152]{2,0,1:T(8,128)(2,1)S(1)} %convolution_convert_fusion.1) | data formatting | bytes 589824 | tf_op jit(solution)/shard_map/convert_element_type | solution.py:138
  9.3 8.6 %all-to-all-start = ((f16[32,4,1152]{2,1,0:T(4,128)(2,1)}), f16[32,4,1152]{2,1,0:T(4,128)(2,1)S(1)}, u32[]{:S(2)}, u32[]{:S(2)}) async-start(f16[32,4,1152]{2,1,0:T(4,128)(2,1)} %copy.17), calls=%async_computation | async-start | bytes 589824 | tf_op jit(solution)/shard_map/all_to_all | solution.py:139
  18.0 2.1 %collective-permute-start.1 = (f32[4,17,256]{2,1,0:T(8,128)S(1)}, f32[4,17,256]{2,1,0:T(8,128)S(1)}, u32[]{:S(2)}, u32[]{:S(2)}) collective-permute-start(f32[4,17,256]{2,1,0:T(8,128)S(1)} %get-tuple-element.37), channel_id=1, source_target_pairs={{1,0},{2,1},{3,2},{4,3},{5,4},{6,5},{7,6},{8,7},{9,8},{10,9},{11,1... | collective-permute-start | bytes 208904 | tf_op jit(solution)/shard_map/ppermute | solution.py:82
  20.2 3.4 %collective-permute-start = (f32[4,17,256]{2,1,0:T(8,128)S(1)}, f32[4,17,256]{2,1,0:T(8,128)S(1)}, u32[]{:S(2)}, u32[]{:S(2)}) collective-permute-start(f32[4,17,256]{2,1,0:T(8,128)S(1)} %get-tuple-element.36), channel_id=1, source_target_pairs={{0,1},{1,2},{2,3},{3,4},{4,5},{5,6},{6,7},{7,8},{8,9},{9,10},{10,1... | collective-permute-start | bytes 208904 | tf_op jit(solution)/shard_map/ppermute | solution.py:81
  23.6 3.5 %all-to-all-done = f16[32,4,1152]{2,1,0:T(4,128)(2,1)S(1)} async-done(((f16[32,4,1152]{2,1,0:T(4,128)(2,1)}), f16[32,4,1152]{2,1,0:T(4,128)(2,1)S(1)}, u32[]{:S(2)}, u32[]{:S(2)}) %all-to-all-start) | async-done | bytes 294944 | tf_op jit(solution)/shard_map/all_to_all | solution.py:139
  27.1 0.1 reshape.121
  27.2 0.1 convert_reduce_fusion
  27.3 0.4 fusion.20
  27.7 1.3 %collective-permute-start.3 = (f16[32,1024]{1,0:T(8,128)(2,1)S(1)}, f16[32,1024]{1,0:T(8,128)(2,1)S(1)}, u32[]{:S(2)}, u32[]{:S(2)}) collective-permute-start(f16[32,1024]{1,0:T(8,128)(2,1)S(1)} %get-tuple-element.39), channel_id=1, source_target_pairs={{32,0},{33,1},{34,2},{35,3},{36,4},{37,5},{38,6},{39,7},{40,8},{41... | collective-permute-start | bytes 196616 | tf_op jit(solution)/shard_map/ppermute | solution.py:149
  29.0 0.7 collective-permute-start.2
  29.7 0.6 pad_add_fusion.bounds_ref
  30.3 2.8 %collective-permute-done.3 = f16[32,1024]{1,0:T(8,128)(2,1)S(1)} collective-permute-done((f16[32,1024]{1,0:T(8,128)(2,1)S(1)}, f16[32,1024]{1,0:T(8,128)(2,1)S(1)}, u32[]{:S(2)}, u32[]{:S(2)}) %collective-permute-start.3) | collective-permute-done | bytes 65568 | tf_op jit(solution)/shard_map/ppermute | solution.py:149
  33.1 0.0 collective-permute-done.2
  33.2 1.3 %collective-permute-start.5 = (f16[64,1024]{1,0:T(8,128)(2,1)S(1)}, f16[64,1024]{1,0:T(8,128)(2,1)S(1)}, u32[]{:S(2)}, u32[]{:S(2)}) collective-permute-start(f16[64,1024]{1,0:T(8,128)(2,1)S(1)} %add_convert_fusion), channel_id=1, source_target_pairs={{0,96},{1,97},{2,98},{3,99},{4,100},{5,101},{6,102},{7,103},{8,104... | collective-permute-start | bytes 393224 | tf_op jit(solution)/shard_map/ppermute | solution.py:153
  34.5 0.7 collective-permute-start.4
  35.1 0.0 collective-permute-done.1
  35.2 1.4 %pad_maximum_fusion.p_ref = f32[72,17,256]{2,1,0:T(8,128)} fusion(f32[4,17,256]{2,1,0:T(8,128)S(1)} %collective-permute-done.1, f32[64,1,256]{2,1,0:T(1,128)S(1)} %broadcast_in_dim_squeeze.4, f32[64,16,256]{2,1,0:T(8,128)S(1)} %bitcast.44, f32[4,17,256]{2,1,0:T(8,128)S(1)} %collective-permute-done), kind=kLoop, calls=%fused_computation.5 | loop fusion | flops 940032 | bytes 2506752 | tf_op jit(solution)/shard_map/concatenate | solution.py:83
  36.6 7.4 %shard_map.68 = f32[64,16,256]{2,1,0:T(8,128)} custom-call(s32[2]{0:T(128)} %pad_add_fusion.bounds_ref, f32[72,17,256]{2,1,0:T(8,128)} %pad_maximum_fusion.p_ref), custom_call_target="tpu_custom_call" | custom-call | tf_op jit(solution)/shard_map/pallas_call | solution.py:87
  44.0 0.1 reshape.122
  44.2 1.1 %fusion.9 = bf16[64,4,256]{2,1,0:T(4,128)(2,1)S(1)} fusion(f32[64,4,256]{2,1,0:T(4,128)S(1)} %reshape.122, f32[64,16,256]{2,1,0:T(8,128)} %shard_map.68), kind=kLoop, calls=%fused_computation.27 | loop fusion | flops 131072 | bytes 655360 | tf_op jit(solution)/shard_map/convert_element_type | solution.py:165
  45.3 0.1 conditional.3
  45.3 0.0 copy-start.1
  45.4 0.8 %collective-permute-start.8 = (bf16[64,4,256]{2,1,0:T(4,128)(2,1)S(1)}, bf16[64,4,256]{2,1,0:T(4,128)(2,1)S(1)}, u32[]{:S(2)}, u32[]{:S(2)}) collective-permute-start(bf16[64,4,256]{2,1,0:T(4,128)(2,1)S(1)} %get-tuple-element.45), channel_id=1, source_target_pairs={{96,64},{97,65},{98,66},{99,67},{100,68},{101,69},{102,70},{103,71... | collective-permute-start | bytes 393224 | tf_op jit(solution)/shard_map/ppermute | solution.py:176
  46.2 0.7 collective-permute-start.7
  46.8 1.3 %collective-permute-start.6 = (bf16[64,4,256]{2,1,0:T(4,128)(2,1)S(1)}, bf16[64,4,256]{2,1,0:T(4,128)(2,1)S(1)}, u32[]{:S(2)}, u32[]{:S(2)}) collective-permute-start(bf16[64,4,256]{2,1,0:T(4,128)(2,1)S(1)} %get-tuple-element.45), channel_id=1, source_target_pairs={{96,0},{97,1},{98,2},{99,3},{100,4},{101,5},{102,6},{103,7},{104,8... | collective-permute-start | bytes 393224 | tf_op jit(solution)/shard_map/ppermute | solution.py:176
  48.1 0.0 collective-permute-done.8
  48.2 0.0 collective-permute-done.7
  48.2 8.7 %collective-permute-done.6 = bf16[64,4,256]{2,1,0:T(4,128)(2,1)S(1)} collective-permute-done((bf16[64,4,256]{2,1,0:T(4,128)(2,1)S(1)}, bf16[64,4,256]{2,1,0:T(4,128)(2,1)S(1)}, u32[]{:S(2)}, u32[]{:S(2)}) %collective-permute-start.6) | collective-permute-done | bytes 131104 | tf_op jit(solution)/shard_map/ppermute | solution.py:176
  57.0 0.3 convolution_convert_fusion.2
  57.2 0.8 %reshape.124 = bf16[32,4,1024]{2,1,0:T(4,128)(2,1)} reshape(bf16[128,1024]{1,0:T(8,128)(2,1)S(1)} %convolution_convert_fusion.2) | data formatting | bytes 524288 | tf_op jit(solution)/shard_map/reshape | solution.py:181
  58.0 7.1 %all-to-all-start.1 = ((bf16[32,4,1024]{2,1,0:T(4,128)(2,1)}), bf16[32,4,1024]{2,1,0:T(4,128)(2,1)S(1)}, u32[]{:S(2)}, u32[]{:S(2)}) async-start(bf16[32,4,1024]{2,1,0:T(4,128)(2,1)} %reshape.124), calls=%async_computation.1 | async-start | bytes 524288 | tf_op jit(solution)/shard_map/all_to_all | solution.py:182
  65.1 0.1 copy.30
  65.2 0.1 bitcast_dynamic-update-slice_fusion
  65.3 0.0 copy-start.2
  65.3 8.6 %all-to-all-done.1 = bf16[32,4,1024]{2,1,0:T(4,128)(2,1)S(1)} async-done(((bf16[32,4,1024]{2,1,0:T(4,128)(2,1)}), bf16[32,4,1024]{2,1,0:T(4,128)(2,1)S(1)}, u32[]{:S(2)}, u32[]{:S(2)}) %all-to-all-start.1) | async-done | bytes 262176 | tf_op jit(solution)/shard_map/all_to_all | solution.py:182
  74.0 0.2 fusion.3
  74.2 0.1 reshape.125
  74.3 0.7 select_bitcast_fusion
  (18 shorter events, 0.3 us)
Async XLA Ops:
  7.7 10.2 %copy-start.3 = (f32[1,64,256]{2,1,0:T(8,128)S(1)}, f32[1,64,256]{2,1,0:T(8,128)}, u32[]{:S(2)}) copy-start(f32[1,64,256]{2,1,0:T(8,128)} %param.12) | copy-start | bytes 196612
  7.7 10.3 %copy-start = (f32[1,64,16,256]{3,2,1,0:T(8,128)S(1)}, f32[1,64,16,256]{3,2,1,0:T(8,128)}, u32[]{:S(2)}) copy-start(f32[1,64,16,256]{3,2,1,0:T(8,128)} %param.11) | copy-start | bytes 3145732
  9.3 17.8 %all-to-all-start = ((f16[32,4,1152]{2,1,0:T(4,128)(2,1)}), f16[32,4,1152]{2,1,0:T(4,128)(2,1)S(1)}, u32[]{:S(2)}, u32[]{:S(2)}) async-start(f16[32,4,1152]{2,1,0:T(4,128)(2,1)} %copy.17), calls=%async_computation | async-start | bytes 589824 | tf_op jit(solution)/shard_map/all_to_all | solution.py:139
  18.0 17.1 %collective-permute-start.1 = (f32[4,17,256]{2,1,0:T(8,128)S(1)}, f32[4,17,256]{2,1,0:T(8,128)S(1)}, u32[]{:S(2)}, u32[]{:S(2)}) collective-permute-start(f32[4,17,256]{2,1,0:T(8,128)S(1)} %get-tuple-element.37), channel_id=1, source_target_pairs={{1,0},{2,1},{3,2},{4,3},{5,4},{6,5},{7,6},{8,7},{9,8},{10,9},{11,1... | collective-permute-start | bytes 208904 | tf_op jit(solution)/shard_map/ppermute | solution.py:82
  20.2 15.0 %collective-permute-start = (f32[4,17,256]{2,1,0:T(8,128)S(1)}, f32[4,17,256]{2,1,0:T(8,128)S(1)}, u32[]{:S(2)}, u32[]{:S(2)}) collective-permute-start(f32[4,17,256]{2,1,0:T(8,128)S(1)} %get-tuple-element.36), channel_id=1, source_target_pairs={{0,1},{1,2},{2,3},{3,4},{4,5},{5,6},{6,7},{7,8},{8,9},{9,10},{10,1... | collective-permute-start | bytes 208904 | tf_op jit(solution)/shard_map/ppermute | solution.py:81
  27.7 5.4 %collective-permute-start.3 = (f16[32,1024]{1,0:T(8,128)(2,1)S(1)}, f16[32,1024]{1,0:T(8,128)(2,1)S(1)}, u32[]{:S(2)}, u32[]{:S(2)}) collective-permute-start(f16[32,1024]{1,0:T(8,128)(2,1)S(1)} %get-tuple-element.39), channel_id=1, source_target_pairs={{32,0},{33,1},{34,2},{35,3},{36,4},{37,5},{38,6},{39,7},{40,8},{41... | collective-permute-start | bytes 196616 | tf_op jit(solution)/shard_map/ppermute | solution.py:149
  29.0 4.1 %collective-permute-start.2 = (f16[32,1024]{1,0:T(8,128)(2,1)S(1)}, f16[32,1024]{1,0:T(8,128)(2,1)S(1)}, u32[]{:S(2)}, u32[]{:S(2)}) collective-permute-start(f16[32,1024]{1,0:T(8,128)(2,1)S(1)} %get-tuple-element.38), channel_id=1, source_target_pairs={{32,64},{33,65},{34,66},{35,67},{36,68},{37,69},{38,70},{39,71},{4... | collective-permute-start | bytes 196616 | tf_op jit(solution)/shard_map/ppermute | solution.py:148
  33.2 10.8 %collective-permute-start.5 = (f16[64,1024]{1,0:T(8,128)(2,1)S(1)}, f16[64,1024]{1,0:T(8,128)(2,1)S(1)}, u32[]{:S(2)}, u32[]{:S(2)}) collective-permute-start(f16[64,1024]{1,0:T(8,128)(2,1)S(1)} %add_convert_fusion), channel_id=1, source_target_pairs={{0,96},{1,97},{2,98},{3,99},{4,100},{5,101},{6,102},{7,103},{8,104... | collective-permute-start | bytes 393224 | tf_op jit(solution)/shard_map/ppermute | solution.py:153
  34.5 9.5 %collective-permute-start.4 = (f16[64,1024]{1,0:T(8,128)(2,1)S(1)}, f16[64,1024]{1,0:T(8,128)(2,1)S(1)}, u32[]{:S(2)}, u32[]{:S(2)}) collective-permute-start(f16[64,1024]{1,0:T(8,128)(2,1)S(1)} %add_convert_fusion), channel_id=1, source_target_pairs={{64,96},{65,97},{66,98},{67,99},{68,100},{69,101},{70,102},{71,103... | collective-permute-start | bytes 393224 | tf_op jit(solution)/shard_map/ppermute | solution.py:152
  45.3 19.8 %copy-start.1 = (f32[64,16,256]{2,1,0:T(8,128)S(1)}, f32[64,16,256]{2,1,0:T(8,128)}, u32[]{:S(2)}) copy-start(f32[64,16,256]{2,1,0:T(8,128)} %shard_map.68) | copy-start | bytes 3145732
  45.4 2.8 %collective-permute-start.8 = (bf16[64,4,256]{2,1,0:T(4,128)(2,1)S(1)}, bf16[64,4,256]{2,1,0:T(4,128)(2,1)S(1)}, u32[]{:S(2)}, u32[]{:S(2)}) collective-permute-start(bf16[64,4,256]{2,1,0:T(4,128)(2,1)S(1)} %get-tuple-element.45), channel_id=1, source_target_pairs={{96,64},{97,65},{98,66},{99,67},{100,68},{101,69},{102,70},{103,71... | collective-permute-start | bytes 393224 | tf_op jit(solution)/shard_map/ppermute | solution.py:176
  46.2 2.0 %collective-permute-start.7 = (bf16[64,4,256]{2,1,0:T(4,128)(2,1)S(1)}, bf16[64,4,256]{2,1,0:T(4,128)(2,1)S(1)}, u32[]{:S(2)}, u32[]{:S(2)}) collective-permute-start(bf16[64,4,256]{2,1,0:T(4,128)(2,1)S(1)} %get-tuple-element.45), channel_id=1, source_target_pairs={{96,32},{97,33},{98,34},{99,35},{100,36},{101,37},{102,38},{103,39... | collective-permute-start | bytes 393224 | tf_op jit(solution)/shard_map/ppermute | solution.py:176
  46.8 10.1 %collective-permute-start.6 = (bf16[64,4,256]{2,1,0:T(4,128)(2,1)S(1)}, bf16[64,4,256]{2,1,0:T(4,128)(2,1)S(1)}, u32[]{:S(2)}, u32[]{:S(2)}) collective-permute-start(bf16[64,4,256]{2,1,0:T(4,128)(2,1)S(1)} %get-tuple-element.45), channel_id=1, source_target_pairs={{96,0},{97,1},{98,2},{99,3},{100,4},{101,5},{102,6},{103,7},{104,8... | collective-permute-start | bytes 393224 | tf_op jit(solution)/shard_map/ppermute | solution.py:176
  58.0 16.0 %all-to-all-start.1 = ((bf16[32,4,1024]{2,1,0:T(4,128)(2,1)}), bf16[32,4,1024]{2,1,0:T(4,128)(2,1)S(1)}, u32[]{:S(2)}, u32[]{:S(2)}) async-start(bf16[32,4,1024]{2,1,0:T(4,128)(2,1)} %reshape.124), calls=%async_computation.1 | async-start | bytes 524288 | tf_op jit(solution)/shard_map/all_to_all | solution.py:182
  65.3 9.7 %copy-start.2 = (f32[1,64,16,256]{3,2,1,0:T(8,128)}, f32[1,64,16,256]{3,2,1,0:T(8,128)S(1)}, u32[]{:S(2)}) copy-start(f32[1,64,16,256]{3,2,1,0:T(8,128)S(1)} %bitcast_dynamic-update-slice_fusion) | copy-start | bytes 3145732

commit v10 on v8

--- a/solution.py
+++ b/solution.py
@@ -150,11 +150,13 @@
     fields = diffuse(layer_temp, diffusivity)
     heating = jnp.where(is_ocean, heating, 0.0).reshape(rows, NF, cols)
     temp_out = fields.at[:, :NF].add(heating)
-    sea_surface = temp_out[:, :NF].astype(jnp.bfloat16)
     returned = lax.cond(
         is_ocean,
         lambda: jnp.einsum(
-            "rfc,rcd->rfd", sea_surface, weights_local, preferred_element_type=jnp.float32
+            "rfc,rcd->rfd",
+            (fields[:, :NF] + heating).astype(jnp.bfloat16),
+            weights_local,
+            preferred_element_type=jnp.float32,
         ).astype(jnp.bfloat16),
         lambda: jnp.zeros((rows, NF, cols), jnp.bfloat16),
     )

time: 70.3 us -> 69 us (0.982)
  other arithmetic: 5.59 us -> 4.38 us
  waiting for transfers between devices: 21.1 us -> 22.2 us
  Pallas kernels: 7.42 us -> 6.45 us
    convert_element_type x1 -> x0, other arithmetic: 1.11 us -> none  [body(): sea_surface = temp_out[:, :NF].astype(jnp.bfloat16)]
    pallas_call x1, Pallas kernels: 7.42 us -> 6.45 us  [diffuse(): pl.pallas_call(_diffusion_kernel, out_shape=jax.ShapeDtypeStruct((rows, l...]
    ppermute x3, waiting for transfers between devices: 9.61 us -> 10.6 us  [body(): ocean_rows = ocean_rows + lax.ppermute(returned, 'comp', [(last, target)])]
  transfers between devices with their start and end apart: 10 -> 10, of which waited for: 3 -> 3; matrix products, arithmetic and copies ran while one was open for 4% -> 4% of each run, Pallas kernels for 11% -> 9%
where the time goes in v10:
time: 69 us; the launch traced here: 68.5 us
  starting transfers between devices  25.1 us (36%)
  waiting for transfers between devices  22.2 us (32%)
  matrix products  7.09 us (10%)
  Pallas kernels  6.45 us (9%)
  other arithmetic  4.38 us (6%)
  local copies, waits for them, and re-layouts  2.32 us (3%)
  between operations  0.95 us (1%)
    ppermute x3, waiting for transfers between devices, body(): ocean_rows = ocean_rows + lax.ppermute(returned, 'comp', [(last, target)])  10.6 us
    all_to_all x1, waiting for transfers between devices, body(): came_back = lax.all_to_all(reply, 'band', 0, 0, tiled=True)  8.66 us
    all_to_all x1, starting transfers between devices, body(): received = lax.all_to_all(sending, 'band', 0, 0, tiled=True)  8.58 us
    pallas_call x1, Pallas kernels, diffuse(): pl.pallas_call(_diffusion_kernel, out_shape=jax.ShapeDtypeStruct((rows, l...  6.45 us
    all_to_all x1, starting transfers between devices, body(): came_back = lax.all_to_all(reply, 'band', 0, 0, tiled=True)  4.89 us
    dot_general x1, matrix products, body(): jnp.einsum('rfc,rcd->rfd', surface_layers, weights_local, preferred_eleme...  4.76 us
    ppermute x3, starting transfers between devices, body(): lax.ppermute(scaled, 'comp', [(source, last)]).astype(jnp.float32)  3.46 us
    ppermute x1, starting transfers between devices, diffuse(): above = lax.ppermute(comb[rows - halo:], 'band', forward)  3.42 us
  transfers between devices with their start and end apart: 10, of which 3 were waited for; matrix products, arithmetic and copies ran while one was open for 4% of the time, Pallas kernels for 9%

profile of v10, /device:TPU:1, one launch (start us, length us, event | category | flops | bytes accessed | tf_op | source)
XLA Modules:
  0.0 68.5 jit_solution(15538046652286215719)
XLA Ops:
  0.6 0.9 %fusion.5 = f32[64]{0:T(128)S(1)} fusion(s32[64]{0:T(128)} %bitcast.55), kind=kOutput, calls=%fused_computation.13 | convolution fusion | flops 286656 | bytes 512 | tf_op jit(solution)/shard_map/dot_general | solution.py:124
  1.5 0.7 fusion.16
  2.2 0.7 convert_bitcast_fusion
  2.9 4.8 %conditional.2 = (f32[64,1024]{1,0:T(8,128)S(1)}) conditional(s32[]{:T(128)} %convert_element_type.100, (f32[1,64,16,256]{3,2,1,0:T(8,128)}, bf16[64,256,256]{2,1,0:T(8,128)(2,1)}) %tuple.37, () %tuple.27), branch_computations={%region_1.0_spmd, %region_2.0_spmd} | conditional | flops 33554432 | bytes 9306120 | solution.py:110
  2.9 4.8 %fusion.1 = f32[64,4,256]{2,1,0:T(4,128)S(1)} fusion(bf16[64,256,256]{2,1,0:T(8,128)(2,1)} %get-tuple-element.33, f32[1,64,16,256]{3,2,1,0:T(8,128)} %get-tuple-element.32), kind=kOutput, calls=%fused_computation.2 | convolution fusion | flops 33554432 | bytes 8781824 | tf_op jit(solution)/shard_map/cond/branch_0_fun/rfc,rcd->rfd/dot_general | solution.py:113
  7.6 0.1 copy.20
  7.7 0.0 copy-start.2
  7.7 0.0 copy-start
  7.7 0.1 broadcast_in_dim.12
  7.8 0.6 convolution_convert_fusion.1
  8.4 0.9 %copy.17 = f16[32,4,1152]{2,1,0:T(4,128)(2,1)} copy(f16[32,4,1152]{2,0,1:T(8,128)(2,1)S(1)} %convolution_convert_fusion.1) | data formatting | bytes 589824 | tf_op jit(solution)/shard_map/convert_element_type | solution.py:138
  9.3 8.6 %all-to-all-start = ((f16[32,4,1152]{2,1,0:T(4,128)(2,1)}), f16[32,4,1152]{2,1,0:T(4,128)(2,1)S(1)}, u32[]{:S(2)}, u32[]{:S(2)}) async-start(f16[32,4,1152]{2,1,0:T(4,128)(2,1)} %copy.17), calls=%async_computation | async-start | bytes 589824 | tf_op jit(solution)/shard_map/all_to_all | solution.py:139
  18.0 2.1 %collective-permute-start.1 = (f32[4,17,256]{2,1,0:T(8,128)S(1)}, f32[4,17,256]{2,1,0:T(8,128)S(1)}, u32[]{:S(2)}, u32[]{:S(2)}) collective-permute-start(f32[4,17,256]{2,1,0:T(8,128)S(1)} %get-tuple-element.40), channel_id=1, source_target_pairs={{1,0},{2,1},{3,2},{4,3},{5,4},{6,5},{7,6},{8,7},{9,8},{10,9},{11,1... | collective-permute-start | bytes 208904 | tf_op jit(solution)/shard_map/ppermute | solution.py:82
  20.2 3.4 %collective-permute-start = (f32[4,17,256]{2,1,0:T(8,128)S(1)}, f32[4,17,256]{2,1,0:T(8,128)S(1)}, u32[]{:S(2)}, u32[]{:S(2)}) collective-permute-start(f32[4,17,256]{2,1,0:T(8,128)S(1)} %get-tuple-element.39), channel_id=1, source_target_pairs={{0,1},{1,2},{2,3},{3,4},{4,5},{5,6},{6,7},{7,8},{8,9},{9,10},{10,1... | collective-permute-start | bytes 208904 | tf_op jit(solution)/shard_map/ppermute | solution.py:81
  23.6 0.6 pad_add_fusion.bounds_ref
  24.2 2.9 %all-to-all-done = f16[32,4,1152]{2,1,0:T(4,128)(2,1)S(1)} async-done(((f16[32,4,1152]{2,1,0:T(4,128)(2,1)}), f16[32,4,1152]{2,1,0:T(4,128)(2,1)S(1)}, u32[]{:S(2)}, u32[]{:S(2)}) %all-to-all-start) | async-done | bytes 294944 | tf_op jit(solution)/shard_map/all_to_all | solution.py:139
  27.1 0.1 reshape.121
  27.2 0.1 convert_reduce_fusion
  27.3 0.4 fusion.4
  27.7 0.7 collective-permute-start.4
  28.4 0.7 collective-permute-start.3
  29.1 2.1 %collective-permute-start.2 = (f16[64,1024]{1,0:T(8,128)(2,1)S(1)}, f16[64,1024]{1,0:T(8,128)(2,1)S(1)}, u32[]{:S(2)}, u32[]{:S(2)}) collective-permute-start(f16[64,1024]{1,0:T(8,128)(2,1)S(1)} %fusion.4), channel_id=1, source_target_pairs={{0,96},{1,97},{2,98},{3,99},{4,100},{5,101},{6,102},{7,103},{8,104... | collective-permute-start | bytes 393224 | tf_op jit(solution)/shard_map/ppermute | solution.py:148
  31.2 0.0 collective-permute-done.1
  31.2 0.0 collective-permute-done
  31.2 1.4 %pad_maximum_fusion.p_ref = f32[72,17,256]{2,1,0:T(8,128)} fusion(f32[4,17,256]{2,1,0:T(8,128)S(1)} %collective-permute-done.1, f32[64,1,256]{2,1,0:T(1,128)S(1)} %broadcast_in_dim_squeeze.4, f32[64,16,256]{2,1,0:T(8,128)S(1)} %bitcast.46, f32[4,17,256]{2,1,0:T(8,128)S(1)} %collective-permute-done), kind=kLoop, calls=%fused_computation.6 | loop fusion | flops 940032 | bytes 2506752 | tf_op jit(solution)/shard_map/concatenate | solution.py:83
  32.6 6.4 %shard_map.68 = f32[64,16,256]{2,1,0:T(8,128)S(1)} custom-call(s32[2]{0:T(128)} %pad_add_fusion.bounds_ref, f32[72,17,256]{2,1,0:T(8,128)} %pad_maximum_fusion.p_ref), custom_call_target="tpu_custom_call" | custom-call | tf_op jit(solution)/shard_map/pallas_call | solution.py:87
  39.1 0.0 collective-permute-done.4
  39.1 0.0 collective-permute-done.3
  39.1 0.0 collective-permute-done.2
  39.1 0.1 add_select_fusion
  39.2 0.1 reshape.122
  39.3 0.1 conditional.3
  39.4 0.7 collective-permute-start.7
  40.0 0.7 collective-permute-start.6
  40.7 1.3 %collective-permute-start.5 = (bf16[64,4,256]{2,1,0:T(4,128)(2,1)S(1)}, bf16[64,4,256]{2,1,0:T(4,128)(2,1)S(1)}, u32[]{:S(2)}, u32[]{:S(2)}) collective-permute-start(bf16[64,4,256]{2,1,0:T(4,128)(2,1)S(1)} %get-tuple-element.44), channel_id=1, source_target_pairs={{96,0},{97,1},{98,2},{99,3},{100,4},{101,5},{102,6},{103,7},{104,8... | collective-permute-start | bytes 393224 | tf_op jit(solution)/shard_map/ppermute | solution.py:166
  42.0 0.0 collective-permute-done.7
  42.0 0.0 collective-permute-done.6
  42.0 10.6 %collective-permute-done.5 = bf16[64,4,256]{2,1,0:T(4,128)(2,1)S(1)} collective-permute-done((bf16[64,4,256]{2,1,0:T(4,128)(2,1)S(1)}, bf16[64,4,256]{2,1,0:T(4,128)(2,1)S(1)}, u32[]{:S(2)}, u32[]{:S(2)}) %collective-permute-start.5) | collective-permute-done | bytes 131104 | tf_op jit(solution)/shard_map/ppermute | solution.py:166
  52.7 0.3 convolution_convert_fusion.2
  52.9 0.8 %reshape.124 = bf16[32,4,1024]{2,1,0:T(4,128)(2,1)} reshape(bf16[128,1024]{1,0:T(8,128)(2,1)S(1)} %convolution_convert_fusion.2) | data formatting | bytes 524288 | tf_op jit(solution)/shard_map/reshape | solution.py:171
  53.7 4.9 %all-to-all-start.1 = ((bf16[32,4,1024]{2,1,0:T(4,128)(2,1)}), bf16[32,4,1024]{2,1,0:T(4,128)(2,1)S(1)}, u32[]{:S(2)}, u32[]{:S(2)}) async-start(bf16[32,4,1024]{2,1,0:T(4,128)(2,1)} %reshape.124), calls=%async_computation.1 | async-start | bytes 524288 | tf_op jit(solution)/shard_map/all_to_all | solution.py:172
  58.6 0.1 copy.30
  58.7 0.1 fusion.10
  58.8 0.0 copy-start.1
  58.9 8.7 %all-to-all-done.1 = bf16[32,4,1024]{2,1,0:T(4,128)(2,1)S(1)} async-done(((bf16[32,4,1024]{2,1,0:T(4,128)(2,1)}), bf16[32,4,1024]{2,1,0:T(4,128)(2,1)S(1)}, u32[]{:S(2)}, u32[]{:S(2)}) %all-to-all-start.1) | async-done | bytes 262176 | tf_op jit(solution)/shard_map/all_to_all | solution.py:172
  67.5 0.2 fusion.3
  67.7 0.1 reshape.125
  67.8 0.7 %select_bitcast_fusion = bf16[1,64,4,256]{3,2,1,0:T(4,128)(2,1)} fusion(bf16[64,4,256]{2,1,0:T(4,128)(2,1)S(1)} %get-tuple-element.44, bf16[64,4,256]{2,1,0:T(4,128)(2,1)S(1)} %reshape.125, pred[]{:T(512)S(6)} %eq.62), kind=kLoop, calls=%fused_computation.23 | loop fusion | flops 65536 | bytes 393217 | tf_op jit(solution)/shard_map/broadcast_in_dim | solution.py:178
  (11 shorter events, 0.2 us)
Async XLA Ops:
  7.7 10.2 %copy-start.2 = (f32[1,64,256]{2,1,0:T(8,128)S(1)}, f32[1,64,256]{2,1,0:T(8,128)}, u32[]{:S(2)}) copy-start(f32[1,64,256]{2,1,0:T(8,128)} %param.12) | copy-start | bytes 196612
  7.7 10.3 %copy-start = (f32[1,64,16,256]{3,2,1,0:T(8,128)S(1)}, f32[1,64,16,256]{3,2,1,0:T(8,128)}, u32[]{:S(2)}) copy-start(f32[1,64,16,256]{3,2,1,0:T(8,128)} %param.11) | copy-start | bytes 3145732
  9.3 17.8 %all-to-all-start = ((f16[32,4,1152]{2,1,0:T(4,128)(2,1)}), f16[32,4,1152]{2,1,0:T(4,128)(2,1)S(1)}, u32[]{:S(2)}, u32[]{:S(2)}) async-start(f16[32,4,1152]{2,1,0:T(4,128)(2,1)} %copy.17), calls=%async_computation | async-start | bytes 589824 | tf_op jit(solution)/shard_map/all_to_all | solution.py:139
  18.0 13.2 %collective-permute-start.1 = (f32[4,17,256]{2,1,0:T(8,128)S(1)}, f32[4,17,256]{2,1,0:T(8,128)S(1)}, u32[]{:S(2)}, u32[]{:S(2)}) collective-permute-start(f32[4,17,256]{2,1,0:T(8,128)S(1)} %get-tuple-element.40), channel_id=1, source_target_pairs={{1,0},{2,1},{3,2},{4,3},{5,4},{6,5},{7,6},{8,7},{9,8},{10,9},{11,1... | collective-permute-start | bytes 208904 | tf_op jit(solution)/shard_map/ppermute | solution.py:82
  20.2 11.0 %collective-permute-start = (f32[4,17,256]{2,1,0:T(8,128)S(1)}, f32[4,17,256]{2,1,0:T(8,128)S(1)}, u32[]{:S(2)}, u32[]{:S(2)}) collective-permute-start(f32[4,17,256]{2,1,0:T(8,128)S(1)} %get-tuple-element.39), channel_id=1, source_target_pairs={{0,1},{1,2},{2,3},{3,4},{4,5},{5,6},{6,7},{7,8},{8,9},{9,10},{10,1... | collective-permute-start | bytes 208904 | tf_op jit(solution)/shard_map/ppermute | solution.py:81
  27.7 11.4 %collective-permute-start.4 = (f16[64,1024]{1,0:T(8,128)(2,1)S(1)}, f16[64,1024]{1,0:T(8,128)(2,1)S(1)}, u32[]{:S(2)}, u32[]{:S(2)}) collective-permute-start(f16[64,1024]{1,0:T(8,128)(2,1)S(1)} %fusion.4), channel_id=1, source_target_pairs={{64,96},{65,97},{66,98},{67,99},{68,100},{69,101},{70,102},{71,103... | collective-permute-start | bytes 393224 | tf_op jit(solution)/shard_map/ppermute | solution.py:148
  28.4 10.7 %collective-permute-start.3 = (f16[64,1024]{1,0:T(8,128)(2,1)S(1)}, f16[64,1024]{1,0:T(8,128)(2,1)S(1)}, u32[]{:S(2)}, u32[]{:S(2)}) collective-permute-start(f16[64,1024]{1,0:T(8,128)(2,1)S(1)} %fusion.4), channel_id=1, source_target_pairs={{32,96},{33,97},{34,98},{35,99},{36,100},{37,101},{38,102},{39,103... | collective-permute-start | bytes 393224 | tf_op jit(solution)/shard_map/ppermute | solution.py:148
  29.1 10.0 %collective-permute-start.2 = (f16[64,1024]{1,0:T(8,128)(2,1)S(1)}, f16[64,1024]{1,0:T(8,128)(2,1)S(1)}, u32[]{:S(2)}, u32[]{:S(2)}) collective-permute-start(f16[64,1024]{1,0:T(8,128)(2,1)S(1)} %fusion.4), channel_id=1, source_target_pairs={{0,96},{1,97},{2,98},{3,99},{4,100},{5,101},{6,102},{7,103},{8,104... | collective-permute-start | bytes 393224 | tf_op jit(solution)/shard_map/ppermute | solution.py:148
  39.4 2.7 %collective-permute-start.7 = (bf16[64,4,256]{2,1,0:T(4,128)(2,1)S(1)}, bf16[64,4,256]{2,1,0:T(4,128)(2,1)S(1)}, u32[]{:S(2)}, u32[]{:S(2)}) collective-permute-start(bf16[64,4,256]{2,1,0:T(4,128)(2,1)S(1)} %get-tuple-element.44), channel_id=1, source_target_pairs={{96,64},{97,65},{98,66},{99,67},{100,68},{101,69},{102,70},{103,71... | collective-permute-start | bytes 393224 | tf_op jit(solution)/shard_map/ppermute | solution.py:166
  40.0 2.0 %collective-permute-start.6 = (bf16[64,4,256]{2,1,0:T(4,128)(2,1)S(1)}, bf16[64,4,256]{2,1,0:T(4,128)(2,1)S(1)}, u32[]{:S(2)}, u32[]{:S(2)}) collective-permute-start(bf16[64,4,256]{2,1,0:T(4,128)(2,1)S(1)} %get-tuple-element.44), channel_id=1, source_target_pairs={{96,32},{97,33},{98,34},{99,35},{100,36},{101,37},{102,38},{103,39... | collective-permute-start | bytes 393224 | tf_op jit(solution)/shard_map/ppermute | solution.py:166
  40.7 11.9 %collective-permute-start.5 = (bf16[64,4,256]{2,1,0:T(4,128)(2,1)S(1)}, bf16[64,4,256]{2,1,0:T(4,128)(2,1)S(1)}, u32[]{:S(2)}, u32[]{:S(2)}) collective-permute-start(bf16[64,4,256]{2,1,0:T(4,128)(2,1)S(1)} %get-tuple-element.44), channel_id=1, source_target_pairs={{96,0},{97,1},{98,2},{99,3},{100,4},{101,5},{102,6},{103,7},{104,8... | collective-permute-start | bytes 393224 | tf_op jit(solution)/shard_map/ppermute | solution.py:166
  53.7 13.8 %all-to-all-start.1 = ((bf16[32,4,1024]{2,1,0:T(4,128)(2,1)}), bf16[32,4,1024]{2,1,0:T(4,128)(2,1)S(1)}, u32[]{:S(2)}, u32[]{:S(2)}) async-start(bf16[32,4,1024]{2,1,0:T(4,128)(2,1)} %reshape.124), calls=%async_computation.1 | async-start | bytes 524288 | tf_op jit(solution)/shard_map/all_to_all | solution.py:172
  58.8 9.7 %copy-start.1 = (f32[1,64,16,256]{3,2,1,0:T(8,128)}, f32[1,64,16,256]{3,2,1,0:T(8,128)S(1)}, u32[]{:S(2)}) copy-start(f32[1,64,16,256]{3,2,1,0:T(8,128)S(1)} %fusion.10) | copy-start | bytes 3145732

commit v11 on v10

--- a/solution.py
+++ b/solution.py
@@ -165,16 +165,11 @@
     for target in range(last):
         ocean_rows = ocean_rows + lax.ppermute(returned, "comp", [(last, target)])
     ocean_rows = ocean_rows.reshape(rows, width)
-    reply = jnp.einsum(
-        "kr,rx->kx", match.astype(jnp.bfloat16), ocean_rows, preferred_element_type=jnp.float32
-    ).astype(jnp.bfloat16)
-    reply = reply.reshape(n_bands, CAP, width)
+    reply = jnp.take(ocean_rows, got_index.reshape(n_bands, CAP), axis=0)
     came_back = lax.all_to_all(reply, "band", 0, 0, tiled=True)
-    came_back = came_back.reshape(n_bands * CAP, width)
-    seen = jnp.einsum(
-        "rk,kx->rx", selector.astype(jnp.bfloat16), came_back, preferred_element_type=jnp.float32
-    ).astype(jnp.bfloat16)
-    surface_temp = jnp.where(is_ocean, returned, seen.reshape(rows, NF, cols))
+    came_back = came_back.reshape(n_bands, CAP, NF, cols)
+    seen = came_back[destination, slot_rank]
+    surface_temp = jnp.where(is_ocean, returned, seen)
     return temp_out[None], surface_temp[None]
 
 

time: 69 us -> 81.1 us (1.18)
  starting transfers between devices: 25.1 us -> 31.3 us
  waiting for transfers between devices: 22.2 us -> 26.3 us
  local copies, waits for them, and re-layouts: 2.32 us -> 3.6 us
  other arithmetic: 4.38 us -> 5.3 us
    all_to_all x1, starting transfers between devices: 4.89 us -> 11.1 us  [body(): came_back = lax.all_to_all(reply, 'band', 0, 0, tiled=True)]
    ppermute x3, waiting for transfers between devices: 0.01 us -> 4.25 us  [body(): lax.ppermute(scaled, 'comp', [(source, last)]).astype(jnp.float32)]
    all_to_all x1, waiting for transfers between devices: 2.95 us -> 0.01 us  [body(): received = lax.all_to_all(sending, 'band', 0, 0, tiled=True)]
    ppermute x3, waiting for transfers between devices: 10.6 us -> 12.3 us  [body(): ocean_rows = ocean_rows + lax.ppermute(returned, 'comp', [(last, target)])]
    gather x0 -> x3, local copies, waits for them, and re-layouts: none -> 1.76 us  [the longest x2 0.97 us: body(): reply = jnp.take(ocean_rows, got_index.reshape(n_bands, CAP), axis=0)]
    select_n x0 -> x2, other arithmetic: none -> 0.91 us  [body(): reply = jnp.take(ocean_rows, got_index.reshape(n_bands, CAP), axis=0)]
  transfers between devices with their start and end apart: 10 -> 10, of which waited for: 3 -> 5; matrix products, arithmetic and copies ran while one was open for 4% -> 3% of each run, Pallas kernels for 9% -> 8%
where the time goes in v11:
time: 81.1 us; the launch traced here: 80.6 us
  starting transfers between devices  31.3 us (39%)
  waiting for transfers between devices  26.3 us (32%)
  matrix products  6.62 us (8%)
  Pallas kernels  6.45 us (8%)
  other arithmetic  5.3 us (7%)
  local copies, waits for them, and re-layouts  3.6 us (4%)
  between operations  0.99 us (1%)
    ppermute x3, waiting for transfers between devices, body(): ocean_rows = ocean_rows + lax.ppermute(returned, 'comp', [(last, target)])  12.3 us
    all_to_all x1, starting transfers between devices, body(): came_back = lax.all_to_all(reply, 'band', 0, 0, tiled=True)  11.1 us
    all_to_all x1, waiting for transfers between devices, body(): came_back = lax.all_to_all(reply, 'band', 0, 0, tiled=True)  8.63 us
    all_to_all x1, starting transfers between devices, body(): received = lax.all_to_all(sending, 'band', 0, 0, tiled=True)  8.58 us
    pallas_call x1, Pallas kernels, diffuse(): pl.pallas_call(_diffusion_kernel, out_shape=jax.ShapeDtypeStruct((rows, l...  6.45 us
    dot_general x1, matrix products, body(): jnp.einsum('rfc,rcd->rfd', surface_layers, weights_local, preferred_eleme...  4.76 us
    ppermute x3, waiting for transfers between devices, body(): lax.ppermute(scaled, 'comp', [(source, last)]).astype(jnp.float32)  4.25 us
    ppermute x3, starting transfers between devices, body(): lax.ppermute(scaled, 'comp', [(source, last)]).astype(jnp.float32)  3.46 us
  transfers between devices with their start and end apart: 10, of which 5 were waited for; matrix products, arithmetic and copies ran while one was open for 3% of the time, Pallas kernels for 8%

profile of v11, /device:TPU:1, one launch (start us, length us, event | category | flops | bytes accessed | tf_op | source)
XLA Modules:
  0.0 80.6 jit_solution(10195179390866247949)
XLA Ops:
  0.6 0.9 %fusion.4 = f32[64]{0:T(128)S(1)} fusion(s32[64]{0:T(128)} %bitcast.62), kind=kOutput, calls=%fused_computation.12 | convolution fusion | flops 286656 | bytes 512 | tf_op jit(solution)/shard_map/dot_general | solution.py:124
  1.5 0.7 fusion.12
  2.2 0.7 convert_bitcast_fusion
  2.9 4.8 %conditional.2 = (f32[64,1024]{1,0:T(8,128)S(1)}) conditional(s32[]{:T(128)} %convert_element_type.110, (f32[1,64,16,256]{3,2,1,0:T(8,128)}, bf16[64,256,256]{2,1,0:T(8,128)(2,1)}) %tuple.36, () %tuple.27), branch_computations={%region_1.0_spmd, %region_2.0_spmd} | conditional | flops 33554432 | bytes 9306120 | solution.py:110
  2.9 4.8 %fusion.1 = f32[64,4,256]{2,1,0:T(4,128)S(1)} fusion(bf16[64,256,256]{2,1,0:T(8,128)(2,1)} %get-tuple-element.33, f32[1,64,16,256]{3,2,1,0:T(8,128)} %get-tuple-element.32), kind=kOutput, calls=%fused_computation.4 | convolution fusion | flops 33554432 | bytes 8781824 | tf_op jit(solution)/shard_map/cond/branch_0_fun/rfc,rcd->rfd/dot_general | solution.py:113
  7.6 0.1 copy.14
  7.7 0.0 copy-start.2
  7.7 0.0 copy-start
  7.7 0.1 broadcast_in_dim.23
  7.8 0.6 convolution_convert_fusion.1
  8.4 0.9 %copy.13 = f16[32,4,1152]{2,1,0:T(4,128)(2,1)} copy(f16[32,4,1152]{2,0,1:T(8,128)(2,1)S(1)} %convolution_convert_fusion.1) | data formatting | bytes 589824 | tf_op jit(solution)/shard_map/convert_element_type | solution.py:138
  9.3 8.6 %all-to-all-start = ((f16[32,4,1152]{2,1,0:T(4,128)(2,1)}), f16[32,4,1152]{2,1,0:T(4,128)(2,1)S(1)}, u32[]{:S(2)}, u32[]{:S(2)}) async-start(f16[32,4,1152]{2,1,0:T(4,128)(2,1)} %copy.13), calls=%async_computation | async-start | bytes 589824 | tf_op jit(solution)/shard_map/all_to_all | solution.py:139
  18.0 2.1 %collective-permute-start.1 = (f32[4,17,256]{2,1,0:T(8,128)S(1)}, f32[4,17,256]{2,1,0:T(8,128)S(1)}, u32[]{:S(2)}, u32[]{:S(2)}) collective-permute-start(f32[4,17,256]{2,1,0:T(8,128)S(1)} %get-tuple-element.40), channel_id=1, source_target_pairs={{1,0},{2,1},{3,2},{4,3},{5,4},{6,5},{7,6},{8,7},{9,8},{10,9},{11,1... | collective-permute-start | bytes 208904 | tf_op jit(solution)/shard_map/ppermute | solution.py:82
  20.2 3.4 %collective-permute-start = (f32[4,17,256]{2,1,0:T(8,128)S(1)}, f32[4,17,256]{2,1,0:T(8,128)S(1)}, u32[]{:S(2)}, u32[]{:S(2)}) collective-permute-start(f32[4,17,256]{2,1,0:T(8,128)S(1)} %get-tuple-element.39), channel_id=1, source_target_pairs={{0,1},{1,2},{2,3},{3,4},{4,5},{5,6},{6,7},{7,8},{8,9},{9,10},{10,1... | collective-permute-start | bytes 208904 | tf_op jit(solution)/shard_map/ppermute | solution.py:81
  23.6 0.6 pad_add_fusion.bounds_ref
  24.2 0.7 collective-permute-done.1
  24.8 0.4 collective-permute-done
  25.2 1.4 %pad_maximum_fusion.p_ref = f32[72,17,256]{2,1,0:T(8,128)} fusion(f32[4,17,256]{2,1,0:T(8,128)S(1)} %collective-permute-done.1, f32[64,1,256]{2,1,0:T(1,128)S(1)} %broadcast_in_dim_squeeze.4, f32[64,16,256]{2,1,0:T(8,128)S(1)} %bitcast.54, f32[4,17,256]{2,1,0:T(8,128)S(1)} %collective-permute-done), kind=kLoop, calls=%fused_computation.8 | loop fusion | flops 940032 | bytes 2506752 | tf_op jit(solution)/shard_map/concatenate | solution.py:83
  26.6 6.4 %shard_map.68 = f32[64,16,256]{2,1,0:T(8,128)S(1)} custom-call(s32[2]{0:T(128)} %pad_add_fusion.bounds_ref, f32[72,17,256]{2,1,0:T(8,128)} %pad_maximum_fusion.p_ref), custom_call_target="tpu_custom_call" | custom-call | tf_op jit(solution)/shard_map/pallas_call | solution.py:87
  33.1 0.1 reshape.189
  33.2 0.1 convert_reduce_fusion
  33.3 0.4 fusion.3
  33.7 0.7 collective-permute-start.4
  34.3 0.7 collective-permute-start.3
  35.0 2.1 %collective-permute-start.2 = (f16[64,1024]{1,0:T(8,128)(2,1)S(1)}, f16[64,1024]{1,0:T(8,128)(2,1)S(1)}, u32[]{:S(2)}, u32[]{:S(2)}) collective-permute-start(f16[64,1024]{1,0:T(8,128)(2,1)S(1)} %fusion.3), channel_id=1, source_target_pairs={{0,96},{1,97},{2,98},{3,99},{4,100},{5,101},{6,102},{7,103},{8,104... | collective-permute-start | bytes 393224 | tf_op jit(solution)/shard_map/ppermute | solution.py:148
  37.1 0.1 convert_element_type.121
  37.2 0.1 convert_element_type.120
  37.4 4.2 %collective-permute-done.2 = f16[64,1024]{1,0:T(8,128)(2,1)S(1)} collective-permute-done((f16[64,1024]{1,0:T(8,128)(2,1)S(1)}, f16[64,1024]{1,0:T(8,128)(2,1)S(1)}, u32[]{:S(2)}, u32[]{:S(2)}) %collective-permute-start.2) | collective-permute-done | bytes 131104 | tf_op jit(solution)/shard_map/ppermute | solution.py:148
  41.6 0.1 add_select_fusion
  41.7 0.1 reshape.190
  41.8 0.1 conditional.3
  41.9 0.7 collective-permute-start.7
  42.6 0.7 collective-permute-start.6
  43.3 1.3 %collective-permute-start.5 = (bf16[64,4,256]{2,1,0:T(4,128)(2,1)S(1)}, bf16[64,4,256]{2,1,0:T(4,128)(2,1)S(1)}, u32[]{:S(2)}, u32[]{:S(2)}) collective-permute-start(bf16[64,4,256]{2,1,0:T(4,128)(2,1)S(1)} %get-tuple-element.42), channel_id=1, source_target_pairs={{96,0},{97,1},{98,2},{99,3},{100,4},{101,5},{102,6},{103,7},{104,8... | collective-permute-start | bytes 393224 | tf_op jit(solution)/shard_map/ppermute | solution.py:166
  44.6 0.1 reshape.195
  44.7 12.3 %collective-permute-done.5 = bf16[64,4,256]{2,1,0:T(4,128)(2,1)S(1)} collective-permute-done((bf16[64,4,256]{2,1,0:T(4,128)(2,1)S(1)}, bf16[64,4,256]{2,1,0:T(4,128)(2,1)S(1)}, u32[]{:S(2)}, u32[]{:S(2)}) %collective-permute-start.5) | collective-permute-done | bytes 131104 | tf_op jit(solution)/shard_map/ppermute | solution.py:166
  57.1 0.0 copy-start.3
  57.1 0.9 %gather_fusion = bf16[128,1024]{1,0:T(8,128)(2,1)S(1)} fusion(bf16[64,1024]{1,0:T(8,128)(2,1)S(1)} %bitcast.49, s32[1024]{0:T(1024)S(1)} %pad_clamp_fusion), kind=kCustom, calls=%fused_computation | custom fusion | bytes 524800 | tf_op jit(solution)/shard_map/jit(_take)/gather | solution.py:168
  58.0 0.1 reshape.194
  58.1 0.9 %broadcast_select_fusion = bf16[32,4,1024]{2,1,0:T(4,128)(2,1)} fusion(bf16[32,4,1024]{2,1,0:T(4,128)(2,1)S(1)} %reshape.194, pred[32,4]{1,0:T(8,128)(4,1)S(1)} %compare_and_fusion), kind=kLoop, calls=%fused_computation.21 | loop fusion | flops 131072 | bytes 524416 | tf_op jit(solution)/shard_map/jit(_take)/select_n | solution.py:168
  59.0 11.1 %all-to-all-start.1 = ((bf16[32,4,1024]{2,1,0:T(4,128)(2,1)}), bf16[32,4,1024]{2,1,0:T(4,128)(2,1)S(1)}, u32[]{:S(2)}, u32[]{:S(2)}) async-start(bf16[32,4,1024]{2,1,0:T(4,128)(2,1)} %broadcast_select_fusion), calls=%async_computation.1 | async-start | bytes 524288 | tf_op jit(solution)/shard_map/all_to_all | solution.py:169
  70.1 0.1 copy.20
  70.2 0.1 fusion.9
  70.3 0.0 copy-start.1
  70.3 8.6 %all-to-all-done.1 = bf16[32,4,1024]{2,1,0:T(4,128)(2,1)S(1)} async-done(((bf16[32,4,1024]{2,1,0:T(4,128)(2,1)}), bf16[32,4,1024]{2,1,0:T(4,128)(2,1)S(1)}, u32[]{:S(2)}, u32[]{:S(2)}) %all-to-all-start.1) | async-done | bytes 262176 | tf_op jit(solution)/shard_map/all_to_all | solution.py:169
  79.0 0.1 reshape.192
  79.1 0.8 gather_fusion.1
  79.9 0.7 select_bitcast_fusion
  (21 shorter events, 0.2 us)
Async XLA Ops:
  7.7 10.2 %copy-start.2 = (f32[1,64,256]{2,1,0:T(8,128)S(1)}, f32[1,64,256]{2,1,0:T(8,128)}, u32[]{:S(2)}) copy-start(f32[1,64,256]{2,1,0:T(8,128)} %param.12) | copy-start | bytes 196612
  7.7 10.3 %copy-start = (f32[1,64,16,256]{3,2,1,0:T(8,128)S(1)}, f32[1,64,16,256]{3,2,1,0:T(8,128)}, u32[]{:S(2)}) copy-start(f32[1,64,16,256]{3,2,1,0:T(8,128)} %param.11) | copy-start | bytes 3145732
  9.3 23.7 %all-to-all-start = ((f16[32,4,1152]{2,1,0:T(4,128)(2,1)}), f16[32,4,1152]{2,1,0:T(4,128)(2,1)S(1)}, u32[]{:S(2)}, u32[]{:S(2)}) async-start(f16[32,4,1152]{2,1,0:T(4,128)(2,1)} %copy.13), calls=%async_computation | async-start | bytes 589824 | tf_op jit(solution)/shard_map/all_to_all | solution.py:139
  18.0 6.8 %collective-permute-start.1 = (f32[4,17,256]{2,1,0:T(8,128)S(1)}, f32[4,17,256]{2,1,0:T(8,128)S(1)}, u32[]{:S(2)}, u32[]{:S(2)}) collective-permute-start(f32[4,17,256]{2,1,0:T(8,128)S(1)} %get-tuple-element.40), channel_id=1, source_target_pairs={{1,0},{2,1},{3,2},{4,3},{5,4},{6,5},{7,6},{8,7},{9,8},{10,9},{11,1... | collective-permute-start | bytes 208904 | tf_op jit(solution)/shard_map/ppermute | solution.py:82
  20.2 5.0 %collective-permute-start = (f32[4,17,256]{2,1,0:T(8,128)S(1)}, f32[4,17,256]{2,1,0:T(8,128)S(1)}, u32[]{:S(2)}, u32[]{:S(2)}) collective-permute-start(f32[4,17,256]{2,1,0:T(8,128)S(1)} %get-tuple-element.39), channel_id=1, source_target_pairs={{0,1},{1,2},{2,3},{3,4},{4,5},{5,6},{6,7},{7,8},{8,9},{9,10},{10,1... | collective-permute-start | bytes 208904 | tf_op jit(solution)/shard_map/ppermute | solution.py:81
  33.7 3.7 %collective-permute-start.4 = (f16[64,1024]{1,0:T(8,128)(2,1)S(1)}, f16[64,1024]{1,0:T(8,128)(2,1)S(1)}, u32[]{:S(2)}, u32[]{:S(2)}) collective-permute-start(f16[64,1024]{1,0:T(8,128)(2,1)S(1)} %fusion.3), channel_id=1, source_target_pairs={{64,96},{65,97},{66,98},{67,99},{68,100},{69,101},{70,102},{71,103... | collective-permute-start | bytes 393224 | tf_op jit(solution)/shard_map/ppermute | solution.py:148
  34.3 3.0 %collective-permute-start.3 = (f16[64,1024]{1,0:T(8,128)(2,1)S(1)}, f16[64,1024]{1,0:T(8,128)(2,1)S(1)}, u32[]{:S(2)}, u32[]{:S(2)}) collective-permute-start(f16[64,1024]{1,0:T(8,128)(2,1)S(1)} %fusion.3), channel_id=1, source_target_pairs={{32,96},{33,97},{34,98},{35,99},{36,100},{37,101},{38,102},{39,103... | collective-permute-start | bytes 393224 | tf_op jit(solution)/shard_map/ppermute | solution.py:148
  35.0 6.6 %collective-permute-start.2 = (f16[64,1024]{1,0:T(8,128)(2,1)S(1)}, f16[64,1024]{1,0:T(8,128)(2,1)S(1)}, u32[]{:S(2)}, u32[]{:S(2)}) collective-permute-start(f16[64,1024]{1,0:T(8,128)(2,1)S(1)} %fusion.3), channel_id=1, source_target_pairs={{0,96},{1,97},{2,98},{3,99},{4,100},{5,101},{6,102},{7,103},{8,104... | collective-permute-start | bytes 393224 | tf_op jit(solution)/shard_map/ppermute | solution.py:148
  41.9 2.8 %collective-permute-start.7 = (bf16[64,4,256]{2,1,0:T(4,128)(2,1)S(1)}, bf16[64,4,256]{2,1,0:T(4,128)(2,1)S(1)}, u32[]{:S(2)}, u32[]{:S(2)}) collective-permute-start(bf16[64,4,256]{2,1,0:T(4,128)(2,1)S(1)} %get-tuple-element.42), channel_id=1, source_target_pairs={{96,64},{97,65},{98,66},{99,67},{100,68},{101,69},{102,70},{103,71... | collective-permute-start | bytes 393224 | tf_op jit(solution)/shard_map/ppermute | solution.py:166
  42.6 2.1 %collective-permute-start.6 = (bf16[64,4,256]{2,1,0:T(4,128)(2,1)S(1)}, bf16[64,4,256]{2,1,0:T(4,128)(2,1)S(1)}, u32[]{:S(2)}, u32[]{:S(2)}) collective-permute-start(bf16[64,4,256]{2,1,0:T(4,128)(2,1)S(1)} %get-tuple-element.42), channel_id=1, source_target_pairs={{96,32},{97,33},{98,34},{99,35},{100,36},{101,37},{102,38},{103,39... | collective-permute-start | bytes 393224 | tf_op jit(solution)/shard_map/ppermute | solution.py:166
  43.3 13.8 %collective-permute-start.5 = (bf16[64,4,256]{2,1,0:T(4,128)(2,1)S(1)}, bf16[64,4,256]{2,1,0:T(4,128)(2,1)S(1)}, u32[]{:S(2)}, u32[]{:S(2)}) collective-permute-start(bf16[64,4,256]{2,1,0:T(4,128)(2,1)S(1)} %get-tuple-element.42), channel_id=1, source_target_pairs={{96,0},{97,1},{98,2},{99,3},{100,4},{101,5},{102,6},{103,7},{104,8... | collective-permute-start | bytes 393224 | tf_op jit(solution)/shard_map/ppermute | solution.py:166
  57.1 13.0 %copy-start.3 = (s32[1,64,1]{1,2,0:T(1,128)S(1)}, s32[1,64,1]{1,2,0:T(1,128)}, u32[]{:S(2)}) copy-start(s32[1,64,1]{1,2,0:T(1,128)} %param.13) | copy-start | bytes 772
  59.0 20.0 %all-to-all-start.1 = ((bf16[32,4,1024]{2,1,0:T(4,128)(2,1)}), bf16[32,4,1024]{2,1,0:T(4,128)(2,1)S(1)}, u32[]{:S(2)}, u32[]{:S(2)}) async-start(bf16[32,4,1024]{2,1,0:T(4,128)(2,1)} %broadcast_select_fusion), calls=%async_computation.1 | async-start | bytes 524288 | tf_op jit(solution)/shard_map/all_to_all | solution.py:169
  70.3 10.3 %copy-start.1 = (f32[1,64,16,256]{3,2,1,0:T(8,128)}, f32[1,64,16,256]{3,2,1,0:T(8,128)S(1)}, u32[]{:S(2)}) copy-start(f32[1,64,16,256]{3,2,1,0:T(8,128)S(1)} %fusion.9) | copy-start | bytes 3145732

commit v12 on v10

--- a/solution.py
+++ b/solution.py
@@ -144,7 +144,7 @@
     last = n_sections - 1
     scaled = (COUPLING * partial).astype(LINK)
     heating = scaled.astype(jnp.float32)
-    for source in range(last):
+    for source in sorted(range(last), key=lambda t: (t + 1) % last):
         heating = heating + lax.ppermute(scaled, "comp", [(source, last)]).astype(jnp.float32)
 
     fields = diffuse(layer_temp, diffusivity)

time: 69 us -> 68.1 us (0.987)
  waiting for transfers between devices: 22.2 us -> 20.6 us
  starting transfers between devices: 25.1 us -> 25.8 us
    ppermute x3, waiting for transfers between devices: 10.6 us -> 9.01 us  [body(): ocean_rows = ocean_rows + lax.ppermute(returned, 'comp', [(last, target)])]
    all_to_all x1, starting transfers between devices: 4.89 us -> 6.16 us  [body(): came_back = lax.all_to_all(reply, 'band', 0, 0, tiled=True)]
  transfers between devices with their start and end apart: 10 -> 10, of which waited for: 3 -> 3; matrix products, arithmetic and copies ran while one was open for 4% -> 4% of each run, Pallas kernels for 9% -> 10%
where the time goes in v12:
time: 68.1 us; the launch traced here: 67.6 us
  starting transfers between devices  25.8 us (38%)
  waiting for transfers between devices  20.6 us (30%)
  matrix products  7.09 us (10%)
  Pallas kernels  6.45 us (9%)
  other arithmetic  4.39 us (6%)
  local copies, waits for them, and re-layouts  2.32 us (3%)
  between operations  0.95 us (1%)
    ppermute x3, waiting for transfers between devices, body(): ocean_rows = ocean_rows + lax.ppermute(returned, 'comp', [(last, target)])  9.01 us
    all_to_all x1, waiting for transfers between devices, body(): came_back = lax.all_to_all(reply, 'band', 0, 0, tiled=True)  8.66 us
    all_to_all x1, starting transfers between devices, body(): received = lax.all_to_all(sending, 'band', 0, 0, tiled=True)  8.58 us
    pallas_call x1, Pallas kernels, diffuse(): pl.pallas_call(_diffusion_kernel, out_shape=jax.ShapeDtypeStruct((rows, l...  6.45 us
    all_to_all x1, starting transfers between devices, body(): came_back = lax.all_to_all(reply, 'band', 0, 0, tiled=True)  6.16 us
    dot_general x1, matrix products, body(): jnp.einsum('rfc,rcd->rfd', surface_layers, weights_local, preferred_eleme...  4.76 us
    ppermute x1, starting transfers between devices, diffuse(): above = lax.ppermute(comb[rows - halo:], 'band', forward)  3.42 us
    all_to_all x1, waiting for transfers between devices, body(): received = lax.all_to_all(sending, 'band', 0, 0, tiled=True)  2.95 us
  transfers between devices with their start and end apart: 10, of which 3 were waited for; matrix products, arithmetic and copies ran while one was open for 4% of the time, Pallas kernels for 10%

profile of v12, /device:TPU:1, one launch (start us, length us, event | category | flops | bytes accessed | tf_op | source)
XLA Modules:
  0.0 67.6 jit_solution(3595809804801243147)
XLA Ops:
  0.6 0.9 %fusion.5 = f32[64]{0:T(128)S(1)} fusion(s32[64]{0:T(128)} %bitcast.55), kind=kOutput, calls=%fused_computation.13 | convolution fusion | flops 286656 | bytes 512 | tf_op jit(solution)/shard_map/dot_general | solution.py:124
  1.5 0.7 fusion.16
  2.2 0.7 convert_bitcast_fusion
  2.9 4.8 %conditional.2 = (f32[64,1024]{1,0:T(8,128)S(1)}) conditional(s32[]{:T(128)} %convert_element_type.100, (f32[1,64,16,256]{3,2,1,0:T(8,128)}, bf16[64,256,256]{2,1,0:T(8,128)(2,1)}) %tuple.37, () %tuple.27), branch_computations={%region_1.0_spmd, %region_2.0_spmd} | conditional | flops 33554432 | bytes 9306120 | solution.py:110
  2.9 4.8 %fusion.1 = f32[64,4,256]{2,1,0:T(4,128)S(1)} fusion(bf16[64,256,256]{2,1,0:T(8,128)(2,1)} %get-tuple-element.33, f32[1,64,16,256]{3,2,1,0:T(8,128)} %get-tuple-element.32), kind=kOutput, calls=%fused_computation.2 | convolution fusion | flops 33554432 | bytes 8781824 | tf_op jit(solution)/shard_map/cond/branch_0_fun/rfc,rcd->rfd/dot_general | solution.py:113
  7.6 0.1 copy.20
  7.7 0.0 copy-start.2
  7.7 0.0 copy-start
  7.7 0.1 broadcast_in_dim.12
  7.8 0.6 convolution_convert_fusion.1
  8.4 0.9 %copy.17 = f16[32,4,1152]{2,1,0:T(4,128)(2,1)} copy(f16[32,4,1152]{2,0,1:T(8,128)(2,1)S(1)} %convolution_convert_fusion.1) | data formatting | bytes 589824 | tf_op jit(solution)/shard_map/convert_element_type | solution.py:138
  9.3 8.6 %all-to-all-start = ((f16[32,4,1152]{2,1,0:T(4,128)(2,1)}), f16[32,4,1152]{2,1,0:T(4,128)(2,1)S(1)}, u32[]{:S(2)}, u32[]{:S(2)}) async-start(f16[32,4,1152]{2,1,0:T(4,128)(2,1)} %copy.17), calls=%async_computation | async-start | bytes 589824 | tf_op jit(solution)/shard_map/all_to_all | solution.py:139
  18.0 2.1 %collective-permute-start.1 = (f32[4,17,256]{2,1,0:T(8,128)S(1)}, f32[4,17,256]{2,1,0:T(8,128)S(1)}, u32[]{:S(2)}, u32[]{:S(2)}) collective-permute-start(f32[4,17,256]{2,1,0:T(8,128)S(1)} %get-tuple-element.40), channel_id=1, source_target_pairs={{1,0},{2,1},{3,2},{4,3},{5,4},{6,5},{7,6},{8,7},{9,8},{10,9},{11,1... | collective-permute-start | bytes 208904 | tf_op jit(solution)/shard_map/ppermute | solution.py:82
  20.2 3.4 %collective-permute-start = (f32[4,17,256]{2,1,0:T(8,128)S(1)}, f32[4,17,256]{2,1,0:T(8,128)S(1)}, u32[]{:S(2)}, u32[]{:S(2)}) collective-permute-start(f32[4,17,256]{2,1,0:T(8,128)S(1)} %get-tuple-element.39), channel_id=1, source_target_pairs={{0,1},{1,2},{2,3},{3,4},{4,5},{5,6},{6,7},{7,8},{8,9},{9,10},{10,1... | collective-permute-start | bytes 208904 | tf_op jit(solution)/shard_map/ppermute | solution.py:81
  23.6 0.6 pad_add_fusion.bounds_ref
  24.2 2.9 %all-to-all-done = f16[32,4,1152]{2,1,0:T(4,128)(2,1)S(1)} async-done(((f16[32,4,1152]{2,1,0:T(4,128)(2,1)}), f16[32,4,1152]{2,1,0:T(4,128)(2,1)S(1)}, u32[]{:S(2)}, u32[]{:S(2)}) %all-to-all-start) | async-done | bytes 294944 | tf_op jit(solution)/shard_map/all_to_all | solution.py:139
  27.1 0.1 reshape.121
  27.2 0.1 convert_reduce_fusion
  27.3 0.4 fusion.4
  27.7 0.7 collective-permute-start.4
  28.4 1.5 %collective-permute-start.3 = (f16[64,1024]{1,0:T(8,128)(2,1)S(1)}, f16[64,1024]{1,0:T(8,128)(2,1)S(1)}, u32[]{:S(2)}, u32[]{:S(2)}) collective-permute-start(f16[64,1024]{1,0:T(8,128)(2,1)S(1)} %fusion.4), channel_id=1, source_target_pairs={{0,96},{1,97},{2,98},{3,99},{4,100},{5,101},{6,102},{7,103},{8,104... | collective-permute-start | bytes 393224 | tf_op jit(solution)/shard_map/ppermute | solution.py:148
  29.9 0.7 collective-permute-start.2
  30.6 0.0 collective-permute-done.1
  30.6 0.0 collective-permute-done
  30.6 1.4 %pad_maximum_fusion.p_ref = f32[72,17,256]{2,1,0:T(8,128)} fusion(f32[4,17,256]{2,1,0:T(8,128)S(1)} %collective-permute-done.1, f32[64,1,256]{2,1,0:T(1,128)S(1)} %broadcast_in_dim_squeeze.4, f32[64,16,256]{2,1,0:T(8,128)S(1)} %bitcast.46, f32[4,17,256]{2,1,0:T(8,128)S(1)} %collective-permute-done), kind=kLoop, calls=%fused_computation.6 | loop fusion | flops 940032 | bytes 2506752 | tf_op jit(solution)/shard_map/concatenate | solution.py:83
  32.0 6.4 %shard_map.68 = f32[64,16,256]{2,1,0:T(8,128)S(1)} custom-call(s32[2]{0:T(128)} %pad_add_fusion.bounds_ref, f32[72,17,256]{2,1,0:T(8,128)} %pad_maximum_fusion.p_ref), custom_call_target="tpu_custom_call" | custom-call | tf_op jit(solution)/shard_map/pallas_call | solution.py:87
  38.4 0.0 collective-permute-done.4
  38.4 0.0 collective-permute-done.3
  38.5 0.0 collective-permute-done.2
  38.5 0.1 add_select_fusion
  38.5 0.1 reshape.122
  38.7 0.1 conditional.3
  38.7 0.7 collective-permute-start.7
  39.4 0.7 collective-permute-start.6
  40.1 1.3 %collective-permute-start.5 = (bf16[64,4,256]{2,1,0:T(4,128)(2,1)S(1)}, bf16[64,4,256]{2,1,0:T(4,128)(2,1)S(1)}, u32[]{:S(2)}, u32[]{:S(2)}) collective-permute-start(bf16[64,4,256]{2,1,0:T(4,128)(2,1)S(1)} %get-tuple-element.44), channel_id=1, source_target_pairs={{96,0},{97,1},{98,2},{99,3},{100,4},{101,5},{102,6},{103,7},{104,8... | collective-permute-start | bytes 393224 | tf_op jit(solution)/shard_map/ppermute | solution.py:166
  41.4 0.0 collective-permute-done.7
  41.4 0.0 collective-permute-done.6
  41.4 9.0 %collective-permute-done.5 = bf16[64,4,256]{2,1,0:T(4,128)(2,1)S(1)} collective-permute-done((bf16[64,4,256]{2,1,0:T(4,128)(2,1)S(1)}, bf16[64,4,256]{2,1,0:T(4,128)(2,1)S(1)}, u32[]{:S(2)}, u32[]{:S(2)}) %collective-permute-start.5) | collective-permute-done | bytes 131104 | tf_op jit(solution)/shard_map/ppermute | solution.py:166
  50.5 0.3 convolution_convert_fusion.2
  50.8 0.8 %reshape.124 = bf16[32,4,1024]{2,1,0:T(4,128)(2,1)} reshape(bf16[128,1024]{1,0:T(8,128)(2,1)S(1)} %convolution_convert_fusion.2) | data formatting | bytes 524288 | tf_op jit(solution)/shard_map/reshape | solution.py:171
  51.6 6.2 %all-to-all-start.1 = ((bf16[32,4,1024]{2,1,0:T(4,128)(2,1)}), bf16[32,4,1024]{2,1,0:T(4,128)(2,1)S(1)}, u32[]{:S(2)}, u32[]{:S(2)}) async-start(bf16[32,4,1024]{2,1,0:T(4,128)(2,1)} %reshape.124), calls=%async_computation.1 | async-start | bytes 524288 | tf_op jit(solution)/shard_map/all_to_all | solution.py:172
  57.7 0.1 copy.30
  57.8 0.1 fusion.10
  57.9 0.0 copy-start.1
  57.9 8.7 %all-to-all-done.1 = bf16[32,4,1024]{2,1,0:T(4,128)(2,1)S(1)} async-done(((bf16[32,4,1024]{2,1,0:T(4,128)(2,1)}), bf16[32,4,1024]{2,1,0:T(4,128)(2,1)S(1)}, u32[]{:S(2)}, u32[]{:S(2)}) %all-to-all-start.1) | async-done | bytes 262176 | tf_op jit(solution)/shard_map/all_to_all | solution.py:172
  66.6 0.2 fusion.3
  66.8 0.1 reshape.125
  66.9 0.7 %select_bitcast_fusion = bf16[1,64,4,256]{3,2,1,0:T(4,128)(2,1)} fusion(bf16[64,4,256]{2,1,0:T(4,128)(2,1)S(1)} %get-tuple-element.44, bf16[64,4,256]{2,1,0:T(4,128)(2,1)S(1)} %reshape.125, pred[]{:T(512)S(6)} %eq.62), kind=kLoop, calls=%fused_computation.23 | loop fusion | flops 65536 | bytes 393217 | tf_op jit(solution)/shard_map/broadcast_in_dim | solution.py:178
  (11 shorter events, 0.2 us)
Async XLA Ops:
  7.7 10.2 %copy-start.2 = (f32[1,64,256]{2,1,0:T(8,128)S(1)}, f32[1,64,256]{2,1,0:T(8,128)}, u32[]{:S(2)}) copy-start(f32[1,64,256]{2,1,0:T(8,128)} %param.12) | copy-start | bytes 196612
  7.7 10.3 %copy-start = (f32[1,64,16,256]{3,2,1,0:T(8,128)S(1)}, f32[1,64,16,256]{3,2,1,0:T(8,128)}, u32[]{:S(2)}) copy-start(f32[1,64,16,256]{3,2,1,0:T(8,128)} %param.11) | copy-start | bytes 3145732
  9.3 17.8 %all-to-all-start = ((f16[32,4,1152]{2,1,0:T(4,128)(2,1)}), f16[32,4,1152]{2,1,0:T(4,128)(2,1)S(1)}, u32[]{:S(2)}, u32[]{:S(2)}) async-start(f16[32,4,1152]{2,1,0:T(4,128)(2,1)} %copy.17), calls=%async_computation | async-start | bytes 589824 | tf_op jit(solution)/shard_map/all_to_all | solution.py:139
  18.0 12.5 %collective-permute-start.1 = (f32[4,17,256]{2,1,0:T(8,128)S(1)}, f32[4,17,256]{2,1,0:T(8,128)S(1)}, u32[]{:S(2)}, u32[]{:S(2)}) collective-permute-start(f32[4,17,256]{2,1,0:T(8,128)S(1)} %get-tuple-element.40), channel_id=1, source_target_pairs={{1,0},{2,1},{3,2},{4,3},{5,4},{6,5},{7,6},{8,7},{9,8},{10,9},{11,1... | collective-permute-start | bytes 208904 | tf_op jit(solution)/shard_map/ppermute | solution.py:82
  20.2 10.4 %collective-permute-start = (f32[4,17,256]{2,1,0:T(8,128)S(1)}, f32[4,17,256]{2,1,0:T(8,128)S(1)}, u32[]{:S(2)}, u32[]{:S(2)}) collective-permute-start(f32[4,17,256]{2,1,0:T(8,128)S(1)} %get-tuple-element.39), channel_id=1, source_target_pairs={{0,1},{1,2},{2,3},{3,4},{4,5},{5,6},{6,7},{7,8},{8,9},{9,10},{10,1... | collective-permute-start | bytes 208904 | tf_op jit(solution)/shard_map/ppermute | solution.py:81
  27.7 10.7 %collective-permute-start.4 = (f16[64,1024]{1,0:T(8,128)(2,1)S(1)}, f16[64,1024]{1,0:T(8,128)(2,1)S(1)}, u32[]{:S(2)}, u32[]{:S(2)}) collective-permute-start(f16[64,1024]{1,0:T(8,128)(2,1)S(1)} %fusion.4), channel_id=1, source_target_pairs={{32,96},{33,97},{34,98},{35,99},{36,100},{37,101},{38,102},{39,103... | collective-permute-start | bytes 393224 | tf_op jit(solution)/shard_map/ppermute | solution.py:148
  28.4 10.1 %collective-permute-start.3 = (f16[64,1024]{1,0:T(8,128)(2,1)S(1)}, f16[64,1024]{1,0:T(8,128)(2,1)S(1)}, u32[]{:S(2)}, u32[]{:S(2)}) collective-permute-start(f16[64,1024]{1,0:T(8,128)(2,1)S(1)} %fusion.4), channel_id=1, source_target_pairs={{0,96},{1,97},{2,98},{3,99},{4,100},{5,101},{6,102},{7,103},{8,104... | collective-permute-start | bytes 393224 | tf_op jit(solution)/shard_map/ppermute | solution.py:148
  29.9 8.6 %collective-permute-start.2 = (f16[64,1024]{1,0:T(8,128)(2,1)S(1)}, f16[64,1024]{1,0:T(8,128)(2,1)S(1)}, u32[]{:S(2)}, u32[]{:S(2)}) collective-permute-start(f16[64,1024]{1,0:T(8,128)(2,1)S(1)} %fusion.4), channel_id=1, source_target_pairs={{64,96},{65,97},{66,98},{67,99},{68,100},{69,101},{70,102},{71,103... | collective-permute-start | bytes 393224 | tf_op jit(solution)/shard_map/ppermute | solution.py:148
  38.7 2.7 %collective-permute-start.7 = (bf16[64,4,256]{2,1,0:T(4,128)(2,1)S(1)}, bf16[64,4,256]{2,1,0:T(4,128)(2,1)S(1)}, u32[]{:S(2)}, u32[]{:S(2)}) collective-permute-start(bf16[64,4,256]{2,1,0:T(4,128)(2,1)S(1)} %get-tuple-element.44), channel_id=1, source_target_pairs={{96,64},{97,65},{98,66},{99,67},{100,68},{101,69},{102,70},{103,71... | collective-permute-start | bytes 393224 | tf_op jit(solution)/shard_map/ppermute | solution.py:166
  39.4 2.0 %collective-permute-start.6 = (bf16[64,4,256]{2,1,0:T(4,128)(2,1)S(1)}, bf16[64,4,256]{2,1,0:T(4,128)(2,1)S(1)}, u32[]{:S(2)}, u32[]{:S(2)}) collective-permute-start(bf16[64,4,256]{2,1,0:T(4,128)(2,1)S(1)} %get-tuple-element.44), channel_id=1, source_target_pairs={{96,32},{97,33},{98,34},{99,35},{100,36},{101,37},{102,38},{103,39... | collective-permute-start | bytes 393224 | tf_op jit(solution)/shard_map/ppermute | solution.py:166
  40.1 10.3 %collective-permute-start.5 = (bf16[64,4,256]{2,1,0:T(4,128)(2,1)S(1)}, bf16[64,4,256]{2,1,0:T(4,128)(2,1)S(1)}, u32[]{:S(2)}, u32[]{:S(2)}) collective-permute-start(bf16[64,4,256]{2,1,0:T(4,128)(2,1)S(1)} %get-tuple-element.44), channel_id=1, source_target_pairs={{96,0},{97,1},{98,2},{99,3},{100,4},{101,5},{102,6},{103,7},{104,8... | collective-permute-start | bytes 393224 | tf_op jit(solution)/shard_map/ppermute | solution.py:166
  51.6 15.0 %all-to-all-start.1 = ((bf16[32,4,1024]{2,1,0:T(4,128)(2,1)}), bf16[32,4,1024]{2,1,0:T(4,128)(2,1)S(1)}, u32[]{:S(2)}, u32[]{:S(2)}) async-start(bf16[32,4,1024]{2,1,0:T(4,128)(2,1)} %reshape.124), calls=%async_computation.1 | async-start | bytes 524288 | tf_op jit(solution)/shard_map/all_to_all | solution.py:172
  57.9 9.7 %copy-start.1 = (f32[1,64,16,256]{3,2,1,0:T(8,128)}, f32[1,64,16,256]{3,2,1,0:T(8,128)S(1)}, u32[]{:S(2)}) copy-start(f32[1,64,16,256]{3,2,1,0:T(8,128)S(1)} %fusion.10) | copy-start | bytes 3145732

commit v13 on v12

--- a/solution.py
+++ b/solution.py
@@ -162,7 +162,7 @@
     )
 
     ocean_rows = returned
-    for target in range(last):
+    for target in sorted(range(last), key=lambda t: (t + 1) % last):
         ocean_rows = ocean_rows + lax.ppermute(returned, "comp", [(last, target)])
     ocean_rows = ocean_rows.reshape(rows, width)
     reply = jnp.einsum(

time: 68.1 us -> 66.8 us (0.981)
  waiting for transfers between devices: 20.6 us -> 19.3 us
    ppermute x3, waiting for transfers between devices: 9.01 us -> 7.71 us  [body(): ocean_rows = ocean_rows + lax.ppermute(returned, 'comp', [(last, target)])]
where the time goes in v13:
time: 66.8 us; the launch traced here: 66.3 us
  starting transfers between devices  25.8 us (39%)
  waiting for transfers between devices  19.3 us (29%)
  matrix products  7.09 us (11%)
  Pallas kernels  6.45 us (10%)
  other arithmetic  4.39 us (7%)
  local copies, waits for them, and re-layouts  2.32 us (3%)
  between operations  0.95 us (1%)
    all_to_all x1, waiting for transfers between devices, body(): came_back = lax.all_to_all(reply, 'band', 0, 0, tiled=True)  8.66 us
    all_to_all x1, starting transfers between devices, body(): received = lax.all_to_all(sending, 'band', 0, 0, tiled=True)  8.58 us
    ppermute x3, waiting for transfers between devices, body(): ocean_rows = ocean_rows + lax.ppermute(returned, 'comp', [(last, target)])  7.71 us
    pallas_call x1, Pallas kernels, diffuse(): pl.pallas_call(_diffusion_kernel, out_shape=jax.ShapeDtypeStruct((rows, l...  6.45 us
    all_to_all x1, starting transfers between devices, body(): came_back = lax.all_to_all(reply, 'band', 0, 0, tiled=True)  6.16 us
    dot_general x1, matrix products, body(): jnp.einsum('rfc,rcd->rfd', surface_layers, weights_local, preferred_eleme...  4.76 us
    ppermute x1, starting transfers between devices, diffuse(): above = lax.ppermute(comb[rows - halo:], 'band', forward)  3.42 us
    all_to_all x1, waiting for transfers between devices, body(): received = lax.all_to_all(sending, 'band', 0, 0, tiled=True)  2.95 us
  transfers between devices with their start and end apart: 10, of which 3 were waited for; matrix products, arithmetic and copies ran while one was open for 4% of the time, Pallas kernels for 10%

profile of v13, /device:TPU:1, one launch (start us, length us, event | category | flops | bytes accessed | tf_op | source)
XLA Modules:
  0.0 66.3 jit_solution(805798204102815553)
XLA Ops:
  0.6 0.9 %fusion.5 = f32[64]{0:T(128)S(1)} fusion(s32[64]{0:T(128)} %bitcast.55), kind=kOutput, calls=%fused_computation.13 | convolution fusion | flops 286656 | bytes 512 | tf_op jit(solution)/shard_map/dot_general | solution.py:124
  1.5 0.7 %fusion.16 = f32[64,32]{0,1:T(8,128)S(1)} fusion(s32[64]{0:T(128)} %bitcast.56), kind=kLoop, calls=%fused_computation.39 | loop fusion | flops 4096 | bytes 8448 | tf_op jit(solution)/shard_map/convert_element_type | solution.py:119
  2.2 0.7 convert_bitcast_fusion
  2.9 4.8 %conditional.2 = (f32[64,1024]{1,0:T(8,128)S(1)}) conditional(s32[]{:T(128)} %convert_element_type.100, (f32[1,64,16,256]{3,2,1,0:T(8,128)}, bf16[64,256,256]{2,1,0:T(8,128)(2,1)}) %tuple.37, () %tuple.27), branch_computations={%region_1.0_spmd, %region_2.0_spmd} | conditional | flops 33554432 | bytes 9306120 | solution.py:110
  2.9 4.8 %fusion.1 = f32[64,4,256]{2,1,0:T(4,128)S(1)} fusion(bf16[64,256,256]{2,1,0:T(8,128)(2,1)} %get-tuple-element.33, f32[1,64,16,256]{3,2,1,0:T(8,128)} %get-tuple-element.32), kind=kOutput, calls=%fused_computation.2 | convolution fusion | flops 33554432 | bytes 8781824 | tf_op jit(solution)/shard_map/cond/branch_0_fun/rfc,rcd->rfd/dot_general | solution.py:113
  7.6 0.1 copy.20
  7.7 0.0 copy-start.2
  7.7 0.0 copy-start
  7.7 0.1 broadcast_in_dim.12
  7.8 0.6 convolution_convert_fusion.1
  8.4 0.9 %copy.17 = f16[32,4,1152]{2,1,0:T(4,128)(2,1)} copy(f16[32,4,1152]{2,0,1:T(8,128)(2,1)S(1)} %convolution_convert_fusion.1) | data formatting | bytes 589824 | tf_op jit(solution)/shard_map/convert_element_type | solution.py:138
  9.3 8.6 %all-to-all-start = ((f16[32,4,1152]{2,1,0:T(4,128)(2,1)}), f16[32,4,1152]{2,1,0:T(4,128)(2,1)S(1)}, u32[]{:S(2)}, u32[]{:S(2)}) async-start(f16[32,4,1152]{2,1,0:T(4,128)(2,1)} %copy.17), calls=%async_computation | async-start | bytes 589824 | tf_op jit(solution)/shard_map/all_to_all | solution.py:139
  18.0 2.1 %collective-permute-start.1 = (f32[4,17,256]{2,1,0:T(8,128)S(1)}, f32[4,17,256]{2,1,0:T(8,128)S(1)}, u32[]{:S(2)}, u32[]{:S(2)}) collective-permute-start(f32[4,17,256]{2,1,0:T(8,128)S(1)} %get-tuple-element.40), channel_id=1, source_target_pairs={{1,0},{2,1},{3,2},{4,3},{5,4},{6,5},{7,6},{8,7},{9,8},{10,9},{11,1... | collective-permute-start | bytes 208904 | tf_op jit(solution)/shard_map/ppermute | solution.py:82
  20.2 3.4 %collective-permute-start = (f32[4,17,256]{2,1,0:T(8,128)S(1)}, f32[4,17,256]{2,1,0:T(8,128)S(1)}, u32[]{:S(2)}, u32[]{:S(2)}) collective-permute-start(f32[4,17,256]{2,1,0:T(8,128)S(1)} %get-tuple-element.39), channel_id=1, source_target_pairs={{0,1},{1,2},{2,3},{3,4},{4,5},{5,6},{6,7},{7,8},{8,9},{9,10},{10,1... | collective-permute-start | bytes 208904 | tf_op jit(solution)/shard_map/ppermute | solution.py:81
  23.6 0.6 pad_add_fusion.bounds_ref
  24.2 2.9 %all-to-all-done = f16[32,4,1152]{2,1,0:T(4,128)(2,1)S(1)} async-done(((f16[32,4,1152]{2,1,0:T(4,128)(2,1)}), f16[32,4,1152]{2,1,0:T(4,128)(2,1)S(1)}, u32[]{:S(2)}, u32[]{:S(2)}) %all-to-all-start) | async-done | bytes 294944 | tf_op jit(solution)/shard_map/all_to_all | solution.py:139
  27.1 0.1 reshape.121
  27.2 0.1 convert_reduce_fusion
  27.3 0.4 fusion.4
  27.7 0.7 %collective-permute-start.4 = (f16[64,1024]{1,0:T(8,128)(2,1)S(1)}, f16[64,1024]{1,0:T(8,128)(2,1)S(1)}, u32[]{:S(2)}, u32[]{:S(2)}) collective-permute-start(f16[64,1024]{1,0:T(8,128)(2,1)S(1)} %fusion.4), channel_id=1, source_target_pairs={{32,96},{33,97},{34,98},{35,99},{36,100},{37,101},{38,102},{39,103... | collective-permute-start | bytes 393224 | tf_op jit(solution)/shard_map/ppermute | solution.py:148
  28.4 1.5 %collective-permute-start.3 = (f16[64,1024]{1,0:T(8,128)(2,1)S(1)}, f16[64,1024]{1,0:T(8,128)(2,1)S(1)}, u32[]{:S(2)}, u32[]{:S(2)}) collective-permute-start(f16[64,1024]{1,0:T(8,128)(2,1)S(1)} %fusion.4), channel_id=1, source_target_pairs={{0,96},{1,97},{2,98},{3,99},{4,100},{5,101},{6,102},{7,103},{8,104... | collective-permute-start | bytes 393224 | tf_op jit(solution)/shard_map/ppermute | solution.py:148
  29.9 0.7 %collective-permute-start.2 = (f16[64,1024]{1,0:T(8,128)(2,1)S(1)}, f16[64,1024]{1,0:T(8,128)(2,1)S(1)}, u32[]{:S(2)}, u32[]{:S(2)}) collective-permute-start(f16[64,1024]{1,0:T(8,128)(2,1)S(1)} %fusion.4), channel_id=1, source_target_pairs={{64,96},{65,97},{66,98},{67,99},{68,100},{69,101},{70,102},{71,103... | collective-permute-start | bytes 393224 | tf_op jit(solution)/shard_map/ppermute | solution.py:148
  30.6 0.0 collective-permute-done.1
  30.6 0.0 collective-permute-done
  30.6 1.4 %pad_maximum_fusion.p_ref = f32[72,17,256]{2,1,0:T(8,128)} fusion(f32[4,17,256]{2,1,0:T(8,128)S(1)} %collective-permute-done.1, f32[64,1,256]{2,1,0:T(1,128)S(1)} %broadcast_in_dim_squeeze.4, f32[64,16,256]{2,1,0:T(8,128)S(1)} %bitcast.46, f32[4,17,256]{2,1,0:T(8,128)S(1)} %collective-permute-done), kind=kLoop, calls=%fused_computation.6 | loop fusion | flops 940032 | bytes 2506752 | tf_op jit(solution)/shard_map/concatenate | solution.py:83
  32.0 6.4 %shard_map.68 = f32[64,16,256]{2,1,0:T(8,128)S(1)} custom-call(s32[2]{0:T(128)} %pad_add_fusion.bounds_ref, f32[72,17,256]{2,1,0:T(8,128)} %pad_maximum_fusion.p_ref), custom_call_target="tpu_custom_call" | custom-call | tf_op jit(solution)/shard_map/pallas_call | solution.py:87
  38.4 0.0 collective-permute-done.4
  38.4 0.0 collective-permute-done.3
  38.5 0.0 collective-permute-done.2
  38.5 0.1 add_select_fusion
  38.5 0.1 reshape.122
  38.7 0.1 conditional.3
  38.7 0.7 %collective-permute-start.7 = (bf16[64,4,256]{2,1,0:T(4,128)(2,1)S(1)}, bf16[64,4,256]{2,1,0:T(4,128)(2,1)S(1)}, u32[]{:S(2)}, u32[]{:S(2)}) collective-permute-start(bf16[64,4,256]{2,1,0:T(4,128)(2,1)S(1)} %get-tuple-element.44), channel_id=1, source_target_pairs={{96,32},{97,33},{98,34},{99,35},{100,36},{101,37},{102,38},{103,39... | collective-permute-start | bytes 393224 | tf_op jit(solution)/shard_map/ppermute | solution.py:166
  39.4 1.3 %collective-permute-start.6 = (bf16[64,4,256]{2,1,0:T(4,128)(2,1)S(1)}, bf16[64,4,256]{2,1,0:T(4,128)(2,1)S(1)}, u32[]{:S(2)}, u32[]{:S(2)}) collective-permute-start(bf16[64,4,256]{2,1,0:T(4,128)(2,1)S(1)} %get-tuple-element.44), channel_id=1, source_target_pairs={{96,0},{97,1},{98,2},{99,3},{100,4},{101,5},{102,6},{103,7},{104,8... | collective-permute-start | bytes 393224 | tf_op jit(solution)/shard_map/ppermute | solution.py:166
  40.7 0.7 %collective-permute-start.5 = (bf16[64,4,256]{2,1,0:T(4,128)(2,1)S(1)}, bf16[64,4,256]{2,1,0:T(4,128)(2,1)S(1)}, u32[]{:S(2)}, u32[]{:S(2)}) collective-permute-start(bf16[64,4,256]{2,1,0:T(4,128)(2,1)S(1)} %get-tuple-element.44), channel_id=1, source_target_pairs={{96,64},{97,65},{98,66},{99,67},{100,68},{101,69},{102,70},{103,71... | collective-permute-start | bytes 393224 | tf_op jit(solution)/shard_map/ppermute | solution.py:166
  41.4 0.0 collective-permute-done.7
  41.4 7.7 %collective-permute-done.6 = bf16[64,4,256]{2,1,0:T(4,128)(2,1)S(1)} collective-permute-done((bf16[64,4,256]{2,1,0:T(4,128)(2,1)S(1)}, bf16[64,4,256]{2,1,0:T(4,128)(2,1)S(1)}, u32[]{:S(2)}, u32[]{:S(2)}) %collective-permute-start.6) | collective-permute-done | bytes 131104 | tf_op jit(solution)/shard_map/ppermute | solution.py:166
  49.1 0.0 collective-permute-done.5
  49.2 0.3 convolution_convert_fusion.2
  49.5 0.8 %reshape.124 = bf16[32,4,1024]{2,1,0:T(4,128)(2,1)} reshape(bf16[128,1024]{1,0:T(8,128)(2,1)S(1)} %convolution_convert_fusion.2) | data formatting | bytes 524288 | tf_op jit(solution)/shard_map/reshape | solution.py:171
  50.3 6.2 %all-to-all-start.1 = ((bf16[32,4,1024]{2,1,0:T(4,128)(2,1)}), bf16[32,4,1024]{2,1,0:T(4,128)(2,1)S(1)}, u32[]{:S(2)}, u32[]{:S(2)}) async-start(bf16[32,4,1024]{2,1,0:T(4,128)(2,1)} %reshape.124), calls=%async_computation.1 | async-start | bytes 524288 | tf_op jit(solution)/shard_map/all_to_all | solution.py:172
  56.4 0.1 copy.30
  56.5 0.1 fusion.10
  56.6 0.0 copy-start.1
  56.6 8.7 %all-to-all-done.1 = bf16[32,4,1024]{2,1,0:T(4,128)(2,1)S(1)} async-done(((bf16[32,4,1024]{2,1,0:T(4,128)(2,1)}), bf16[32,4,1024]{2,1,0:T(4,128)(2,1)S(1)}, u32[]{:S(2)}, u32[]{:S(2)}) %all-to-all-start.1) | async-done | bytes 262176 | tf_op jit(solution)/shard_map/all_to_all | solution.py:172
  65.3 0.2 fusion.3
  65.5 0.1 reshape.125
  65.6 0.7 %select_bitcast_fusion = bf16[1,64,4,256]{3,2,1,0:T(4,128)(2,1)} fusion(bf16[64,4,256]{2,1,0:T(4,128)(2,1)S(1)} %get-tuple-element.44, bf16[64,4,256]{2,1,0:T(4,128)(2,1)S(1)} %reshape.125, pred[]{:T(512)S(6)} %eq.62), kind=kLoop, calls=%fused_computation.23 | loop fusion | flops 65536 | bytes 393217 | tf_op jit(solution)/shard_map/broadcast_in_dim | solution.py:178
  (11 shorter events, 0.2 us)
Async XLA Ops:
  7.7 10.2 %copy-start.2 = (f32[1,64,256]{2,1,0:T(8,128)S(1)}, f32[1,64,256]{2,1,0:T(8,128)}, u32[]{:S(2)}) copy-start(f32[1,64,256]{2,1,0:T(8,128)} %param.12) | copy-start | bytes 196612
  7.7 10.3 %copy-start = (f32[1,64,16,256]{3,2,1,0:T(8,128)S(1)}, f32[1,64,16,256]{3,2,1,0:T(8,128)}, u32[]{:S(2)}) copy-start(f32[1,64,16,256]{3,2,1,0:T(8,128)} %param.11) | copy-start | bytes 3145732
  9.3 17.8 %all-to-all-start = ((f16[32,4,1152]{2,1,0:T(4,128)(2,1)}), f16[32,4,1152]{2,1,0:T(4,128)(2,1)S(1)}, u32[]{:S(2)}, u32[]{:S(2)}) async-start(f16[32,4,1152]{2,1,0:T(4,128)(2,1)} %copy.17), calls=%async_computation | async-start | bytes 589824 | tf_op jit(solution)/shard_map/all_to_all | solution.py:139
  18.0 12.5 %collective-permute-start.1 = (f32[4,17,256]{2,1,0:T(8,128)S(1)}, f32[4,17,256]{2,1,0:T(8,128)S(1)}, u32[]{:S(2)}, u32[]{:S(2)}) collective-permute-start(f32[4,17,256]{2,1,0:T(8,128)S(1)} %get-tuple-element.40), channel_id=1, source_target_pairs={{1,0},{2,1},{3,2},{4,3},{5,4},{6,5},{7,6},{8,7},{9,8},{10,9},{11,1... | collective-permute-start | bytes 208904 | tf_op jit(solution)/shard_map/ppermute | solution.py:82
  20.2 10.4 %collective-permute-start = (f32[4,17,256]{2,1,0:T(8,128)S(1)}, f32[4,17,256]{2,1,0:T(8,128)S(1)}, u32[]{:S(2)}, u32[]{:S(2)}) collective-permute-start(f32[4,17,256]{2,1,0:T(8,128)S(1)} %get-tuple-element.39), channel_id=1, source_target_pairs={{0,1},{1,2},{2,3},{3,4},{4,5},{5,6},{6,7},{7,8},{8,9},{9,10},{10,1... | collective-permute-start | bytes 208904 | tf_op jit(solution)/shard_map/ppermute | solution.py:81
  27.7 10.7 %collective-permute-start.4 = (f16[64,1024]{1,0:T(8,128)(2,1)S(1)}, f16[64,1024]{1,0:T(8,128)(2,1)S(1)}, u32[]{:S(2)}, u32[]{:S(2)}) collective-permute-start(f16[64,1024]{1,0:T(8,128)(2,1)S(1)} %fusion.4), channel_id=1, source_target_pairs={{32,96},{33,97},{34,98},{35,99},{36,100},{37,101},{38,102},{39,103... | collective-permute-start | bytes 393224 | tf_op jit(solution)/shard_map/ppermute | solution.py:148
  28.4 10.1 %collective-permute-start.3 = (f16[64,1024]{1,0:T(8,128)(2,1)S(1)}, f16[64,1024]{1,0:T(8,128)(2,1)S(1)}, u32[]{:S(2)}, u32[]{:S(2)}) collective-permute-start(f16[64,1024]{1,0:T(8,128)(2,1)S(1)} %fusion.4), channel_id=1, source_target_pairs={{0,96},{1,97},{2,98},{3,99},{4,100},{5,101},{6,102},{7,103},{8,104... | collective-permute-start | bytes 393224 | tf_op jit(solution)/shard_map/ppermute | solution.py:148
  29.9 8.6 %collective-permute-start.2 = (f16[64,1024]{1,0:T(8,128)(2,1)S(1)}, f16[64,1024]{1,0:T(8,128)(2,1)S(1)}, u32[]{:S(2)}, u32[]{:S(2)}) collective-permute-start(f16[64,1024]{1,0:T(8,128)(2,1)S(1)} %fusion.4), channel_id=1, source_target_pairs={{64,96},{65,97},{66,98},{67,99},{68,100},{69,101},{70,102},{71,103... | collective-permute-start | bytes 393224 | tf_op jit(solution)/shard_map/ppermute | solution.py:148
  38.7 2.7 %collective-permute-start.7 = (bf16[64,4,256]{2,1,0:T(4,128)(2,1)S(1)}, bf16[64,4,256]{2,1,0:T(4,128)(2,1)S(1)}, u32[]{:S(2)}, u32[]{:S(2)}) collective-permute-start(bf16[64,4,256]{2,1,0:T(4,128)(2,1)S(1)} %get-tuple-element.44), channel_id=1, source_target_pairs={{96,32},{97,33},{98,34},{99,35},{100,36},{101,37},{102,38},{103,39... | collective-permute-start | bytes 393224 | tf_op jit(solution)/shard_map/ppermute | solution.py:166
  39.4 9.7 %collective-permute-start.6 = (bf16[64,4,256]{2,1,0:T(4,128)(2,1)S(1)}, bf16[64,4,256]{2,1,0:T(4,128)(2,1)S(1)}, u32[]{:S(2)}, u32[]{:S(2)}) collective-permute-start(bf16[64,4,256]{2,1,0:T(4,128)(2,1)S(1)} %get-tuple-element.44), channel_id=1, source_target_pairs={{96,0},{97,1},{98,2},{99,3},{100,4},{101,5},{102,6},{103,7},{104,8... | collective-permute-start | bytes 393224 | tf_op jit(solution)/shard_map/ppermute | solution.py:166
  40.7 8.4 %collective-permute-start.5 = (bf16[64,4,256]{2,1,0:T(4,128)(2,1)S(1)}, bf16[64,4,256]{2,1,0:T(4,128)(2,1)S(1)}, u32[]{:S(2)}, u32[]{:S(2)}) collective-permute-start(bf16[64,4,256]{2,1,0:T(4,128)(2,1)S(1)} %get-tuple-element.44), channel_id=1, source_target_pairs={{96,64},{97,65},{98,66},{99,67},{100,68},{101,69},{102,70},{103,71... | collective-permute-start | bytes 393224 | tf_op jit(solution)/shard_map/ppermute | solution.py:166
  50.3 15.0 %all-to-all-start.1 = ((bf16[32,4,1024]{2,1,0:T(4,128)(2,1)}), bf16[32,4,1024]{2,1,0:T(4,128)(2,1)S(1)}, u32[]{:S(2)}, u32[]{:S(2)}) async-start(bf16[32,4,1024]{2,1,0:T(4,128)(2,1)} %reshape.124), calls=%async_computation.1 | async-start | bytes 524288 | tf_op jit(solution)/shard_map/all_to_all | solution.py:172
  56.6 9.7 %copy-start.1 = (f32[1,64,16,256]{3,2,1,0:T(8,128)}, f32[1,64,16,256]{3,2,1,0:T(8,128)S(1)}, u32[]{:S(2)}) copy-start(f32[1,64,16,256]{3,2,1,0:T(8,128)S(1)} %fusion.10) | copy-start | bytes 3145732

commit v14 on v13

--- a/solution.py
+++ b/solution.py
@@ -161,10 +161,8 @@
         lambda: jnp.zeros((rows, NF, cols), jnp.bfloat16),
     )
 
-    ocean_rows = returned
-    for target in sorted(range(last), key=lambda t: (t + 1) % last):
-        ocean_rows = ocean_rows + lax.ppermute(returned, "comp", [(last, target)])
-    ocean_rows = ocean_rows.reshape(rows, width)
+    spread = jnp.broadcast_to(returned[None], (n_sections, rows, NF, cols))
+    ocean_rows = lax.all_to_all(spread, "comp", 0, 0, tiled=True)[last].reshape(rows, width)
     reply = jnp.einsum(
         "kr,rx->kx", match.astype(jnp.bfloat16), ocean_rows, preferred_element_type=jnp.float32
     ).astype(jnp.bfloat16)

time: 66.8 us -> 72.4 us (1.084)
  blocking collectives: 0 us -> 14.3 us
  waiting for transfers between devices: 19.3 us -> 11.6 us
  starting transfers between devices: 25.8 us -> 24.7 us
    all_to_all x0 -> x1, blocking collectives: none -> 14.3 us  [body(): lax.all_to_all(spread, 'comp', 0, 0, tiled=True)[last].reshape(rows, width)]
    ppermute x3 -> x0, waiting for transfers between devices: 7.71 us -> none  [body(): ocean_rows = ocean_rows + lax.ppermute(returned, 'comp', [(last, target)])]
    ppermute x3 -> x0, starting transfers between devices: 2.63 us -> none  [body(): ocean_rows = ocean_rows + lax.ppermute(returned, 'comp', [(last, target)])]
    all_to_all x1, starting transfers between devices: 6.16 us -> 7.67 us  [body(): came_back = lax.all_to_all(reply, 'band', 0, 0, tiled=True)]
  transfers between devices with their start and end apart: 10 -> 7, of which waited for: 3 -> 2; matrix products, arithmetic and copies ran while one was open for 4% -> 4% of each run, Pallas kernels for 10% -> 9%
where the time goes in v14:
time: 72.4 us; the launch traced here: 71.9 us
  starting transfers between devices  24.7 us (34%)
  blocking collectives  14.3 us (20%)
  waiting for transfers between devices  11.6 us (16%)
  matrix products  7.09 us (10%)
  Pallas kernels  6.45 us (9%)
  other arithmetic  4.39 us (6%)
  local copies, waits for them, and re-layouts  2.51 us (3%)
  between operations  0.92 us (1%)
    all_to_all x1, blocking collectives, body(): lax.all_to_all(spread, 'comp', 0, 0, tiled=True)[last].reshape(rows, width)  14.3 us
    all_to_all x1, waiting for transfers between devices, body(): came_back = lax.all_to_all(reply, 'band', 0, 0, tiled=True)  8.66 us
    all_to_all x1, starting transfers between devices, body(): received = lax.all_to_all(sending, 'band', 0, 0, tiled=True)  8.58 us
    all_to_all x1, starting transfers between devices, body(): came_back = lax.all_to_all(reply, 'band', 0, 0, tiled=True)  7.67 us
    pallas_call x1, Pallas kernels, diffuse(): pl.pallas_call(_diffusion_kernel, out_shape=jax.ShapeDtypeStruct((rows, l...  6.45 us
    dot_general x1, matrix products, body(): jnp.einsum('rfc,rcd->rfd', surface_layers, weights_local, preferred_eleme...  4.76 us
    ppermute x1, starting transfers between devices, diffuse(): above = lax.ppermute(comb[rows - halo:], 'band', forward)  3.42 us
    all_to_all x1, waiting for transfers between devices, body(): received = lax.all_to_all(sending, 'band', 0, 0, tiled=True)  2.88 us
  transfers between devices with their start and end apart: 7, of which 2 were waited for; matrix products, arithmetic and copies ran while one was open for 4% of the time, Pallas kernels for 9%

profile of v14, /device:TPU:1, one launch (start us, length us, event | category | flops | bytes accessed | tf_op | source)
XLA Modules:
  0.0 71.9 jit_solution(9850890036427304555)
XLA Ops:
  0.6 0.9 %fusion.5 = f32[64]{0:T(128)S(1)} fusion(s32[64]{0:T(128)} %bitcast.47), kind=kOutput, calls=%fused_computation.13 | convolution fusion | flops 286656 | bytes 512 | tf_op jit(solution)/shard_map/dot_general | solution.py:124
  1.5 0.7 fusion.16
  2.2 0.7 convert_bitcast_fusion
  2.9 4.8 %conditional.2 = (f32[64,1024]{1,0:T(8,128)S(1)}) conditional(s32[]{:T(128)} %convert_element_type.100, (f32[1,64,16,256]{3,2,1,0:T(8,128)}, bf16[64,256,256]{2,1,0:T(8,128)(2,1)}) %tuple.37, () %tuple.27), branch_computations={%region_1.0_spmd, %region_2.0_spmd} | conditional | flops 33554432 | bytes 9306120 | solution.py:110
  2.9 4.8 %fusion.1 = f32[64,4,256]{2,1,0:T(4,128)S(1)} fusion(bf16[64,256,256]{2,1,0:T(8,128)(2,1)} %get-tuple-element.33, f32[1,64,16,256]{3,2,1,0:T(8,128)} %get-tuple-element.32), kind=kOutput, calls=%fused_computation.2 | convolution fusion | flops 33554432 | bytes 8781824 | tf_op jit(solution)/shard_map/cond/branch_0_fun/rfc,rcd->rfd/dot_general | solution.py:113
  7.6 0.1 copy.20
  7.7 0.0 copy-start.2
  7.7 0.0 copy-start
  7.7 0.1 broadcast_in_dim.15
  7.8 0.6 convolution_convert_fusion.1
  8.4 0.9 %copy.17 = f16[32,4,1152]{2,1,0:T(4,128)(2,1)} copy(f16[32,4,1152]{2,0,1:T(8,128)(2,1)S(1)} %convolution_convert_fusion.1) | data formatting | bytes 589824 | tf_op jit(solution)/shard_map/convert_element_type | solution.py:138
  9.3 8.6 %all-to-all-start = ((f16[32,4,1152]{2,1,0:T(4,128)(2,1)}), f16[32,4,1152]{2,1,0:T(4,128)(2,1)S(1)}, u32[]{:S(2)}, u32[]{:S(2)}) async-start(f16[32,4,1152]{2,1,0:T(4,128)(2,1)} %copy.17), calls=%async_computation | async-start | bytes 589824 | tf_op jit(solution)/shard_map/all_to_all | solution.py:139
  17.9 0.0 copy-done.2
  18.0 0.0 copy-done
  18.0 2.1 %collective-permute-start.1 = (f32[4,17,256]{2,1,0:T(8,128)S(1)}, f32[4,17,256]{2,1,0:T(8,128)S(1)}, u32[]{:S(2)}, u32[]{:S(2)}) collective-permute-start(f32[4,17,256]{2,1,0:T(8,128)S(1)} %get-tuple-element.40), channel_id=1, source_target_pairs={{1,0},{2,1},{3,2},{4,3},{5,4},{6,5},{7,6},{8,7},{9,8},{10,9},{11,1... | collective-permute-start | bytes 208904 | tf_op jit(solution)/shard_map/ppermute | solution.py:82
  20.2 3.4 %collective-permute-start = (f32[4,17,256]{2,1,0:T(8,128)S(1)}, f32[4,17,256]{2,1,0:T(8,128)S(1)}, u32[]{:S(2)}, u32[]{:S(2)}) collective-permute-start(f32[4,17,256]{2,1,0:T(8,128)S(1)} %get-tuple-element.39), channel_id=1, source_target_pairs={{0,1},{1,2},{2,3},{3,4},{4,5},{5,6},{6,7},{7,8},{8,9},{9,10},{10,1... | collective-permute-start | bytes 208904 | tf_op jit(solution)/shard_map/ppermute | solution.py:81
  23.6 0.6 pad_add_fusion.bounds_ref
  24.2 2.9 %all-to-all-done = f16[32,4,1152]{2,1,0:T(4,128)(2,1)S(1)} async-done(((f16[32,4,1152]{2,1,0:T(4,128)(2,1)}), f16[32,4,1152]{2,1,0:T(4,128)(2,1)S(1)}, u32[]{:S(2)}, u32[]{:S(2)}) %all-to-all-start) | async-done | bytes 294944 | tf_op jit(solution)/shard_map/all_to_all | solution.py:139
  27.1 0.1 reshape.119
  27.2 0.1 convert_reduce_fusion
  27.3 0.4 fusion.4
  27.7 0.7 collective-permute-start.4
  28.4 1.5 %collective-permute-start.3 = (f16[64,1024]{1,0:T(8,128)(2,1)S(1)}, f16[64,1024]{1,0:T(8,128)(2,1)S(1)}, u32[]{:S(2)}, u32[]{:S(2)}) collective-permute-start(f16[64,1024]{1,0:T(8,128)(2,1)S(1)} %fusion.4), channel_id=1, source_target_pairs={{0,96},{1,97},{2,98},{3,99},{4,100},{5,101},{6,102},{7,103},{8,104... | collective-permute-start | bytes 393224 | tf_op jit(solution)/shard_map/ppermute | solution.py:148
  29.9 0.7 collective-permute-start.2
  30.6 0.0 collective-permute-done.1
  30.6 0.0 collective-permute-done
  30.6 1.4 %pad_maximum_fusion.p_ref = f32[72,17,256]{2,1,0:T(8,128)} fusion(f32[4,17,256]{2,1,0:T(8,128)S(1)} %collective-permute-done.1, f32[64,1,256]{2,1,0:T(1,128)S(1)} %broadcast_in_dim_squeeze.4, f32[64,16,256]{2,1,0:T(8,128)S(1)} %bitcast.42, f32[4,17,256]{2,1,0:T(8,128)S(1)} %collective-permute-done), kind=kLoop, calls=%fused_computation.6 | loop fusion | flops 940032 | bytes 2506752 | tf_op jit(solution)/shard_map/concatenate | solution.py:83
  32.0 6.4 %shard_map.68 = f32[64,16,256]{2,1,0:T(8,128)S(1)} custom-call(s32[2]{0:T(128)} %pad_add_fusion.bounds_ref, f32[72,17,256]{2,1,0:T(8,128)} %pad_maximum_fusion.p_ref), custom_call_target="tpu_custom_call" | custom-call | tf_op jit(solution)/shard_map/pallas_call | solution.py:87
  38.4 0.0 collective-permute-done.4
  38.4 0.0 collective-permute-done.3
  38.4 0.0 collective-permute-done.2
  38.4 0.1 add_select_fusion
  38.5 0.1 reshape.120
  38.7 0.1 conditional.3
  38.7 0.1 broadcast_in_dim.18
  38.9 14.3 %all_to_all.15 = bf16[4,64,4,256]{3,2,1,0:T(4,128)(2,1)S(1)} all-to-all(bf16[4,64,4,256]{3,2,1,0:T(4,128)(2,1)S(1)} %broadcast_in_dim.18), channel_id=1, replica_groups=mesh['comp'=4,'band'=32] {'comp'}, dimensions={0} | all-to-all | bytes 1048576 | tf_op jit(solution)/shard_map/all_to_all | solution.py:165
  53.3 0.3 convolution_convert_fusion.2
  53.5 0.8 %reshape.121 = bf16[32,4,1024]{2,1,0:T(4,128)(2,1)} reshape(bf16[128,1024]{1,0:T(8,128)(2,1)S(1)} %convolution_convert_fusion.2) | data formatting | bytes 524288 | tf_op jit(solution)/shard_map/reshape | solution.py:169
  54.3 7.7 %all-to-all-start.2 = ((bf16[32,4,1024]{2,1,0:T(4,128)(2,1)}), bf16[32,4,1024]{2,1,0:T(4,128)(2,1)S(1)}, u32[]{:S(2)}, u32[]{:S(2)}) async-start(bf16[32,4,1024]{2,1,0:T(4,128)(2,1)} %reshape.121), calls=%async_computation.2 | async-start | bytes 524288 | tf_op jit(solution)/shard_map/all_to_all | solution.py:170
  62.0 0.1 copy.30
  62.1 0.1 fusion.10
  62.2 0.0 copy-start.1
  62.2 8.7 %all-to-all-done.2 = bf16[32,4,1024]{2,1,0:T(4,128)(2,1)S(1)} async-done(((bf16[32,4,1024]{2,1,0:T(4,128)(2,1)}), bf16[32,4,1024]{2,1,0:T(4,128)(2,1)S(1)}, u32[]{:S(2)}, u32[]{:S(2)}) %all-to-all-start.2) | async-done | bytes 262176 | tf_op jit(solution)/shard_map/all_to_all | solution.py:170
  70.9 0.2 fusion.3
  71.1 0.1 reshape.122
  71.2 0.7 %select_bitcast_fusion = bf16[1,64,4,256]{3,2,1,0:T(4,128)(2,1)} fusion(bf16[64,4,256]{2,1,0:T(4,128)(2,1)S(1)} %get-tuple-element.44, bf16[64,4,256]{2,1,0:T(4,128)(2,1)S(1)} %reshape.122, pred[]{:T(512)S(6)} %eq.62), kind=kLoop, calls=%fused_computation.23 | loop fusion | flops 65536 | bytes 393217 | tf_op jit(solution)/shard_map/broadcast_in_dim | solution.py:176
  71.9 0.0 copy-done.1
  (8 shorter events, 0.2 us)
Async XLA Ops:
  7.7 10.2 %copy-start.2 = (f32[1,64,256]{2,1,0:T(8,128)S(1)}, f32[1,64,256]{2,1,0:T(8,128)}, u32[]{:S(2)}) copy-start(f32[1,64,256]{2,1,0:T(8,128)} %param.12) | copy-start | bytes 196612
  7.7 10.3 %copy-start = (f32[1,64,16,256]{3,2,1,0:T(8,128)S(1)}, f32[1,64,16,256]{3,2,1,0:T(8,128)}, u32[]{:S(2)}) copy-start(f32[1,64,16,256]{3,2,1,0:T(8,128)} %param.11) | copy-start | bytes 3145732
  9.3 17.8 %all-to-all-start = ((f16[32,4,1152]{2,1,0:T(4,128)(2,1)}), f16[32,4,1152]{2,1,0:T(4,128)(2,1)S(1)}, u32[]{:S(2)}, u32[]{:S(2)}) async-start(f16[32,4,1152]{2,1,0:T(4,128)(2,1)} %copy.17), calls=%async_computation | async-start | bytes 589824 | tf_op jit(solution)/shard_map/all_to_all | solution.py:139
  18.0 12.5 %collective-permute-start.1 = (f32[4,17,256]{2,1,0:T(8,128)S(1)}, f32[4,17,256]{2,1,0:T(8,128)S(1)}, u32[]{:S(2)}, u32[]{:S(2)}) collective-permute-start(f32[4,17,256]{2,1,0:T(8,128)S(1)} %get-tuple-element.40), channel_id=1, source_target_pairs={{1,0},{2,1},{3,2},{4,3},{5,4},{6,5},{7,6},{8,7},{9,8},{10,9},{11,1... | collective-permute-start | bytes 208904 | tf_op jit(solution)/shard_map/ppermute | solution.py:82
  20.2 10.4 %collective-permute-start = (f32[4,17,256]{2,1,0:T(8,128)S(1)}, f32[4,17,256]{2,1,0:T(8,128)S(1)}, u32[]{:S(2)}, u32[]{:S(2)}) collective-permute-start(f32[4,17,256]{2,1,0:T(8,128)S(1)} %get-tuple-element.39), channel_id=1, source_target_pairs={{0,1},{1,2},{2,3},{3,4},{4,5},{5,6},{6,7},{7,8},{8,9},{9,10},{10,1... | collective-permute-start | bytes 208904 | tf_op jit(solution)/shard_map/ppermute | solution.py:81
  27.7 10.7 %collective-permute-start.4 = (f16[64,1024]{1,0:T(8,128)(2,1)S(1)}, f16[64,1024]{1,0:T(8,128)(2,1)S(1)}, u32[]{:S(2)}, u32[]{:S(2)}) collective-permute-start(f16[64,1024]{1,0:T(8,128)(2,1)S(1)} %fusion.4), channel_id=1, source_target_pairs={{32,96},{33,97},{34,98},{35,99},{36,100},{37,101},{38,102},{39,103... | collective-permute-start | bytes 393224 | tf_op jit(solution)/shard_map/ppermute | solution.py:148
  28.4 10.0 %collective-permute-start.3 = (f16[64,1024]{1,0:T(8,128)(2,1)S(1)}, f16[64,1024]{1,0:T(8,128)(2,1)S(1)}, u32[]{:S(2)}, u32[]{:S(2)}) collective-permute-start(f16[64,1024]{1,0:T(8,128)(2,1)S(1)} %fusion.4), channel_id=1, source_target_pairs={{0,96},{1,97},{2,98},{3,99},{4,100},{5,101},{6,102},{7,103},{8,104... | collective-permute-start | bytes 393224 | tf_op jit(solution)/shard_map/ppermute | solution.py:148
  29.9 8.5 %collective-permute-start.2 = (f16[64,1024]{1,0:T(8,128)(2,1)S(1)}, f16[64,1024]{1,0:T(8,128)(2,1)S(1)}, u32[]{:S(2)}, u32[]{:S(2)}) collective-permute-start(f16[64,1024]{1,0:T(8,128)(2,1)S(1)} %fusion.4), channel_id=1, source_target_pairs={{64,96},{65,97},{66,98},{67,99},{68,100},{69,101},{70,102},{71,103... | collective-permute-start | bytes 393224 | tf_op jit(solution)/shard_map/ppermute | solution.py:148
  54.3 16.5 %all-to-all-start.2 = ((bf16[32,4,1024]{2,1,0:T(4,128)(2,1)}), bf16[32,4,1024]{2,1,0:T(4,128)(2,1)S(1)}, u32[]{:S(2)}, u32[]{:S(2)}) async-start(bf16[32,4,1024]{2,1,0:T(4,128)(2,1)} %reshape.121), calls=%async_computation.2 | async-start | bytes 524288 | tf_op jit(solution)/shard_map/all_to_all | solution.py:170
  62.2 9.7 %copy-start.1 = (f32[1,64,16,256]{3,2,1,0:T(8,128)}, f32[1,64,16,256]{3,2,1,0:T(8,128)S(1)}, u32[]{:S(2)}) copy-start(f32[1,64,16,256]{3,2,1,0:T(8,128)S(1)} %fusion.10) | copy-start | bytes 3145732

commit v15 on v13

--- a/solution.py
+++ b/solution.py
@@ -120,13 +120,10 @@
         jnp.float32
     )
     positions = jnp.arange(rows, dtype=jnp.int32)
-    earlier_mask = (positions[:, None] > positions[None, :]).astype(jnp.float32)
-    earlier = jnp.dot(
-        earlier_mask.astype(jnp.bfloat16),
-        dest_onehot.astype(jnp.bfloat16),
-        preferred_element_type=jnp.float32,
+    same_earlier = (destination[:, None] == destination[None, :]) & (
+        positions[:, None] > positions[None, :]
     )
-    slot_rank = jnp.sum(earlier * dest_onehot, axis=1).astype(jnp.int32)
+    slot_rank = jnp.sum(same_earlier.astype(jnp.int32), axis=1)
     slot_onehot = (slot_rank[:, None] == jnp.arange(CAP, dtype=jnp.int32)[None, :]).astype(
         jnp.float32
     )

time: 66.8 us -> 66.9 us (level)
  other arithmetic: 4.39 us -> 5.29 us
  matrix products: 7.09 us -> 6.23 us
    reduce_sum x0 -> x1, other arithmetic: none -> 0.91 us  [body(): slot_rank = jnp.sum(same_earlier.astype(jnp.int32), axis=1)]
    dot_general x1 -> x0, matrix products: 0.87 us -> none  [body(): jnp.dot(earlier_mask.astype(jnp.bfloat16), dest_onehot.astype(jnp.bfloat1...]
where the time goes in v15:
time: 66.9 us; the launch traced here: 66.4 us
  starting transfers between devices  25.8 us (39%)
  waiting for transfers between devices  19.3 us (29%)
  Pallas kernels  6.45 us (10%)
  matrix products  6.23 us (9%)
  other arithmetic  5.29 us (8%)
  local copies, waits for them, and re-layouts  2.32 us (3%)
  between operations  0.95 us (1%)
    all_to_all x1, waiting for transfers between devices, body(): came_back = lax.all_to_all(reply, 'band', 0, 0, tiled=True)  8.66 us
    all_to_all x1, starting transfers between devices, body(): received = lax.all_to_all(sending, 'band', 0, 0, tiled=True)  8.58 us
    ppermute x3, waiting for transfers between devices, body(): ocean_rows = ocean_rows + lax.ppermute(returned, 'comp', [(last, target)])  7.71 us
    pallas_call x1, Pallas kernels, diffuse(): pl.pallas_call(_diffusion_kernel, out_shape=jax.ShapeDtypeStruct((rows, l...  6.45 us
    all_to_all x1, starting transfers between devices, body(): came_back = lax.all_to_all(reply, 'band', 0, 0, tiled=True)  6.15 us
    dot_general x1, matrix products, body(): jnp.einsum('rfc,rcd->rfd', surface_layers, weights_local, preferred_eleme...  4.76 us
    ppermute x1, starting transfers between devices, diffuse(): above = lax.ppermute(comb[rows - halo:], 'band', forward)  3.42 us
    all_to_all x1, waiting for transfers between devices, body(): received = lax.all_to_all(sending, 'band', 0, 0, tiled=True)  2.95 us
  transfers between devices with their start and end apart: 10, of which 3 were waited for; matrix products, arithmetic and copies ran while one was open for 4% of the time, Pallas kernels for 10%

profile of v15, /device:TPU:1, one launch (start us, length us, event | category | flops | bytes accessed | tf_op | source)
XLA Modules:
  0.0 66.4 jit_solution(13599404760102975183)
XLA Ops:
  0.6 0.9 %convert_reduce_fusion.1 = s32[64]{0:T(128)S(1)} fusion(s32[64]{0:T(128)} %bitcast.55), kind=kLoop, calls=%fused_computation.34 | loop fusion | flops 20416 | bytes 512 | tf_op jit(solution)/shard_map/reduce_sum | solution.py:126
  1.5 0.7 %fusion.16 = f32[64,32]{0,1:T(8,128)S(1)} fusion(s32[64]{0:T(128)} %bitcast.56), kind=kLoop, calls=%fused_computation.38 | loop fusion | flops 4096 | bytes 8448 | tf_op jit(solution)/shard_map/convert_element_type | solution.py:119
  2.2 0.7 convert_bitcast_fusion
  2.9 4.8 %conditional.2 = (f32[64,1024]{1,0:T(8,128)S(1)}) conditional(s32[]{:T(128)} %convert_element_type.84, (f32[1,64,16,256]{3,2,1,0:T(8,128)}, bf16[64,256,256]{2,1,0:T(8,128)(2,1)}) %tuple.37, () %tuple.27), branch_computations={%region_1.0_spmd, %region_2.0_spmd} | conditional | flops 33554432 | bytes 9306120 | solution.py:110
  2.9 4.8 %fusion.1 = f32[64,4,256]{2,1,0:T(4,128)S(1)} fusion(bf16[64,256,256]{2,1,0:T(8,128)(2,1)} %get-tuple-element.33, f32[1,64,16,256]{3,2,1,0:T(8,128)} %get-tuple-element.32), kind=kOutput, calls=%fused_computation.2 | convolution fusion | flops 33554432 | bytes 8781824 | tf_op jit(solution)/shard_map/cond/branch_0_fun/rfc,rcd->rfd/dot_general | solution.py:113
  7.7 0.1 copy.24
  7.7 0.0 copy-start.2
  7.8 0.0 copy-start
  7.8 0.1 broadcast_in_dim.12
  7.8 0.6 convolution_convert_fusion.1
  8.5 0.9 %copy.21 = f16[32,4,1152]{2,1,0:T(4,128)(2,1)} copy(f16[32,4,1152]{2,0,1:T(8,128)(2,1)S(1)} %convolution_convert_fusion.1) | data formatting | bytes 589824 | tf_op jit(solution)/shard_map/convert_element_type | solution.py:135
  9.4 8.6 %all-to-all-start = ((f16[32,4,1152]{2,1,0:T(4,128)(2,1)}), f16[32,4,1152]{2,1,0:T(4,128)(2,1)S(1)}, u32[]{:S(2)}, u32[]{:S(2)}) async-start(f16[32,4,1152]{2,1,0:T(4,128)(2,1)} %copy.21), calls=%async_computation | async-start | bytes 589824 | tf_op jit(solution)/shard_map/all_to_all | solution.py:136
  18.1 2.1 %collective-permute-start.1 = (f32[4,17,256]{2,1,0:T(8,128)S(1)}, f32[4,17,256]{2,1,0:T(8,128)S(1)}, u32[]{:S(2)}, u32[]{:S(2)}) collective-permute-start(f32[4,17,256]{2,1,0:T(8,128)S(1)} %get-tuple-element.40), channel_id=1, source_target_pairs={{1,0},{2,1},{3,2},{4,3},{5,4},{6,5},{7,6},{8,7},{9,8},{10,9},{11,1... | collective-permute-start | bytes 208904 | tf_op jit(solution)/shard_map/ppermute | solution.py:82
  20.2 3.4 %collective-permute-start = (f32[4,17,256]{2,1,0:T(8,128)S(1)}, f32[4,17,256]{2,1,0:T(8,128)S(1)}, u32[]{:S(2)}, u32[]{:S(2)}) collective-permute-start(f32[4,17,256]{2,1,0:T(8,128)S(1)} %get-tuple-element.39), channel_id=1, source_target_pairs={{0,1},{1,2},{2,3},{3,4},{4,5},{5,6},{6,7},{7,8},{8,9},{9,10},{10,1... | collective-permute-start | bytes 208904 | tf_op jit(solution)/shard_map/ppermute | solution.py:81
  23.6 0.6 pad_add_fusion.bounds_ref
  24.2 2.9 %all-to-all-done = f16[32,4,1152]{2,1,0:T(4,128)(2,1)S(1)} async-done(((f16[32,4,1152]{2,1,0:T(4,128)(2,1)}), f16[32,4,1152]{2,1,0:T(4,128)(2,1)S(1)}, u32[]{:S(2)}, u32[]{:S(2)}) %all-to-all-start) | async-done | bytes 294944 | tf_op jit(solution)/shard_map/all_to_all | solution.py:136
  27.2 0.1 reshape.119
  27.3 0.1 convert_reduce_fusion
  27.4 0.4 fusion.4
  27.7 0.7 %collective-permute-start.4 = (f16[64,1024]{1,0:T(8,128)(2,1)S(1)}, f16[64,1024]{1,0:T(8,128)(2,1)S(1)}, u32[]{:S(2)}, u32[]{:S(2)}) collective-permute-start(f16[64,1024]{1,0:T(8,128)(2,1)S(1)} %fusion.4), channel_id=1, source_target_pairs={{32,96},{33,97},{34,98},{35,99},{36,100},{37,101},{38,102},{39,103... | collective-permute-start | bytes 393224 | tf_op jit(solution)/shard_map/ppermute | solution.py:145
  28.4 1.5 %collective-permute-start.3 = (f16[64,1024]{1,0:T(8,128)(2,1)S(1)}, f16[64,1024]{1,0:T(8,128)(2,1)S(1)}, u32[]{:S(2)}, u32[]{:S(2)}) collective-permute-start(f16[64,1024]{1,0:T(8,128)(2,1)S(1)} %fusion.4), channel_id=1, source_target_pairs={{0,96},{1,97},{2,98},{3,99},{4,100},{5,101},{6,102},{7,103},{8,104... | collective-permute-start | bytes 393224 | tf_op jit(solution)/shard_map/ppermute | solution.py:145
  29.9 0.7 %collective-permute-start.2 = (f16[64,1024]{1,0:T(8,128)(2,1)S(1)}, f16[64,1024]{1,0:T(8,128)(2,1)S(1)}, u32[]{:S(2)}, u32[]{:S(2)}) collective-permute-start(f16[64,1024]{1,0:T(8,128)(2,1)S(1)} %fusion.4), channel_id=1, source_target_pairs={{64,96},{65,97},{66,98},{67,99},{68,100},{69,101},{70,102},{71,103... | collective-permute-start | bytes 393224 | tf_op jit(solution)/shard_map/ppermute | solution.py:145
  30.6 0.0 collective-permute-done.1
  30.6 0.0 collective-permute-done
  30.6 1.4 %pad_maximum_fusion.p_ref = f32[72,17,256]{2,1,0:T(8,128)} fusion(f32[4,17,256]{2,1,0:T(8,128)S(1)} %collective-permute-done.1, f32[64,1,256]{2,1,0:T(1,128)S(1)} %broadcast_in_dim_squeeze.2, f32[64,16,256]{2,1,0:T(8,128)S(1)} %bitcast.46, f32[4,17,256]{2,1,0:T(8,128)S(1)} %collective-permute-done), kind=kLoop, calls=%fused_computation.6 | loop fusion | flops 940032 | bytes 2506752 | tf_op jit(solution)/shard_map/concatenate | solution.py:83
  32.0 6.4 %shard_map.68 = f32[64,16,256]{2,1,0:T(8,128)S(1)} custom-call(s32[2]{0:T(128)} %pad_add_fusion.bounds_ref, f32[72,17,256]{2,1,0:T(8,128)} %pad_maximum_fusion.p_ref), custom_call_target="tpu_custom_call" | custom-call | tf_op jit(solution)/shard_map/pallas_call | solution.py:87
  38.5 0.0 collective-permute-done.4
  38.5 0.0 collective-permute-done.3
  38.5 0.0 collective-permute-done.2
  38.5 0.1 add_select_fusion
  38.6 0.1 reshape.120
  38.7 0.1 conditional.3
  38.8 0.7 %collective-permute-start.7 = (bf16[64,4,256]{2,1,0:T(4,128)(2,1)S(1)}, bf16[64,4,256]{2,1,0:T(4,128)(2,1)S(1)}, u32[]{:S(2)}, u32[]{:S(2)}) collective-permute-start(bf16[64,4,256]{2,1,0:T(4,128)(2,1)S(1)} %get-tuple-element.44), channel_id=1, source_target_pairs={{96,32},{97,33},{98,34},{99,35},{100,36},{101,37},{102,38},{103,39... | collective-permute-start | bytes 393224 | tf_op jit(solution)/shard_map/ppermute | solution.py:163
  39.5 1.3 %collective-permute-start.6 = (bf16[64,4,256]{2,1,0:T(4,128)(2,1)S(1)}, bf16[64,4,256]{2,1,0:T(4,128)(2,1)S(1)}, u32[]{:S(2)}, u32[]{:S(2)}) collective-permute-start(bf16[64,4,256]{2,1,0:T(4,128)(2,1)S(1)} %get-tuple-element.44), channel_id=1, source_target_pairs={{96,0},{97,1},{98,2},{99,3},{100,4},{101,5},{102,6},{103,7},{104,8... | collective-permute-start | bytes 393224 | tf_op jit(solution)/shard_map/ppermute | solution.py:163
  40.8 0.7 %collective-permute-start.5 = (bf16[64,4,256]{2,1,0:T(4,128)(2,1)S(1)}, bf16[64,4,256]{2,1,0:T(4,128)(2,1)S(1)}, u32[]{:S(2)}, u32[]{:S(2)}) collective-permute-start(bf16[64,4,256]{2,1,0:T(4,128)(2,1)S(1)} %get-tuple-element.44), channel_id=1, source_target_pairs={{96,64},{97,65},{98,66},{99,67},{100,68},{101,69},{102,70},{103,71... | collective-permute-start | bytes 393224 | tf_op jit(solution)/shard_map/ppermute | solution.py:163
  41.4 0.0 collective-permute-done.7
  41.4 7.7 %collective-permute-done.6 = bf16[64,4,256]{2,1,0:T(4,128)(2,1)S(1)} collective-permute-done((bf16[64,4,256]{2,1,0:T(4,128)(2,1)S(1)}, bf16[64,4,256]{2,1,0:T(4,128)(2,1)S(1)}, u32[]{:S(2)}, u32[]{:S(2)}) %collective-permute-start.6) | collective-permute-done | bytes 131104 | tf_op jit(solution)/shard_map/ppermute | solution.py:163
  49.1 0.0 collective-permute-done.5
  49.2 0.3 convolution_convert_fusion.2
  49.5 0.8 %reshape.122 = bf16[32,4,1024]{2,1,0:T(4,128)(2,1)} reshape(bf16[128,1024]{1,0:T(8,128)(2,1)S(1)} %convolution_convert_fusion.2) | data formatting | bytes 524288 | tf_op jit(solution)/shard_map/reshape | solution.py:168
  50.3 6.2 %all-to-all-start.1 = ((bf16[32,4,1024]{2,1,0:T(4,128)(2,1)}), bf16[32,4,1024]{2,1,0:T(4,128)(2,1)S(1)}, u32[]{:S(2)}, u32[]{:S(2)}) async-start(bf16[32,4,1024]{2,1,0:T(4,128)(2,1)} %reshape.122), calls=%async_computation.1 | async-start | bytes 524288 | tf_op jit(solution)/shard_map/all_to_all | solution.py:169
  56.5 0.1 copy.34
  56.5 0.1 fusion.9
  56.7 0.0 copy-start.1
  56.7 8.7 %all-to-all-done.1 = bf16[32,4,1024]{2,1,0:T(4,128)(2,1)S(1)} async-done(((bf16[32,4,1024]{2,1,0:T(4,128)(2,1)}), bf16[32,4,1024]{2,1,0:T(4,128)(2,1)S(1)}, u32[]{:S(2)}, u32[]{:S(2)}) %all-to-all-start.1) | async-done | bytes 262176 | tf_op jit(solution)/shard_map/all_to_all | solution.py:169
  65.3 0.2 fusion.3
  65.6 0.1 reshape.123
  65.6 0.7 %select_bitcast_fusion = bf16[1,64,4,256]{3,2,1,0:T(4,128)(2,1)} fusion(bf16[64,4,256]{2,1,0:T(4,128)(2,1)S(1)} %get-tuple-element.44, bf16[64,4,256]{2,1,0:T(4,128)(2,1)S(1)} %reshape.123, pred[]{:T(512)S(6)} %eq.75), kind=kLoop, calls=%fused_computation.21 | loop fusion | flops 65536 | bytes 393217 | tf_op jit(solution)/shard_map/broadcast_in_dim | solution.py:175
  (10 shorter events, 0.2 us)
Async XLA Ops:
  7.7 10.2 %copy-start.2 = (f32[1,64,256]{2,1,0:T(8,128)S(1)}, f32[1,64,256]{2,1,0:T(8,128)}, u32[]{:S(2)}) copy-start(f32[1,64,256]{2,1,0:T(8,128)} %param.12) | copy-start | bytes 196612
  7.8 10.3 %copy-start = (f32[1,64,16,256]{3,2,1,0:T(8,128)S(1)}, f32[1,64,16,256]{3,2,1,0:T(8,128)}, u32[]{:S(2)}) copy-start(f32[1,64,16,256]{3,2,1,0:T(8,128)} %param.11) | copy-start | bytes 3145732
  9.4 17.8 %all-to-all-start = ((f16[32,4,1152]{2,1,0:T(4,128)(2,1)}), f16[32,4,1152]{2,1,0:T(4,128)(2,1)S(1)}, u32[]{:S(2)}, u32[]{:S(2)}) async-start(f16[32,4,1152]{2,1,0:T(4,128)(2,1)} %copy.21), calls=%async_computation | async-start | bytes 589824 | tf_op jit(solution)/shard_map/all_to_all | solution.py:136
  18.1 12.5 %collective-permute-start.1 = (f32[4,17,256]{2,1,0:T(8,128)S(1)}, f32[4,17,256]{2,1,0:T(8,128)S(1)}, u32[]{:S(2)}, u32[]{:S(2)}) collective-permute-start(f32[4,17,256]{2,1,0:T(8,128)S(1)} %get-tuple-element.40), channel_id=1, source_target_pairs={{1,0},{2,1},{3,2},{4,3},{5,4},{6,5},{7,6},{8,7},{9,8},{10,9},{11,1... | collective-permute-start | bytes 208904 | tf_op jit(solution)/shard_map/ppermute | solution.py:82
  20.2 10.4 %collective-permute-start = (f32[4,17,256]{2,1,0:T(8,128)S(1)}, f32[4,17,256]{2,1,0:T(8,128)S(1)}, u32[]{:S(2)}, u32[]{:S(2)}) collective-permute-start(f32[4,17,256]{2,1,0:T(8,128)S(1)} %get-tuple-element.39), channel_id=1, source_target_pairs={{0,1},{1,2},{2,3},{3,4},{4,5},{5,6},{6,7},{7,8},{8,9},{9,10},{10,1... | collective-permute-start | bytes 208904 | tf_op jit(solution)/shard_map/ppermute | solution.py:81
  27.7 10.7 %collective-permute-start.4 = (f16[64,1024]{1,0:T(8,128)(2,1)S(1)}, f16[64,1024]{1,0:T(8,128)(2,1)S(1)}, u32[]{:S(2)}, u32[]{:S(2)}) collective-permute-start(f16[64,1024]{1,0:T(8,128)(2,1)S(1)} %fusion.4), channel_id=1, source_target_pairs={{32,96},{33,97},{34,98},{35,99},{36,100},{37,101},{38,102},{39,103... | collective-permute-start | bytes 393224 | tf_op jit(solution)/shard_map/ppermute | solution.py:145
  28.4 10.1 %collective-permute-start.3 = (f16[64,1024]{1,0:T(8,128)(2,1)S(1)}, f16[64,1024]{1,0:T(8,128)(2,1)S(1)}, u32[]{:S(2)}, u32[]{:S(2)}) collective-permute-start(f16[64,1024]{1,0:T(8,128)(2,1)S(1)} %fusion.4), channel_id=1, source_target_pairs={{0,96},{1,97},{2,98},{3,99},{4,100},{5,101},{6,102},{7,103},{8,104... | collective-permute-start | bytes 393224 | tf_op jit(solution)/shard_map/ppermute | solution.py:145
  29.9 8.6 %collective-permute-start.2 = (f16[64,1024]{1,0:T(8,128)(2,1)S(1)}, f16[64,1024]{1,0:T(8,128)(2,1)S(1)}, u32[]{:S(2)}, u32[]{:S(2)}) collective-permute-start(f16[64,1024]{1,0:T(8,128)(2,1)S(1)} %fusion.4), channel_id=1, source_target_pairs={{64,96},{65,97},{66,98},{67,99},{68,100},{69,101},{70,102},{71,103... | collective-permute-start | bytes 393224 | tf_op jit(solution)/shard_map/ppermute | solution.py:145
  38.8 2.7 %collective-permute-start.7 = (bf16[64,4,256]{2,1,0:T(4,128)(2,1)S(1)}, bf16[64,4,256]{2,1,0:T(4,128)(2,1)S(1)}, u32[]{:S(2)}, u32[]{:S(2)}) collective-permute-start(bf16[64,4,256]{2,1,0:T(4,128)(2,1)S(1)} %get-tuple-element.44), channel_id=1, source_target_pairs={{96,32},{97,33},{98,34},{99,35},{100,36},{101,37},{102,38},{103,39... | collective-permute-start | bytes 393224 | tf_op jit(solution)/shard_map/ppermute | solution.py:163
  39.5 9.7 %collective-permute-start.6 = (bf16[64,4,256]{2,1,0:T(4,128)(2,1)S(1)}, bf16[64,4,256]{2,1,0:T(4,128)(2,1)S(1)}, u32[]{:S(2)}, u32[]{:S(2)}) collective-permute-start(bf16[64,4,256]{2,1,0:T(4,128)(2,1)S(1)} %get-tuple-element.44), channel_id=1, source_target_pairs={{96,0},{97,1},{98,2},{99,3},{100,4},{101,5},{102,6},{103,7},{104,8... | collective-permute-start | bytes 393224 | tf_op jit(solution)/shard_map/ppermute | solution.py:163
  40.8 8.4 %collective-permute-start.5 = (bf16[64,4,256]{2,1,0:T(4,128)(2,1)S(1)}, bf16[64,4,256]{2,1,0:T(4,128)(2,1)S(1)}, u32[]{:S(2)}, u32[]{:S(2)}) collective-permute-start(bf16[64,4,256]{2,1,0:T(4,128)(2,1)S(1)} %get-tuple-element.44), channel_id=1, source_target_pairs={{96,64},{97,65},{98,66},{99,67},{100,68},{101,69},{102,70},{103,71... | collective-permute-start | bytes 393224 | tf_op jit(solution)/shard_map/ppermute | solution.py:163
  50.3 15.0 %all-to-all-start.1 = ((bf16[32,4,1024]{2,1,0:T(4,128)(2,1)}), bf16[32,4,1024]{2,1,0:T(4,128)(2,1)S(1)}, u32[]{:S(2)}, u32[]{:S(2)}) async-start(bf16[32,4,1024]{2,1,0:T(4,128)(2,1)} %reshape.122), calls=%async_computation.1 | async-start | bytes 524288 | tf_op jit(solution)/shard_map/all_to_all | solution.py:169
  56.7 9.7 %copy-start.1 = (f32[1,64,16,256]{3,2,1,0:T(8,128)}, f32[1,64,16,256]{3,2,1,0:T(8,128)S(1)}, u32[]{:S(2)}) copy-start(f32[1,64,16,256]{3,2,1,0:T(8,128)S(1)} %fusion.9) | copy-start | bytes 3145732

commit v16 on v13

--- a/solution.py
+++ b/solution.py
@@ -162,7 +162,7 @@
     )
 
     ocean_rows = returned
-    for target in sorted(range(last), key=lambda t: (t + 1) % last):
+    for target in sorted(range(last), reverse=True):
         ocean_rows = ocean_rows + lax.ppermute(returned, "comp", [(last, target)])
     ocean_rows = ocean_rows.reshape(rows, width)
     reply = jnp.einsum(

time: 66.8 us -> 66.4 us (level)
  the two profiles are of different devices: /device:TPU:1 before, /device:TPU:65 now
where the time goes in v16:
time: 66.4 us; the launch traced here: 65.9 us
  starting transfers between devices  24.7 us (37%)
  waiting for transfers between devices  19.9 us (30%)
  matrix products  7.1 us (11%)
  Pallas kernels  6.45 us (10%)
  other arithmetic  4.38 us (7%)
  local copies, waits for them, and re-layouts  2.32 us (3%)
  between operations  0.95 us (1%)
    all_to_all x1, waiting for transfers between devices, body(): came_back = lax.all_to_all(reply, 'band', 0, 0, tiled=True)  8.66 us
    ppermute x3, waiting for transfers between devices, body(): ocean_rows = ocean_rows + lax.ppermute(returned, 'comp', [(last, target)])  8.3 us
    all_to_all x1, starting transfers between devices, body(): received = lax.all_to_all(sending, 'band', 0, 0, tiled=True)  7.76 us
    pallas_call x1, Pallas kernels, diffuse(): pl.pallas_call(_diffusion_kernel, out_shape=jax.ShapeDtypeStruct((rows, l...  6.45 us
    all_to_all x1, starting transfers between devices, body(): came_back = lax.all_to_all(reply, 'band', 0, 0, tiled=True)  6.15 us
    dot_general x1, matrix products, body(): jnp.einsum('rfc,rcd->rfd', surface_layers, weights_local, preferred_eleme...  4.76 us
    ppermute x1, starting transfers between devices, diffuse(): above = lax.ppermute(comb[rows - halo:], 'band', forward)  3.42 us
    all_to_all x1, waiting for transfers between devices, body(): received = lax.all_to_all(sending, 'band', 0, 0, tiled=True)  2.95 us
  transfers between devices with their start and end apart: 10, of which 3 were waited for; matrix products, arithmetic and copies ran while one was open for 4% of the time, Pallas kernels for 10%

profile of v16, /device:TPU:65, one launch (start us, length us, event | category | flops | bytes accessed | tf_op | source)
XLA Modules:
  0.0 65.9 jit_solution(17189487639528398356)
XLA Ops:
  0.6 0.9 %fusion.5 = f32[64]{0:T(128)S(1)} fusion(s32[64]{0:T(128)} %bitcast.55), kind=kOutput, calls=%fused_computation.13 | convolution fusion | flops 286656 | bytes 512 | tf_op jit(solution)/shard_map/dot_general | solution.py:124
  1.5 0.7 %fusion.16 = f32[64,32]{0,1:T(8,128)S(1)} fusion(s32[64]{0:T(128)} %bitcast.56), kind=kLoop, calls=%fused_computation.39 | loop fusion | flops 4096 | bytes 8448 | tf_op jit(solution)/shard_map/convert_element_type | solution.py:119
  2.2 0.7 convert_bitcast_fusion
  2.9 4.8 %conditional.2 = (f32[64,1024]{1,0:T(8,128)S(1)}) conditional(s32[]{:T(128)} %convert_element_type.100, (f32[1,64,16,256]{3,2,1,0:T(8,128)}, bf16[64,256,256]{2,1,0:T(8,128)(2,1)}) %tuple.37, () %tuple.27), branch_computations={%region_1.0_spmd, %region_2.0_spmd} | conditional | flops 33554432 | bytes 9306120 | solution.py:110
  2.9 4.8 %fusion.1 = f32[64,4,256]{2,1,0:T(4,128)S(1)} fusion(bf16[64,256,256]{2,1,0:T(8,128)(2,1)} %get-tuple-element.33, f32[1,64,16,256]{3,2,1,0:T(8,128)} %get-tuple-element.32), kind=kOutput, calls=%fused_computation.2 | convolution fusion | flops 33554432 | bytes 8781824 | tf_op jit(solution)/shard_map/cond/branch_0_fun/rfc,rcd->rfd/dot_general | solution.py:113
  7.6 0.1 copy.20
  7.7 0.0 copy-start.2
  7.7 0.0 copy-start
  7.7 0.1 broadcast_in_dim.12
  7.8 0.6 convolution_convert_fusion.1
  8.4 0.9 %copy.17 = f16[32,4,1152]{2,1,0:T(4,128)(2,1)} copy(f16[32,4,1152]{2,0,1:T(8,128)(2,1)S(1)} %convolution_convert_fusion.1) | data formatting | bytes 589824 | tf_op jit(solution)/shard_map/convert_element_type | solution.py:138
  9.3 7.8 %all-to-all-start = ((f16[32,4,1152]{2,1,0:T(4,128)(2,1)}), f16[32,4,1152]{2,1,0:T(4,128)(2,1)S(1)}, u32[]{:S(2)}, u32[]{:S(2)}) async-start(f16[32,4,1152]{2,1,0:T(4,128)(2,1)} %copy.17), calls=%async_computation | async-start | bytes 589824 | tf_op jit(solution)/shard_map/all_to_all | solution.py:139
  17.2 2.1 %collective-permute-start.1 = (f32[4,17,256]{2,1,0:T(8,128)S(1)}, f32[4,17,256]{2,1,0:T(8,128)S(1)}, u32[]{:S(2)}, u32[]{:S(2)}) collective-permute-start(f32[4,17,256]{2,1,0:T(8,128)S(1)} %get-tuple-element.40), channel_id=1, source_target_pairs={{1,0},{2,1},{3,2},{4,3},{5,4},{6,5},{7,6},{8,7},{9,8},{10,9},{11,1... | collective-permute-start | bytes 208904 | tf_op jit(solution)/shard_map/ppermute | solution.py:82
  19.4 3.4 %collective-permute-start = (f32[4,17,256]{2,1,0:T(8,128)S(1)}, f32[4,17,256]{2,1,0:T(8,128)S(1)}, u32[]{:S(2)}, u32[]{:S(2)}) collective-permute-start(f32[4,17,256]{2,1,0:T(8,128)S(1)} %get-tuple-element.39), channel_id=1, source_target_pairs={{0,1},{1,2},{2,3},{3,4},{4,5},{5,6},{6,7},{7,8},{8,9},{9,10},{10,1... | collective-permute-start | bytes 208904 | tf_op jit(solution)/shard_map/ppermute | solution.py:81
  22.8 0.6 pad_add_fusion.bounds_ref
  23.4 2.9 %all-to-all-done = f16[32,4,1152]{2,1,0:T(4,128)(2,1)S(1)} async-done(((f16[32,4,1152]{2,1,0:T(4,128)(2,1)}), f16[32,4,1152]{2,1,0:T(4,128)(2,1)S(1)}, u32[]{:S(2)}, u32[]{:S(2)}) %all-to-all-start) | async-done | bytes 294944 | tf_op jit(solution)/shard_map/all_to_all | solution.py:139
  26.3 0.1 reshape.121
  26.4 0.1 convert_reduce_fusion
  26.5 0.4 fusion.4
  26.9 0.7 %collective-permute-start.4 = (f16[64,1024]{1,0:T(8,128)(2,1)S(1)}, f16[64,1024]{1,0:T(8,128)(2,1)S(1)}, u32[]{:S(2)}, u32[]{:S(2)}) collective-permute-start(f16[64,1024]{1,0:T(8,128)(2,1)S(1)} %fusion.4), channel_id=1, source_target_pairs={{32,96},{33,97},{34,98},{35,99},{36,100},{37,101},{38,102},{39,103... | collective-permute-start | bytes 393224 | tf_op jit(solution)/shard_map/ppermute | solution.py:148
  27.6 0.7 %collective-permute-start.3 = (f16[64,1024]{1,0:T(8,128)(2,1)S(1)}, f16[64,1024]{1,0:T(8,128)(2,1)S(1)}, u32[]{:S(2)}, u32[]{:S(2)}) collective-permute-start(f16[64,1024]{1,0:T(8,128)(2,1)S(1)} %fusion.4), channel_id=1, source_target_pairs={{0,96},{1,97},{2,98},{3,99},{4,100},{5,101},{6,102},{7,103},{8,104... | collective-permute-start | bytes 393224 | tf_op jit(solution)/shard_map/ppermute | solution.py:148
  28.2 1.3 %collective-permute-start.2 = (f16[64,1024]{1,0:T(8,128)(2,1)S(1)}, f16[64,1024]{1,0:T(8,128)(2,1)S(1)}, u32[]{:S(2)}, u32[]{:S(2)}) collective-permute-start(f16[64,1024]{1,0:T(8,128)(2,1)S(1)} %fusion.4), channel_id=1, source_target_pairs={{64,96},{65,97},{66,98},{67,99},{68,100},{69,101},{70,102},{71,103... | collective-permute-start | bytes 393224 | tf_op jit(solution)/shard_map/ppermute | solution.py:148
  29.5 0.0 collective-permute-done.1
  29.6 0.0 collective-permute-done
  29.6 1.4 %pad_maximum_fusion.p_ref = f32[72,17,256]{2,1,0:T(8,128)} fusion(f32[4,17,256]{2,1,0:T(8,128)S(1)} %collective-permute-done.1, f32[64,1,256]{2,1,0:T(1,128)S(1)} %broadcast_in_dim_squeeze.4, f32[64,16,256]{2,1,0:T(8,128)S(1)} %bitcast.46, f32[4,17,256]{2,1,0:T(8,128)S(1)} %collective-permute-done), kind=kLoop, calls=%fused_computation.6 | loop fusion | flops 940032 | bytes 2506752 | tf_op jit(solution)/shard_map/concatenate | solution.py:83
  31.0 6.4 %shard_map.68 = f32[64,16,256]{2,1,0:T(8,128)S(1)} custom-call(s32[2]{0:T(128)} %pad_add_fusion.bounds_ref, f32[72,17,256]{2,1,0:T(8,128)} %pad_maximum_fusion.p_ref), custom_call_target="tpu_custom_call" | custom-call | tf_op jit(solution)/shard_map/pallas_call | solution.py:87
  37.4 0.0 collective-permute-done.4
  37.4 0.0 collective-permute-done.3
  37.4 0.0 collective-permute-done.2
  37.4 0.1 add_select_fusion
  37.5 0.1 reshape.122
  37.7 0.1 conditional.3
  37.7 0.7 %collective-permute-start.7 = (bf16[64,4,256]{2,1,0:T(4,128)(2,1)S(1)}, bf16[64,4,256]{2,1,0:T(4,128)(2,1)S(1)}, u32[]{:S(2)}, u32[]{:S(2)}) collective-permute-start(bf16[64,4,256]{2,1,0:T(4,128)(2,1)S(1)} %get-tuple-element.44), channel_id=1, source_target_pairs={{96,0},{97,1},{98,2},{99,3},{100,4},{101,5},{102,6},{103,7},{104,8... | collective-permute-start | bytes 393224 | tf_op jit(solution)/shard_map/ppermute | solution.py:166
  38.4 0.7 %collective-permute-start.6 = (bf16[64,4,256]{2,1,0:T(4,128)(2,1)S(1)}, bf16[64,4,256]{2,1,0:T(4,128)(2,1)S(1)}, u32[]{:S(2)}, u32[]{:S(2)}) collective-permute-start(bf16[64,4,256]{2,1,0:T(4,128)(2,1)S(1)} %get-tuple-element.44), channel_id=1, source_target_pairs={{96,32},{97,33},{98,34},{99,35},{100,36},{101,37},{102,38},{103,39... | collective-permute-start | bytes 393224 | tf_op jit(solution)/shard_map/ppermute | solution.py:166
  39.1 1.3 %collective-permute-start.5 = (bf16[64,4,256]{2,1,0:T(4,128)(2,1)S(1)}, bf16[64,4,256]{2,1,0:T(4,128)(2,1)S(1)}, u32[]{:S(2)}, u32[]{:S(2)}) collective-permute-start(bf16[64,4,256]{2,1,0:T(4,128)(2,1)S(1)} %get-tuple-element.44), channel_id=1, source_target_pairs={{96,64},{97,65},{98,66},{99,67},{100,68},{101,69},{102,70},{103,71... | collective-permute-start | bytes 393224 | tf_op jit(solution)/shard_map/ppermute | solution.py:166
  40.4 0.0 collective-permute-done.7
  40.4 0.0 collective-permute-done.6
  40.4 8.3 %collective-permute-done.5 = bf16[64,4,256]{2,1,0:T(4,128)(2,1)S(1)} collective-permute-done((bf16[64,4,256]{2,1,0:T(4,128)(2,1)S(1)}, bf16[64,4,256]{2,1,0:T(4,128)(2,1)S(1)}, u32[]{:S(2)}, u32[]{:S(2)}) %collective-permute-start.5) | collective-permute-done | bytes 131104 | tf_op jit(solution)/shard_map/ppermute | solution.py:166
  48.8 0.3 convolution_convert_fusion.2
  49.0 0.8 %reshape.124 = bf16[32,4,1024]{2,1,0:T(4,128)(2,1)} reshape(bf16[128,1024]{1,0:T(8,128)(2,1)S(1)} %convolution_convert_fusion.2) | data formatting | bytes 524288 | tf_op jit(solution)/shard_map/reshape | solution.py:171
  49.8 6.2 %all-to-all-start.1 = ((bf16[32,4,1024]{2,1,0:T(4,128)(2,1)}), bf16[32,4,1024]{2,1,0:T(4,128)(2,1)S(1)}, u32[]{:S(2)}, u32[]{:S(2)}) async-start(bf16[32,4,1024]{2,1,0:T(4,128)(2,1)} %reshape.124), calls=%async_computation.1 | async-start | bytes 524288 | tf_op jit(solution)/shard_map/all_to_all | solution.py:172
  56.0 0.1 copy.30
  56.1 0.1 fusion.10
  56.2 0.0 copy-start.1
  56.2 8.7 %all-to-all-done.1 = bf16[32,4,1024]{2,1,0:T(4,128)(2,1)S(1)} async-done(((bf16[32,4,1024]{2,1,0:T(4,128)(2,1)}), bf16[32,4,1024]{2,1,0:T(4,128)(2,1)S(1)}, u32[]{:S(2)}, u32[]{:S(2)}) %all-to-all-start.1) | async-done | bytes 262176 | tf_op jit(solution)/shard_map/all_to_all | solution.py:172
  64.9 0.2 fusion.3
  65.1 0.1 reshape.125
  65.2 0.7 %select_bitcast_fusion = bf16[1,64,4,256]{3,2,1,0:T(4,128)(2,1)} fusion(bf16[64,4,256]{2,1,0:T(4,128)(2,1)S(1)} %get-tuple-element.44, bf16[64,4,256]{2,1,0:T(4,128)(2,1)S(1)} %reshape.125, pred[]{:T(512)S(6)} %eq.62), kind=kLoop, calls=%fused_computation.23 | loop fusion | flops 65536 | bytes 393217 | tf_op jit(solution)/shard_map/broadcast_in_dim | solution.py:178
  (11 shorter events, 0.2 us)
Async XLA Ops:
  7.7 9.4 %copy-start.2 = (f32[1,64,256]{2,1,0:T(8,128)S(1)}, f32[1,64,256]{2,1,0:T(8,128)}, u32[]{:S(2)}) copy-start(f32[1,64,256]{2,1,0:T(8,128)} %param.12) | copy-start | bytes 196612
  7.7 9.5 %copy-start = (f32[1,64,16,256]{3,2,1,0:T(8,128)S(1)}, f32[1,64,16,256]{3,2,1,0:T(8,128)}, u32[]{:S(2)}) copy-start(f32[1,64,16,256]{3,2,1,0:T(8,128)} %param.11) | copy-start | bytes 3145732
  9.3 17.0 %all-to-all-start = ((f16[32,4,1152]{2,1,0:T(4,128)(2,1)}), f16[32,4,1152]{2,1,0:T(4,128)(2,1)S(1)}, u32[]{:S(2)}, u32[]{:S(2)}) async-start(f16[32,4,1152]{2,1,0:T(4,128)(2,1)} %copy.17), calls=%async_computation | async-start | bytes 589824 | tf_op jit(solution)/shard_map/all_to_all | solution.py:139
  17.2 12.3 %collective-permute-start.1 = (f32[4,17,256]{2,1,0:T(8,128)S(1)}, f32[4,17,256]{2,1,0:T(8,128)S(1)}, u32[]{:S(2)}, u32[]{:S(2)}) collective-permute-start(f32[4,17,256]{2,1,0:T(8,128)S(1)} %get-tuple-element.40), channel_id=1, source_target_pairs={{1,0},{2,1},{3,2},{4,3},{5,4},{6,5},{7,6},{8,7},{9,8},{10,9},{11,1... | collective-permute-start | bytes 208904 | tf_op jit(solution)/shard_map/ppermute | solution.py:82
  19.4 10.2 %collective-permute-start = (f32[4,17,256]{2,1,0:T(8,128)S(1)}, f32[4,17,256]{2,1,0:T(8,128)S(1)}, u32[]{:S(2)}, u32[]{:S(2)}) collective-permute-start(f32[4,17,256]{2,1,0:T(8,128)S(1)} %get-tuple-element.39), channel_id=1, source_target_pairs={{0,1},{1,2},{2,3},{3,4},{4,5},{5,6},{6,7},{7,8},{8,9},{9,10},{10,1... | collective-permute-start | bytes 208904 | tf_op jit(solution)/shard_map/ppermute | solution.py:81
  26.9 10.5 %collective-permute-start.4 = (f16[64,1024]{1,0:T(8,128)(2,1)S(1)}, f16[64,1024]{1,0:T(8,128)(2,1)S(1)}, u32[]{:S(2)}, u32[]{:S(2)}) collective-permute-start(f16[64,1024]{1,0:T(8,128)(2,1)S(1)} %fusion.4), channel_id=1, source_target_pairs={{32,96},{33,97},{34,98},{35,99},{36,100},{37,101},{38,102},{39,103... | collective-permute-start | bytes 393224 | tf_op jit(solution)/shard_map/ppermute | solution.py:148
  27.6 9.9 %collective-permute-start.3 = (f16[64,1024]{1,0:T(8,128)(2,1)S(1)}, f16[64,1024]{1,0:T(8,128)(2,1)S(1)}, u32[]{:S(2)}, u32[]{:S(2)}) collective-permute-start(f16[64,1024]{1,0:T(8,128)(2,1)S(1)} %fusion.4), channel_id=1, source_target_pairs={{0,96},{1,97},{2,98},{3,99},{4,100},{5,101},{6,102},{7,103},{8,104... | collective-permute-start | bytes 393224 | tf_op jit(solution)/shard_map/ppermute | solution.py:148
  28.2 9.2 %collective-permute-start.2 = (f16[64,1024]{1,0:T(8,128)(2,1)S(1)}, f16[64,1024]{1,0:T(8,128)(2,1)S(1)}, u32[]{:S(2)}, u32[]{:S(2)}) collective-permute-start(f16[64,1024]{1,0:T(8,128)(2,1)S(1)} %fusion.4), channel_id=1, source_target_pairs={{64,96},{65,97},{66,98},{67,99},{68,100},{69,101},{70,102},{71,103... | collective-permute-start | bytes 393224 | tf_op jit(solution)/shard_map/ppermute | solution.py:148
  37.7 2.7 %collective-permute-start.7 = (bf16[64,4,256]{2,1,0:T(4,128)(2,1)S(1)}, bf16[64,4,256]{2,1,0:T(4,128)(2,1)S(1)}, u32[]{:S(2)}, u32[]{:S(2)}) collective-permute-start(bf16[64,4,256]{2,1,0:T(4,128)(2,1)S(1)} %get-tuple-element.44), channel_id=1, source_target_pairs={{96,0},{97,1},{98,2},{99,3},{100,4},{101,5},{102,6},{103,7},{104,8... | collective-permute-start | bytes 393224 | tf_op jit(solution)/shard_map/ppermute | solution.py:166
  38.4 2.0 %collective-permute-start.6 = (bf16[64,4,256]{2,1,0:T(4,128)(2,1)S(1)}, bf16[64,4,256]{2,1,0:T(4,128)(2,1)S(1)}, u32[]{:S(2)}, u32[]{:S(2)}) collective-permute-start(bf16[64,4,256]{2,1,0:T(4,128)(2,1)S(1)} %get-tuple-element.44), channel_id=1, source_target_pairs={{96,32},{97,33},{98,34},{99,35},{100,36},{101,37},{102,38},{103,39... | collective-permute-start | bytes 393224 | tf_op jit(solution)/shard_map/ppermute | solution.py:166
  39.1 9.6 %collective-permute-start.5 = (bf16[64,4,256]{2,1,0:T(4,128)(2,1)S(1)}, bf16[64,4,256]{2,1,0:T(4,128)(2,1)S(1)}, u32[]{:S(2)}, u32[]{:S(2)}) collective-permute-start(bf16[64,4,256]{2,1,0:T(4,128)(2,1)S(1)} %get-tuple-element.44), channel_id=1, source_target_pairs={{96,64},{97,65},{98,66},{99,67},{100,68},{101,69},{102,70},{103,71... | collective-permute-start | bytes 393224 | tf_op jit(solution)/shard_map/ppermute | solution.py:166
  49.8 15.0 %all-to-all-start.1 = ((bf16[32,4,1024]{2,1,0:T(4,128)(2,1)}), bf16[32,4,1024]{2,1,0:T(4,128)(2,1)S(1)}, u32[]{:S(2)}, u32[]{:S(2)}) async-start(bf16[32,4,1024]{2,1,0:T(4,128)(2,1)} %reshape.124), calls=%async_computation.1 | async-start | bytes 524288 | tf_op jit(solution)/shard_map/all_to_all | solution.py:172
  56.2 9.7 %copy-start.1 = (f32[1,64,16,256]{3,2,1,0:T(8,128)}, f32[1,64,16,256]{3,2,1,0:T(8,128)S(1)}, u32[]{:S(2)}) copy-start(f32[1,64,16,256]{3,2,1,0:T(8,128)S(1)} %fusion.10) | copy-start | bytes 3145732

commit v17 on v16

--- a/solution.py
+++ b/solution.py
@@ -144,7 +144,7 @@
     last = n_sections - 1
     scaled = (COUPLING * partial).astype(LINK)
     heating = scaled.astype(jnp.float32)
-    for source in sorted(range(last), key=lambda t: (t + 1) % last):
+    for source in sorted(range(last), reverse=True):
         heating = heating + lax.ppermute(scaled, "comp", [(source, last)]).astype(jnp.float32)
 
     fields = diffuse(layer_temp, diffusivity)

time: 66.4 us -> 65.5 us (0.986)
  starting transfers between devices: 24.7 us -> 23.7 us
    all_to_all x1, starting transfers between devices: 6.15 us -> 5.09 us  [body(): came_back = lax.all_to_all(reply, 'band', 0, 0, tiled=True)]
where the time goes in v17:
time: 65.5 us; the launch traced here: 65 us
  starting transfers between devices  23.7 us (36%)
  waiting for transfers between devices  20.1 us (31%)
  matrix products  7.09 us (11%)
  Pallas kernels  6.45 us (10%)
  other arithmetic  4.38 us (7%)
  local copies, waits for them, and re-layouts  2.32 us (4%)
  between operations  0.95 us (1%)
    all_to_all x1, waiting for transfers between devices, body(): came_back = lax.all_to_all(reply, 'band', 0, 0, tiled=True)  8.66 us
    ppermute x3, waiting for transfers between devices, body(): ocean_rows = ocean_rows + lax.ppermute(returned, 'comp', [(last, target)])  8.46 us
    all_to_all x1, starting transfers between devices, body(): received = lax.all_to_all(sending, 'band', 0, 0, tiled=True)  7.76 us
    pallas_call x1, Pallas kernels, diffuse(): pl.pallas_call(_diffusion_kernel, out_shape=jax.ShapeDtypeStruct((rows, l...  6.45 us
    all_to_all x1, starting transfers between devices, body(): came_back = lax.all_to_all(reply, 'band', 0, 0, tiled=True)  5.09 us
    dot_general x1, matrix products, body(): jnp.einsum('rfc,rcd->rfd', surface_layers, weights_local, preferred_eleme...  4.76 us
    ppermute x1, starting transfers between devices, diffuse(): above = lax.ppermute(comb[rows - halo:], 'band', forward)  3.42 us
    all_to_all x1, waiting for transfers between devices, body(): received = lax.all_to_all(sending, 'band', 0, 0, tiled=True)  2.95 us
  transfers between devices with their start and end apart: 10, of which 3 were waited for; matrix products, arithmetic and copies ran while one was open for 4% of the time, Pallas kernels for 10%

profile of v17, /device:TPU:65, one launch (start us, length us, event | category | flops | bytes accessed | tf_op | source)
XLA Modules:
  0.0 65.0 jit_solution(13280226543398551626)
XLA Ops:
  0.6 0.9 %fusion.5 = f32[64]{0:T(128)S(1)} fusion(s32[64]{0:T(128)} %bitcast.55), kind=kOutput, calls=%fused_computation.13 | convolution fusion | flops 286656 | bytes 512 | tf_op jit(solution)/shard_map/dot_general | solution.py:124
  1.5 0.7 %fusion.16 = f32[64,32]{0,1:T(8,128)S(1)} fusion(s32[64]{0:T(128)} %bitcast.56), kind=kLoop, calls=%fused_computation.39 | loop fusion | flops 4096 | bytes 8448 | tf_op jit(solution)/shard_map/convert_element_type | solution.py:119
  2.2 0.7 %convert_bitcast_fusion = f32[64]{0:T(128)S(1)} fusion(s32[1,64]{1,0:T(1,128)} %param.14), kind=kLoop, calls=%fused_computation.44 | loop fusion | flops 64 | bytes 512 | tf_op jit(solution)/shard_map/convert_element_type | solution.py:135
  2.9 4.8 %conditional.2 = (f32[64,1024]{1,0:T(8,128)S(1)}) conditional(s32[]{:T(128)} %convert_element_type.100, (f32[1,64,16,256]{3,2,1,0:T(8,128)}, bf16[64,256,256]{2,1,0:T(8,128)(2,1)}) %tuple.37, () %tuple.27), branch_computations={%region_1.0_spmd, %region_2.0_spmd} | conditional | flops 33554432 | bytes 9306120 | solution.py:110
  2.9 4.8 %fusion.1 = f32[64,4,256]{2,1,0:T(4,128)S(1)} fusion(bf16[64,256,256]{2,1,0:T(8,128)(2,1)} %get-tuple-element.33, f32[1,64,16,256]{3,2,1,0:T(8,128)} %get-tuple-element.32), kind=kOutput, calls=%fused_computation.2 | convolution fusion | flops 33554432 | bytes 8781824 | tf_op jit(solution)/shard_map/cond/branch_0_fun/rfc,rcd->rfd/dot_general | solution.py:113
  7.6 0.1 copy.20
  7.7 0.0 copy-start.2
  7.7 0.0 copy-start
  7.7 0.1 broadcast_in_dim.12
  7.8 0.6 convolution_convert_fusion.1
  8.4 0.9 %copy.17 = f16[32,4,1152]{2,1,0:T(4,128)(2,1)} copy(f16[32,4,1152]{2,0,1:T(8,128)(2,1)S(1)} %convolution_convert_fusion.1) | data formatting | bytes 589824 | tf_op jit(solution)/shard_map/convert_element_type | solution.py:138
  9.3 7.8 %all-to-all-start = ((f16[32,4,1152]{2,1,0:T(4,128)(2,1)}), f16[32,4,1152]{2,1,0:T(4,128)(2,1)S(1)}, u32[]{:S(2)}, u32[]{:S(2)}) async-start(f16[32,4,1152]{2,1,0:T(4,128)(2,1)} %copy.17), calls=%async_computation | async-start | bytes 589824 | tf_op jit(solution)/shard_map/all_to_all | solution.py:139
  17.2 2.1 %collective-permute-start.1 = (f32[4,17,256]{2,1,0:T(8,128)S(1)}, f32[4,17,256]{2,1,0:T(8,128)S(1)}, u32[]{:S(2)}, u32[]{:S(2)}) collective-permute-start(f32[4,17,256]{2,1,0:T(8,128)S(1)} %get-tuple-element.40), channel_id=1, source_target_pairs={{1,0},{2,1},{3,2},{4,3},{5,4},{6,5},{7,6},{8,7},{9,8},{10,9},{11,1... | collective-permute-start | bytes 208904 | tf_op jit(solution)/shard_map/ppermute | solution.py:82
  19.4 3.4 %collective-permute-start = (f32[4,17,256]{2,1,0:T(8,128)S(1)}, f32[4,17,256]{2,1,0:T(8,128)S(1)}, u32[]{:S(2)}, u32[]{:S(2)}) collective-permute-start(f32[4,17,256]{2,1,0:T(8,128)S(1)} %get-tuple-element.39), channel_id=1, source_target_pairs={{0,1},{1,2},{2,3},{3,4},{4,5},{5,6},{6,7},{7,8},{8,9},{9,10},{10,1... | collective-permute-start | bytes 208904 | tf_op jit(solution)/shard_map/ppermute | solution.py:81
  22.8 0.6 pad_add_fusion.bounds_ref
  23.4 2.9 %all-to-all-done = f16[32,4,1152]{2,1,0:T(4,128)(2,1)S(1)} async-done(((f16[32,4,1152]{2,1,0:T(4,128)(2,1)}), f16[32,4,1152]{2,1,0:T(4,128)(2,1)S(1)}, u32[]{:S(2)}, u32[]{:S(2)}) %all-to-all-start) | async-done | bytes 294944 | tf_op jit(solution)/shard_map/all_to_all | solution.py:139
  26.3 0.1 reshape.121
  26.4 0.1 convert_reduce_fusion
  26.5 0.4 fusion.4
  26.9 0.7 %collective-permute-start.4 = (f16[64,1024]{1,0:T(8,128)(2,1)S(1)}, f16[64,1024]{1,0:T(8,128)(2,1)S(1)}, u32[]{:S(2)}, u32[]{:S(2)}) collective-permute-start(f16[64,1024]{1,0:T(8,128)(2,1)S(1)} %fusion.4), channel_id=1, source_target_pairs={{0,96},{1,97},{2,98},{3,99},{4,100},{5,101},{6,102},{7,103},{8,104... | collective-permute-start | bytes 393224 | tf_op jit(solution)/shard_map/ppermute | solution.py:148
  27.6 0.7 %collective-permute-start.3 = (f16[64,1024]{1,0:T(8,128)(2,1)S(1)}, f16[64,1024]{1,0:T(8,128)(2,1)S(1)}, u32[]{:S(2)}, u32[]{:S(2)}) collective-permute-start(f16[64,1024]{1,0:T(8,128)(2,1)S(1)} %fusion.4), channel_id=1, source_target_pairs={{32,96},{33,97},{34,98},{35,99},{36,100},{37,101},{38,102},{39,103... | collective-permute-start | bytes 393224 | tf_op jit(solution)/shard_map/ppermute | solution.py:148
  28.2 1.3 %collective-permute-start.2 = (f16[64,1024]{1,0:T(8,128)(2,1)S(1)}, f16[64,1024]{1,0:T(8,128)(2,1)S(1)}, u32[]{:S(2)}, u32[]{:S(2)}) collective-permute-start(f16[64,1024]{1,0:T(8,128)(2,1)S(1)} %fusion.4), channel_id=1, source_target_pairs={{64,96},{65,97},{66,98},{67,99},{68,100},{69,101},{70,102},{71,103... | collective-permute-start | bytes 393224 | tf_op jit(solution)/shard_map/ppermute | solution.py:148
  29.5 0.0 collective-permute-done.1
  29.6 0.0 collective-permute-done
  29.6 1.4 %pad_maximum_fusion.p_ref = f32[72,17,256]{2,1,0:T(8,128)} fusion(f32[4,17,256]{2,1,0:T(8,128)S(1)} %collective-permute-done.1, f32[64,1,256]{2,1,0:T(1,128)S(1)} %broadcast_in_dim_squeeze.4, f32[64,16,256]{2,1,0:T(8,128)S(1)} %bitcast.46, f32[4,17,256]{2,1,0:T(8,128)S(1)} %collective-permute-done), kind=kLoop, calls=%fused_computation.6 | loop fusion | flops 940032 | bytes 2506752 | tf_op jit(solution)/shard_map/concatenate | solution.py:83
  31.0 6.4 %shard_map.68 = f32[64,16,256]{2,1,0:T(8,128)S(1)} custom-call(s32[2]{0:T(128)} %pad_add_fusion.bounds_ref, f32[72,17,256]{2,1,0:T(8,128)} %pad_maximum_fusion.p_ref), custom_call_target="tpu_custom_call" | custom-call | tf_op jit(solution)/shard_map/pallas_call | solution.py:87
  37.4 0.0 collective-permute-done.4
  37.4 0.0 collective-permute-done.3
  37.4 0.0 collective-permute-done.2
  37.4 0.1 add_select_fusion
  37.5 0.1 reshape.122
  37.7 0.1 conditional.3
  37.7 0.7 %collective-permute-start.7 = (bf16[64,4,256]{2,1,0:T(4,128)(2,1)S(1)}, bf16[64,4,256]{2,1,0:T(4,128)(2,1)S(1)}, u32[]{:S(2)}, u32[]{:S(2)}) collective-permute-start(bf16[64,4,256]{2,1,0:T(4,128)(2,1)S(1)} %get-tuple-element.44), channel_id=1, source_target_pairs={{96,0},{97,1},{98,2},{99,3},{100,4},{101,5},{102,6},{103,7},{104,8... | collective-permute-start | bytes 393224 | tf_op jit(solution)/shard_map/ppermute | solution.py:166
  38.4 0.7 %collective-permute-start.6 = (bf16[64,4,256]{2,1,0:T(4,128)(2,1)S(1)}, bf16[64,4,256]{2,1,0:T(4,128)(2,1)S(1)}, u32[]{:S(2)}, u32[]{:S(2)}) collective-permute-start(bf16[64,4,256]{2,1,0:T(4,128)(2,1)S(1)} %get-tuple-element.44), channel_id=1, source_target_pairs={{96,32},{97,33},{98,34},{99,35},{100,36},{101,37},{102,38},{103,39... | collective-permute-start | bytes 393224 | tf_op jit(solution)/shard_map/ppermute | solution.py:166
  39.1 1.3 %collective-permute-start.5 = (bf16[64,4,256]{2,1,0:T(4,128)(2,1)S(1)}, bf16[64,4,256]{2,1,0:T(4,128)(2,1)S(1)}, u32[]{:S(2)}, u32[]{:S(2)}) collective-permute-start(bf16[64,4,256]{2,1,0:T(4,128)(2,1)S(1)} %get-tuple-element.44), channel_id=1, source_target_pairs={{96,64},{97,65},{98,66},{99,67},{100,68},{101,69},{102,70},{103,71... | collective-permute-start | bytes 393224 | tf_op jit(solution)/shard_map/ppermute | solution.py:166
  40.4 0.0 collective-permute-done.7
  40.4 0.0 collective-permute-done.6
  40.4 8.5 %collective-permute-done.5 = bf16[64,4,256]{2,1,0:T(4,128)(2,1)S(1)} collective-permute-done((bf16[64,4,256]{2,1,0:T(4,128)(2,1)S(1)}, bf16[64,4,256]{2,1,0:T(4,128)(2,1)S(1)}, u32[]{:S(2)}, u32[]{:S(2)}) %collective-permute-start.5) | collective-permute-done | bytes 131104 | tf_op jit(solution)/shard_map/ppermute | solution.py:166
  48.9 0.3 convolution_convert_fusion.2
  49.2 0.8 %reshape.124 = bf16[32,4,1024]{2,1,0:T(4,128)(2,1)} reshape(bf16[128,1024]{1,0:T(8,128)(2,1)S(1)} %convolution_convert_fusion.2) | data formatting | bytes 524288 | tf_op jit(solution)/shard_map/reshape | solution.py:171
  50.0 5.1 %all-to-all-start.1 = ((bf16[32,4,1024]{2,1,0:T(4,128)(2,1)}), bf16[32,4,1024]{2,1,0:T(4,128)(2,1)S(1)}, u32[]{:S(2)}, u32[]{:S(2)}) async-start(bf16[32,4,1024]{2,1,0:T(4,128)(2,1)} %reshape.124), calls=%async_computation.1 | async-start | bytes 524288 | tf_op jit(solution)/shard_map/all_to_all | solution.py:172
  55.1 0.1 copy.30
  55.2 0.1 fusion.10
  55.3 0.0 copy-start.1
  55.3 8.7 %all-to-all-done.1 = bf16[32,4,1024]{2,1,0:T(4,128)(2,1)S(1)} async-done(((bf16[32,4,1024]{2,1,0:T(4,128)(2,1)}), bf16[32,4,1024]{2,1,0:T(4,128)(2,1)S(1)}, u32[]{:S(2)}, u32[]{:S(2)}) %all-to-all-start.1) | async-done | bytes 262176 | tf_op jit(solution)/shard_map/all_to_all | solution.py:172
  64.0 0.2 fusion.3
  64.2 0.1 reshape.125
  64.3 0.7 %select_bitcast_fusion = bf16[1,64,4,256]{3,2,1,0:T(4,128)(2,1)} fusion(bf16[64,4,256]{2,1,0:T(4,128)(2,1)S(1)} %get-tuple-element.44, bf16[64,4,256]{2,1,0:T(4,128)(2,1)S(1)} %reshape.125, pred[]{:T(512)S(6)} %eq.62), kind=kLoop, calls=%fused_computation.23 | loop fusion | flops 65536 | bytes 393217 | tf_op jit(solution)/shard_map/broadcast_in_dim | solution.py:178
  (11 shorter events, 0.2 us)
Async XLA Ops:
  7.7 9.4 %copy-start.2 = (f32[1,64,256]{2,1,0:T(8,128)S(1)}, f32[1,64,256]{2,1,0:T(8,128)}, u32[]{:S(2)}) copy-start(f32[1,64,256]{2,1,0:T(8,128)} %param.12) | copy-start | bytes 196612
  7.7 9.5 %copy-start = (f32[1,64,16,256]{3,2,1,0:T(8,128)S(1)}, f32[1,64,16,256]{3,2,1,0:T(8,128)}, u32[]{:S(2)}) copy-start(f32[1,64,16,256]{3,2,1,0:T(8,128)} %param.11) | copy-start | bytes 3145732
  9.3 17.0 %all-to-all-start = ((f16[32,4,1152]{2,1,0:T(4,128)(2,1)}), f16[32,4,1152]{2,1,0:T(4,128)(2,1)S(1)}, u32[]{:S(2)}, u32[]{:S(2)}) async-start(f16[32,4,1152]{2,1,0:T(4,128)(2,1)} %copy.17), calls=%async_computation | async-start | bytes 589824 | tf_op jit(solution)/shard_map/all_to_all | solution.py:139
  17.2 12.3 %collective-permute-start.1 = (f32[4,17,256]{2,1,0:T(8,128)S(1)}, f32[4,17,256]{2,1,0:T(8,128)S(1)}, u32[]{:S(2)}, u32[]{:S(2)}) collective-permute-start(f32[4,17,256]{2,1,0:T(8,128)S(1)} %get-tuple-element.40), channel_id=1, source_target_pairs={{1,0},{2,1},{3,2},{4,3},{5,4},{6,5},{7,6},{8,7},{9,8},{10,9},{11,1... | collective-permute-start | bytes 208904 | tf_op jit(solution)/shard_map/ppermute | solution.py:82
  19.4 10.2 %collective-permute-start = (f32[4,17,256]{2,1,0:T(8,128)S(1)}, f32[4,17,256]{2,1,0:T(8,128)S(1)}, u32[]{:S(2)}, u32[]{:S(2)}) collective-permute-start(f32[4,17,256]{2,1,0:T(8,128)S(1)} %get-tuple-element.39), channel_id=1, source_target_pairs={{0,1},{1,2},{2,3},{3,4},{4,5},{5,6},{6,7},{7,8},{8,9},{9,10},{10,1... | collective-permute-start | bytes 208904 | tf_op jit(solution)/shard_map/ppermute | solution.py:81
  26.9 10.5 %collective-permute-start.4 = (f16[64,1024]{1,0:T(8,128)(2,1)S(1)}, f16[64,1024]{1,0:T(8,128)(2,1)S(1)}, u32[]{:S(2)}, u32[]{:S(2)}) collective-permute-start(f16[64,1024]{1,0:T(8,128)(2,1)S(1)} %fusion.4), channel_id=1, source_target_pairs={{0,96},{1,97},{2,98},{3,99},{4,100},{5,101},{6,102},{7,103},{8,104... | collective-permute-start | bytes 393224 | tf_op jit(solution)/shard_map/ppermute | solution.py:148
  27.6 9.9 %collective-permute-start.3 = (f16[64,1024]{1,0:T(8,128)(2,1)S(1)}, f16[64,1024]{1,0:T(8,128)(2,1)S(1)}, u32[]{:S(2)}, u32[]{:S(2)}) collective-permute-start(f16[64,1024]{1,0:T(8,128)(2,1)S(1)} %fusion.4), channel_id=1, source_target_pairs={{32,96},{33,97},{34,98},{35,99},{36,100},{37,101},{38,102},{39,103... | collective-permute-start | bytes 393224 | tf_op jit(solution)/shard_map/ppermute | solution.py:148
  28.2 9.2 %collective-permute-start.2 = (f16[64,1024]{1,0:T(8,128)(2,1)S(1)}, f16[64,1024]{1,0:T(8,128)(2,1)S(1)}, u32[]{:S(2)}, u32[]{:S(2)}) collective-permute-start(f16[64,1024]{1,0:T(8,128)(2,1)S(1)} %fusion.4), channel_id=1, source_target_pairs={{64,96},{65,97},{66,98},{67,99},{68,100},{69,101},{70,102},{71,103... | collective-permute-start | bytes 393224 | tf_op jit(solution)/shard_map/ppermute | solution.py:148
  37.7 2.7 %collective-permute-start.7 = (bf16[64,4,256]{2,1,0:T(4,128)(2,1)S(1)}, bf16[64,4,256]{2,1,0:T(4,128)(2,1)S(1)}, u32[]{:S(2)}, u32[]{:S(2)}) collective-permute-start(bf16[64,4,256]{2,1,0:T(4,128)(2,1)S(1)} %get-tuple-element.44), channel_id=1, source_target_pairs={{96,0},{97,1},{98,2},{99,3},{100,4},{101,5},{102,6},{103,7},{104,8... | collective-permute-start | bytes 393224 | tf_op jit(solution)/shard_map/ppermute | solution.py:166
  38.4 2.0 %collective-permute-start.6 = (bf16[64,4,256]{2,1,0:T(4,128)(2,1)S(1)}, bf16[64,4,256]{2,1,0:T(4,128)(2,1)S(1)}, u32[]{:S(2)}, u32[]{:S(2)}) collective-permute-start(bf16[64,4,256]{2,1,0:T(4,128)(2,1)S(1)} %get-tuple-element.44), channel_id=1, source_target_pairs={{96,32},{97,33},{98,34},{99,35},{100,36},{101,37},{102,38},{103,39... | collective-permute-start | bytes 393224 | tf_op jit(solution)/shard_map/ppermute | solution.py:166
  39.1 9.8 %collective-permute-start.5 = (bf16[64,4,256]{2,1,0:T(4,128)(2,1)S(1)}, bf16[64,4,256]{2,1,0:T(4,128)(2,1)S(1)}, u32[]{:S(2)}, u32[]{:S(2)}) collective-permute-start(bf16[64,4,256]{2,1,0:T(4,128)(2,1)S(1)} %get-tuple-element.44), channel_id=1, source_target_pairs={{96,64},{97,65},{98,66},{99,67},{100,68},{101,69},{102,70},{103,71... | collective-permute-start | bytes 393224 | tf_op jit(solution)/shard_map/ppermute | solution.py:166
  50.0 14.0 %all-to-all-start.1 = ((bf16[32,4,1024]{2,1,0:T(4,128)(2,1)}), bf16[32,4,1024]{2,1,0:T(4,128)(2,1)S(1)}, u32[]{:S(2)}, u32[]{:S(2)}) async-start(bf16[32,4,1024]{2,1,0:T(4,128)(2,1)} %reshape.124), calls=%async_computation.1 | async-start | bytes 524288 | tf_op jit(solution)/shard_map/all_to_all | solution.py:172
  55.3 9.7 %copy-start.1 = (f32[1,64,16,256]{3,2,1,0:T(8,128)}, f32[1,64,16,256]{3,2,1,0:T(8,128)S(1)}, u32[]{:S(2)}) copy-start(f32[1,64,16,256]{3,2,1,0:T(8,128)S(1)} %fusion.10) | copy-start | bytes 3145732

commit v18 on v17

--- a/solution.py
+++ b/solution.py
@@ -38,8 +38,12 @@
     return max(k for k in range(1, limit + 1) if n % k == 0)
 
 
-def _diffusion_kernel(bounds_ref, p_ref, o_ref, buf_a, buf_b):
+def _diffusion_kernel(bounds_ref, above_ref, comb_ref, below_ref, o_ref, p_ref, buf_a, buf_b):
     total = p_ref.shape[0]
+    halo_rows = above_ref.shape[0]
+    p_ref[pl.ds(0, halo_rows)] = above_ref[...]
+    p_ref[pl.ds(halo_rows, comb_ref.shape[0])] = comb_ref[...]
+    p_ref[pl.ds(total - halo_rows, halo_rows)] = below_ref[...]
     rows, lev = o_ref.shape[0], o_ref.shape[1]
     halo = (total - rows) // 2
     bounds = (bounds_ref[0], bounds_ref[1])
@@ -80,7 +84,6 @@
     backward = [(i + 1, i) for i in range(n_bands - 1)]
     above = lax.ppermute(comb[rows - halo:], "band", forward)
     below = lax.ppermute(comb[:halo], "band", backward)
-    padded = jnp.concatenate([above, comb, below], axis=0)
     first = jnp.where(band == 0, halo, 0)
     stop = jnp.where(band == n_bands - 1, halo + rows, total)
     bounds = jnp.stack([first, stop]).astype(jnp.int32)
@@ -90,10 +93,13 @@
         in_specs=[
             pl.BlockSpec(memory_space=pltpu.SMEM),
             pl.BlockSpec(memory_space=pltpu.VMEM),
+            pl.BlockSpec(memory_space=pltpu.VMEM),
+            pl.BlockSpec(memory_space=pltpu.VMEM),
         ],
         out_specs=pl.BlockSpec(memory_space=pltpu.VMEM),
-        scratch_shapes=[pltpu.VMEM((total, lev, cols), jnp.float32)] * 2,
-    )(bounds, padded)
+        scratch_shapes=[pltpu.VMEM((total, lev + 1, cols), jnp.float32)]
+        + [pltpu.VMEM((total, lev, cols), jnp.float32)] * 2,
+    )(bounds, above, comb, below)
 
 
 def body(layer_temp, diffusivity, owner_band, block_index, remap_blocks):

time: 65.5 us -> 66.9 us (1.021)
  local copies, waits for them, and re-layouts: 2.32 us -> 3.59 us
  waiting for transfers between devices: 20.1 us -> 21.1 us
  starting transfers between devices: 23.7 us -> 22.8 us
    unnamed x8 -> x12, local copies, waits for them, and re-layouts: 0.11 us -> 1.38 us
    all_to_all x1, starting transfers between devices: 5.09 us -> 4.28 us  [body(): came_back = lax.all_to_all(reply, 'band', 0, 0, tiled=True)]
    concatenate x1 -> x2, other arithmetic: 1.39 us -> 1.32 us  [diffuse(): comb = jnp.concatenate([layer_temp[0], diffusivity[0][:, None, :]], axis=1)]
where the time goes in v18:
time: 66.9 us; the launch traced here: 66.4 us
  starting transfers between devices  22.8 us (34%)
  waiting for transfers between devices  21.1 us (32%)
  matrix products  7.09 us (11%)
  Pallas kernels  6.49 us (10%)
  other arithmetic  4.38 us (7%)
  local copies, waits for them, and re-layouts  3.59 us (5%)
  between operations  0.93 us (1%)
    all_to_all x1, waiting for transfers between devices, body(): came_back = lax.all_to_all(reply, 'band', 0, 0, tiled=True)  8.77 us
    ppermute x3, waiting for transfers between devices, body(): ocean_rows = ocean_rows + lax.ppermute(returned, 'comp', [(last, target)])  8.73 us
    all_to_all x1, starting transfers between devices, body(): received = lax.all_to_all(sending, 'band', 0, 0, tiled=True)  7.76 us
    pallas_call x1, Pallas kernels, diffuse(): pl.pallas_call(_diffusion_kernel, out_shape=jax.ShapeDtypeStruct((rows, l...  6.49 us
    dot_general x1, matrix products, body(): jnp.einsum('rfc,rcd->rfd', surface_layers, weights_local, preferred_eleme...  4.76 us
    all_to_all x1, starting transfers between devices, body(): came_back = lax.all_to_all(reply, 'band', 0, 0, tiled=True)  4.28 us
    all_to_all x1, waiting for transfers between devices, body(): received = lax.all_to_all(sending, 'band', 0, 0, tiled=True)  3.62 us
    ppermute x1, starting transfers between devices, diffuse(): above = lax.ppermute(comb[rows - halo:], 'band', forward)  3.54 us
  transfers between devices with their start and end apart: 10, of which 3 were waited for; matrix products, arithmetic and copies ran while one was open for 4% of the time, Pallas kernels for 10%

profile of v18, /device:TPU:65, one launch (start us, length us, event | category | flops | bytes accessed | tf_op | source)
XLA Modules:
  0.0 66.4 jit_solution(1617762653749535388)
XLA Ops:
  0.6 0.9 %fusion.5 = f32[64]{0:T(128)S(1)} fusion(s32[64]{0:T(128)} %bitcast.55), kind=kOutput, calls=%fused_computation.17 | convolution fusion | flops 286656 | bytes 512 | tf_op jit(solution)/shard_map/dot_general | solution.py:130
  1.5 0.7 %fusion.18 = f32[64,32]{0,1:T(8,128)S(1)} fusion(s32[64]{0:T(128)} %bitcast.56), kind=kLoop, calls=%fused_computation.43 | loop fusion | flops 4096 | bytes 8448 | tf_op jit(solution)/shard_map/convert_element_type | solution.py:125
  2.2 0.7 convert_bitcast_fusion
  2.9 4.8 %conditional.2 = (f32[64,1024]{1,0:T(8,128)S(1)}) conditional(s32[]{:T(128)} %convert_element_type.100, (f32[1,64,16,256]{3,2,1,0:T(8,128)}, bf16[64,256,256]{2,1,0:T(8,128)(2,1)}) %tuple.37, () %tuple.27), branch_computations={%region_1.0_spmd, %region_2.0_spmd} | conditional | flops 33554432 | bytes 9306120 | solution.py:116
  2.9 4.8 %fusion.1 = f32[64,4,256]{2,1,0:T(4,128)S(1)} fusion(bf16[64,256,256]{2,1,0:T(8,128)(2,1)} %get-tuple-element.33, f32[1,64,16,256]{3,2,1,0:T(8,128)} %get-tuple-element.32), kind=kOutput, calls=%fused_computation.2 | convolution fusion | flops 33554432 | bytes 8781824 | tf_op jit(solution)/shard_map/cond/branch_0_fun/rfc,rcd->rfd/dot_general | solution.py:119
  7.6 0.1 copy.20
  7.7 0.0 copy-start.4
  7.7 0.0 copy-start
  7.7 0.1 broadcast_in_dim.12
  7.8 0.6 convolution_convert_fusion.1
  8.4 0.9 %copy.17 = f16[32,4,1152]{2,1,0:T(4,128)(2,1)} copy(f16[32,4,1152]{2,0,1:T(8,128)(2,1)S(1)} %convolution_convert_fusion.1) | data formatting | bytes 589824 | tf_op jit(solution)/shard_map/convert_element_type | solution.py:144
  9.3 7.8 %all-to-all-start = ((f16[32,4,1152]{2,1,0:T(4,128)(2,1)}), f16[32,4,1152]{2,1,0:T(4,128)(2,1)S(1)}, u32[]{:S(2)}, u32[]{:S(2)}) async-start(f16[32,4,1152]{2,1,0:T(4,128)(2,1)} %copy.17), calls=%async_computation | async-start | bytes 589824 | tf_op jit(solution)/shard_map/all_to_all | solution.py:145
  17.2 3.5 %collective-permute-start = (f32[4,17,256]{2,1,0:T(8,128)S(1)}, f32[4,17,256]{2,1,0:T(8,128)S(1)}, u32[]{:S(2)}, u32[]{:S(2)}) collective-permute-start(f32[4,17,256]{2,1,0:T(8,128)S(1)} %get-tuple-element.40), channel_id=1, source_target_pairs={{0,1},{1,2},{2,3},{3,4},{4,5},{5,6},{6,7},{7,8},{8,9},{9,10},{10,1... | collective-permute-start | bytes 208904 | tf_op jit(solution)/shard_map/ppermute | solution.py:85
  20.8 1.9 %collective-permute-start.1 = (f32[4,17,256]{2,1,0:T(8,128)S(1)}, f32[4,17,256]{2,1,0:T(8,128)S(1)}, u32[]{:S(2)}, u32[]{:S(2)}) collective-permute-start(f32[4,17,256]{2,1,0:T(8,128)S(1)} %get-tuple-element.39), channel_id=1, source_target_pairs={{1,0},{2,1},{3,2},{4,3},{5,4},{6,5},{7,6},{8,7},{9,8},{10,9},{11,1... | collective-permute-start | bytes 208904 | tf_op jit(solution)/shard_map/ppermute | solution.py:86
  22.7 3.6 %all-to-all-done = f16[32,4,1152]{2,1,0:T(4,128)(2,1)S(1)} async-done(((f16[32,4,1152]{2,1,0:T(4,128)(2,1)}), f16[32,4,1152]{2,1,0:T(4,128)(2,1)S(1)}, u32[]{:S(2)}, u32[]{:S(2)}) %all-to-all-start) | async-done | bytes 294944 | tf_op jit(solution)/shard_map/all_to_all | solution.py:145
  26.3 0.1 reshape.121
  26.4 0.1 convert_reduce_fusion
  26.5 0.4 fusion.4
  26.9 0.7 %collective-permute-start.4 = (f16[64,1024]{1,0:T(8,128)(2,1)S(1)}, f16[64,1024]{1,0:T(8,128)(2,1)S(1)}, u32[]{:S(2)}, u32[]{:S(2)}) collective-permute-start(f16[64,1024]{1,0:T(8,128)(2,1)S(1)} %fusion.4), channel_id=1, source_target_pairs={{0,96},{1,97},{2,98},{3,99},{4,100},{5,101},{6,102},{7,103},{8,104... | collective-permute-start | bytes 393224 | tf_op jit(solution)/shard_map/ppermute | solution.py:154
  27.6 0.7 %collective-permute-start.3 = (f16[64,1024]{1,0:T(8,128)(2,1)S(1)}, f16[64,1024]{1,0:T(8,128)(2,1)S(1)}, u32[]{:S(2)}, u32[]{:S(2)}) collective-permute-start(f16[64,1024]{1,0:T(8,128)(2,1)S(1)} %fusion.4), channel_id=1, source_target_pairs={{32,96},{33,97},{34,98},{35,99},{36,100},{37,101},{38,102},{39,103... | collective-permute-start | bytes 393224 | tf_op jit(solution)/shard_map/ppermute | solution.py:154
  28.2 1.3 %collective-permute-start.2 = (f16[64,1024]{1,0:T(8,128)(2,1)S(1)}, f16[64,1024]{1,0:T(8,128)(2,1)S(1)}, u32[]{:S(2)}, u32[]{:S(2)}) collective-permute-start(f16[64,1024]{1,0:T(8,128)(2,1)S(1)} %fusion.4), channel_id=1, source_target_pairs={{64,96},{65,97},{66,98},{67,99},{68,100},{69,101},{70,102},{71,103... | collective-permute-start | bytes 393224 | tf_op jit(solution)/shard_map/ppermute | solution.py:154
  29.5 1.3 %pad_maximum_fusion.comb_ref = f32[64,17,256]{2,1,0:T(8,128)} fusion(f32[64,1,256]{2,1,0:T(1,128)S(1)} %broadcast_in_dim_squeeze.4, f32[64,16,256]{2,1,0:T(8,128)S(1)} %bitcast.46), kind=kLoop, calls=%fused_computation.7 | loop fusion | flops 278528 | bytes 2228224 | tf_op jit(solution)/shard_map/concatenate | solution.py:82
  30.8 0.6 pad_add_fusion.bounds_ref
  31.5 0.0 collective-permute-done.above_ref
  31.5 0.0 collective-permute-done.1.below_ref
  31.5 0.6 copy-done.2
  32.1 0.6 copy-done.3
  32.8 6.5 %shard_map.68 = f32[64,16,256]{2,1,0:T(8,128)S(1)} custom-call(s32[2]{0:T(128)} %pad_add_fusion.bounds_ref, f32[4,17,256]{2,1,0:T(8,128)} %copy-done.2, f32[64,17,256]{2,1,0:T(8,128)} %pad_maximum_fusion.comb_ref, f32[4,17,256]{2,1,0:T(8,128)} %copy-done.3), custom_call_target="tpu_custom_call" | custom-call | tf_op jit(solution)/shard_map/pallas_call | solution.py:90
  39.3 0.0 collective-permute-done.4
  39.3 0.0 collective-permute-done.2
  39.3 0.1 add_select_fusion
  39.4 0.1 reshape.122
  39.5 0.1 conditional.3
  39.6 0.7 %collective-permute-start.7 = (bf16[64,4,256]{2,1,0:T(4,128)(2,1)S(1)}, bf16[64,4,256]{2,1,0:T(4,128)(2,1)S(1)}, u32[]{:S(2)}, u32[]{:S(2)}) collective-permute-start(bf16[64,4,256]{2,1,0:T(4,128)(2,1)S(1)} %get-tuple-element.44), channel_id=1, source_target_pairs={{96,0},{97,1},{98,2},{99,3},{100,4},{101,5},{102,6},{103,7},{104,8... | collective-permute-start | bytes 393224 | tf_op jit(solution)/shard_map/ppermute | solution.py:172
  40.3 0.7 %collective-permute-start.6 = (bf16[64,4,256]{2,1,0:T(4,128)(2,1)S(1)}, bf16[64,4,256]{2,1,0:T(4,128)(2,1)S(1)}, u32[]{:S(2)}, u32[]{:S(2)}) collective-permute-start(bf16[64,4,256]{2,1,0:T(4,128)(2,1)S(1)} %get-tuple-element.44), channel_id=1, source_target_pairs={{96,32},{97,33},{98,34},{99,35},{100,36},{101,37},{102,38},{103,39... | collective-permute-start | bytes 393224 | tf_op jit(solution)/shard_map/ppermute | solution.py:172
  40.9 1.3 %collective-permute-start.5 = (bf16[64,4,256]{2,1,0:T(4,128)(2,1)S(1)}, bf16[64,4,256]{2,1,0:T(4,128)(2,1)S(1)}, u32[]{:S(2)}, u32[]{:S(2)}) collective-permute-start(bf16[64,4,256]{2,1,0:T(4,128)(2,1)S(1)} %get-tuple-element.44), channel_id=1, source_target_pairs={{96,64},{97,65},{98,66},{99,67},{100,68},{101,69},{102,70},{103,71... | collective-permute-start | bytes 393224 | tf_op jit(solution)/shard_map/ppermute | solution.py:172
  42.3 0.0 collective-permute-done.6
  42.3 8.7 %collective-permute-done.5 = bf16[64,4,256]{2,1,0:T(4,128)(2,1)S(1)} collective-permute-done((bf16[64,4,256]{2,1,0:T(4,128)(2,1)S(1)}, bf16[64,4,256]{2,1,0:T(4,128)(2,1)S(1)}, u32[]{:S(2)}, u32[]{:S(2)}) %collective-permute-start.5) | collective-permute-done | bytes 131104 | tf_op jit(solution)/shard_map/ppermute | solution.py:172
  51.1 0.3 convolution_convert_fusion.2
  51.3 0.8 %reshape.124 = bf16[32,4,1024]{2,1,0:T(4,128)(2,1)} reshape(bf16[128,1024]{1,0:T(8,128)(2,1)S(1)} %convolution_convert_fusion.2) | data formatting | bytes 524288 | tf_op jit(solution)/shard_map/reshape | solution.py:177
  52.1 4.3 %all-to-all-start.1 = ((bf16[32,4,1024]{2,1,0:T(4,128)(2,1)}), bf16[32,4,1024]{2,1,0:T(4,128)(2,1)S(1)}, u32[]{:S(2)}, u32[]{:S(2)}) async-start(bf16[32,4,1024]{2,1,0:T(4,128)(2,1)} %reshape.124), calls=%async_computation.1 | async-start | bytes 524288 | tf_op jit(solution)/shard_map/all_to_all | solution.py:178
  56.4 0.1 copy.30
  56.5 0.1 fusion.10
  56.6 0.0 copy-start.1
  56.6 8.8 %all-to-all-done.1 = bf16[32,4,1024]{2,1,0:T(4,128)(2,1)S(1)} async-done(((bf16[32,4,1024]{2,1,0:T(4,128)(2,1)}), bf16[32,4,1024]{2,1,0:T(4,128)(2,1)S(1)}, u32[]{:S(2)}, u32[]{:S(2)}) %all-to-all-start.1) | async-done | bytes 262176 | tf_op jit(solution)/shard_map/all_to_all | solution.py:178
  65.4 0.2 fusion.3
  65.6 0.1 reshape.125
  65.7 0.7 %select_bitcast_fusion = bf16[1,64,4,256]{3,2,1,0:T(4,128)(2,1)} fusion(bf16[64,4,256]{2,1,0:T(4,128)(2,1)S(1)} %get-tuple-element.44, bf16[64,4,256]{2,1,0:T(4,128)(2,1)S(1)} %reshape.125, pred[]{:T(512)S(6)} %eq.62), kind=kLoop, calls=%fused_computation.27 | loop fusion | flops 65536 | bytes 393217 | tf_op jit(solution)/shard_map/broadcast_in_dim | solution.py:184
  (15 shorter events, 0.2 us)
Async XLA Ops:
  7.7 9.4 %copy-start.4 = (f32[1,64,256]{2,1,0:T(8,128)S(1)}, f32[1,64,256]{2,1,0:T(8,128)}, u32[]{:S(2)}) copy-start(f32[1,64,256]{2,1,0:T(8,128)} %param.12) | copy-start | bytes 196612
  7.7 9.5 %copy-start = (f32[1,64,16,256]{3,2,1,0:T(8,128)S(1)}, f32[1,64,16,256]{3,2,1,0:T(8,128)}, u32[]{:S(2)}) copy-start(f32[1,64,16,256]{3,2,1,0:T(8,128)} %param.11) | copy-start | bytes 3145732
  9.3 17.0 %all-to-all-start = ((f16[32,4,1152]{2,1,0:T(4,128)(2,1)}), f16[32,4,1152]{2,1,0:T(4,128)(2,1)S(1)}, u32[]{:S(2)}, u32[]{:S(2)}) async-start(f16[32,4,1152]{2,1,0:T(4,128)(2,1)} %copy.17), calls=%async_computation | async-start | bytes 589824 | tf_op jit(solution)/shard_map/all_to_all | solution.py:145
  17.2 14.3 %collective-permute-start = (f32[4,17,256]{2,1,0:T(8,128)S(1)}, f32[4,17,256]{2,1,0:T(8,128)S(1)}, u32[]{:S(2)}, u32[]{:S(2)}) collective-permute-start(f32[4,17,256]{2,1,0:T(8,128)S(1)} %get-tuple-element.40), channel_id=1, source_target_pairs={{0,1},{1,2},{2,3},{3,4},{4,5},{5,6},{6,7},{7,8},{8,9},{9,10},{10,1... | collective-permute-start | bytes 208904 | tf_op jit(solution)/shard_map/ppermute | solution.py:85
  20.8 10.7 %collective-permute-start.1 = (f32[4,17,256]{2,1,0:T(8,128)S(1)}, f32[4,17,256]{2,1,0:T(8,128)S(1)}, u32[]{:S(2)}, u32[]{:S(2)}) collective-permute-start(f32[4,17,256]{2,1,0:T(8,128)S(1)} %get-tuple-element.39), channel_id=1, source_target_pairs={{1,0},{2,1},{3,2},{4,3},{5,4},{6,5},{7,6},{8,7},{9,8},{10,9},{11,1... | collective-permute-start | bytes 208904 | tf_op jit(solution)/shard_map/ppermute | solution.py:86
  26.9 12.4 %collective-permute-start.4 = (f16[64,1024]{1,0:T(8,128)(2,1)S(1)}, f16[64,1024]{1,0:T(8,128)(2,1)S(1)}, u32[]{:S(2)}, u32[]{:S(2)}) collective-permute-start(f16[64,1024]{1,0:T(8,128)(2,1)S(1)} %fusion.4), channel_id=1, source_target_pairs={{0,96},{1,97},{2,98},{3,99},{4,100},{5,101},{6,102},{7,103},{8,104... | collective-permute-start | bytes 393224 | tf_op jit(solution)/shard_map/ppermute | solution.py:154
  27.6 11.7 %collective-permute-start.3 = (f16[64,1024]{1,0:T(8,128)(2,1)S(1)}, f16[64,1024]{1,0:T(8,128)(2,1)S(1)}, u32[]{:S(2)}, u32[]{:S(2)}) collective-permute-start(f16[64,1024]{1,0:T(8,128)(2,1)S(1)} %fusion.4), channel_id=1, source_target_pairs={{32,96},{33,97},{34,98},{35,99},{36,100},{37,101},{38,102},{39,103... | collective-permute-start | bytes 393224 | tf_op jit(solution)/shard_map/ppermute | solution.py:154
  28.2 11.1 %collective-permute-start.2 = (f16[64,1024]{1,0:T(8,128)(2,1)S(1)}, f16[64,1024]{1,0:T(8,128)(2,1)S(1)}, u32[]{:S(2)}, u32[]{:S(2)}) collective-permute-start(f16[64,1024]{1,0:T(8,128)(2,1)S(1)} %fusion.4), channel_id=1, source_target_pairs={{64,96},{65,97},{66,98},{67,99},{68,100},{69,101},{70,102},{71,103... | collective-permute-start | bytes 393224 | tf_op jit(solution)/shard_map/ppermute | solution.py:154
  31.5 0.6 copy-start.2
  32.1 0.6 copy-start.3
  39.6 2.7 %collective-permute-start.7 = (bf16[64,4,256]{2,1,0:T(4,128)(2,1)S(1)}, bf16[64,4,256]{2,1,0:T(4,128)(2,1)S(1)}, u32[]{:S(2)}, u32[]{:S(2)}) collective-permute-start(bf16[64,4,256]{2,1,0:T(4,128)(2,1)S(1)} %get-tuple-element.44), channel_id=1, source_target_pairs={{96,0},{97,1},{98,2},{99,3},{100,4},{101,5},{102,6},{103,7},{104,8... | collective-permute-start | bytes 393224 | tf_op jit(solution)/shard_map/ppermute | solution.py:172
  40.3 2.0 %collective-permute-start.6 = (bf16[64,4,256]{2,1,0:T(4,128)(2,1)S(1)}, bf16[64,4,256]{2,1,0:T(4,128)(2,1)S(1)}, u32[]{:S(2)}, u32[]{:S(2)}) collective-permute-start(bf16[64,4,256]{2,1,0:T(4,128)(2,1)S(1)} %get-tuple-element.44), channel_id=1, source_target_pairs={{96,32},{97,33},{98,34},{99,35},{100,36},{101,37},{102,38},{103,39... | collective-permute-start | bytes 393224 | tf_op jit(solution)/shard_map/ppermute | solution.py:172
  40.9 10.0 %collective-permute-start.5 = (bf16[64,4,256]{2,1,0:T(4,128)(2,1)S(1)}, bf16[64,4,256]{2,1,0:T(4,128)(2,1)S(1)}, u32[]{:S(2)}, u32[]{:S(2)}) collective-permute-start(bf16[64,4,256]{2,1,0:T(4,128)(2,1)S(1)} %get-tuple-element.44), channel_id=1, source_target_pairs={{96,64},{97,65},{98,66},{99,67},{100,68},{101,69},{102,70},{103,71... | collective-permute-start | bytes 393224 | tf_op jit(solution)/shard_map/ppermute | solution.py:172
  52.1 13.3 %all-to-all-start.1 = ((bf16[32,4,1024]{2,1,0:T(4,128)(2,1)}), bf16[32,4,1024]{2,1,0:T(4,128)(2,1)S(1)}, u32[]{:S(2)}, u32[]{:S(2)}) async-start(bf16[32,4,1024]{2,1,0:T(4,128)(2,1)} %reshape.124), calls=%async_computation.1 | async-start | bytes 524288 | tf_op jit(solution)/shard_map/all_to_all | solution.py:178
  56.6 9.8 %copy-start.1 = (f32[1,64,16,256]{3,2,1,0:T(8,128)}, f32[1,64,16,256]{3,2,1,0:T(8,128)S(1)}, u32[]{:S(2)}) copy-start(f32[1,64,16,256]{3,2,1,0:T(8,128)S(1)} %fusion.10) | copy-start | bytes 3145732

commit v19 on v17

--- a/solution.py
+++ b/solution.py
@@ -162,7 +162,7 @@
     )
 
     ocean_rows = returned
-    for target in sorted(range(last), reverse=True):
+    for target in sorted(range(last), key=lambda t: (t + 1) % last):
         ocean_rows = ocean_rows + lax.ppermute(returned, "comp", [(last, target)])
     ocean_rows = ocean_rows.reshape(rows, width)
     reply = jnp.einsum(

time: 65.5 us -> 65.9 us (level)
  the two profiles are of different devices: /device:TPU:65 before, /device:TPU:1 now
where the time goes in v19:
time: 65.9 us; the launch traced here: 65.4 us
  starting transfers between devices  24.5 us (37%)
  waiting for transfers between devices  19.7 us (30%)
  matrix products  7.09 us (11%)
  Pallas kernels  6.45 us (10%)
  other arithmetic  4.38 us (7%)
  local copies, waits for them, and re-layouts  2.32 us (4%)
  between operations  0.95 us (1%)
    all_to_all x1, waiting for transfers between devices, body(): came_back = lax.all_to_all(reply, 'band', 0, 0, tiled=True)  8.66 us
    all_to_all x1, starting transfers between devices, body(): received = lax.all_to_all(sending, 'band', 0, 0, tiled=True)  8.58 us
    ppermute x3, waiting for transfers between devices, body(): ocean_rows = ocean_rows + lax.ppermute(returned, 'comp', [(last, target)])  8.07 us
    pallas_call x1, Pallas kernels, diffuse(): pl.pallas_call(_diffusion_kernel, out_shape=jax.ShapeDtypeStruct((rows, l...  6.45 us
    all_to_all x1, starting transfers between devices, body(): came_back = lax.all_to_all(reply, 'band', 0, 0, tiled=True)  5.08 us
    dot_general x1, matrix products, body(): jnp.einsum('rfc,rcd->rfd', surface_layers, weights_local, preferred_eleme...  4.76 us
    ppermute x1, starting transfers between devices, diffuse(): above = lax.ppermute(comb[rows - halo:], 'band', forward)  3.42 us
    all_to_all x1, waiting for transfers between devices, body(): received = lax.all_to_all(sending, 'band', 0, 0, tiled=True)  2.95 us
  transfers between devices with their start and end apart: 10, of which 3 were waited for; matrix products, arithmetic and copies ran while one was open for 4% of the time, Pallas kernels for 10%

profile of v19, /device:TPU:1, one launch (start us, length us, event | category | flops | bytes accessed | tf_op | source)
XLA Modules:
  0.0 65.4 jit_solution(8158787230608550152)
XLA Ops:
  0.6 0.9 %fusion.5 = f32[64]{0:T(128)S(1)} fusion(s32[64]{0:T(128)} %bitcast.55), kind=kOutput, calls=%fused_computation.13 | convolution fusion | flops 286656 | bytes 512 | tf_op jit(solution)/shard_map/dot_general | solution.py:124
  1.5 0.7 %fusion.16 = f32[64,32]{0,1:T(8,128)S(1)} fusion(s32[64]{0:T(128)} %bitcast.56), kind=kLoop, calls=%fused_computation.39 | loop fusion | flops 4096 | bytes 8448 | tf_op jit(solution)/shard_map/convert_element_type | solution.py:119
  2.2 0.7 %convert_bitcast_fusion = f32[64]{0:T(128)S(1)} fusion(s32[1,64]{1,0:T(1,128)} %param.14), kind=kLoop, calls=%fused_computation.44 | loop fusion | flops 64 | bytes 512 | tf_op jit(solution)/shard_map/convert_element_type | solution.py:135
  2.9 4.8 %conditional.2 = (f32[64,1024]{1,0:T(8,128)S(1)}) conditional(s32[]{:T(128)} %convert_element_type.100, (f32[1,64,16,256]{3,2,1,0:T(8,128)}, bf16[64,256,256]{2,1,0:T(8,128)(2,1)}) %tuple.37, () %tuple.27), branch_computations={%region_1.0_spmd, %region_2.0_spmd} | conditional | flops 33554432 | bytes 9306120 | solution.py:110
  2.9 4.8 %fusion.1 = f32[64,4,256]{2,1,0:T(4,128)S(1)} fusion(bf16[64,256,256]{2,1,0:T(8,128)(2,1)} %get-tuple-element.33, f32[1,64,16,256]{3,2,1,0:T(8,128)} %get-tuple-element.32), kind=kOutput, calls=%fused_computation.2 | convolution fusion | flops 33554432 | bytes 8781824 | tf_op jit(solution)/shard_map/cond/branch_0_fun/rfc,rcd->rfd/dot_general | solution.py:113
  7.6 0.1 copy.20
  7.7 0.0 copy-start.2
  7.7 0.0 copy-start
  7.7 0.1 broadcast_in_dim.12
  7.8 0.6 convolution_convert_fusion.1
  8.4 0.9 %copy.17 = f16[32,4,1152]{2,1,0:T(4,128)(2,1)} copy(f16[32,4,1152]{2,0,1:T(8,128)(2,1)S(1)} %convolution_convert_fusion.1) | data formatting | bytes 589824 | tf_op jit(solution)/shard_map/convert_element_type | solution.py:138
  9.3 8.6 %all-to-all-start = ((f16[32,4,1152]{2,1,0:T(4,128)(2,1)}), f16[32,4,1152]{2,1,0:T(4,128)(2,1)S(1)}, u32[]{:S(2)}, u32[]{:S(2)}) async-start(f16[32,4,1152]{2,1,0:T(4,128)(2,1)} %copy.17), calls=%async_computation | async-start | bytes 589824 | tf_op jit(solution)/shard_map/all_to_all | solution.py:139
  18.0 2.1 %collective-permute-start.1 = (f32[4,17,256]{2,1,0:T(8,128)S(1)}, f32[4,17,256]{2,1,0:T(8,128)S(1)}, u32[]{:S(2)}, u32[]{:S(2)}) collective-permute-start(f32[4,17,256]{2,1,0:T(8,128)S(1)} %get-tuple-element.40), channel_id=1, source_target_pairs={{1,0},{2,1},{3,2},{4,3},{5,4},{6,5},{7,6},{8,7},{9,8},{10,9},{11,1... | collective-permute-start | bytes 208904 | tf_op jit(solution)/shard_map/ppermute | solution.py:82
  20.2 3.4 %collective-permute-start = (f32[4,17,256]{2,1,0:T(8,128)S(1)}, f32[4,17,256]{2,1,0:T(8,128)S(1)}, u32[]{:S(2)}, u32[]{:S(2)}) collective-permute-start(f32[4,17,256]{2,1,0:T(8,128)S(1)} %get-tuple-element.39), channel_id=1, source_target_pairs={{0,1},{1,2},{2,3},{3,4},{4,5},{5,6},{6,7},{7,8},{8,9},{9,10},{10,1... | collective-permute-start | bytes 208904 | tf_op jit(solution)/shard_map/ppermute | solution.py:81
  23.6 0.6 pad_add_fusion.bounds_ref
  24.2 2.9 %all-to-all-done = f16[32,4,1152]{2,1,0:T(4,128)(2,1)S(1)} async-done(((f16[32,4,1152]{2,1,0:T(4,128)(2,1)}), f16[32,4,1152]{2,1,0:T(4,128)(2,1)S(1)}, u32[]{:S(2)}, u32[]{:S(2)}) %all-to-all-start) | async-done | bytes 294944 | tf_op jit(solution)/shard_map/all_to_all | solution.py:139
  27.1 0.1 reshape.121
  27.2 0.1 convert_reduce_fusion
  27.3 0.4 fusion.4
  27.7 1.3 %collective-permute-start.4 = (f16[64,1024]{1,0:T(8,128)(2,1)S(1)}, f16[64,1024]{1,0:T(8,128)(2,1)S(1)}, u32[]{:S(2)}, u32[]{:S(2)}) collective-permute-start(f16[64,1024]{1,0:T(8,128)(2,1)S(1)} %fusion.4), channel_id=1, source_target_pairs={{0,96},{1,97},{2,98},{3,99},{4,100},{5,101},{6,102},{7,103},{8,104... | collective-permute-start | bytes 393224 | tf_op jit(solution)/shard_map/ppermute | solution.py:148
  29.0 0.7 %collective-permute-start.3 = (f16[64,1024]{1,0:T(8,128)(2,1)S(1)}, f16[64,1024]{1,0:T(8,128)(2,1)S(1)}, u32[]{:S(2)}, u32[]{:S(2)}) collective-permute-start(f16[64,1024]{1,0:T(8,128)(2,1)S(1)} %fusion.4), channel_id=1, source_target_pairs={{32,96},{33,97},{34,98},{35,99},{36,100},{37,101},{38,102},{39,103... | collective-permute-start | bytes 393224 | tf_op jit(solution)/shard_map/ppermute | solution.py:148
  29.7 0.7 %collective-permute-start.2 = (f16[64,1024]{1,0:T(8,128)(2,1)S(1)}, f16[64,1024]{1,0:T(8,128)(2,1)S(1)}, u32[]{:S(2)}, u32[]{:S(2)}) collective-permute-start(f16[64,1024]{1,0:T(8,128)(2,1)S(1)} %fusion.4), channel_id=1, source_target_pairs={{64,96},{65,97},{66,98},{67,99},{68,100},{69,101},{70,102},{71,103... | collective-permute-start | bytes 393224 | tf_op jit(solution)/shard_map/ppermute | solution.py:148
  30.4 0.0 collective-permute-done.1
  30.4 0.0 collective-permute-done
  30.4 1.4 %pad_maximum_fusion.p_ref = f32[72,17,256]{2,1,0:T(8,128)} fusion(f32[4,17,256]{2,1,0:T(8,128)S(1)} %collective-permute-done.1, f32[64,1,256]{2,1,0:T(1,128)S(1)} %broadcast_in_dim_squeeze.4, f32[64,16,256]{2,1,0:T(8,128)S(1)} %bitcast.46, f32[4,17,256]{2,1,0:T(8,128)S(1)} %collective-permute-done), kind=kLoop, calls=%fused_computation.6 | loop fusion | flops 940032 | bytes 2506752 | tf_op jit(solution)/shard_map/concatenate | solution.py:83
  31.8 6.4 %shard_map.68 = f32[64,16,256]{2,1,0:T(8,128)S(1)} custom-call(s32[2]{0:T(128)} %pad_add_fusion.bounds_ref, f32[72,17,256]{2,1,0:T(8,128)} %pad_maximum_fusion.p_ref), custom_call_target="tpu_custom_call" | custom-call | tf_op jit(solution)/shard_map/pallas_call | solution.py:87
  38.2 0.0 collective-permute-done.4
  38.2 0.0 collective-permute-done.3
  38.2 0.0 collective-permute-done.2
  38.3 0.1 add_select_fusion
  38.3 0.1 reshape.122
  38.5 0.1 conditional.3
  38.5 0.7 %collective-permute-start.7 = (bf16[64,4,256]{2,1,0:T(4,128)(2,1)S(1)}, bf16[64,4,256]{2,1,0:T(4,128)(2,1)S(1)}, u32[]{:S(2)}, u32[]{:S(2)}) collective-permute-start(bf16[64,4,256]{2,1,0:T(4,128)(2,1)S(1)} %get-tuple-element.44), channel_id=1, source_target_pairs={{96,32},{97,33},{98,34},{99,35},{100,36},{101,37},{102,38},{103,39... | collective-permute-start | bytes 393224 | tf_op jit(solution)/shard_map/ppermute | solution.py:166
  39.2 1.3 %collective-permute-start.6 = (bf16[64,4,256]{2,1,0:T(4,128)(2,1)S(1)}, bf16[64,4,256]{2,1,0:T(4,128)(2,1)S(1)}, u32[]{:S(2)}, u32[]{:S(2)}) collective-permute-start(bf16[64,4,256]{2,1,0:T(4,128)(2,1)S(1)} %get-tuple-element.44), channel_id=1, source_target_pairs={{96,0},{97,1},{98,2},{99,3},{100,4},{101,5},{102,6},{103,7},{104,8... | collective-permute-start | bytes 393224 | tf_op jit(solution)/shard_map/ppermute | solution.py:166
  40.5 0.7 %collective-permute-start.5 = (bf16[64,4,256]{2,1,0:T(4,128)(2,1)S(1)}, bf16[64,4,256]{2,1,0:T(4,128)(2,1)S(1)}, u32[]{:S(2)}, u32[]{:S(2)}) collective-permute-start(bf16[64,4,256]{2,1,0:T(4,128)(2,1)S(1)} %get-tuple-element.44), channel_id=1, source_target_pairs={{96,64},{97,65},{98,66},{99,67},{100,68},{101,69},{102,70},{103,71... | collective-permute-start | bytes 393224 | tf_op jit(solution)/shard_map/ppermute | solution.py:166
  41.2 0.0 collective-permute-done.7
  41.2 8.1 %collective-permute-done.6 = bf16[64,4,256]{2,1,0:T(4,128)(2,1)S(1)} collective-permute-done((bf16[64,4,256]{2,1,0:T(4,128)(2,1)S(1)}, bf16[64,4,256]{2,1,0:T(4,128)(2,1)S(1)}, u32[]{:S(2)}, u32[]{:S(2)}) %collective-permute-start.6) | collective-permute-done | bytes 131104 | tf_op jit(solution)/shard_map/ppermute | solution.py:166
  49.3 0.0 collective-permute-done.5
  49.3 0.3 convolution_convert_fusion.2
  49.6 0.8 %reshape.124 = bf16[32,4,1024]{2,1,0:T(4,128)(2,1)} reshape(bf16[128,1024]{1,0:T(8,128)(2,1)S(1)} %convolution_convert_fusion.2) | data formatting | bytes 524288 | tf_op jit(solution)/shard_map/reshape | solution.py:171
  50.4 5.1 %all-to-all-start.1 = ((bf16[32,4,1024]{2,1,0:T(4,128)(2,1)}), bf16[32,4,1024]{2,1,0:T(4,128)(2,1)S(1)}, u32[]{:S(2)}, u32[]{:S(2)}) async-start(bf16[32,4,1024]{2,1,0:T(4,128)(2,1)} %reshape.124), calls=%async_computation.1 | async-start | bytes 524288 | tf_op jit(solution)/shard_map/all_to_all | solution.py:172
  55.5 0.1 copy.30
  55.6 0.1 fusion.10
  55.7 0.0 copy-start.1
  55.7 8.7 %all-to-all-done.1 = bf16[32,4,1024]{2,1,0:T(4,128)(2,1)S(1)} async-done(((bf16[32,4,1024]{2,1,0:T(4,128)(2,1)}), bf16[32,4,1024]{2,1,0:T(4,128)(2,1)S(1)}, u32[]{:S(2)}, u32[]{:S(2)}) %all-to-all-start.1) | async-done | bytes 262176 | tf_op jit(solution)/shard_map/all_to_all | solution.py:172
  64.4 0.2 fusion.3
  64.6 0.1 reshape.125
  64.7 0.7 %select_bitcast_fusion = bf16[1,64,4,256]{3,2,1,0:T(4,128)(2,1)} fusion(bf16[64,4,256]{2,1,0:T(4,128)(2,1)S(1)} %get-tuple-element.44, bf16[64,4,256]{2,1,0:T(4,128)(2,1)S(1)} %reshape.125, pred[]{:T(512)S(6)} %eq.62), kind=kLoop, calls=%fused_computation.23 | loop fusion | flops 65536 | bytes 393217 | tf_op jit(solution)/shard_map/broadcast_in_dim | solution.py:178
  (11 shorter events, 0.2 us)
Async XLA Ops:
  7.7 10.2 %copy-start.2 = (f32[1,64,256]{2,1,0:T(8,128)S(1)}, f32[1,64,256]{2,1,0:T(8,128)}, u32[]{:S(2)}) copy-start(f32[1,64,256]{2,1,0:T(8,128)} %param.12) | copy-start | bytes 196612
  7.7 10.3 %copy-start = (f32[1,64,16,256]{3,2,1,0:T(8,128)S(1)}, f32[1,64,16,256]{3,2,1,0:T(8,128)}, u32[]{:S(2)}) copy-start(f32[1,64,16,256]{3,2,1,0:T(8,128)} %param.11) | copy-start | bytes 3145732
  9.3 17.8 %all-to-all-start = ((f16[32,4,1152]{2,1,0:T(4,128)(2,1)}), f16[32,4,1152]{2,1,0:T(4,128)(2,1)S(1)}, u32[]{:S(2)}, u32[]{:S(2)}) async-start(f16[32,4,1152]{2,1,0:T(4,128)(2,1)} %copy.17), calls=%async_computation | async-start | bytes 589824 | tf_op jit(solution)/shard_map/all_to_all | solution.py:139
  18.0 12.3 %collective-permute-start.1 = (f32[4,17,256]{2,1,0:T(8,128)S(1)}, f32[4,17,256]{2,1,0:T(8,128)S(1)}, u32[]{:S(2)}, u32[]{:S(2)}) collective-permute-start(f32[4,17,256]{2,1,0:T(8,128)S(1)} %get-tuple-element.40), channel_id=1, source_target_pairs={{1,0},{2,1},{3,2},{4,3},{5,4},{6,5},{7,6},{8,7},{9,8},{10,9},{11,1... | collective-permute-start | bytes 208904 | tf_op jit(solution)/shard_map/ppermute | solution.py:82
  20.2 10.2 %collective-permute-start = (f32[4,17,256]{2,1,0:T(8,128)S(1)}, f32[4,17,256]{2,1,0:T(8,128)S(1)}, u32[]{:S(2)}, u32[]{:S(2)}) collective-permute-start(f32[4,17,256]{2,1,0:T(8,128)S(1)} %get-tuple-element.39), channel_id=1, source_target_pairs={{0,1},{1,2},{2,3},{3,4},{4,5},{5,6},{6,7},{7,8},{8,9},{9,10},{10,1... | collective-permute-start | bytes 208904 | tf_op jit(solution)/shard_map/ppermute | solution.py:81
  27.7 10.5 %collective-permute-start.4 = (f16[64,1024]{1,0:T(8,128)(2,1)S(1)}, f16[64,1024]{1,0:T(8,128)(2,1)S(1)}, u32[]{:S(2)}, u32[]{:S(2)}) collective-permute-start(f16[64,1024]{1,0:T(8,128)(2,1)S(1)} %fusion.4), channel_id=1, source_target_pairs={{0,96},{1,97},{2,98},{3,99},{4,100},{5,101},{6,102},{7,103},{8,104... | collective-permute-start | bytes 393224 | tf_op jit(solution)/shard_map/ppermute | solution.py:148
  29.0 9.2 %collective-permute-start.3 = (f16[64,1024]{1,0:T(8,128)(2,1)S(1)}, f16[64,1024]{1,0:T(8,128)(2,1)S(1)}, u32[]{:S(2)}, u32[]{:S(2)}) collective-permute-start(f16[64,1024]{1,0:T(8,128)(2,1)S(1)} %fusion.4), channel_id=1, source_target_pairs={{32,96},{33,97},{34,98},{35,99},{36,100},{37,101},{38,102},{39,103... | collective-permute-start | bytes 393224 | tf_op jit(solution)/shard_map/ppermute | solution.py:148
  29.7 8.6 %collective-permute-start.2 = (f16[64,1024]{1,0:T(8,128)(2,1)S(1)}, f16[64,1024]{1,0:T(8,128)(2,1)S(1)}, u32[]{:S(2)}, u32[]{:S(2)}) collective-permute-start(f16[64,1024]{1,0:T(8,128)(2,1)S(1)} %fusion.4), channel_id=1, source_target_pairs={{64,96},{65,97},{66,98},{67,99},{68,100},{69,101},{70,102},{71,103... | collective-permute-start | bytes 393224 | tf_op jit(solution)/shard_map/ppermute | solution.py:148
  38.5 2.7 %collective-permute-start.7 = (bf16[64,4,256]{2,1,0:T(4,128)(2,1)S(1)}, bf16[64,4,256]{2,1,0:T(4,128)(2,1)S(1)}, u32[]{:S(2)}, u32[]{:S(2)}) collective-permute-start(bf16[64,4,256]{2,1,0:T(4,128)(2,1)S(1)} %get-tuple-element.44), channel_id=1, source_target_pairs={{96,32},{97,33},{98,34},{99,35},{100,36},{101,37},{102,38},{103,39... | collective-permute-start | bytes 393224 | tf_op jit(solution)/shard_map/ppermute | solution.py:166
  39.2 10.1 %collective-permute-start.6 = (bf16[64,4,256]{2,1,0:T(4,128)(2,1)S(1)}, bf16[64,4,256]{2,1,0:T(4,128)(2,1)S(1)}, u32[]{:S(2)}, u32[]{:S(2)}) collective-permute-start(bf16[64,4,256]{2,1,0:T(4,128)(2,1)S(1)} %get-tuple-element.44), channel_id=1, source_target_pairs={{96,0},{97,1},{98,2},{99,3},{100,4},{101,5},{102,6},{103,7},{104,8... | collective-permute-start | bytes 393224 | tf_op jit(solution)/shard_map/ppermute | solution.py:166
  40.5 8.8 %collective-permute-start.5 = (bf16[64,4,256]{2,1,0:T(4,128)(2,1)S(1)}, bf16[64,4,256]{2,1,0:T(4,128)(2,1)S(1)}, u32[]{:S(2)}, u32[]{:S(2)}) collective-permute-start(bf16[64,4,256]{2,1,0:T(4,128)(2,1)S(1)} %get-tuple-element.44), channel_id=1, source_target_pairs={{96,64},{97,65},{98,66},{99,67},{100,68},{101,69},{102,70},{103,71... | collective-permute-start | bytes 393224 | tf_op jit(solution)/shard_map/ppermute | solution.py:166
  50.4 14.0 %all-to-all-start.1 = ((bf16[32,4,1024]{2,1,0:T(4,128)(2,1)}), bf16[32,4,1024]{2,1,0:T(4,128)(2,1)S(1)}, u32[]{:S(2)}, u32[]{:S(2)}) async-start(bf16[32,4,1024]{2,1,0:T(4,128)(2,1)} %reshape.124), calls=%async_computation.1 | async-start | bytes 524288 | tf_op jit(solution)/shard_map/all_to_all | solution.py:172
  55.7 9.7 %copy-start.1 = (f32[1,64,16,256]{3,2,1,0:T(8,128)}, f32[1,64,16,256]{3,2,1,0:T(8,128)S(1)}, u32[]{:S(2)}) copy-start(f32[1,64,16,256]{3,2,1,0:T(8,128)S(1)} %fusion.10) | copy-start | bytes 3145732

commit v20 on v19

--- a/solution.py
+++ b/solution.py
@@ -162,7 +162,7 @@
     )
 
     ocean_rows = returned
-    for target in sorted(range(last), key=lambda t: (t + 1) % last):
+    for target in (1, 2, 0):
         ocean_rows = ocean_rows + lax.ppermute(returned, "comp", [(last, target)])
     ocean_rows = ocean_rows.reshape(rows, width)
     reply = jnp.einsum(

time: 65.9 us -> 66.8 us (1.014)
  the two profiles are of different devices: /device:TPU:1 before, /device:TPU:33 now
where the time goes in v20:
time: 66.8 us; the launch traced here: 66.3 us
  starting transfers between devices  23.7 us (35%)
  waiting for transfers between devices  21.4 us (32%)
  matrix products  7.1 us (11%)
  Pallas kernels  6.45 us (10%)
  other arithmetic  4.39 us (7%)
  local copies, waits for them, and re-layouts  2.32 us (3%)
  between operations  0.95 us (1%)
    ppermute x3, waiting for transfers between devices, body(): ocean_rows = ocean_rows + lax.ppermute(returned, 'comp', [(last, target)])  9.81 us
    all_to_all x1, waiting for transfers between devices, body(): came_back = lax.all_to_all(reply, 'band', 0, 0, tiled=True)  8.66 us
    all_to_all x1, starting transfers between devices, body(): received = lax.all_to_all(sending, 'band', 0, 0, tiled=True)  7.76 us
    pallas_call x1, Pallas kernels, diffuse(): pl.pallas_call(_diffusion_kernel, out_shape=jax.ShapeDtypeStruct((rows, l...  6.45 us
    all_to_all x1, starting transfers between devices, body(): came_back = lax.all_to_all(reply, 'band', 0, 0, tiled=True)  5.07 us
    dot_general x1, matrix products, body(): jnp.einsum('rfc,rcd->rfd', surface_layers, weights_local, preferred_eleme...  4.76 us
    ppermute x1, starting transfers between devices, diffuse(): above = lax.ppermute(comb[rows - halo:], 'band', forward)  3.42 us
    all_to_all x1, waiting for transfers between devices, body(): received = lax.all_to_all(sending, 'band', 0, 0, tiled=True)  2.95 us
  transfers between devices with their start and end apart: 10, of which 3 were waited for; matrix products, arithmetic and copies ran while one was open for 4% of the time, Pallas kernels for 10%

profile of v20, /device:TPU:33, one launch (start us, length us, event | category | flops | bytes accessed | tf_op | source)
XLA Modules:
  0.0 66.3 jit_solution(12698424924231231580)
XLA Ops:
  0.6 0.9 %fusion.5 = f32[64]{0:T(128)S(1)} fusion(s32[64]{0:T(128)} %bitcast.55), kind=kOutput, calls=%fused_computation.13 | convolution fusion | flops 286656 | bytes 512 | tf_op jit(solution)/shard_map/dot_general | solution.py:124
  1.5 0.7 %fusion.16 = f32[64,32]{0,1:T(8,128)S(1)} fusion(s32[64]{0:T(128)} %bitcast.56), kind=kLoop, calls=%fused_computation.39 | loop fusion | flops 4096 | bytes 8448 | tf_op jit(solution)/shard_map/convert_element_type | solution.py:119
  2.2 0.7 convert_bitcast_fusion
  2.9 4.8 %conditional.2 = (f32[64,1024]{1,0:T(8,128)S(1)}) conditional(s32[]{:T(128)} %convert_element_type.100, (f32[1,64,16,256]{3,2,1,0:T(8,128)}, bf16[64,256,256]{2,1,0:T(8,128)(2,1)}) %tuple.37, () %tuple.27), branch_computations={%region_1.0_spmd, %region_2.0_spmd} | conditional | flops 33554432 | bytes 9306120 | solution.py:110
  2.9 4.8 %fusion.1 = f32[64,4,256]{2,1,0:T(4,128)S(1)} fusion(bf16[64,256,256]{2,1,0:T(8,128)(2,1)} %get-tuple-element.33, f32[1,64,16,256]{3,2,1,0:T(8,128)} %get-tuple-element.32), kind=kOutput, calls=%fused_computation.2 | convolution fusion | flops 33554432 | bytes 8781824 | tf_op jit(solution)/shard_map/cond/branch_0_fun/rfc,rcd->rfd/dot_general | solution.py:113
  7.6 0.1 copy.20
  7.7 0.0 copy-start.2
  7.7 0.0 copy-start
  7.7 0.1 broadcast_in_dim.12
  7.8 0.6 convolution_convert_fusion.1
  8.4 0.9 %copy.17 = f16[32,4,1152]{2,1,0:T(4,128)(2,1)} copy(f16[32,4,1152]{2,0,1:T(8,128)(2,1)S(1)} %convolution_convert_fusion.1) | data formatting | bytes 589824 | tf_op jit(solution)/shard_map/convert_element_type | solution.py:138
  9.3 7.8 %all-to-all-start = ((f16[32,4,1152]{2,1,0:T(4,128)(2,1)}), f16[32,4,1152]{2,1,0:T(4,128)(2,1)S(1)}, u32[]{:S(2)}, u32[]{:S(2)}) async-start(f16[32,4,1152]{2,1,0:T(4,128)(2,1)} %copy.17), calls=%async_computation | async-start | bytes 589824 | tf_op jit(solution)/shard_map/all_to_all | solution.py:139
  17.2 2.1 %collective-permute-start.1 = (f32[4,17,256]{2,1,0:T(8,128)S(1)}, f32[4,17,256]{2,1,0:T(8,128)S(1)}, u32[]{:S(2)}, u32[]{:S(2)}) collective-permute-start(f32[4,17,256]{2,1,0:T(8,128)S(1)} %get-tuple-element.40), channel_id=1, source_target_pairs={{1,0},{2,1},{3,2},{4,3},{5,4},{6,5},{7,6},{8,7},{9,8},{10,9},{11,1... | collective-permute-start | bytes 208904 | tf_op jit(solution)/shard_map/ppermute | solution.py:82
  19.4 3.4 %collective-permute-start = (f32[4,17,256]{2,1,0:T(8,128)S(1)}, f32[4,17,256]{2,1,0:T(8,128)S(1)}, u32[]{:S(2)}, u32[]{:S(2)}) collective-permute-start(f32[4,17,256]{2,1,0:T(8,128)S(1)} %get-tuple-element.39), channel_id=1, source_target_pairs={{0,1},{1,2},{2,3},{3,4},{4,5},{5,6},{6,7},{7,8},{8,9},{9,10},{10,1... | collective-permute-start | bytes 208904 | tf_op jit(solution)/shard_map/ppermute | solution.py:81
  22.8 0.6 pad_add_fusion.bounds_ref
  23.4 2.9 %all-to-all-done = f16[32,4,1152]{2,1,0:T(4,128)(2,1)S(1)} async-done(((f16[32,4,1152]{2,1,0:T(4,128)(2,1)}), f16[32,4,1152]{2,1,0:T(4,128)(2,1)S(1)}, u32[]{:S(2)}, u32[]{:S(2)}) %all-to-all-start) | async-done | bytes 294944 | tf_op jit(solution)/shard_map/all_to_all | solution.py:139
  26.3 0.1 reshape.121
  26.4 0.1 convert_reduce_fusion
  26.5 0.4 fusion.4
  26.9 0.7 %collective-permute-start.4 = (f16[64,1024]{1,0:T(8,128)(2,1)S(1)}, f16[64,1024]{1,0:T(8,128)(2,1)S(1)}, u32[]{:S(2)}, u32[]{:S(2)}) collective-permute-start(f16[64,1024]{1,0:T(8,128)(2,1)S(1)} %fusion.4), channel_id=1, source_target_pairs={{0,96},{1,97},{2,98},{3,99},{4,100},{5,101},{6,102},{7,103},{8,104... | collective-permute-start | bytes 393224 | tf_op jit(solution)/shard_map/ppermute | solution.py:148
  27.6 1.3 %collective-permute-start.3 = (f16[64,1024]{1,0:T(8,128)(2,1)S(1)}, f16[64,1024]{1,0:T(8,128)(2,1)S(1)}, u32[]{:S(2)}, u32[]{:S(2)}) collective-permute-start(f16[64,1024]{1,0:T(8,128)(2,1)S(1)} %fusion.4), channel_id=1, source_target_pairs={{32,96},{33,97},{34,98},{35,99},{36,100},{37,101},{38,102},{39,103... | collective-permute-start | bytes 393224 | tf_op jit(solution)/shard_map/ppermute | solution.py:148
  28.9 0.7 %collective-permute-start.2 = (f16[64,1024]{1,0:T(8,128)(2,1)S(1)}, f16[64,1024]{1,0:T(8,128)(2,1)S(1)}, u32[]{:S(2)}, u32[]{:S(2)}) collective-permute-start(f16[64,1024]{1,0:T(8,128)(2,1)S(1)} %fusion.4), channel_id=1, source_target_pairs={{64,96},{65,97},{66,98},{67,99},{68,100},{69,101},{70,102},{71,103... | collective-permute-start | bytes 393224 | tf_op jit(solution)/shard_map/ppermute | solution.py:148
  29.5 0.0 collective-permute-done.1
  29.6 0.0 collective-permute-done
  29.6 1.4 %pad_maximum_fusion.p_ref = f32[72,17,256]{2,1,0:T(8,128)} fusion(f32[4,17,256]{2,1,0:T(8,128)S(1)} %collective-permute-done.1, f32[64,1,256]{2,1,0:T(1,128)S(1)} %broadcast_in_dim_squeeze.4, f32[64,16,256]{2,1,0:T(8,128)S(1)} %bitcast.46, f32[4,17,256]{2,1,0:T(8,128)S(1)} %collective-permute-done), kind=kLoop, calls=%fused_computation.6 | loop fusion | flops 940032 | bytes 2506752 | tf_op jit(solution)/shard_map/concatenate | solution.py:83
  31.0 6.4 %shard_map.68 = f32[64,16,256]{2,1,0:T(8,128)S(1)} custom-call(s32[2]{0:T(128)} %pad_add_fusion.bounds_ref, f32[72,17,256]{2,1,0:T(8,128)} %pad_maximum_fusion.p_ref), custom_call_target="tpu_custom_call" | custom-call | tf_op jit(solution)/shard_map/pallas_call | solution.py:87
  37.4 0.0 collective-permute-done.4
  37.4 0.0 collective-permute-done.3
  37.4 0.0 collective-permute-done.2
  37.4 0.1 add_select_fusion
  37.5 0.1 reshape.122
  37.7 0.1 conditional.3
  37.7 0.7 %collective-permute-start.7 = (bf16[64,4,256]{2,1,0:T(4,128)(2,1)S(1)}, bf16[64,4,256]{2,1,0:T(4,128)(2,1)S(1)}, u32[]{:S(2)}, u32[]{:S(2)}) collective-permute-start(bf16[64,4,256]{2,1,0:T(4,128)(2,1)S(1)} %get-tuple-element.44), channel_id=1, source_target_pairs={{96,0},{97,1},{98,2},{99,3},{100,4},{101,5},{102,6},{103,7},{104,8... | collective-permute-start | bytes 393224 | tf_op jit(solution)/shard_map/ppermute | solution.py:166
  38.4 0.7 %collective-permute-start.6 = (bf16[64,4,256]{2,1,0:T(4,128)(2,1)S(1)}, bf16[64,4,256]{2,1,0:T(4,128)(2,1)S(1)}, u32[]{:S(2)}, u32[]{:S(2)}) collective-permute-start(bf16[64,4,256]{2,1,0:T(4,128)(2,1)S(1)} %get-tuple-element.44), channel_id=1, source_target_pairs={{96,64},{97,65},{98,66},{99,67},{100,68},{101,69},{102,70},{103,71... | collective-permute-start | bytes 393224 | tf_op jit(solution)/shard_map/ppermute | solution.py:166
  39.1 1.3 %collective-permute-start.5 = (bf16[64,4,256]{2,1,0:T(4,128)(2,1)S(1)}, bf16[64,4,256]{2,1,0:T(4,128)(2,1)S(1)}, u32[]{:S(2)}, u32[]{:S(2)}) collective-permute-start(bf16[64,4,256]{2,1,0:T(4,128)(2,1)S(1)} %get-tuple-element.44), channel_id=1, source_target_pairs={{96,32},{97,33},{98,34},{99,35},{100,36},{101,37},{102,38},{103,39... | collective-permute-start | bytes 393224 | tf_op jit(solution)/shard_map/ppermute | solution.py:166
  40.4 0.0 collective-permute-done.7
  40.4 0.0 collective-permute-done.6
  40.4 9.8 %collective-permute-done.5 = bf16[64,4,256]{2,1,0:T(4,128)(2,1)S(1)} collective-permute-done((bf16[64,4,256]{2,1,0:T(4,128)(2,1)S(1)}, bf16[64,4,256]{2,1,0:T(4,128)(2,1)S(1)}, u32[]{:S(2)}, u32[]{:S(2)}) %collective-permute-start.5) | collective-permute-done | bytes 131104 | tf_op jit(solution)/shard_map/ppermute | solution.py:166
  50.3 0.3 convolution_convert_fusion.2
  50.5 0.8 %reshape.124 = bf16[32,4,1024]{2,1,0:T(4,128)(2,1)} reshape(bf16[128,1024]{1,0:T(8,128)(2,1)S(1)} %convolution_convert_fusion.2) | data formatting | bytes 524288 | tf_op jit(solution)/shard_map/reshape | solution.py:171
  51.4 5.1 %all-to-all-start.1 = ((bf16[32,4,1024]{2,1,0:T(4,128)(2,1)}), bf16[32,4,1024]{2,1,0:T(4,128)(2,1)S(1)}, u32[]{:S(2)}, u32[]{:S(2)}) async-start(bf16[32,4,1024]{2,1,0:T(4,128)(2,1)} %reshape.124), calls=%async_computation.1 | async-start | bytes 524288 | tf_op jit(solution)/shard_map/all_to_all | solution.py:172
  56.4 0.1 copy.30
  56.5 0.1 fusion.10
  56.6 0.0 copy-start.1
  56.6 8.7 %all-to-all-done.1 = bf16[32,4,1024]{2,1,0:T(4,128)(2,1)S(1)} async-done(((bf16[32,4,1024]{2,1,0:T(4,128)(2,1)}), bf16[32,4,1024]{2,1,0:T(4,128)(2,1)S(1)}, u32[]{:S(2)}, u32[]{:S(2)}) %all-to-all-start.1) | async-done | bytes 262176 | tf_op jit(solution)/shard_map/all_to_all | solution.py:172
  65.3 0.2 fusion.3
  65.5 0.1 reshape.125
  65.6 0.7 %select_bitcast_fusion = bf16[1,64,4,256]{3,2,1,0:T(4,128)(2,1)} fusion(bf16[64,4,256]{2,1,0:T(4,128)(2,1)S(1)} %get-tuple-element.44, bf16[64,4,256]{2,1,0:T(4,128)(2,1)S(1)} %reshape.125, pred[]{:T(512)S(6)} %eq.62), kind=kLoop, calls=%fused_computation.23 | loop fusion | flops 65536 | bytes 393217 | tf_op jit(solution)/shard_map/broadcast_in_dim | solution.py:178
  (11 shorter events, 0.2 us)
Async XLA Ops:
  7.7 9.4 %copy-start.2 = (f32[1,64,256]{2,1,0:T(8,128)S(1)}, f32[1,64,256]{2,1,0:T(8,128)}, u32[]{:S(2)}) copy-start(f32[1,64,256]{2,1,0:T(8,128)} %param.12) | copy-start | bytes 196612
  7.7 9.5 %copy-start = (f32[1,64,16,256]{3,2,1,0:T(8,128)S(1)}, f32[1,64,16,256]{3,2,1,0:T(8,128)}, u32[]{:S(2)}) copy-start(f32[1,64,16,256]{3,2,1,0:T(8,128)} %param.11) | copy-start | bytes 3145732
  9.3 17.0 %all-to-all-start = ((f16[32,4,1152]{2,1,0:T(4,128)(2,1)}), f16[32,4,1152]{2,1,0:T(4,128)(2,1)S(1)}, u32[]{:S(2)}, u32[]{:S(2)}) async-start(f16[32,4,1152]{2,1,0:T(4,128)(2,1)} %copy.17), calls=%async_computation | async-start | bytes 589824 | tf_op jit(solution)/shard_map/all_to_all | solution.py:139
  17.2 12.3 %collective-permute-start.1 = (f32[4,17,256]{2,1,0:T(8,128)S(1)}, f32[4,17,256]{2,1,0:T(8,128)S(1)}, u32[]{:S(2)}, u32[]{:S(2)}) collective-permute-start(f32[4,17,256]{2,1,0:T(8,128)S(1)} %get-tuple-element.40), channel_id=1, source_target_pairs={{1,0},{2,1},{3,2},{4,3},{5,4},{6,5},{7,6},{8,7},{9,8},{10,9},{11,1... | collective-permute-start | bytes 208904 | tf_op jit(solution)/shard_map/ppermute | solution.py:82
  19.4 10.2 %collective-permute-start = (f32[4,17,256]{2,1,0:T(8,128)S(1)}, f32[4,17,256]{2,1,0:T(8,128)S(1)}, u32[]{:S(2)}, u32[]{:S(2)}) collective-permute-start(f32[4,17,256]{2,1,0:T(8,128)S(1)} %get-tuple-element.39), channel_id=1, source_target_pairs={{0,1},{1,2},{2,3},{3,4},{4,5},{5,6},{6,7},{7,8},{8,9},{9,10},{10,1... | collective-permute-start | bytes 208904 | tf_op jit(solution)/shard_map/ppermute | solution.py:81
  26.9 10.5 %collective-permute-start.4 = (f16[64,1024]{1,0:T(8,128)(2,1)S(1)}, f16[64,1024]{1,0:T(8,128)(2,1)S(1)}, u32[]{:S(2)}, u32[]{:S(2)}) collective-permute-start(f16[64,1024]{1,0:T(8,128)(2,1)S(1)} %fusion.4), channel_id=1, source_target_pairs={{0,96},{1,97},{2,98},{3,99},{4,100},{5,101},{6,102},{7,103},{8,104... | collective-permute-start | bytes 393224 | tf_op jit(solution)/shard_map/ppermute | solution.py:148
  27.6 9.9 %collective-permute-start.3 = (f16[64,1024]{1,0:T(8,128)(2,1)S(1)}, f16[64,1024]{1,0:T(8,128)(2,1)S(1)}, u32[]{:S(2)}, u32[]{:S(2)}) collective-permute-start(f16[64,1024]{1,0:T(8,128)(2,1)S(1)} %fusion.4), channel_id=1, source_target_pairs={{32,96},{33,97},{34,98},{35,99},{36,100},{37,101},{38,102},{39,103... | collective-permute-start | bytes 393224 | tf_op jit(solution)/shard_map/ppermute | solution.py:148
  28.9 8.6 %collective-permute-start.2 = (f16[64,1024]{1,0:T(8,128)(2,1)S(1)}, f16[64,1024]{1,0:T(8,128)(2,1)S(1)}, u32[]{:S(2)}, u32[]{:S(2)}) collective-permute-start(f16[64,1024]{1,0:T(8,128)(2,1)S(1)} %fusion.4), channel_id=1, source_target_pairs={{64,96},{65,97},{66,98},{67,99},{68,100},{69,101},{70,102},{71,103... | collective-permute-start | bytes 393224 | tf_op jit(solution)/shard_map/ppermute | solution.py:148
  37.7 2.7 %collective-permute-start.7 = (bf16[64,4,256]{2,1,0:T(4,128)(2,1)S(1)}, bf16[64,4,256]{2,1,0:T(4,128)(2,1)S(1)}, u32[]{:S(2)}, u32[]{:S(2)}) collective-permute-start(bf16[64,4,256]{2,1,0:T(4,128)(2,1)S(1)} %get-tuple-element.44), channel_id=1, source_target_pairs={{96,0},{97,1},{98,2},{99,3},{100,4},{101,5},{102,6},{103,7},{104,8... | collective-permute-start | bytes 393224 | tf_op jit(solution)/shard_map/ppermute | solution.py:166
  38.4 2.0 %collective-permute-start.6 = (bf16[64,4,256]{2,1,0:T(4,128)(2,1)S(1)}, bf16[64,4,256]{2,1,0:T(4,128)(2,1)S(1)}, u32[]{:S(2)}, u32[]{:S(2)}) collective-permute-start(bf16[64,4,256]{2,1,0:T(4,128)(2,1)S(1)} %get-tuple-element.44), channel_id=1, source_target_pairs={{96,64},{97,65},{98,66},{99,67},{100,68},{101,69},{102,70},{103,71... | collective-permute-start | bytes 393224 | tf_op jit(solution)/shard_map/ppermute | solution.py:166
  39.1 11.1 %collective-permute-start.5 = (bf16[64,4,256]{2,1,0:T(4,128)(2,1)S(1)}, bf16[64,4,256]{2,1,0:T(4,128)(2,1)S(1)}, u32[]{:S(2)}, u32[]{:S(2)}) collective-permute-start(bf16[64,4,256]{2,1,0:T(4,128)(2,1)S(1)} %get-tuple-element.44), channel_id=1, source_target_pairs={{96,32},{97,33},{98,34},{99,35},{100,36},{101,37},{102,38},{103,39... | collective-permute-start | bytes 393224 | tf_op jit(solution)/shard_map/ppermute | solution.py:166
  51.4 14.0 %all-to-all-start.1 = ((bf16[32,4,1024]{2,1,0:T(4,128)(2,1)}), bf16[32,4,1024]{2,1,0:T(4,128)(2,1)S(1)}, u32[]{:S(2)}, u32[]{:S(2)}) async-start(bf16[32,4,1024]{2,1,0:T(4,128)(2,1)} %reshape.124), calls=%async_computation.1 | async-start | bytes 524288 | tf_op jit(solution)/shard_map/all_to_all | solution.py:172
  56.6 9.7 %copy-start.1 = (f32[1,64,16,256]{3,2,1,0:T(8,128)}, f32[1,64,16,256]{3,2,1,0:T(8,128)S(1)}, u32[]{:S(2)}) copy-start(f32[1,64,16,256]{3,2,1,0:T(8,128)S(1)} %fusion.10) | copy-start | bytes 3145732

commit v21 on v17

--- a/solution.py
+++ b/solution.py
@@ -144,7 +144,7 @@
     last = n_sections - 1
     scaled = (COUPLING * partial).astype(LINK)
     heating = scaled.astype(jnp.float32)
-    for source in sorted(range(last), reverse=True):
+    for source in (1, 2, 0):
         heating = heating + lax.ppermute(scaled, "comp", [(source, last)]).astype(jnp.float32)
 
     fields = diffuse(layer_temp, diffusivity)

time: 65.5 us -> 65.5 us (level)
  no operation moved by 1% of the time
where the time goes in v21:
time: 65.5 us; the launch traced here: 65 us
  starting transfers between devices  23.7 us (36%)
  waiting for transfers between devices  20.1 us (31%)
  matrix products  7.1 us (11%)
  Pallas kernels  6.45 us (10%)
  other arithmetic  4.39 us (7%)
  local copies, waits for them, and re-layouts  2.32 us (4%)
  between operations  0.95 us (1%)
    all_to_all x1, waiting for transfers between devices, body(): came_back = lax.all_to_all(reply, 'band', 0, 0, tiled=True)  8.66 us
    ppermute x3, waiting for transfers between devices, body(): ocean_rows = ocean_rows + lax.ppermute(returned, 'comp', [(last, target)])  8.47 us
    all_to_all x1, starting transfers between devices, body(): received = lax.all_to_all(sending, 'band', 0, 0, tiled=True)  7.76 us
    pallas_call x1, Pallas kernels, diffuse(): pl.pallas_call(_diffusion_kernel, out_shape=jax.ShapeDtypeStruct((rows, l...  6.45 us
    all_to_all x1, starting transfers between devices, body(): came_back = lax.all_to_all(reply, 'band', 0, 0, tiled=True)  5.07 us
    dot_general x1, matrix products, body(): jnp.einsum('rfc,rcd->rfd', surface_layers, weights_local, preferred_eleme...  4.76 us
    ppermute x1, starting transfers between devices, diffuse(): above = lax.ppermute(comb[rows - halo:], 'band', forward)  3.42 us
    all_to_all x1, waiting for transfers between devices, body(): received = lax.all_to_all(sending, 'band', 0, 0, tiled=True)  2.95 us
  transfers between devices with their start and end apart: 10, of which 3 were waited for; matrix products, arithmetic and copies ran while one was open for 4% of the time, Pallas kernels for 10%

profile of v21, /device:TPU:65, one launch (start us, length us, event | category | flops | bytes accessed | tf_op | source)
XLA Modules:
  0.0 65.0 jit_solution(8577855317007935606)
XLA Ops:
  0.6 0.9 %fusion.5 = f32[64]{0:T(128)S(1)} fusion(s32[64]{0:T(128)} %bitcast.55), kind=kOutput, calls=%fused_computation.13 | convolution fusion | flops 286656 | bytes 512 | tf_op jit(solution)/shard_map/dot_general | solution.py:124
  1.5 0.7 %fusion.16 = f32[64,32]{0,1:T(8,128)S(1)} fusion(s32[64]{0:T(128)} %bitcast.56), kind=kLoop, calls=%fused_computation.39 | loop fusion | flops 4096 | bytes 8448 | tf_op jit(solution)/shard_map/convert_element_type | solution.py:119
  2.2 0.7 %convert_bitcast_fusion = f32[64]{0:T(128)S(1)} fusion(s32[1,64]{1,0:T(1,128)} %param.14), kind=kLoop, calls=%fused_computation.44 | loop fusion | flops 64 | bytes 512 | tf_op jit(solution)/shard_map/convert_element_type | solution.py:135
  2.9 4.8 %conditional.2 = (f32[64,1024]{1,0:T(8,128)S(1)}) conditional(s32[]{:T(128)} %convert_element_type.100, (f32[1,64,16,256]{3,2,1,0:T(8,128)}, bf16[64,256,256]{2,1,0:T(8,128)(2,1)}) %tuple.37, () %tuple.27), branch_computations={%region_1.0_spmd, %region_2.0_spmd} | conditional | flops 33554432 | bytes 9306120 | solution.py:110
  2.9 4.8 %fusion.1 = f32[64,4,256]{2,1,0:T(4,128)S(1)} fusion(bf16[64,256,256]{2,1,0:T(8,128)(2,1)} %get-tuple-element.33, f32[1,64,16,256]{3,2,1,0:T(8,128)} %get-tuple-element.32), kind=kOutput, calls=%fused_computation.2 | convolution fusion | flops 33554432 | bytes 8781824 | tf_op jit(solution)/shard_map/cond/branch_0_fun/rfc,rcd->rfd/dot_general | solution.py:113
  7.6 0.1 copy.20
  7.7 0.0 copy-start.2
  7.7 0.0 copy-start
  7.7 0.1 broadcast_in_dim.12
  7.8 0.6 convolution_convert_fusion.1
  8.4 0.9 %copy.17 = f16[32,4,1152]{2,1,0:T(4,128)(2,1)} copy(f16[32,4,1152]{2,0,1:T(8,128)(2,1)S(1)} %convolution_convert_fusion.1) | data formatting | bytes 589824 | tf_op jit(solution)/shard_map/convert_element_type | solution.py:138
  9.3 7.8 %all-to-all-start = ((f16[32,4,1152]{2,1,0:T(4,128)(2,1)}), f16[32,4,1152]{2,1,0:T(4,128)(2,1)S(1)}, u32[]{:S(2)}, u32[]{:S(2)}) async-start(f16[32,4,1152]{2,1,0:T(4,128)(2,1)} %copy.17), calls=%async_computation | async-start | bytes 589824 | tf_op jit(solution)/shard_map/all_to_all | solution.py:139
  17.2 2.1 %collective-permute-start.1 = (f32[4,17,256]{2,1,0:T(8,128)S(1)}, f32[4,17,256]{2,1,0:T(8,128)S(1)}, u32[]{:S(2)}, u32[]{:S(2)}) collective-permute-start(f32[4,17,256]{2,1,0:T(8,128)S(1)} %get-tuple-element.40), channel_id=1, source_target_pairs={{1,0},{2,1},{3,2},{4,3},{5,4},{6,5},{7,6},{8,7},{9,8},{10,9},{11,1... | collective-permute-start | bytes 208904 | tf_op jit(solution)/shard_map/ppermute | solution.py:82
  19.4 3.4 %collective-permute-start = (f32[4,17,256]{2,1,0:T(8,128)S(1)}, f32[4,17,256]{2,1,0:T(8,128)S(1)}, u32[]{:S(2)}, u32[]{:S(2)}) collective-permute-start(f32[4,17,256]{2,1,0:T(8,128)S(1)} %get-tuple-element.39), channel_id=1, source_target_pairs={{0,1},{1,2},{2,3},{3,4},{4,5},{5,6},{6,7},{7,8},{8,9},{9,10},{10,1... | collective-permute-start | bytes 208904 | tf_op jit(solution)/shard_map/ppermute | solution.py:81
  22.8 0.6 pad_add_fusion.bounds_ref
  23.4 2.9 %all-to-all-done = f16[32,4,1152]{2,1,0:T(4,128)(2,1)S(1)} async-done(((f16[32,4,1152]{2,1,0:T(4,128)(2,1)}), f16[32,4,1152]{2,1,0:T(4,128)(2,1)S(1)}, u32[]{:S(2)}, u32[]{:S(2)}) %all-to-all-start) | async-done | bytes 294944 | tf_op jit(solution)/shard_map/all_to_all | solution.py:139
  26.3 0.1 reshape.121
  26.4 0.1 convert_reduce_fusion
  26.5 0.4 fusion.4
  26.9 0.7 %collective-permute-start.4 = (f16[64,1024]{1,0:T(8,128)(2,1)S(1)}, f16[64,1024]{1,0:T(8,128)(2,1)S(1)}, u32[]{:S(2)}, u32[]{:S(2)}) collective-permute-start(f16[64,1024]{1,0:T(8,128)(2,1)S(1)} %fusion.4), channel_id=1, source_target_pairs={{0,96},{1,97},{2,98},{3,99},{4,100},{5,101},{6,102},{7,103},{8,104... | collective-permute-start | bytes 393224 | tf_op jit(solution)/shard_map/ppermute | solution.py:148
  27.6 1.3 %collective-permute-start.3 = (f16[64,1024]{1,0:T(8,128)(2,1)S(1)}, f16[64,1024]{1,0:T(8,128)(2,1)S(1)}, u32[]{:S(2)}, u32[]{:S(2)}) collective-permute-start(f16[64,1024]{1,0:T(8,128)(2,1)S(1)} %fusion.4), channel_id=1, source_target_pairs={{64,96},{65,97},{66,98},{67,99},{68,100},{69,101},{70,102},{71,103... | collective-permute-start | bytes 393224 | tf_op jit(solution)/shard_map/ppermute | solution.py:148
  28.9 0.7 %collective-permute-start.2 = (f16[64,1024]{1,0:T(8,128)(2,1)S(1)}, f16[64,1024]{1,0:T(8,128)(2,1)S(1)}, u32[]{:S(2)}, u32[]{:S(2)}) collective-permute-start(f16[64,1024]{1,0:T(8,128)(2,1)S(1)} %fusion.4), channel_id=1, source_target_pairs={{32,96},{33,97},{34,98},{35,99},{36,100},{37,101},{38,102},{39,103... | collective-permute-start | bytes 393224 | tf_op jit(solution)/shard_map/ppermute | solution.py:148
  29.5 0.0 collective-permute-done.1
  29.6 0.0 collective-permute-done
  29.6 1.4 %pad_maximum_fusion.p_ref = f32[72,17,256]{2,1,0:T(8,128)} fusion(f32[4,17,256]{2,1,0:T(8,128)S(1)} %collective-permute-done.1, f32[64,1,256]{2,1,0:T(1,128)S(1)} %broadcast_in_dim_squeeze.4, f32[64,16,256]{2,1,0:T(8,128)S(1)} %bitcast.46, f32[4,17,256]{2,1,0:T(8,128)S(1)} %collective-permute-done), kind=kLoop, calls=%fused_computation.6 | loop fusion | flops 940032 | bytes 2506752 | tf_op jit(solution)/shard_map/concatenate | solution.py:83
  31.0 6.4 %shard_map.68 = f32[64,16,256]{2,1,0:T(8,128)S(1)} custom-call(s32[2]{0:T(128)} %pad_add_fusion.bounds_ref, f32[72,17,256]{2,1,0:T(8,128)} %pad_maximum_fusion.p_ref), custom_call_target="tpu_custom_call" | custom-call | tf_op jit(solution)/shard_map/pallas_call | solution.py:87
  37.4 0.0 collective-permute-done.4
  37.4 0.0 collective-permute-done.3
  37.4 0.0 collective-permute-done.2
  37.4 0.1 add_select_fusion
  37.5 0.1 reshape.122
  37.7 0.1 conditional.3
  37.7 0.7 %collective-permute-start.7 = (bf16[64,4,256]{2,1,0:T(4,128)(2,1)S(1)}, bf16[64,4,256]{2,1,0:T(4,128)(2,1)S(1)}, u32[]{:S(2)}, u32[]{:S(2)}) collective-permute-start(bf16[64,4,256]{2,1,0:T(4,128)(2,1)S(1)} %get-tuple-element.44), channel_id=1, source_target_pairs={{96,0},{97,1},{98,2},{99,3},{100,4},{101,5},{102,6},{103,7},{104,8... | collective-permute-start | bytes 393224 | tf_op jit(solution)/shard_map/ppermute | solution.py:166
  38.4 0.7 %collective-permute-start.6 = (bf16[64,4,256]{2,1,0:T(4,128)(2,1)S(1)}, bf16[64,4,256]{2,1,0:T(4,128)(2,1)S(1)}, u32[]{:S(2)}, u32[]{:S(2)}) collective-permute-start(bf16[64,4,256]{2,1,0:T(4,128)(2,1)S(1)} %get-tuple-element.44), channel_id=1, source_target_pairs={{96,32},{97,33},{98,34},{99,35},{100,36},{101,37},{102,38},{103,39... | collective-permute-start | bytes 393224 | tf_op jit(solution)/shard_map/ppermute | solution.py:166
  39.1 1.3 %collective-permute-start.5 = (bf16[64,4,256]{2,1,0:T(4,128)(2,1)S(1)}, bf16[64,4,256]{2,1,0:T(4,128)(2,1)S(1)}, u32[]{:S(2)}, u32[]{:S(2)}) collective-permute-start(bf16[64,4,256]{2,1,0:T(4,128)(2,1)S(1)} %get-tuple-element.44), channel_id=1, source_target_pairs={{96,64},{97,65},{98,66},{99,67},{100,68},{101,69},{102,70},{103,71... | collective-permute-start | bytes 393224 | tf_op jit(solution)/shard_map/ppermute | solution.py:166
  40.4 0.0 collective-permute-done.7
  40.4 0.0 collective-permute-done.6
  40.4 8.5 %collective-permute-done.5 = bf16[64,4,256]{2,1,0:T(4,128)(2,1)S(1)} collective-permute-done((bf16[64,4,256]{2,1,0:T(4,128)(2,1)S(1)}, bf16[64,4,256]{2,1,0:T(4,128)(2,1)S(1)}, u32[]{:S(2)}, u32[]{:S(2)}) %collective-permute-start.5) | collective-permute-done | bytes 131104 | tf_op jit(solution)/shard_map/ppermute | solution.py:166
  48.9 0.3 convolution_convert_fusion.2
  49.2 0.8 %reshape.124 = bf16[32,4,1024]{2,1,0:T(4,128)(2,1)} reshape(bf16[128,1024]{1,0:T(8,128)(2,1)S(1)} %convolution_convert_fusion.2) | data formatting | bytes 524288 | tf_op jit(solution)/shard_map/reshape | solution.py:171
  50.0 5.1 %all-to-all-start.1 = ((bf16[32,4,1024]{2,1,0:T(4,128)(2,1)}), bf16[32,4,1024]{2,1,0:T(4,128)(2,1)S(1)}, u32[]{:S(2)}, u32[]{:S(2)}) async-start(bf16[32,4,1024]{2,1,0:T(4,128)(2,1)} %reshape.124), calls=%async_computation.1 | async-start | bytes 524288 | tf_op jit(solution)/shard_map/all_to_all | solution.py:172
  55.1 0.1 copy.30
  55.2 0.1 fusion.10
  55.3 0.0 copy-start.1
  55.3 8.7 %all-to-all-done.1 = bf16[32,4,1024]{2,1,0:T(4,128)(2,1)S(1)} async-done(((bf16[32,4,1024]{2,1,0:T(4,128)(2,1)}), bf16[32,4,1024]{2,1,0:T(4,128)(2,1)S(1)}, u32[]{:S(2)}, u32[]{:S(2)}) %all-to-all-start.1) | async-done | bytes 262176 | tf_op jit(solution)/shard_map/all_to_all | solution.py:172
  64.0 0.2 fusion.3
  64.2 0.1 reshape.125
  64.3 0.7 %select_bitcast_fusion = bf16[1,64,4,256]{3,2,1,0:T(4,128)(2,1)} fusion(bf16[64,4,256]{2,1,0:T(4,128)(2,1)S(1)} %get-tuple-element.44, bf16[64,4,256]{2,1,0:T(4,128)(2,1)S(1)} %reshape.125, pred[]{:T(512)S(6)} %eq.62), kind=kLoop, calls=%fused_computation.23 | loop fusion | flops 65536 | bytes 393217 | tf_op jit(solution)/shard_map/broadcast_in_dim | solution.py:178
  (11 shorter events, 0.2 us)
Async XLA Ops:
  7.7 9.4 %copy-start.2 = (f32[1,64,256]{2,1,0:T(8,128)S(1)}, f32[1,64,256]{2,1,0:T(8,128)}, u32[]{:S(2)}) copy-start(f32[1,64,256]{2,1,0:T(8,128)} %param.12) | copy-start | bytes 196612
  7.7 9.5 %copy-start = (f32[1,64,16,256]{3,2,1,0:T(8,128)S(1)}, f32[1,64,16,256]{3,2,1,0:T(8,128)}, u32[]{:S(2)}) copy-start(f32[1,64,16,256]{3,2,1,0:T(8,128)} %param.11) | copy-start | bytes 3145732
  9.3 17.0 %all-to-all-start = ((f16[32,4,1152]{2,1,0:T(4,128)(2,1)}), f16[32,4,1152]{2,1,0:T(4,128)(2,1)S(1)}, u32[]{:S(2)}, u32[]{:S(2)}) async-start(f16[32,4,1152]{2,1,0:T(4,128)(2,1)} %copy.17), calls=%async_computation | async-start | bytes 589824 | tf_op jit(solution)/shard_map/all_to_all | solution.py:139
  17.2 12.3 %collective-permute-start.1 = (f32[4,17,256]{2,1,0:T(8,128)S(1)}, f32[4,17,256]{2,1,0:T(8,128)S(1)}, u32[]{:S(2)}, u32[]{:S(2)}) collective-permute-start(f32[4,17,256]{2,1,0:T(8,128)S(1)} %get-tuple-element.40), channel_id=1, source_target_pairs={{1,0},{2,1},{3,2},{4,3},{5,4},{6,5},{7,6},{8,7},{9,8},{10,9},{11,1... | collective-permute-start | bytes 208904 | tf_op jit(solution)/shard_map/ppermute | solution.py:82
  19.4 10.2 %collective-permute-start = (f32[4,17,256]{2,1,0:T(8,128)S(1)}, f32[4,17,256]{2,1,0:T(8,128)S(1)}, u32[]{:S(2)}, u32[]{:S(2)}) collective-permute-start(f32[4,17,256]{2,1,0:T(8,128)S(1)} %get-tuple-element.39), channel_id=1, source_target_pairs={{0,1},{1,2},{2,3},{3,4},{4,5},{5,6},{6,7},{7,8},{8,9},{9,10},{10,1... | collective-permute-start | bytes 208904 | tf_op jit(solution)/shard_map/ppermute | solution.py:81
  26.9 10.5 %collective-permute-start.4 = (f16[64,1024]{1,0:T(8,128)(2,1)S(1)}, f16[64,1024]{1,0:T(8,128)(2,1)S(1)}, u32[]{:S(2)}, u32[]{:S(2)}) collective-permute-start(f16[64,1024]{1,0:T(8,128)(2,1)S(1)} %fusion.4), channel_id=1, source_target_pairs={{0,96},{1,97},{2,98},{3,99},{4,100},{5,101},{6,102},{7,103},{8,104... | collective-permute-start | bytes 393224 | tf_op jit(solution)/shard_map/ppermute | solution.py:148
  27.6 9.9 %collective-permute-start.3 = (f16[64,1024]{1,0:T(8,128)(2,1)S(1)}, f16[64,1024]{1,0:T(8,128)(2,1)S(1)}, u32[]{:S(2)}, u32[]{:S(2)}) collective-permute-start(f16[64,1024]{1,0:T(8,128)(2,1)S(1)} %fusion.4), channel_id=1, source_target_pairs={{64,96},{65,97},{66,98},{67,99},{68,100},{69,101},{70,102},{71,103... | collective-permute-start | bytes 393224 | tf_op jit(solution)/shard_map/ppermute | solution.py:148
  28.9 8.6 %collective-permute-start.2 = (f16[64,1024]{1,0:T(8,128)(2,1)S(1)}, f16[64,1024]{1,0:T(8,128)(2,1)S(1)}, u32[]{:S(2)}, u32[]{:S(2)}) collective-permute-start(f16[64,1024]{1,0:T(8,128)(2,1)S(1)} %fusion.4), channel_id=1, source_target_pairs={{32,96},{33,97},{34,98},{35,99},{36,100},{37,101},{38,102},{39,103... | collective-permute-start | bytes 393224 | tf_op jit(solution)/shard_map/ppermute | solution.py:148
  37.7 2.7 %collective-permute-start.7 = (bf16[64,4,256]{2,1,0:T(4,128)(2,1)S(1)}, bf16[64,4,256]{2,1,0:T(4,128)(2,1)S(1)}, u32[]{:S(2)}, u32[]{:S(2)}) collective-permute-start(bf16[64,4,256]{2,1,0:T(4,128)(2,1)S(1)} %get-tuple-element.44), channel_id=1, source_target_pairs={{96,0},{97,1},{98,2},{99,3},{100,4},{101,5},{102,6},{103,7},{104,8... | collective-permute-start | bytes 393224 | tf_op jit(solution)/shard_map/ppermute | solution.py:166
  38.4 2.0 %collective-permute-start.6 = (bf16[64,4,256]{2,1,0:T(4,128)(2,1)S(1)}, bf16[64,4,256]{2,1,0:T(4,128)(2,1)S(1)}, u32[]{:S(2)}, u32[]{:S(2)}) collective-permute-start(bf16[64,4,256]{2,1,0:T(4,128)(2,1)S(1)} %get-tuple-element.44), channel_id=1, source_target_pairs={{96,32},{97,33},{98,34},{99,35},{100,36},{101,37},{102,38},{103,39... | collective-permute-start | bytes 393224 | tf_op jit(solution)/shard_map/ppermute | solution.py:166
  39.1 9.8 %collective-permute-start.5 = (bf16[64,4,256]{2,1,0:T(4,128)(2,1)S(1)}, bf16[64,4,256]{2,1,0:T(4,128)(2,1)S(1)}, u32[]{:S(2)}, u32[]{:S(2)}) collective-permute-start(bf16[64,4,256]{2,1,0:T(4,128)(2,1)S(1)} %get-tuple-element.44), channel_id=1, source_target_pairs={{96,64},{97,65},{98,66},{99,67},{100,68},{101,69},{102,70},{103,71... | collective-permute-start | bytes 393224 | tf_op jit(solution)/shard_map/ppermute | solution.py:166
  50.0 13.9 %all-to-all-start.1 = ((bf16[32,4,1024]{2,1,0:T(4,128)(2,1)}), bf16[32,4,1024]{2,1,0:T(4,128)(2,1)S(1)}, u32[]{:S(2)}, u32[]{:S(2)}) async-start(bf16[32,4,1024]{2,1,0:T(4,128)(2,1)} %reshape.124), calls=%async_computation.1 | async-start | bytes 524288 | tf_op jit(solution)/shard_map/all_to_all | solution.py:172
  55.3 9.7 %copy-start.1 = (f32[1,64,16,256]{3,2,1,0:T(8,128)}, f32[1,64,16,256]{3,2,1,0:T(8,128)S(1)}, u32[]{:S(2)}) copy-start(f32[1,64,16,256]{3,2,1,0:T(8,128)S(1)} %fusion.10) | copy-start | bytes 3145732
